TPU v7x, 128 devices: a whole 4x4x4 slice. The times are simulated.
128 devices in a mesh: tm: 64 (over x, z, y_lo, core), row: 2 (over y_hi).
Axes of the slice: x: 4, y: 4 (y_hi: 2, y_lo: 2; y = y_hi * 2 + y_lo), z: 4, core: 2. Of those that a mesh axis runs over, the one named last changes fastest.
Arguments:
- slice_ops: bfloat16 [64, 2048, 2048], P('tm', 'row'), may hold values from -6 to 6
- base_op: bfloat16 [2048, 2048], replicated, may hold values from -6 to 6
- load_table: float32 [16, 2048], replicated, may hold values from -1 to 1
- phase_idx: int32 [64, 2], P('tm'), may hold values from 0 to 15
- step_counts: int32 [64, 2], P('tm'), may hold values from 1 to 8
Outputs:
- windows: bfloat16 [64, 2048, 2048], P('tm', 'row')
All inputs are finite; a program needn't handle non-finite values.
Results may differ from a plain program's by a relative error of at most 0.012.
Values may be sent and summed in bfloat16 or wider, within the bound.
No kernel may reach another device: no remote copies, remote signals or barrier semaphores. Data moves between devices by JAX's collectives and lax.ppermute only.
A program may use at most 128 MiB of HBM per device.

v0:
```python
import math

import jax
import jax.numpy as jnp
from jax import lax
from jax.sharding import PartitionSpec as P

LEVELS = 2


def shifted(value, axis, steps):
    count = lax.axis_size(axis)
    pairs = [(source, (source + steps) % count) for source in range(count)]
    return lax.ppermute(value, axis, pairs)


def shards(slice_ops, base_op, load_table, phase_idx, step_counts):
    state_size = base_op.shape[0]
    norm_scale = 1.0 / math.sqrt(state_size)
    phase_count = load_table.shape[0]
    index_row = phase_idx[0]
    count_row = step_counts[0].astype(jnp.float32)
    one_hot = (
        index_row[:, None] == lax.broadcasted_iota(jnp.int32, (index_row.shape[0], phase_count), 1)
    ).astype(jnp.float32)
    table_rows = jnp.dot(one_hot, load_table, precision=lax.Precision.HIGHEST)
    gain_rows = jnp.exp(0.1 * count_row[:, None] * table_rows)
    right_factor = (base_op * gain_rows[0]).astype(jnp.bfloat16)
    left_factor = (slice_ops[0] * gain_rows[1]).astype(jnp.bfloat16)
    product = jnp.dot(left_factor, right_factor, preferred_element_type=jnp.float32)
    current = (product * norm_scale).astype(jnp.bfloat16)
    for depth_level in range(LEVELS):
        distance = 2**depth_level
        whole = lax.all_gather(current, "row", axis=0, tiled=True)
        earlier = shifted(whole, "tm", distance)
        combined = jnp.dot(current, earlier, preferred_element_type=jnp.float32)
        current = (combined * norm_scale).astype(jnp.bfloat16)
    return current[None]


def solution(mesh):
    return jax.shard_map(
        shards,
        mesh=mesh,
        in_specs=(P("tm", "row", None), P(), P(), P("tm", None), P("tm", None)),
        out_specs=P("tm", "row", None),
        check_vma=False,
    )
```

profile of v0, /device:TPU:96, one launch (start us, length us, event | category | flops | bytes accessed | tf_op | source)
XLA Modules:
  0.0 547.1 jit_solution(3729319134731721616)
XLA Ops:
  6.5 0.0 copy-start
  6.5 0.0 all-gather.3.cloned.1.call-start
  6.5 0.7 multiply_bitcast_fusion
  7.2 0.2 copy-done
  7.5 0.9 fusion.7
  8.4 13.8 %multiply_convert_fusion.4 = bf16[1024,2048]{1,0:T(8,128)(2,1)} fusion(bf16[2048,2048]{1,0:T(8,128)(2,1)} %param.6, f32[2048]{0:T(1024)S(1)} %bitcast.19, bf16[1,1024,2048]{2,1,0:T(8,128)(2,1)} %param.5, f32[2048]{0:T(1024)S(1)} %bitcast.18), kind=kOutput, calls=%fused_computation.6 | convolution fusion | flops 8613003264 | bytes 16793600 | tf_op jit(solution)/shard_map/dot_general | solution.py:30
  22.2 0.0 all-gather.3.cloned.1.call-update
  22.2 0.0 all-gather.5.cloned.1.call-start
  22.3 109.5 %all-gather.3.cloned.1.call-done = bf16[2048,2048]{1,0:T(8,128)(2,1)} async-done(((bf16[1024,2048]{1,0:T(8,128)(2,1)}), bf16[2048,2048]{1,0:T(8,128)(2,1)}) %all-gather.3.cloned.1.call-update) | async-done | bytes 8388624 | tf_op jit(solution)/shard_map/all_gather | solution.py:34
  131.7 0.0 collective-permute-start
  131.7 94.0 %collective-permute-done = bf16[2048,2048]{1,0:T(8,128)(2,1)S(1)} collective-permute-done((bf16[2048,2048]{1,0:T(8,128)(2,1)}, bf16[2048,2048]{1,0:T(8,128)(2,1)S(1)}, u32[]{:S(2)}, u32[]{:S(2)}) %collective-permute-start) | collective-permute-done | bytes 8388640 | tf_op jit(solution)/shard_map/ppermute | solution.py:14
  225.7 12.1 %multiply_convert_fusion.3 = bf16[1024,2048]{1,0:T(8,128)(2,1)} fusion(bf16[1024,2048]{1,0:T(8,128)(2,1)} %multiply_convert_fusion.4, bf16[2048,2048]{1,0:T(8,128)(2,1)S(1)} %collective-permute-done), kind=kOutput, calls=%fused_computation.5 | convolution fusion | flops 8594128896 | bytes 16777216 | tf_op jit(solution)/shard_map/dot_general | solution.py:36
  237.8 0.0 all-gather.5.cloned.1.call-update
  237.9 107.0 %all-gather.5.cloned.1.call-done = bf16[2048,2048]{1,0:T(8,128)(2,1)} async-done(((bf16[1024,2048]{1,0:T(8,128)(2,1)}), bf16[2048,2048]{1,0:T(8,128)(2,1)}) %all-gather.5.cloned.1.call-update) | async-done | bytes 8388624 | tf_op jit(solution)/shard_map/all_gather | solution.py:34
  344.9 0.6 collective-permute-start.1
  345.5 182.7 %collective-permute-done.1 = bf16[2048,2048]{1,0:T(8,128)(2,1)S(1)} collective-permute-done((bf16[2048,2048]{1,0:T(8,128)(2,1)}, bf16[2048,2048]{1,0:T(8,128)(2,1)S(1)}, u32[]{:S(2)}, u32[]{:S(2)}) %collective-permute-start.1) | collective-permute-done | bytes 8388640 | tf_op jit(solution)/shard_map/ppermute | solution.py:14
  528.2 12.1 %fusion.6 = bf16[1,1024,2048]{2,1,0:T(8,128)(2,1)} fusion(bf16[1024,2048]{1,0:T(8,128)(2,1)} %multiply_convert_fusion.3, bf16[2048,2048]{1,0:T(8,128)(2,1)S(1)} %collective-permute-done.1), kind=kOutput, calls=%fused_computation.10 | convolution fusion | flops 8594128896 | bytes 16777216 | tf_op jit(solution)/shard_map/dot_general | solution.py:36
  (1 shorter events, 0.0 us)
Async XLA Ops:
  6.5 0.9 copy-start
  6.5 125.2 %all-gather.3.cloned.1.call-start = ((), (), s32[]{:S(2)}) async-start(), calls=%async_computation | async-start | bytes 12582912 | tf_op jit(solution)/shard_map/all_gather | solution.py:34
  22.2 322.7 %all-gather.5.cloned.1.call-start = ((), (), s32[]{:S(2)}) async-start(), calls=%async_computation.1 | async-start | bytes 12582912 | tf_op jit(solution)/shard_map/all_gather | solution.py:34
  131.7 94.0 %collective-permute-start = (bf16[2048,2048]{1,0:T(8,128)(2,1)}, bf16[2048,2048]{1,0:T(8,128)(2,1)S(1)}, u32[]{:S(2)}, u32[]{:S(2)}) collective-permute-start(bf16[2048,2048]{1,0:T(8,128)(2,1)} %all-gather.3.cloned.1.call-done), channel_id=1, source_target_pairs={{0,2},{2,4},{4,6},{6,8},{8,10},{10,12},{12,14},{14,16},{16,18},{18... | collective-permute-start | bytes 25165832 | tf_op jit(solution)/shard_map/ppermute | solution.py:14
  344.9 183.3 %collective-permute-start.1 = (bf16[2048,2048]{1,0:T(8,128)(2,1)}, bf16[2048,2048]{1,0:T(8,128)(2,1)S(1)}, u32[]{:S(2)}, u32[]{:S(2)}) collective-permute-start(bf16[2048,2048]{1,0:T(8,128)(2,1)} %all-gather.5.cloned.1.call-done), channel_id=1, source_target_pairs={{0,4},{2,6},{4,8},{6,10},{8,12},{10,14},{12,16},{14,18},{16,20},{1... | collective-permute-start | bytes 25165832 | tf_op jit(solution)/shard_map/ppermute | solution.py:14
Sparse Core Ops, SparseCore 0:
  22.3 109.3 all-gather.2
  238.0 106.8 all-gather.4
where the time goes:
time: 552 us; the launch traced here: 547 us
  waiting for transfers between devices  493 us (89%)
  matrix products  38.9 us (7%)
  between operations  13.4 us (2%)
    ppermute x2, waiting for transfers between devices, shifted(): return lax.ppermute(value, axis, pairs)  277 us
    all_gather x2, waiting for transfers between devices, shards(): whole = lax.all_gather(current, 'row', axis=0, tiled=True)  216 us
    dot_general x2, matrix products, shards(): combined = jnp.dot(current, earlier, preferred_element_type=jnp.float32)  24.2 us
    dot_general x1, matrix products, shards(): jnp.dot(left_factor, right_factor, preferred_element_type=jnp.float32)  13.8 us
  transfers between devices with their start and end apart: 4, of which 4 were waited for; matrix products, arithmetic and copies ran while one was open for 0% of the time, Pallas kernels for 0%

commit v1 on v0

--- a/solution.py
+++ b/solution.py
@@ -8,16 +8,25 @@
 LEVELS = 2
 
 
-def shifted(value, axis, steps):
-    count = lax.axis_size(axis)
-    pairs = [(source, (source + steps) % count) for source in range(count)]
-    return lax.ppermute(value, axis, pairs)
+def moved(value, distance, row_offset):
+    tm_count = lax.axis_size("tm")
+    row_count = lax.axis_size("row")
+    pairs = []
+    for t in range(tm_count):
+        for r in range(row_count):
+            source = t * row_count + r
+            target = ((t + distance) % tm_count) * row_count + (r + row_offset) % row_count
+            pairs.append((source, target))
+    return lax.ppermute(value, ("tm", "row"), pairs)
 
 
 def shards(slice_ops, base_op, load_table, phase_idx, step_counts):
     state_size = base_op.shape[0]
     norm_scale = 1.0 / math.sqrt(state_size)
     phase_count = load_table.shape[0]
+    row_count = lax.axis_size("row")
+    half = slice_ops.shape[1]
+    row = lax.axis_index("row")
     index_row = phase_idx[0]
     count_row = step_counts[0].astype(jnp.float32)
     one_hot = (
@@ -31,10 +40,14 @@
     current = (product * norm_scale).astype(jnp.bfloat16)
     for depth_level in range(LEVELS):
         distance = 2**depth_level
-        whole = lax.all_gather(current, "row", axis=0, tiled=True)
-        earlier = shifted(whole, "tm", distance)
-        combined = jnp.dot(current, earlier, preferred_element_type=jnp.float32)
-        current = (combined * norm_scale).astype(jnp.bfloat16)
+        total = None
+        for offset in range(row_count):
+            earlier_rows = moved(current, distance, offset)
+            source_row = (row - offset) % row_count
+            columns = lax.dynamic_slice_in_dim(current, source_row * half, half, axis=1)
+            part = jnp.dot(columns, earlier_rows, preferred_element_type=jnp.float32)
+            total = part if total is None else total + part
+        current = (total * norm_scale).astype(jnp.bfloat16)
     return current[None]
 
 

time: 552 us -> 350 us (0.63)
  the two profiles are of different devices: /device:TPU:96 before, /device:TPU:6 now
where the time goes in v1:
time: 350 us
  waiting for transfers between devices  306 us (87%)
  matrix products  39.5 us (11%)
    ppermute x4, waiting for transfers between devices, moved(): return lax.ppermute(value, ('tm', 'row'), pairs)  306 us
    dot_general x4, matrix products, shards(): part = jnp.dot(columns, earlier_rows, preferred_element_type=jnp.float32)  24.7 us
    dot_general x1, matrix products, shards(): jnp.dot(left_factor, right_factor, preferred_element_type=jnp.float32)  13.8 us
  transfers between devices with their start and end apart: 4, of which 4 were waited for; matrix products, arithmetic and copies ran while one was open for 3% of the time, Pallas kernels for 0%

profile of v1, /device:TPU:6, one launch (start us, length us, event | category | flops | bytes accessed | tf_op | source)
XLA Modules:
  0.0 350.2 jit_solution(12929273822915945449)
XLA Ops:
  0.0 0.0 copy-start
  0.0 0.7 multiply_bitcast_fusion
  0.7 0.2 copy-done
  0.9 0.9 fusion.7
  1.8 13.8 %multiply_convert_fusion.4 = bf16[1024,2048]{1,0:T(8,128)(2,1)} fusion(bf16[2048,2048]{1,0:T(8,128)(2,1)} %param.6, f32[2048]{0:T(1024)S(1)} %bitcast.19, bf16[1,1024,2048]{2,1,0:T(8,128)(2,1)} %param.5, f32[2048]{0:T(1024)S(1)} %bitcast.18), kind=kOutput, calls=%fused_computation.6 | convolution fusion | flops 8613003264 | bytes 16793600 | tf_op jit(solution)/shard_map/dot_general | solution.py:39
  15.7 2.6 collective-permute-start.1
  18.3 0.5 collective-permute-start
  18.8 94.3 %collective-permute-done.1 = bf16[1024,2048]{1,0:T(8,128)(2,1)} collective-permute-done((bf16[1024,2048]{1,0:T(8,128)(2,1)}, bf16[1024,2048]{1,0:T(8,128)(2,1)}, u32[]{:S(2)}, u32[]{:S(2)}) %collective-permute-start.1) | collective-permute-done | bytes 4194336 | tf_op jit(solution)/shard_map/ppermute | solution.py:20
  113.1 6.9 %fusion.11 = f32[1024,2048]{1,0:T(8,128)S(1)} fusion(bf16[1024,2048]{1,0:T(8,128)(2,1)} %collective-permute-done.1, bf16[1024,2048]{1,0:T(8,128)(2,1)} %multiply_convert_fusion.4, s32[]{:T(128)S(6)} %select_n.26), kind=kOutput, calls=%fused_computation.16 | convolution fusion | flops 4294967296 | bytes 14680068 | tf_op jit(solution)/shard_map/dot_general | solution.py:48
  120.0 35.7 %collective-permute-done = bf16[1024,2048]{1,0:T(8,128)(2,1)} collective-permute-done((bf16[1024,2048]{1,0:T(8,128)(2,1)}, bf16[1024,2048]{1,0:T(8,128)(2,1)}, u32[]{:S(2)}, u32[]{:S(2)}) %collective-permute-start) | collective-permute-done | bytes 4194336 | tf_op jit(solution)/shard_map/ppermute | solution.py:20
  155.8 7.3 %multiply_convert_fusion.3 = bf16[1024,2048]{1,0:T(8,128)(2,1)S(1)} fusion(f32[1024,2048]{1,0:T(8,128)S(1)} %fusion.11, bf16[1024,2048]{1,0:T(8,128)(2,1)} %collective-permute-done, bf16[1024,2048]{1,0:T(8,128)(2,1)} %multiply_convert_fusion.4, s32[]{:T(128)S(6)} %select_n.24), kind=kOutput, calls=%fused_computation.5 | convolution fusion | flops 4301258752 | bytes 18874372 | tf_op jit(solution)/shard_map/dot_general | solution.py:48
  163.1 0.1 collective-permute-start.3
  163.2 0.3 collective-permute-start.2
  163.4 98.2 %collective-permute-done.3 = bf16[1024,2048]{1,0:T(8,128)(2,1)S(1)} collective-permute-done((bf16[1024,2048]{1,0:T(8,128)(2,1)S(1)}, bf16[1024,2048]{1,0:T(8,128)(2,1)S(1)}, u32[]{:S(2)}, u32[]{:S(2)}) %collective-permute-start.3) | collective-permute-done | bytes 4194336 | tf_op jit(solution)/shard_map/ppermute | solution.py:20
  261.6 4.5 %fusion.8 = f32[1024,2048]{1,0:T(8,128)S(1)} fusion(bf16[1024,2048]{1,0:T(8,128)(2,1)S(1)} %collective-permute-done.3, bf16[1024,2048]{1,0:T(8,128)(2,1)S(1)} %multiply_convert_fusion.3, s32[]{:T(128)S(6)} %select_n.26), kind=kOutput, calls=%fused_computation.13 | convolution fusion | flops 4294967296 | bytes 14680068 | tf_op jit(solution)/shard_map/dot_general | solution.py:48
  266.1 78.1 %collective-permute-done.2 = bf16[1024,2048]{1,0:T(8,128)(2,1)S(1)} collective-permute-done((bf16[1024,2048]{1,0:T(8,128)(2,1)S(1)}, bf16[1024,2048]{1,0:T(8,128)(2,1)S(1)}, u32[]{:S(2)}, u32[]{:S(2)}) %collective-permute-start.2) | collective-permute-done | bytes 4194336 | tf_op jit(solution)/shard_map/ppermute | solution.py:20
  344.1 6.0 %fusion.3 = bf16[1,1024,2048]{2,1,0:T(8,128)(2,1)} fusion(f32[1024,2048]{1,0:T(8,128)S(1)} %fusion.8, bf16[1024,2048]{1,0:T(8,128)(2,1)S(1)} %collective-permute-done.2, bf16[1024,2048]{1,0:T(8,128)(2,1)S(1)} %multiply_convert_fusion.3, s32[]{:T(128)S(6)} %select_n.24), kind=kOutput, calls=%fused_computation.8 | convolution fusion | flops 4301258752 | bytes 18874372 | tf_op jit(solution)/shard_map/dot_general | solution.py:48
  (1 shorter events, 0.0 us)
Async XLA Ops:
  0.0 0.9 copy-start
  15.7 97.5 %collective-permute-start.1 = (bf16[1024,2048]{1,0:T(8,128)(2,1)}, bf16[1024,2048]{1,0:T(8,128)(2,1)}, u32[]{:S(2)}, u32[]{:S(2)}) collective-permute-start(bf16[1024,2048]{1,0:T(8,128)(2,1)} %multiply_convert_fusion.4), channel_id=1, source_target_pairs={{0,3},{1,2},{2,5},{3,4},{4,7},{5,6},{6,9},{7,8},{8,11},{9,10},{10,... | collective-permute-start | bytes 12582920 | tf_op jit(solution)/shard_map/ppermute | solution.py:20
  18.3 137.5 %collective-permute-start = (bf16[1024,2048]{1,0:T(8,128)(2,1)}, bf16[1024,2048]{1,0:T(8,128)(2,1)}, u32[]{:S(2)}, u32[]{:S(2)}) collective-permute-start(bf16[1024,2048]{1,0:T(8,128)(2,1)} %multiply_convert_fusion.4), channel_id=1, source_target_pairs={{0,2},{1,3},{2,4},{3,5},{4,6},{5,7},{6,8},{7,9},{8,10},{9,11},{10,... | collective-permute-start | bytes 12582920 | tf_op jit(solution)/shard_map/ppermute | solution.py:20
  163.1 98.5 %collective-permute-start.3 = (bf16[1024,2048]{1,0:T(8,128)(2,1)S(1)}, bf16[1024,2048]{1,0:T(8,128)(2,1)S(1)}, u32[]{:S(2)}, u32[]{:S(2)}) collective-permute-start(bf16[1024,2048]{1,0:T(8,128)(2,1)S(1)} %multiply_convert_fusion.3), channel_id=1, source_target_pairs={{0,5},{1,4},{2,7},{3,6},{4,9},{5,8},{6,11},{7,10},{8,13},{9,12},{1... | collective-permute-start | bytes 12582920 | tf_op jit(solution)/shard_map/ppermute | solution.py:20
  163.2 181.0 %collective-permute-start.2 = (bf16[1024,2048]{1,0:T(8,128)(2,1)S(1)}, bf16[1024,2048]{1,0:T(8,128)(2,1)S(1)}, u32[]{:S(2)}, u32[]{:S(2)}) collective-permute-start(bf16[1024,2048]{1,0:T(8,128)(2,1)S(1)} %multiply_convert_fusion.3), channel_id=1, source_target_pairs={{0,4},{1,5},{2,6},{3,7},{4,8},{5,9},{6,10},{7,11},{8,12},{9,13},{1... | collective-permute-start | bytes 12582920 | tf_op jit(solution)/shard_map/ppermute | solution.py:20

commit v2 on v1

--- a/solution.py
+++ b/solution.py
@@ -6,18 +6,31 @@
 from jax.sharding import PartitionSpec as P
 
 LEVELS = 2
+CHUNKS = 4
 
 
-def moved(value, distance, row_offset):
+def sent(value, route):
     tm_count = lax.axis_size("tm")
     row_count = lax.axis_size("row")
     pairs = []
     for t in range(tm_count):
         for r in range(row_count):
-            source = t * row_count + r
-            target = ((t + distance) % tm_count) * row_count + (r + row_offset) % row_count
-            pairs.append((source, target))
+            target = route(t, r, tm_count, row_count)
+            if target is not None:
+                pairs.append((t * row_count + r, target[0] * row_count + target[1]))
     return lax.ppermute(value, ("tm", "row"), pairs)
+
+
+def y_low(t):
+    return (t // 2) % 2
+
+
+def direct(distance, row_offset):
+    return lambda t, r, n, m: ((t + distance) % n, (r + row_offset) % m)
+
+
+def when_low(low, route):
+    return lambda t, r, n, m: route(t, r, n, m) if y_low(t) == low else None
 
 
 def shards(slice_ops, base_op, load_table, phase_idx, step_counts):
@@ -38,16 +51,35 @@
     left_factor = (slice_ops[0] * gain_rows[1]).astype(jnp.bfloat16)
     product = jnp.dot(left_factor, right_factor, preferred_element_type=jnp.float32)
     current = (product * norm_scale).astype(jnp.bfloat16)
-    for depth_level in range(LEVELS):
-        distance = 2**depth_level
-        total = None
-        for offset in range(row_count):
-            earlier_rows = moved(current, distance, offset)
-            source_row = (row - offset) % row_count
-            columns = lax.dynamic_slice_in_dim(current, source_row * half, half, axis=1)
-            part = jnp.dot(columns, earlier_rows, preferred_element_type=jnp.float32)
-            total = part if total is None else total + part
-        current = (total * norm_scale).astype(jnp.bfloat16)
+
+    total = None
+    for offset in range(row_count):
+        earlier_rows = sent(current, direct(1, offset))
+        source_row = (row - offset) % row_count
+        columns = lax.dynamic_slice_in_dim(current, source_row * half, half, axis=1)
+        part = jnp.dot(columns, earlier_rows, preferred_element_type=jnp.float32)
+        total = part if total is None else total + part
+    current = (total * norm_scale).astype(jnp.bfloat16)
+
+    own_columns = lax.dynamic_slice_in_dim(current, row * half, half, axis=1)
+    other_columns = lax.dynamic_slice_in_dim(current, (1 - row) * half, half, axis=1)
+    rows_each = half // CHUNKS
+    total = None
+    for chunk in range(CHUNKS):
+        block = current[chunk * rows_each:(chunk + 1) * rows_each]
+        same_near = sent(block, when_low(0, direct(2, 0)))
+        other_near = sent(block, when_low(0, direct(2, 1)))
+        ring_first = sent(block, when_low(1, direct(4, 0)))
+        same_far = sent(ring_first, when_low(1, direct(-2, 0)))
+        y_first = sent(block, when_low(1, direct(-2, 1)))
+        other_far = sent(y_first, when_low(0, direct(4, 0)))
+        same = same_near + same_far
+        other = other_near + other_far
+        span = slice(chunk * rows_each, (chunk + 1) * rows_each)
+        part = jnp.dot(own_columns[:, span], same, preferred_element_type=jnp.float32)
+        part = part + jnp.dot(other_columns[:, span], other, preferred_element_type=jnp.float32)
+        total = part if total is None else total + part
+    current = (total * norm_scale).astype(jnp.bfloat16)
     return current[None]
 
 

time: 350 us -> 361 us (1.031)
  the two profiles are of different devices: /device:TPU:6 before, /device:TPU:96 now
where the time goes in v2:
time: 361 us; the launch traced here: 355 us
  waiting for transfers between devices  147 us (41%)
  starting transfers between devices  117 us (32%)
  matrix products  86.5 us (24%)
  local copies, waits for them, and re-layouts  3.67 us (1%)
    ppermute x26, waiting for transfers between devices, sent(): return lax.ppermute(value, ('tm', 'row'), pairs)  147 us
    ppermute x26, starting transfers between devices, sent(): return lax.ppermute(value, ('tm', 'row'), pairs)  117 us
    dot_general x4, matrix products, shards(): jnp.dot(own_columns[:, span], same, preferred_element_type=jnp.float32)  38.2 us
    dot_general x4, matrix products, shards(): jnp.dot(other_columns[:, span], other, preferred_element_type=jnp.float32)  19.3 us
    dot_general x2, matrix products, shards(): part = jnp.dot(columns, earlier_rows, preferred_element_type=jnp.float32)  14.2 us
    dot_general x1, matrix products, shards(): jnp.dot(left_factor, right_factor, preferred_element_type=jnp.float32)  13.8 us
  transfers between devices with their start and end apart: 26, of which 6 were waited for; matrix products, arithmetic and copies ran while one was open for 12% of the time, Pallas kernels for 0%

profile of v2, /device:TPU:96, one launch (start us, length us, event | category | flops | bytes accessed | tf_op | source)
XLA Modules:
  0.0 355.2 jit_solution(6541925153300510113)
XLA Ops:
  0.0 0.7 multiply_bitcast_fusion
  0.7 0.2 copy-done
  0.9 0.9 fusion.7
  1.8 13.8 %multiply_convert_fusion.4 = bf16[1024,2048]{1,0:T(8,128)(2,1)} fusion(bf16[2048,2048]{1,0:T(8,128)(2,1)} %param.6, f32[2048]{0:T(1024)S(1)} %bitcast.17, bf16[1,1024,2048]{2,1,0:T(8,128)(2,1)} %param.5, f32[2048]{0:T(1024)S(1)} %bitcast.16), kind=kOutput, calls=%fused_computation.6 | convolution fusion | flops 8613003264 | bytes 16793600 | tf_op jit(solution)/shard_map/dot_general | solution.py:52
  15.7 2.6 collective-permute-start.1
  18.3 0.5 collective-permute-start
  18.8 104.9 %collective-permute-done.1 = bf16[1024,2048]{1,0:T(8,128)(2,1)} collective-permute-done((bf16[1024,2048]{1,0:T(8,128)(2,1)}, bf16[1024,2048]{1,0:T(8,128)(2,1)}, u32[]{:S(2)}, u32[]{:S(2)}) %collective-permute-start.1) | collective-permute-done | bytes 4194336 | tf_op jit(solution)/shard_map/ppermute | solution.py:21
  123.7 6.9 %fusion.8 = f32[1024,2048]{1,0:T(8,128)S(1)} fusion(bf16[1024,2048]{1,0:T(8,128)(2,1)} %collective-permute-done.1, bf16[1024,2048]{1,0:T(8,128)(2,1)} %multiply_convert_fusion.4, s32[]{:T(128)S(6)} %select_n.26), kind=kOutput, calls=%fused_computation.13 | convolution fusion | flops 4294967296 | bytes 14680068 | tf_op jit(solution)/shard_map/dot_general | solution.py:60
  130.6 0.0 collective-permute-done
  130.6 7.3 %multiply_convert_fusion.3 = bf16[1024,2048]{1,0:T(8,128)(2,1)S(1)} fusion(f32[1024,2048]{1,0:T(8,128)S(1)} %fusion.8, bf16[1024,2048]{1,0:T(8,128)(2,1)} %collective-permute-done, bf16[1024,2048]{1,0:T(8,128)(2,1)} %multiply_convert_fusion.4, s32[]{:T(128)S(6)} %select_n.24), kind=kOutput, calls=%fused_computation.5 | convolution fusion | flops 4301258752 | bytes 18874372 | tf_op jit(solution)/shard_map/dot_general | solution.py:60
  138.0 0.0 copy-start.2
  138.0 2.0 copy-done.2
  140.0 1.4 fusion.47
  141.3 1.3 collective-permute-start.6
  142.6 6.8 %collective-permute-start.5 = (bf16[256,2048]{1,0:T(8,128)(2,1)S(1)}, bf16[256,2048]{1,0:T(8,128)(2,1)S(1)}, u32[]{:S(2)}, u32[]{:S(2)}) collective-permute-start(bf16[256,2048]{1,0:T(8,128)(2,1)S(1)} %get-tuple-element.5), channel_id=1, source_target_pairs={{0,5},{1,4},{2,7},{3,6},{8,13},{9,12},{10,15},{11,14},{16,21},{17,... | collective-permute-start | bytes 3145736 | tf_op jit(solution)/shard_map/ppermute | solution.py:21
  149.4 1.6 collective-permute-start.3
  151.1 25.2 %collective-permute-start.2 = (bf16[256,2048]{1,0:T(8,128)(2,1)S(1)}, bf16[256,2048]{1,0:T(8,128)(2,1)S(1)}, u32[]{:S(2)}, u32[]{:S(2)}) collective-permute-start(bf16[256,2048]{1,0:T(8,128)(2,1)S(1)} %get-tuple-element.5), channel_id=1, source_target_pairs={{0,4},{1,5},{2,6},{3,7},{8,12},{9,13},{10,14},{11,15},{16,20},{17,... | collective-permute-start | bytes 3145736 | tf_op jit(solution)/shard_map/ppermute | solution.py:21
  176.3 1.3 collective-permute-start.24
  177.6 0.0 collective-permute-done.6
  177.6 0.7 collective-permute-start.21
  178.3 0.0 collective-permute-done.5
  178.4 1.3 collective-permute-start.18
  179.7 0.0 collective-permute-done.3
  179.7 21.5 %collective-permute-start.17 = (bf16[256,2048]{1,0:T(8,128)(2,1)S(1)}, bf16[256,2048]{1,0:T(8,128)(2,1)S(1)}, u32[]{:S(2)}, u32[]{:S(2)}) collective-permute-start(bf16[256,2048]{1,0:T(8,128)(2,1)S(1)} %get-tuple-element.7), channel_id=1, source_target_pairs={{0,5},{1,4},{2,7},{3,6},{8,13},{9,12},{10,15},{11,14},{16,21},{17,... | collective-permute-start | bytes 3145736 | tf_op jit(solution)/shard_map/ppermute | solution.py:21
  201.2 0.0 collective-permute-done.2
  201.2 0.7 collective-permute-start.15
  202.0 3.5 collective-permute-done.24
  205.5 1.7 collective-permute-start.9
  207.2 0.0 collective-permute-done.21
  207.2 1.3 collective-permute-start.12
  208.5 19.5 %collective-permute-done.18 = bf16[256,2048]{1,0:T(8,128)(2,1)S(1)} collective-permute-done((bf16[256,2048]{1,0:T(8,128)(2,1)S(1)}, bf16[256,2048]{1,0:T(8,128)(2,1)S(1)}, u32[]{:S(2)}, u32[]{:S(2)}) %collective-permute-start.18) | collective-permute-done | bytes 1048608 | tf_op jit(solution)/shard_map/ppermute | solution.py:21
  228.0 1.3 collective-permute-start.4
  229.3 6.5 %collective-permute-start.8 = (bf16[256,2048]{1,0:T(8,128)(2,1)}, bf16[256,2048]{1,0:T(8,128)(2,1)}, u32[]{:S(2)}, u32[]{:S(2)}) collective-permute-start(bf16[256,2048]{1,0:T(8,128)(2,1)} %get-tuple-element.8), channel_id=1, source_target_pairs={{0,4},{1,5},{2,6},{3,7},{8,12},{9,13},{10,14},{11,15},{16,20},{17,... | collective-permute-start | bytes 3145736 | tf_op jit(solution)/shard_map/ppermute | solution.py:21
  235.8 0.0 collective-permute-done.15
  235.8 1.9 collective-permute-start.7
  237.8 0.0 collective-permute-done.9
  237.8 1.3 collective-permute-start.10
  239.1 0.0 copy-start.3
  239.2 4.6 %collective-permute-done.12 = bf16[256,2048]{1,0:T(8,128)(2,1)} collective-permute-done((bf16[256,2048]{1,0:T(8,128)(2,1)}, bf16[256,2048]{1,0:T(8,128)(2,1)}, u32[]{:S(2)}, u32[]{:S(2)}) %collective-permute-start.12) | collective-permute-done | bytes 1048608 | tf_op jit(solution)/shard_map/ppermute | solution.py:21
  243.8 19.5 %collective-permute-start.11 = (bf16[256,2048]{1,0:T(8,128)(2,1)}, bf16[256,2048]{1,0:T(8,128)(2,1)S(1)}, u32[]{:S(2)}, u32[]{:S(2)}) collective-permute-start(bf16[256,2048]{1,0:T(8,128)(2,1)} %get-tuple-element.8), channel_id=1, source_target_pairs={{0,5},{1,4},{2,7},{3,6},{8,13},{9,12},{10,15},{11,14},{16,21},{17,... | collective-permute-start | bytes 3145736 | tf_op jit(solution)/shard_map/ppermute | solution.py:21
  263.3 0.0 collective-permute-done.4
  263.3 6.7 %collective-permute-start.13 = (bf16[256,2048]{1,0:T(8,128)(2,1)}, bf16[256,2048]{1,0:T(8,128)(2,1)S(1)}, u32[]{:S(2)}, u32[]{:S(2)}) collective-permute-start(bf16[256,2048]{1,0:T(8,128)(2,1)} %collective-permute-done.12), channel_id=1, source_target_pairs={{0,8},{1,9},{2,10},{3,11},{8,16},{9,17},{10,18},{11,19},{16,24},{1... | collective-permute-start | bytes 3145736 | tf_op jit(solution)/shard_map/ppermute | solution.py:21
  270.0 6.3 %fusion.24 = f32[1024,2048]{1,0:T(8,128)} fusion(bf16[256,2048]{1,0:T(8,128)(2,1)} %copy-done.8, bf16[256,2048]{1,0:T(8,128)(2,1)} %collective-permute-done.4, bf16[1024,2048]{1,0:T(8,128)(2,1)} %copy-done.2, s32[]{:T(128)S(6)} %select_n.27), kind=kOutput, calls=%fused_computation.29 | convolution fusion | flops 1074266112 | bytes 11010052 | tf_op jit(solution)/shard_map/dot_general | solution.py:79
  276.3 0.0 collective-permute-done.8
  276.3 1.5 collective-permute-start.14
  277.7 0.0 collective-permute-done.7
  277.8 1.3 collective-permute-start.16
  279.1 5.8 %fusion.22 = f32[1024,2048]{1,0:T(8,128)} fusion(bf16[256,2048]{1,0:T(8,128)(2,1)S(1)} %copy-done.7, bf16[256,2048]{1,0:T(8,128)(2,1)} %collective-permute-done.7, bf16[1024,2048]{1,0:T(8,128)(2,1)S(1)} %copy-done.3, s32[]{:T(128)S(6)} %select_n.28), kind=kOutput, calls=%fused_computation.27 | convolution fusion | flops 1074266112 | bytes 11010052 | tf_op jit(solution)/shard_map/dot_general | solution.py:80
  284.8 0.0 collective-permute-done.10
  284.9 3.8 %collective-permute-start.19 = (bf16[256,2048]{1,0:T(8,128)(2,1)S(1)}, bf16[256,2048]{1,0:T(8,128)(2,1)S(1)}, u32[]{:S(2)}, u32[]{:S(2)}) collective-permute-start(bf16[256,2048]{1,0:T(8,128)(2,1)S(1)} %copy-done.14), channel_id=1, source_target_pairs={{0,8},{1,9},{2,10},{3,11},{8,16},{9,17},{10,18},{11,19},{16,24},{1... | collective-permute-start | bytes 3145736 | tf_op jit(solution)/shard_map/ppermute | solution.py:21
  288.7 6.1 %fusion.20 = f32[1024,2048]{1,0:T(8,128)} fusion(bf16[256,2048]{1,0:T(8,128)(2,1)} %collective-permute-done.8, bf16[256,2048]{1,0:T(8,128)(2,1)} %collective-permute-done.10, bf16[1024,2048]{1,0:T(8,128)(2,1)S(1)} %copy-done.3, s32[]{:T(128)S(6)} %add.90), kind=kOutput, calls=%fused_computation.25 | convolution fusion | flops 1074266112 | bytes 11010052 | tf_op jit(solution)/shard_map/dot_general | solution.py:79
  294.8 0.0 collective-permute-done.11
  294.8 1.9 collective-permute-start.23
  296.6 0.0 collective-permute-done.13
  296.7 1.9 collective-permute-start.25
  298.6 4.5 %fusion.18 = f32[1024,2048]{1,0:T(8,128)} fusion(bf16[256,2048]{1,0:T(8,128)(2,1)S(1)} %collective-permute-done.11, bf16[256,2048]{1,0:T(8,128)(2,1)S(1)} %collective-permute-done.13, bf16[1024,2048]{1,0:T(8,128)(2,1)S(1)} %copy-done.3, s32[]{:T(128)S(6)} %add.91), kind=kOutput, calls=%fused_computation.23 | convolution fusion | flops 1074266112 | bytes 11010052 | tf_op jit(solution)/shard_map/dot_general | solution.py:80
  303.1 1.3 collective-permute-start.20
  304.5 1.3 collective-permute-start.22
  305.8 4.5 %fusion.16 = f32[1024,2048]{1,0:T(8,128)} fusion(bf16[256,2048]{1,0:T(8,128)(2,1)S(1)} %collective-permute-done.14, bf16[256,2048]{1,0:T(8,128)(2,1)S(1)} %collective-permute-done.16, bf16[1024,2048]{1,0:T(8,128)(2,1)S(1)} %copy-done.3, s32[]{:T(128)S(6)} %add.92), kind=kOutput, calls=%fused_computation.21 | convolution fusion | flops 1074266112 | bytes 11010052 | tf_op jit(solution)/shard_map/dot_general | solution.py:79
  310.3 2.7 collective-permute-done.19
  313.0 4.5 %fusion.14 = f32[1024,2048]{1,0:T(8,128)} fusion(bf16[256,2048]{1,0:T(8,128)(2,1)S(1)} %copy-done.5, bf16[256,2048]{1,0:T(8,128)(2,1)S(1)} %collective-permute-done.19, bf16[1024,2048]{1,0:T(8,128)(2,1)S(1)} %copy-done.3, s32[]{:T(128)S(6)} %add.93), kind=kOutput, calls=%fused_computation.19 | convolution fusion | flops 1074266112 | bytes 11010052 | tf_op jit(solution)/shard_map/dot_general | solution.py:80
  317.5 11.8 %collective-permute-done.25 = bf16[256,2048]{1,0:T(8,128)(2,1)S(1)} collective-permute-done((bf16[256,2048]{1,0:T(8,128)(2,1)S(1)}, bf16[256,2048]{1,0:T(8,128)(2,1)S(1)}, u32[]{:S(2)}, u32[]{:S(2)}) %collective-permute-start.25) | collective-permute-done | bytes 1048608 | tf_op jit(solution)/shard_map/ppermute | solution.py:21
  329.3 4.5 %fusion.11 = f32[1024,2048]{1,0:T(8,128)} fusion(bf16[256,2048]{1,0:T(8,128)(2,1)S(1)} %collective-permute-done.23, bf16[256,2048]{1,0:T(8,128)(2,1)S(1)} %collective-permute-done.25, bf16[1024,2048]{1,0:T(8,128)(2,1)S(1)} %copy-done.3, s32[]{:T(128)S(6)} %add.95), kind=kOutput, calls=%fused_computation.16 | convolution fusion | flops 1074266112 | bytes 11010052 | tf_op jit(solution)/shard_map/dot_general | solution.py:80
  333.9 21.3 %fusion.6 = bf16[1,1024,2048]{2,1,0:T(8,128)(2,1)} fusion(f32[1024,2048]{1,0:T(8,128)} %fusion.11, f32[1024,2048]{1,0:T(8,128)} %fusion.16, f32[1024,2048]{1,0:T(8,128)} %fusion.14, f32[1024,2048]{1,0:T(8,128)} %fusion.20, f32[1024,2048]{1,0:T(8,128)} %fusion.18, f32[1024,2048]{1,0:T(8,128)} %fusion.24, f32[1024,2048]{1,0:T(8,128)} %fusion.22, ...), kind=kOutput, calls=%fused_computation.10 | convolution fusion | flops 1093140480 | bytes 65536004 | tf_op jit(solution)/shard_map/dot_general | solution.py:79
  (37 shorter events, 0.1 us)
Async XLA Ops:
  0.0 0.9 copy-start
  15.7 108.0 %collective-permute-start.1 = (bf16[1024,2048]{1,0:T(8,128)(2,1)}, bf16[1024,2048]{1,0:T(8,128)(2,1)}, u32[]{:S(2)}, u32[]{:S(2)}) collective-permute-start(bf16[1024,2048]{1,0:T(8,128)(2,1)} %multiply_convert_fusion.4), channel_id=1, source_target_pairs={{0,3},{1,2},{2,5},{3,4},{4,7},{5,6},{6,9},{7,8},{8,11},{9,10},{10,... | collective-permute-start | bytes 12582920 | tf_op jit(solution)/shard_map/ppermute | solution.py:21
  18.3 112.3 %collective-permute-start = (bf16[1024,2048]{1,0:T(8,128)(2,1)}, bf16[1024,2048]{1,0:T(8,128)(2,1)}, u32[]{:S(2)}, u32[]{:S(2)}) collective-permute-start(bf16[1024,2048]{1,0:T(8,128)(2,1)} %multiply_convert_fusion.4), channel_id=1, source_target_pairs={{0,2},{1,3},{2,4},{3,5},{4,6},{5,7},{6,8},{7,9},{8,10},{9,11},{10,... | collective-permute-start | bytes 12582920 | tf_op jit(solution)/shard_map/ppermute | solution.py:21
  138.0 2.0 copy-start.2
  141.3 36.3 %collective-permute-start.6 = (bf16[256,2048]{1,0:T(8,128)(2,1)S(1)}, bf16[256,2048]{1,0:T(8,128)(2,1)}, u32[]{:S(2)}, u32[]{:S(2)}) collective-permute-start(bf16[256,2048]{1,0:T(8,128)(2,1)S(1)} %get-tuple-element.5), channel_id=1, source_target_pairs={{4,1},{5,0},{6,3},{7,2},{12,9},{13,8},{14,11},{15,10},{20,17},{21,... | collective-permute-start | bytes 3145736 | tf_op jit(solution)/shard_map/ppermute | solution.py:21
  142.6 35.7 %collective-permute-start.5 = (bf16[256,2048]{1,0:T(8,128)(2,1)S(1)}, bf16[256,2048]{1,0:T(8,128)(2,1)S(1)}, u32[]{:S(2)}, u32[]{:S(2)}) collective-permute-start(bf16[256,2048]{1,0:T(8,128)(2,1)S(1)} %get-tuple-element.5), channel_id=1, source_target_pairs={{0,5},{1,4},{2,7},{3,6},{8,13},{9,12},{10,15},{11,14},{16,21},{17,... | collective-permute-start | bytes 3145736 | tf_op jit(solution)/shard_map/ppermute | solution.py:21
  149.4 30.3 %collective-permute-start.3 = (bf16[256,2048]{1,0:T(8,128)(2,1)S(1)}, bf16[256,2048]{1,0:T(8,128)(2,1)}, u32[]{:S(2)}, u32[]{:S(2)}) collective-permute-start(bf16[256,2048]{1,0:T(8,128)(2,1)S(1)} %get-tuple-element.5), channel_id=1, source_target_pairs={{4,12},{5,13},{6,14},{7,15},{12,20},{13,21},{14,22},{15,23},{20,28... | collective-permute-start | bytes 3145736 | tf_op jit(solution)/shard_map/ppermute | solution.py:21
  151.1 50.2 %collective-permute-start.2 = (bf16[256,2048]{1,0:T(8,128)(2,1)S(1)}, bf16[256,2048]{1,0:T(8,128)(2,1)S(1)}, u32[]{:S(2)}, u32[]{:S(2)}) collective-permute-start(bf16[256,2048]{1,0:T(8,128)(2,1)S(1)} %get-tuple-element.5), channel_id=1, source_target_pairs={{0,4},{1,5},{2,6},{3,7},{8,12},{9,13},{10,14},{11,15},{16,20},{17,... | collective-permute-start | bytes 3145736 | tf_op jit(solution)/shard_map/ppermute | solution.py:21
  176.3 29.2 %collective-permute-start.24 = (bf16[256,2048]{1,0:T(8,128)(2,1)S(1)}, bf16[256,2048]{1,0:T(8,128)(2,1)S(1)}, u32[]{:S(2)}, u32[]{:S(2)}) collective-permute-start(bf16[256,2048]{1,0:T(8,128)(2,1)S(1)} %get-tuple-element.6), channel_id=1, source_target_pairs={{4,1},{5,0},{6,3},{7,2},{12,9},{13,8},{14,11},{15,10},{20,17},{21,... | collective-permute-start | bytes 3145736 | tf_op jit(solution)/shard_map/ppermute | solution.py:21
  177.6 29.6 %collective-permute-start.21 = (bf16[256,2048]{1,0:T(8,128)(2,1)S(1)}, bf16[256,2048]{1,0:T(8,128)(2,1)S(1)}, u32[]{:S(2)}, u32[]{:S(2)}) collective-permute-start(bf16[256,2048]{1,0:T(8,128)(2,1)S(1)} %get-tuple-element.6), channel_id=1, source_target_pairs={{4,12},{5,13},{6,14},{7,15},{12,20},{13,21},{14,22},{15,23},{20,28... | collective-permute-start | bytes 3145736 | tf_op jit(solution)/shard_map/ppermute | solution.py:21
  178.4 1.3 copy-start.6
  178.4 49.6 %collective-permute-start.18 = (bf16[256,2048]{1,0:T(8,128)(2,1)S(1)}, bf16[256,2048]{1,0:T(8,128)(2,1)S(1)}, u32[]{:S(2)}, u32[]{:S(2)}) collective-permute-start(bf16[256,2048]{1,0:T(8,128)(2,1)S(1)} %get-tuple-element.7), channel_id=1, source_target_pairs={{4,1},{5,0},{6,3},{7,2},{12,9},{13,8},{14,11},{15,10},{20,17},{21,... | collective-permute-start | bytes 3145736 | tf_op jit(solution)/shard_map/ppermute | solution.py:21
  179.7 49.6 %collective-permute-start.17 = (bf16[256,2048]{1,0:T(8,128)(2,1)S(1)}, bf16[256,2048]{1,0:T(8,128)(2,1)S(1)}, u32[]{:S(2)}, u32[]{:S(2)}) collective-permute-start(bf16[256,2048]{1,0:T(8,128)(2,1)S(1)} %get-tuple-element.7), channel_id=1, source_target_pairs={{0,5},{1,4},{2,7},{3,6},{8,13},{9,12},{10,15},{11,14},{16,21},{17,... | collective-permute-start | bytes 3145736 | tf_op jit(solution)/shard_map/ppermute | solution.py:21
  201.2 36.5 %copy-start.8 = (bf16[256,2048]{1,0:T(8,128)(2,1)}, bf16[256,2048]{1,0:T(8,128)(2,1)S(1)}, u32[]{:S(2)}) copy-start(bf16[256,2048]{1,0:T(8,128)(2,1)S(1)} %collective-permute-done.2) | copy-start | bytes 3145732
  201.2 34.6 %collective-permute-start.15 = (bf16[256,2048]{1,0:T(8,128)(2,1)S(1)}, bf16[256,2048]{1,0:T(8,128)(2,1)S(1)}, u32[]{:S(2)}, u32[]{:S(2)}) collective-permute-start(bf16[256,2048]{1,0:T(8,128)(2,1)S(1)} %get-tuple-element.7), channel_id=1, source_target_pairs={{4,12},{5,13},{6,14},{7,15},{12,20},{13,21},{14,22},{15,23},{20,28... | collective-permute-start | bytes 3145736 | tf_op jit(solution)/shard_map/ppermute | solution.py:21
  205.5 32.3 %copy-start.11 = (bf16[256,2048]{1,0:T(8,128)(2,1)}, bf16[256,2048]{1,0:T(8,128)(2,1)S(1)}, u32[]{:S(2)}) copy-start(bf16[256,2048]{1,0:T(8,128)(2,1)S(1)} %collective-permute-done.24) | copy-start | bytes 3145732
  205.5 32.3 %collective-permute-start.9 = (bf16[256,2048]{1,0:T(8,128)(2,1)}, bf16[256,2048]{1,0:T(8,128)(2,1)}, u32[]{:S(2)}, u32[]{:S(2)}) collective-permute-start(bf16[256,2048]{1,0:T(8,128)(2,1)} %get-tuple-element.8), channel_id=1, source_target_pairs={{4,12},{5,13},{6,14},{7,15},{12,20},{13,21},{14,22},{15,23},{20,28... | collective-permute-start | bytes 3145736 | tf_op jit(solution)/shard_map/ppermute | solution.py:21
  207.2 30.6 %copy-start.9 = (bf16[256,2048]{1,0:T(8,128)(2,1)}, bf16[256,2048]{1,0:T(8,128)(2,1)S(1)}, u32[]{:S(2)}) copy-start(bf16[256,2048]{1,0:T(8,128)(2,1)S(1)} %collective-permute-done.21) | copy-start | bytes 3145732
  207.2 36.6 %collective-permute-start.12 = (bf16[256,2048]{1,0:T(8,128)(2,1)}, bf16[256,2048]{1,0:T(8,128)(2,1)}, u32[]{:S(2)}, u32[]{:S(2)}) collective-permute-start(bf16[256,2048]{1,0:T(8,128)(2,1)} %get-tuple-element.8), channel_id=1, source_target_pairs={{4,1},{5,0},{6,3},{7,2},{12,9},{13,8},{14,11},{15,10},{20,17},{21,... | collective-permute-start | bytes 3145736 | tf_op jit(solution)/shard_map/ppermute | solution.py:21
  228.0 9.8 %copy-start.13 = (bf16[256,2048]{1,0:T(8,128)(2,1)}, bf16[256,2048]{1,0:T(8,128)(2,1)S(1)}, u32[]{:S(2)}) copy-start(bf16[256,2048]{1,0:T(8,128)(2,1)S(1)} %collective-permute-done.18) | copy-start | bytes 3145732
  228.0 35.3 %collective-permute-start.4 = (bf16[256,2048]{1,0:T(8,128)(2,1)}, bf16[256,2048]{1,0:T(8,128)(2,1)}, u32[]{:S(2)}, u32[]{:S(2)}) collective-permute-start(bf16[256,2048]{1,0:T(8,128)(2,1)} %collective-permute-done.3), channel_id=1, source_target_pairs={{4,0},{5,1},{6,2},{7,3},{12,8},{13,9},{14,10},{15,11},{20,16},{21,... | collective-permute-start | bytes 3145736 | tf_op jit(solution)/shard_map/ppermute | solution.py:21
  229.3 6.6 %copy-start.4 = (bf16[256,2048]{1,0:T(8,128)(2,1)}, bf16[256,2048]{1,0:T(8,128)(2,1)S(1)}, u32[]{:S(2)}) copy-start(bf16[256,2048]{1,0:T(8,128)(2,1)S(1)} %collective-permute-done.17) | copy-start | bytes 3145732
  229.3 47.0 %collective-permute-start.8 = (bf16[256,2048]{1,0:T(8,128)(2,1)}, bf16[256,2048]{1,0:T(8,128)(2,1)}, u32[]{:S(2)}, u32[]{:S(2)}) collective-permute-start(bf16[256,2048]{1,0:T(8,128)(2,1)} %get-tuple-element.8), channel_id=1, source_target_pairs={{0,4},{1,5},{2,6},{3,7},{8,12},{9,13},{10,14},{11,15},{16,20},{17,... | collective-permute-start | bytes 3145736 | tf_op jit(solution)/shard_map/ppermute | solution.py:21
  235.8 2.0 copy-start.15
  235.8 41.9 %collective-permute-start.7 = (bf16[256,2048]{1,0:T(8,128)(2,1)}, bf16[256,2048]{1,0:T(8,128)(2,1)}, u32[]{:S(2)}, u32[]{:S(2)}) collective-permute-start(bf16[256,2048]{1,0:T(8,128)(2,1)} %collective-permute-done.6), channel_id=1, source_target_pairs={{0,8},{1,9},{2,10},{3,11},{8,16},{9,17},{10,18},{11,19},{16,24},{1... | collective-permute-start | bytes 3145736 | tf_op jit(solution)/shard_map/ppermute | solution.py:21
  237.8 47.0 %collective-permute-start.10 = (bf16[256,2048]{1,0:T(8,128)(2,1)}, bf16[256,2048]{1,0:T(8,128)(2,1)}, u32[]{:S(2)}, u32[]{:S(2)}) collective-permute-start(bf16[256,2048]{1,0:T(8,128)(2,1)} %collective-permute-done.9), channel_id=1, source_target_pairs={{4,0},{5,1},{6,2},{7,3},{12,8},{13,9},{14,10},{15,11},{20,16},{21,... | collective-permute-start | bytes 3145736 | tf_op jit(solution)/shard_map/ppermute | solution.py:21
  239.1 38.6 %copy-start.16 = (bf16[256,2048]{1,0:T(8,128)(2,1)S(1)}, bf16[256,2048]{1,0:T(8,128)(2,1)}, u32[]{:S(2)}) copy-start(bf16[256,2048]{1,0:T(8,128)(2,1)} %copy-done.15) | copy-start | bytes 3145732
  239.1 39.9 %copy-start.3 = (bf16[1024,2048]{1,0:T(8,128)(2,1)S(1)}, bf16[1024,2048]{1,0:T(8,128)(2,1)}, u32[]{:S(2)}) copy-start(bf16[1024,2048]{1,0:T(8,128)(2,1)} %copy-done.2) | copy-start | bytes 12582916
  239.1 39.9 %copy-start.7 = (bf16[256,2048]{1,0:T(8,128)(2,1)S(1)}, bf16[256,2048]{1,0:T(8,128)(2,1)}, u32[]{:S(2)}) copy-start(bf16[256,2048]{1,0:T(8,128)(2,1)} %copy-done.6) | copy-start | bytes 3145732
  239.2 45.7 %copy-start.14 = (bf16[256,2048]{1,0:T(8,128)(2,1)S(1)}, bf16[256,2048]{1,0:T(8,128)(2,1)}, u32[]{:S(2)}) copy-start(bf16[256,2048]{1,0:T(8,128)(2,1)} %copy-done.13) | copy-start | bytes 3145732
  243.8 51.0 %collective-permute-start.11 = (bf16[256,2048]{1,0:T(8,128)(2,1)}, bf16[256,2048]{1,0:T(8,128)(2,1)S(1)}, u32[]{:S(2)}, u32[]{:S(2)}) collective-permute-start(bf16[256,2048]{1,0:T(8,128)(2,1)} %get-tuple-element.8), channel_id=1, source_target_pairs={{0,5},{1,4},{2,7},{3,6},{8,13},{9,12},{10,15},{11,14},{16,21},{17,... | collective-permute-start | bytes 3145736 | tf_op jit(solution)/shard_map/ppermute | solution.py:21
  263.3 33.3 %collective-permute-start.13 = (bf16[256,2048]{1,0:T(8,128)(2,1)}, bf16[256,2048]{1,0:T(8,128)(2,1)S(1)}, u32[]{:S(2)}, u32[]{:S(2)}) collective-permute-start(bf16[256,2048]{1,0:T(8,128)(2,1)} %collective-permute-done.12), channel_id=1, source_target_pairs={{0,8},{1,9},{2,10},{3,11},{8,16},{9,17},{10,18},{11,19},{16,24},{1... | collective-permute-start | bytes 3145736 | tf_op jit(solution)/shard_map/ppermute | solution.py:21
  276.3 20.4 %copy-start.12 = (bf16[256,2048]{1,0:T(8,128)(2,1)S(1)}, bf16[256,2048]{1,0:T(8,128)(2,1)}, u32[]{:S(2)}) copy-start(bf16[256,2048]{1,0:T(8,128)(2,1)} %copy-done.11) | copy-start | bytes 3145732
  276.3 26.8 %collective-permute-start.14 = (bf16[256,2048]{1,0:T(8,128)(2,1)S(1)}, bf16[256,2048]{1,0:T(8,128)(2,1)S(1)}, u32[]{:S(2)}, u32[]{:S(2)}) collective-permute-start(bf16[256,2048]{1,0:T(8,128)(2,1)S(1)} %get-tuple-element.7), channel_id=1, source_target_pairs={{0,4},{1,5},{2,6},{3,7},{8,12},{9,13},{10,14},{11,15},{16,20},{17,... | collective-permute-start | bytes 3145736 | tf_op jit(solution)/shard_map/ppermute | solution.py:21
  277.8 26.7 %collective-permute-start.16 = (bf16[256,2048]{1,0:T(8,128)(2,1)S(1)}, bf16[256,2048]{1,0:T(8,128)(2,1)S(1)}, u32[]{:S(2)}, u32[]{:S(2)}) collective-permute-start(bf16[256,2048]{1,0:T(8,128)(2,1)S(1)} %copy-done.16), channel_id=1, source_target_pairs={{4,0},{5,1},{6,2},{7,3},{12,8},{13,9},{14,10},{15,11},{20,16},{21,... | collective-permute-start | bytes 3145736 | tf_op jit(solution)/shard_map/ppermute | solution.py:21
  284.8 19.6 %copy-start.10 = (bf16[256,2048]{1,0:T(8,128)(2,1)S(1)}, bf16[256,2048]{1,0:T(8,128)(2,1)}, u32[]{:S(2)}) copy-start(bf16[256,2048]{1,0:T(8,128)(2,1)} %copy-done.9) | copy-start | bytes 3145732
  284.9 28.1 %collective-permute-start.19 = (bf16[256,2048]{1,0:T(8,128)(2,1)S(1)}, bf16[256,2048]{1,0:T(8,128)(2,1)S(1)}, u32[]{:S(2)}, u32[]{:S(2)}) collective-permute-start(bf16[256,2048]{1,0:T(8,128)(2,1)S(1)} %copy-done.14), channel_id=1, source_target_pairs={{0,8},{1,9},{2,10},{3,11},{8,16},{9,17},{10,18},{11,19},{16,24},{1... | collective-permute-start | bytes 3145736 | tf_op jit(solution)/shard_map/ppermute | solution.py:21
  294.8 18.2 %copy-start.5 = (bf16[256,2048]{1,0:T(8,128)(2,1)S(1)}, bf16[256,2048]{1,0:T(8,128)(2,1)}, u32[]{:S(2)}) copy-start(bf16[256,2048]{1,0:T(8,128)(2,1)} %copy-done.4) | copy-start | bytes 3145732
  294.8 22.7 %collective-permute-start.23 = (bf16[256,2048]{1,0:T(8,128)(2,1)S(1)}, bf16[256,2048]{1,0:T(8,128)(2,1)S(1)}, u32[]{:S(2)}, u32[]{:S(2)}) collective-permute-start(bf16[256,2048]{1,0:T(8,128)(2,1)S(1)} %get-tuple-element.6), channel_id=1, source_target_pairs={{0,5},{1,4},{2,7},{3,6},{8,13},{9,12},{10,15},{11,14},{16,21},{17,... | collective-permute-start | bytes 3145736 | tf_op jit(solution)/shard_map/ppermute | solution.py:21
  296.7 32.7 %collective-permute-start.25 = (bf16[256,2048]{1,0:T(8,128)(2,1)S(1)}, bf16[256,2048]{1,0:T(8,128)(2,1)S(1)}, u32[]{:S(2)}, u32[]{:S(2)}) collective-permute-start(bf16[256,2048]{1,0:T(8,128)(2,1)S(1)} %copy-done.12), channel_id=1, source_target_pairs={{0,8},{1,9},{2,10},{3,11},{8,16},{9,17},{10,18},{11,19},{16,24},{1... | collective-permute-start | bytes 3145736 | tf_op jit(solution)/shard_map/ppermute | solution.py:21
  303.1 30.8 %collective-permute-start.20 = (bf16[256,2048]{1,0:T(8,128)(2,1)S(1)}, bf16[256,2048]{1,0:T(8,128)(2,1)S(1)}, u32[]{:S(2)}, u32[]{:S(2)}) collective-permute-start(bf16[256,2048]{1,0:T(8,128)(2,1)S(1)} %get-tuple-element.6), channel_id=1, source_target_pairs={{0,4},{1,5},{2,6},{3,7},{8,12},{9,13},{10,14},{11,15},{16,20},{17,... | collective-permute-start | bytes 3145736 | tf_op jit(solution)/shard_map/ppermute | solution.py:21
  304.5 29.4 %collective-permute-start.22 = (bf16[256,2048]{1,0:T(8,128)(2,1)S(1)}, bf16[256,2048]{1,0:T(8,128)(2,1)S(1)}, u32[]{:S(2)}, u32[]{:S(2)}) collective-permute-start(bf16[256,2048]{1,0:T(8,128)(2,1)S(1)} %copy-done.10), channel_id=1, source_target_pairs={{4,0},{5,1},{6,2},{7,3},{12,8},{13,9},{14,10},{15,11},{20,16},{21,... | collective-permute-start | bytes 3145736 | tf_op jit(solution)/shard_map/ppermute | solution.py:21
  333.9 21.4 %copy-start.1 = (f32[16,2048]{1,0:T(8,128)S(1)}, f32[16,2048]{1,0:T(8,128)}, u32[]{:S(2)}) copy-start(f32[16,2048]{1,0:T(8,128)} %param.7) | copy-start | bytes 393220

commit v3 on v2

--- a/solution.py
+++ b/solution.py
@@ -6,7 +6,7 @@
 from jax.sharding import PartitionSpec as P
 
 LEVELS = 2
-CHUNKS = 4
+DIRECT_ROWS = 352
 
 
 def sent(value, route):
@@ -61,24 +61,19 @@
         total = part if total is None else total + part
     current = (total * norm_scale).astype(jnp.bfloat16)
 
+    direct_rows = DIRECT_ROWS
+    same = sent(current, direct(2, 0))
+    other_near = sent(current, when_low(0, direct(2, 1)))
+    other_top = sent(current[:direct_rows], when_low(1, direct(2, 1)))
+    ring_first = sent(current[direct_rows:], when_low(1, direct(4, 0)))
+    other_bottom = sent(ring_first, when_low(1, direct(-2, 1)))
+    other_top = other_top + other_near[:direct_rows]
+    other_bottom = other_bottom + other_near[direct_rows:]
     own_columns = lax.dynamic_slice_in_dim(current, row * half, half, axis=1)
     other_columns = lax.dynamic_slice_in_dim(current, (1 - row) * half, half, axis=1)
-    rows_each = half // CHUNKS
-    total = None
-    for chunk in range(CHUNKS):
-        block = current[chunk * rows_each:(chunk + 1) * rows_each]
-        same_near = sent(block, when_low(0, direct(2, 0)))
-        other_near = sent(block, when_low(0, direct(2, 1)))
-        ring_first = sent(block, when_low(1, direct(4, 0)))
-        same_far = sent(ring_first, when_low(1, direct(-2, 0)))
-        y_first = sent(block, when_low(1, direct(-2, 1)))
-        other_far = sent(y_first, when_low(0, direct(4, 0)))
-        same = same_near + same_far
-        other = other_near + other_far
-        span = slice(chunk * rows_each, (chunk + 1) * rows_each)
-        part = jnp.dot(own_columns[:, span], same, preferred_element_type=jnp.float32)
-        part = part + jnp.dot(other_columns[:, span], other, preferred_element_type=jnp.float32)
-        total = part if total is None else total + part
+    total = jnp.dot(own_columns, same, preferred_element_type=jnp.float32)
+    total = total + jnp.dot(other_columns[:, :direct_rows], other_top, preferred_element_type=jnp.float32)
+    total = total + jnp.dot(other_columns[:, direct_rows:], other_bottom, preferred_element_type=jnp.float32)
     current = (total * norm_scale).astype(jnp.bfloat16)
     return current[None]
 

time: 361 us -> 366 us (1.014)
  the two profiles are of different devices: /device:TPU:96 before, /device:TPU:7 now
where the time goes in v3:
time: 366 us; the launch traced here: 365 us
  waiting for transfers between devices  290 us (79%)
  matrix products  56.9 us (16%)
  starting transfers between devices  13.8 us (4%)
  local copies, waits for them, and re-layouts  3.7 us (1%)
    ppermute x7, waiting for transfers between devices, sent(): return lax.ppermute(value, ('tm', 'row'), pairs)  290 us
    dot_general x2, matrix products, shards(): part = jnp.dot(columns, earlier_rows, preferred_element_type=jnp.float32)  16.2 us
    dot_general x1, matrix products, shards(): jnp.dot(left_factor, right_factor, preferred_element_type=jnp.float32)  13.8 us
    ppermute x7, starting transfers between devices, sent(): return lax.ppermute(value, ('tm', 'row'), pairs)  13.8 us
    dot_general x1, matrix products, shards(): jnp.dot(other_columns[:, direct_rows:], other_bottom, preferred_element_t...  11.4 us
    dot_general x1, matrix products, shards(): total = jnp.dot(own_columns, same, preferred_element_type=jnp.float32)  10.6 us
  transfers between devices with their start and end apart: 7, of which 2 were waited for; matrix products, arithmetic and copies ran while one was open for 7% of the time, Pallas kernels for 0%

profile of v3, /device:TPU:7, one launch (start us, length us, event | category | flops | bytes accessed | tf_op | source)
XLA Modules:
  0.0 365.2 jit_solution(999341134261318209)
XLA Ops:
  0.0 0.0 copy-start
  0.0 0.7 multiply_bitcast_fusion
  0.7 0.2 copy-done
  0.9 0.9 fusion.7
  1.8 13.8 %multiply_convert_fusion.4 = bf16[1024,2048]{1,0:T(8,128)(2,1)} fusion(bf16[2048,2048]{1,0:T(8,128)(2,1)} %param.6, f32[2048]{0:T(1024)S(1)} %bitcast.18, bf16[1,1024,2048]{2,1,0:T(8,128)(2,1)} %param.5, f32[2048]{0:T(1024)S(1)} %bitcast.17), kind=kOutput, calls=%fused_computation.6 | convolution fusion | flops 8613003264 | bytes 16793600 | tf_op jit(solution)/shard_map/dot_general | solution.py:52
  15.7 3.3 collective-permute-start.1
  19.0 0.3 collective-permute-start
  19.3 90.4 %collective-permute-done.1 = bf16[1024,2048]{1,0:T(8,128)(2,1)} collective-permute-done((bf16[1024,2048]{1,0:T(8,128)(2,1)}, bf16[1024,2048]{1,0:T(8,128)(2,1)}, u32[]{:S(2)}, u32[]{:S(2)}) %collective-permute-start.1) | collective-permute-done | bytes 4194336 | tf_op jit(solution)/shard_map/ppermute | solution.py:21
  109.7 6.9 %fusion.10 = f32[1024,2048]{1,0:T(8,128)S(1)} fusion(bf16[1024,2048]{1,0:T(8,128)(2,1)} %collective-permute-done.1, bf16[1024,2048]{1,0:T(8,128)(2,1)} %multiply_convert_fusion.4, s32[]{:T(128)S(6)} %select_n.26), kind=kOutput, calls=%fused_computation.16 | convolution fusion | flops 4294967296 | bytes 14680068 | tf_op jit(solution)/shard_map/dot_general | solution.py:60
  116.6 0.0 collective-permute-done
  116.6 9.3 %multiply_convert_fusion.3 = bf16[1024,2048]{1,0:T(8,128)(2,1)} fusion(f32[1024,2048]{1,0:T(8,128)S(1)} %fusion.10, bf16[1024,2048]{1,0:T(8,128)(2,1)} %collective-permute-done, bf16[1024,2048]{1,0:T(8,128)(2,1)} %multiply_convert_fusion.4, s32[]{:T(128)S(6)} %select_n.24), kind=kOutput, calls=%fused_computation.5 | convolution fusion | flops 4301258752 | bytes 18874372 | tf_op jit(solution)/shard_map/dot_general | solution.py:60
  125.9 5.2 %collective-permute-start.4 = (bf16[1024,2048]{1,0:T(8,128)(2,1)}, bf16[1024,2048]{1,0:T(8,128)(2,1)}, u32[]{:S(2)}, u32[]{:S(2)}) collective-permute-start(bf16[1024,2048]{1,0:T(8,128)(2,1)} %multiply_convert_fusion.3), channel_id=1, source_target_pairs={{0,5},{1,4},{2,7},{3,6},{8,13},{9,12},{10,15},{11,14},{16,21},{17,... | collective-permute-start | bytes 12582920 | tf_op jit(solution)/shard_map/ppermute | solution.py:21
  131.1 2.0 slice.36
  133.0 2.3 collective-permute-start.5
  135.3 0.0 collective-permute-start.2
  135.3 1.5 slice.34
  136.8 1.3 collective-permute-start.3
  138.1 0.0 collective-permute-done.5
  138.1 1.5 collective-permute-start.6
  139.6 199.6 %collective-permute-done.3 = bf16[352,2048]{1,0:T(8,128)(2,1)S(1)} collective-permute-done((bf16[352,2048]{1,0:T(8,128)(2,1)S(1)}, bf16[352,2048]{1,0:T(8,128)(2,1)S(1)}, u32[]{:S(2)}, u32[]{:S(2)}) %collective-permute-start.3) | collective-permute-done | bytes 1441824 | tf_op jit(solution)/shard_map/ppermute | solution.py:21
  339.2 0.0 collective-permute-done.4
  339.2 4.1 %fusion.14 = f32[1024,2048]{1,0:T(8,128)S(1)} fusion(bf16[352,2048]{1,0:T(8,128)(2,1)S(1)} %collective-permute-done.3, bf16[1024,2048]{1,0:T(8,128)(2,1)} %collective-permute-done.4, bf16[1024,2048]{1,0:T(8,128)(2,1)} %multiply_convert_fusion.3, s32[]{:T(128)S(6)} %select_n.28), kind=kOutput, calls=%fused_computation.21 | convolution fusion | flops 1477115904 | bytes 12058628 | tf_op jit(solution)/shard_map/dot_general | solution.py:75
  343.3 0.0 collective-permute-done.2
  343.3 10.6 %fusion.8 = f32[1024,2048]{1,0:T(8,128)} fusion(bf16[1024,2048]{1,0:T(8,128)(2,1)} %collective-permute-done.2, bf16[1024,2048]{1,0:T(8,128)(2,1)} %multiply_convert_fusion.3, s32[]{:T(128)S(6)} %select_n.27), kind=kOutput, calls=%fused_computation.14 | convolution fusion | flops 4294967296 | bytes 14680068 | tf_op jit(solution)/shard_map/dot_general | solution.py:74
  353.9 0.0 collective-permute-done.6
  353.9 0.0 copy-start.1
  353.9 11.4 %fusion.3 = bf16[1,1024,2048]{2,1,0:T(8,128)(2,1)} fusion(f32[1024,2048]{1,0:T(8,128)} %fusion.8, f32[1024,2048]{1,0:T(8,128)S(1)} %fusion.14, bf16[672,2048]{1,0:T(8,128)(2,1)} %collective-permute-done.6, bf16[1024,2048]{1,0:T(8,128)(2,1)} %collective-permute-done.4, bf16[1024,2048]{1,0:T(8,128)(2,1)} %multiply_convert_fusion.3, s32[]{:T(128)S(6)} %add.46), kind=kOutput, calls=%fused_computation.8 | convolution fusion | flops 2828337152 | bytes 28049412 | tf_op jit(solution)/shard_map/dot_general | solution.py:76
  365.2 0.0 copy-done.1
  (1 shorter events, 0.0 us)
Async XLA Ops:
  0.0 0.9 copy-start
  15.7 94.0 %collective-permute-start.1 = (bf16[1024,2048]{1,0:T(8,128)(2,1)}, bf16[1024,2048]{1,0:T(8,128)(2,1)}, u32[]{:S(2)}, u32[]{:S(2)}) collective-permute-start(bf16[1024,2048]{1,0:T(8,128)(2,1)} %multiply_convert_fusion.4), channel_id=1, source_target_pairs={{0,3},{1,2},{2,5},{3,4},{4,7},{5,6},{6,9},{7,8},{8,11},{9,10},{10,... | collective-permute-start | bytes 12582920 | tf_op jit(solution)/shard_map/ppermute | solution.py:21
  19.0 97.6 %collective-permute-start = (bf16[1024,2048]{1,0:T(8,128)(2,1)}, bf16[1024,2048]{1,0:T(8,128)(2,1)}, u32[]{:S(2)}, u32[]{:S(2)}) collective-permute-start(bf16[1024,2048]{1,0:T(8,128)(2,1)} %multiply_convert_fusion.4), channel_id=1, source_target_pairs={{0,2},{1,3},{2,4},{3,5},{4,6},{5,7},{6,8},{7,9},{8,10},{9,11},{10,... | collective-permute-start | bytes 12582920 | tf_op jit(solution)/shard_map/ppermute | solution.py:21
  125.9 213.3 %collective-permute-start.4 = (bf16[1024,2048]{1,0:T(8,128)(2,1)}, bf16[1024,2048]{1,0:T(8,128)(2,1)}, u32[]{:S(2)}, u32[]{:S(2)}) collective-permute-start(bf16[1024,2048]{1,0:T(8,128)(2,1)} %multiply_convert_fusion.3), channel_id=1, source_target_pairs={{0,5},{1,4},{2,7},{3,6},{8,13},{9,12},{10,15},{11,14},{16,21},{17,... | collective-permute-start | bytes 12582920 | tf_op jit(solution)/shard_map/ppermute | solution.py:21
  133.0 5.1 %collective-permute-start.5 = (bf16[672,2048]{1,0:T(8,128)(2,1)S(1)}, bf16[672,2048]{1,0:T(8,128)(2,1)}, u32[]{:S(2)}, u32[]{:S(2)}) collective-permute-start(bf16[672,2048]{1,0:T(8,128)(2,1)S(1)} %slice.36), channel_id=1, source_target_pairs={{4,12},{5,13},{6,14},{7,15},{12,20},{13,21},{14,22},{15,23},{20,28... | collective-permute-start | bytes 8257544 | tf_op jit(solution)/shard_map/ppermute | solution.py:21
  135.3 208.0 %collective-permute-start.2 = (bf16[1024,2048]{1,0:T(8,128)(2,1)}, bf16[1024,2048]{1,0:T(8,128)(2,1)}, u32[]{:S(2)}, u32[]{:S(2)}) collective-permute-start(bf16[1024,2048]{1,0:T(8,128)(2,1)} %multiply_convert_fusion.3), channel_id=1, source_target_pairs={{0,4},{1,5},{2,6},{3,7},{4,8},{5,9},{6,10},{7,11},{8,12},{9,13},{1... | collective-permute-start | bytes 12582920 | tf_op jit(solution)/shard_map/ppermute | solution.py:21
  136.8 202.4 %collective-permute-start.3 = (bf16[352,2048]{1,0:T(8,128)(2,1)S(1)}, bf16[352,2048]{1,0:T(8,128)(2,1)S(1)}, u32[]{:S(2)}, u32[]{:S(2)}) collective-permute-start(bf16[352,2048]{1,0:T(8,128)(2,1)S(1)} %slice.34), channel_id=1, source_target_pairs={{4,9},{5,8},{6,11},{7,10},{12,17},{13,16},{14,19},{15,18},{20,25},... | collective-permute-start | bytes 4325384 | tf_op jit(solution)/shard_map/ppermute | solution.py:21
  138.1 215.8 %collective-permute-start.6 = (bf16[672,2048]{1,0:T(8,128)(2,1)}, bf16[672,2048]{1,0:T(8,128)(2,1)}, u32[]{:S(2)}, u32[]{:S(2)}) collective-permute-start(bf16[672,2048]{1,0:T(8,128)(2,1)} %collective-permute-done.5), channel_id=1, source_target_pairs={{4,1},{5,0},{6,3},{7,2},{12,9},{13,8},{14,11},{15,10},{20,17},{21,... | collective-permute-start | bytes 8257544 | tf_op jit(solution)/shard_map/ppermute | solution.py:21
  353.9 11.4 %copy-start.1 = (f32[16,2048]{1,0:T(8,128)S(1)}, f32[16,2048]{1,0:T(8,128)}, u32[]{:S(2)}) copy-start(f32[16,2048]{1,0:T(8,128)} %param.7) | copy-start | bytes 393220

commit v4 on v3

--- a/solution.py
+++ b/solution.py
@@ -27,6 +27,26 @@
 
 def direct(distance, row_offset):
     return lambda t, r, n, m: ((t + distance) % n, (r + row_offset) % m)
+
+
+def ring_of(t):
+    return (t // 4) % 4
+
+
+def ring_first_hop(t, r, n, m):
+    if y_low(t) != 1:
+        return None
+    if ring_of(t) == 3:
+        return ((t - 12) % n, r)
+    return ((t + 4) % n, r)
+
+
+def ring_first_exit(t, r, n, m):
+    if y_low(t) != 1:
+        return None
+    if ring_of(t) == 0:
+        return ((t + 14) % n, 1 - r)
+    return ((t - 2) % n, 1 - r)
 
 
 def when_low(low, route):
@@ -65,8 +85,8 @@
     same = sent(current, direct(2, 0))
     other_near = sent(current, when_low(0, direct(2, 1)))
     other_top = sent(current[:direct_rows], when_low(1, direct(2, 1)))
-    ring_first = sent(current[direct_rows:], when_low(1, direct(4, 0)))
-    other_bottom = sent(ring_first, when_low(1, direct(-2, 1)))
+    ring_first = sent(current[direct_rows:], ring_first_hop)
+    other_bottom = sent(ring_first, ring_first_exit)
     other_top = other_top + other_near[:direct_rows]
     other_bottom = other_bottom + other_near[direct_rows:]
     own_columns = lax.dynamic_slice_in_dim(current, row * half, half, axis=1)

time: 366 us -> 319 us (0.87)
  the two profiles are of different devices: /device:TPU:7 before, /device:TPU:6 now
where the time goes in v4:
time: 319 us
  waiting for transfers between devices  246 us (77%)
  matrix products  56.9 us (18%)
  starting transfers between devices  11.4 us (4%)
  local copies, waits for them, and re-layouts  3.7 us (1%)
    ppermute x7, waiting for transfers between devices, sent(): return lax.ppermute(value, ('tm', 'row'), pairs)  246 us
    dot_general x2, matrix products, shards(): part = jnp.dot(columns, earlier_rows, preferred_element_type=jnp.float32)  16.2 us
    dot_general x1, matrix products, shards(): jnp.dot(left_factor, right_factor, preferred_element_type=jnp.float32)  13.8 us
    ppermute x7, starting transfers between devices, sent(): return lax.ppermute(value, ('tm', 'row'), pairs)  11.4 us
    dot_general x1, matrix products, shards(): jnp.dot(other_columns[:, direct_rows:], other_bottom, preferred_element_t...  11.4 us
    dot_general x1, matrix products, shards(): total = jnp.dot(own_columns, same, preferred_element_type=jnp.float32)  10.6 us
  transfers between devices with their start and end apart: 7, of which 3 were waited for; matrix products, arithmetic and copies ran while one was open for 8% of the time, Pallas kernels for 0%

profile of v4, /device:TPU:6, one launch (start us, length us, event | category | flops | bytes accessed | tf_op | source)
XLA Modules:
  0.0 318.5 jit_solution(4307021620938048312)
XLA Ops:
  0.0 0.0 copy-start
  0.0 0.7 multiply_bitcast_fusion
  0.7 0.2 copy-done
  0.9 0.9 fusion.7
  1.8 13.8 %multiply_convert_fusion.4 = bf16[1024,2048]{1,0:T(8,128)(2,1)} fusion(bf16[2048,2048]{1,0:T(8,128)(2,1)} %param.6, f32[2048]{0:T(1024)S(1)} %bitcast.18, bf16[1,1024,2048]{2,1,0:T(8,128)(2,1)} %param.5, f32[2048]{0:T(1024)S(1)} %bitcast.17), kind=kOutput, calls=%fused_computation.6 | convolution fusion | flops 8613003264 | bytes 16793600 | tf_op jit(solution)/shard_map/dot_general | solution.py:72
  15.7 2.6 collective-permute-start.1
  18.3 0.5 collective-permute-start
  18.8 94.3 %collective-permute-done.1 = bf16[1024,2048]{1,0:T(8,128)(2,1)} collective-permute-done((bf16[1024,2048]{1,0:T(8,128)(2,1)}, bf16[1024,2048]{1,0:T(8,128)(2,1)}, u32[]{:S(2)}, u32[]{:S(2)}) %collective-permute-start.1) | collective-permute-done | bytes 4194336 | tf_op jit(solution)/shard_map/ppermute | solution.py:21
  113.1 6.9 %fusion.10 = f32[1024,2048]{1,0:T(8,128)S(1)} fusion(bf16[1024,2048]{1,0:T(8,128)(2,1)} %collective-permute-done.1, bf16[1024,2048]{1,0:T(8,128)(2,1)} %multiply_convert_fusion.4, s32[]{:T(128)S(6)} %select_n.26), kind=kOutput, calls=%fused_computation.16 | convolution fusion | flops 4294967296 | bytes 14680068 | tf_op jit(solution)/shard_map/dot_general | solution.py:80
  120.0 35.7 %collective-permute-done = bf16[1024,2048]{1,0:T(8,128)(2,1)} collective-permute-done((bf16[1024,2048]{1,0:T(8,128)(2,1)}, bf16[1024,2048]{1,0:T(8,128)(2,1)}, u32[]{:S(2)}, u32[]{:S(2)}) %collective-permute-start) | collective-permute-done | bytes 4194336 | tf_op jit(solution)/shard_map/ppermute | solution.py:21
  155.8 9.3 %multiply_convert_fusion.3 = bf16[1024,2048]{1,0:T(8,128)(2,1)} fusion(f32[1024,2048]{1,0:T(8,128)S(1)} %fusion.10, bf16[1024,2048]{1,0:T(8,128)(2,1)} %collective-permute-done, bf16[1024,2048]{1,0:T(8,128)(2,1)} %multiply_convert_fusion.4, s32[]{:T(128)S(6)} %select_n.24), kind=kOutput, calls=%fused_computation.5 | convolution fusion | flops 4301258752 | bytes 18874372 | tf_op jit(solution)/shard_map/dot_general | solution.py:80
  165.1 3.2 %collective-permute-start.4 = (bf16[1024,2048]{1,0:T(8,128)(2,1)}, bf16[1024,2048]{1,0:T(8,128)(2,1)}, u32[]{:S(2)}, u32[]{:S(2)}) collective-permute-start(bf16[1024,2048]{1,0:T(8,128)(2,1)} %multiply_convert_fusion.3), channel_id=1, source_target_pairs={{0,5},{1,4},{2,7},{3,6},{8,13},{9,12},{10,15},{11,14},{16,21},{17,... | collective-permute-start | bytes 12582920 | tf_op jit(solution)/shard_map/ppermute | solution.py:21
  168.3 2.0 slice.36
  170.2 2.3 collective-permute-start.5
  172.5 0.0 collective-permute-start.2
  172.5 1.5 slice.34
  174.0 1.3 collective-permute-start.3
  175.3 0.0 collective-permute-done.5
  175.3 1.5 collective-permute-start.6
  176.8 115.7 %collective-permute-done.3 = bf16[352,2048]{1,0:T(8,128)(2,1)S(1)} collective-permute-done((bf16[352,2048]{1,0:T(8,128)(2,1)S(1)}, bf16[352,2048]{1,0:T(8,128)(2,1)S(1)}, u32[]{:S(2)}, u32[]{:S(2)}) %collective-permute-start.3) | collective-permute-done | bytes 1441824 | tf_op jit(solution)/shard_map/ppermute | solution.py:21
  292.5 0.0 collective-permute-done.4
  292.5 4.1 %fusion.14 = f32[1024,2048]{1,0:T(8,128)S(1)} fusion(bf16[352,2048]{1,0:T(8,128)(2,1)S(1)} %collective-permute-done.3, bf16[1024,2048]{1,0:T(8,128)(2,1)} %collective-permute-done.4, bf16[1024,2048]{1,0:T(8,128)(2,1)} %multiply_convert_fusion.3, s32[]{:T(128)S(6)} %select_n.28), kind=kOutput, calls=%fused_computation.21 | convolution fusion | flops 1477115904 | bytes 12058628 | tf_op jit(solution)/shard_map/dot_general | solution.py:95
  296.6 0.0 collective-permute-done.2
  296.6 10.6 %fusion.8 = f32[1024,2048]{1,0:T(8,128)} fusion(bf16[1024,2048]{1,0:T(8,128)(2,1)} %collective-permute-done.2, bf16[1024,2048]{1,0:T(8,128)(2,1)} %multiply_convert_fusion.3, s32[]{:T(128)S(6)} %select_n.27), kind=kOutput, calls=%fused_computation.14 | convolution fusion | flops 4294967296 | bytes 14680068 | tf_op jit(solution)/shard_map/dot_general | solution.py:94
  307.2 0.0 collective-permute-done.6
  307.2 0.0 copy-start.1
  307.2 11.4 %fusion.3 = bf16[1,1024,2048]{2,1,0:T(8,128)(2,1)} fusion(f32[1024,2048]{1,0:T(8,128)} %fusion.8, f32[1024,2048]{1,0:T(8,128)S(1)} %fusion.14, bf16[672,2048]{1,0:T(8,128)(2,1)} %collective-permute-done.6, bf16[1024,2048]{1,0:T(8,128)(2,1)} %collective-permute-done.4, bf16[1024,2048]{1,0:T(8,128)(2,1)} %multiply_convert_fusion.3, s32[]{:T(128)S(6)} %add.46), kind=kOutput, calls=%fused_computation.8 | convolution fusion | flops 2828337152 | bytes 28049412 | tf_op jit(solution)/shard_map/dot_general | solution.py:96
  318.5 0.0 copy-done.1
  (1 shorter events, 0.0 us)
Async XLA Ops:
  0.0 0.9 copy-start
  15.7 97.5 %collective-permute-start.1 = (bf16[1024,2048]{1,0:T(8,128)(2,1)}, bf16[1024,2048]{1,0:T(8,128)(2,1)}, u32[]{:S(2)}, u32[]{:S(2)}) collective-permute-start(bf16[1024,2048]{1,0:T(8,128)(2,1)} %multiply_convert_fusion.4), channel_id=1, source_target_pairs={{0,3},{1,2},{2,5},{3,4},{4,7},{5,6},{6,9},{7,8},{8,11},{9,10},{10,... | collective-permute-start | bytes 12582920 | tf_op jit(solution)/shard_map/ppermute | solution.py:21
  18.3 137.5 %collective-permute-start = (bf16[1024,2048]{1,0:T(8,128)(2,1)}, bf16[1024,2048]{1,0:T(8,128)(2,1)}, u32[]{:S(2)}, u32[]{:S(2)}) collective-permute-start(bf16[1024,2048]{1,0:T(8,128)(2,1)} %multiply_convert_fusion.4), channel_id=1, source_target_pairs={{0,2},{1,3},{2,4},{3,5},{4,6},{5,7},{6,8},{7,9},{8,10},{9,11},{10,... | collective-permute-start | bytes 12582920 | tf_op jit(solution)/shard_map/ppermute | solution.py:21
  165.1 127.5 %collective-permute-start.4 = (bf16[1024,2048]{1,0:T(8,128)(2,1)}, bf16[1024,2048]{1,0:T(8,128)(2,1)}, u32[]{:S(2)}, u32[]{:S(2)}) collective-permute-start(bf16[1024,2048]{1,0:T(8,128)(2,1)} %multiply_convert_fusion.3), channel_id=1, source_target_pairs={{0,5},{1,4},{2,7},{3,6},{8,13},{9,12},{10,15},{11,14},{16,21},{17,... | collective-permute-start | bytes 12582920 | tf_op jit(solution)/shard_map/ppermute | solution.py:21
  170.2 5.1 %collective-permute-start.5 = (bf16[672,2048]{1,0:T(8,128)(2,1)S(1)}, bf16[672,2048]{1,0:T(8,128)(2,1)}, u32[]{:S(2)}, u32[]{:S(2)}) collective-permute-start(bf16[672,2048]{1,0:T(8,128)(2,1)S(1)} %slice.36), channel_id=1, source_target_pairs={{4,12},{5,13},{6,14},{7,15},{12,20},{13,21},{14,22},{15,23},{20,28... | collective-permute-start | bytes 8257544 | tf_op jit(solution)/shard_map/ppermute | solution.py:21
  172.5 124.1 %collective-permute-start.2 = (bf16[1024,2048]{1,0:T(8,128)(2,1)}, bf16[1024,2048]{1,0:T(8,128)(2,1)}, u32[]{:S(2)}, u32[]{:S(2)}) collective-permute-start(bf16[1024,2048]{1,0:T(8,128)(2,1)} %multiply_convert_fusion.3), channel_id=1, source_target_pairs={{0,4},{1,5},{2,6},{3,7},{4,8},{5,9},{6,10},{7,11},{8,12},{9,13},{1... | collective-permute-start | bytes 12582920 | tf_op jit(solution)/shard_map/ppermute | solution.py:21
  174.0 118.5 %collective-permute-start.3 = (bf16[352,2048]{1,0:T(8,128)(2,1)S(1)}, bf16[352,2048]{1,0:T(8,128)(2,1)S(1)}, u32[]{:S(2)}, u32[]{:S(2)}) collective-permute-start(bf16[352,2048]{1,0:T(8,128)(2,1)S(1)} %slice.34), channel_id=1, source_target_pairs={{4,9},{5,8},{6,11},{7,10},{12,17},{13,16},{14,19},{15,18},{20,25},... | collective-permute-start | bytes 4325384 | tf_op jit(solution)/shard_map/ppermute | solution.py:21
  175.3 131.9 %collective-permute-start.6 = (bf16[672,2048]{1,0:T(8,128)(2,1)}, bf16[672,2048]{1,0:T(8,128)(2,1)}, u32[]{:S(2)}, u32[]{:S(2)}) collective-permute-start(bf16[672,2048]{1,0:T(8,128)(2,1)} %collective-permute-done.5), channel_id=1, source_target_pairs={{4,33},{5,32},{6,35},{7,34},{12,9},{13,8},{14,11},{15,10},{20,17},... | collective-permute-start | bytes 8257544 | tf_op jit(solution)/shard_map/ppermute | solution.py:21
  307.2 11.4 %copy-start.1 = (f32[16,2048]{1,0:T(8,128)S(1)}, f32[16,2048]{1,0:T(8,128)}, u32[]{:S(2)}) copy-start(f32[16,2048]{1,0:T(8,128)} %param.7) | copy-start | bytes 393220

commit v5 on v4

--- a/solution.py
+++ b/solution.py
@@ -72,13 +72,20 @@
     product = jnp.dot(left_factor, right_factor, preferred_element_type=jnp.float32)
     current = (product * norm_scale).astype(jnp.bfloat16)
 
-    total = None
-    for offset in range(row_count):
-        earlier_rows = sent(current, direct(1, offset))
-        source_row = (row - offset) % row_count
-        columns = lax.dynamic_slice_in_dim(current, source_row * half, half, axis=1)
-        part = jnp.dot(columns, earlier_rows, preferred_element_type=jnp.float32)
-        total = part if total is None else total + part
+    split_rows = half // 2
+    boundary = lambda t, r, n, m: ((t - 12) % n, r) if ring_of(t) == 3 and t % 4 == 3 else None
+    boundary_exit = lambda t, r, n, m: ((t + 13) % n, r) if ring_of(t) == 0 and t % 4 == 3 else None
+    not_boundary = lambda t, r, n, m: None if ring_of(t) == 3 and t % 4 == 3 else ((t + 1) % n, r)
+    same_top = sent(current[:split_rows], direct(1, 0))
+    same_bottom = sent(current[split_rows:], not_boundary)
+    wrapped = sent(current[split_rows:], boundary)
+    same_bottom = same_bottom + sent(wrapped, boundary_exit)
+    other = sent(current, direct(1, 1))
+    own_columns = lax.dynamic_slice_in_dim(current, row * half, half, axis=1)
+    other_columns = lax.dynamic_slice_in_dim(current, (1 - row) * half, half, axis=1)
+    total = jnp.dot(other_columns, other, preferred_element_type=jnp.float32)
+    total = total + jnp.dot(own_columns[:, :split_rows], same_top, preferred_element_type=jnp.float32)
+    total = total + jnp.dot(own_columns[:, split_rows:], same_bottom, preferred_element_type=jnp.float32)
     current = (total * norm_scale).astype(jnp.bfloat16)
 
     direct_rows = DIRECT_ROWS

time: 319 us -> 306 us (0.959)
  the two profiles are of different devices: /device:TPU:6 before, /device:TPU:119 now
where the time goes in v5:
time: 306 us
  waiting for transfers between devices  206 us (67%)
  matrix products  58.2 us (19%)
  starting transfers between devices  31.6 us (10%)
  local copies, waits for them, and re-layouts  8.56 us (3%)
    ppermute x10, waiting for transfers between devices, sent(): return lax.ppermute(value, ('tm', 'row'), pairs)  206 us
    ppermute x10, starting transfers between devices, sent(): return lax.ppermute(value, ('tm', 'row'), pairs)  31.6 us
    dot_general x1, matrix products, shards(): jnp.dot(left_factor, right_factor, preferred_element_type=jnp.float32)  13.8 us
    dot_general x1, matrix products, shards(): jnp.dot(other_columns[:, direct_rows:], other_bottom, preferred_element_t...  11.4 us
    dot_general x1, matrix products, shards(): total = jnp.dot(own_columns, same, preferred_element_type=jnp.float32)  10.5 us
    dot_general x1, matrix products, shards(): total = jnp.dot(other_columns, other, preferred_element_type=jnp.float32)  6.92 us
    dot_general x1, matrix products, shards(): jnp.dot(own_columns[:, split_rows:], same_bottom, preferred_element_type=...  6.29 us
  transfers between devices with their start and end apart: 10, of which 6 were waited for; matrix products, arithmetic and copies ran while one was open for 11% of the time, Pallas kernels for 0%

profile of v5, /device:TPU:119, one launch (start us, length us, event | category | flops | bytes accessed | tf_op | source)
XLA Modules:
  0.0 305.6 jit_solution(12510534392500962752)
XLA Ops:
  0.0 0.0 copy-start
  0.0 0.7 multiply_bitcast_fusion
  0.7 0.2 copy-done
  0.9 0.9 fusion.7
  1.8 13.8 %multiply_convert_fusion.4 = bf16[1024,2048]{1,0:T(8,128)(2,1)} fusion(bf16[2048,2048]{1,0:T(8,128)(2,1)} %param.6, f32[2048]{0:T(1024)S(1)} %bitcast.18, bf16[1,1024,2048]{2,1,0:T(8,128)(2,1)} %param.5, f32[2048]{0:T(1024)S(1)} %bitcast.17), kind=kOutput, calls=%fused_computation.6 | convolution fusion | flops 8613003264 | bytes 16793600 | tf_op jit(solution)/shard_map/dot_general | solution.py:72
  15.7 0.7 collective-permute-start
  16.4 4.9 %fusion.28 = (bf16[512,2048]{1,0:T(8,128)(2,1)}, bf16[512,2048]{1,0:T(8,128)(2,1)}) fusion(bf16[1024,2048]{1,0:T(8,128)(2,1)} %multiply_convert_fusion.4), kind=kLoop, calls=%fused_computation.36 | loop fusion | bytes 8388608 | tf_op jit(solution)/shard_map/slice | solution.py:80
  21.3 2.0 collective-permute-start.3
  23.3 1.5 collective-permute-start.1
  24.8 3.1 %collective-permute-start.2 = (bf16[512,2048]{1,0:T(8,128)(2,1)}, bf16[512,2048]{1,0:T(8,128)(2,1)S(1)}, u32[]{:S(2)}, u32[]{:S(2)}) collective-permute-start(bf16[512,2048]{1,0:T(8,128)(2,1)} %get-tuple-element.5), channel_id=1, source_target_pairs={{0,2},{1,3},{2,4},{3,5},{4,6},{5,7},{6,8},{7,9},{8,10},{9,11},{10,... | collective-permute-start | bytes 6291464 | tf_op jit(solution)/shard_map/ppermute | solution.py:21
  27.9 0.0 collective-permute-done.3
  27.9 2.0 collective-permute-start.4
  29.9 40.8 %collective-permute-done.1 = bf16[512,2048]{1,0:T(8,128)(2,1)} collective-permute-done((bf16[512,2048]{1,0:T(8,128)(2,1)}, bf16[512,2048]{1,0:T(8,128)(2,1)}, u32[]{:S(2)}, u32[]{:S(2)}) %collective-permute-start.1) | collective-permute-done | bytes 2097184 | tf_op jit(solution)/shard_map/ppermute | solution.py:21
  70.7 4.3 %fusion.16 = f32[1024,2048]{1,0:T(8,128)S(1)} fusion(bf16[512,2048]{1,0:T(8,128)(2,1)} %collective-permute-done.1, bf16[1024,2048]{1,0:T(8,128)(2,1)} %multiply_convert_fusion.4, s32[]{:T(128)S(6)} %select_n.9), kind=kOutput, calls=%fused_computation.23 | convolution fusion | flops 2147483648 | bytes 11534340 | tf_op jit(solution)/shard_map/dot_general | solution.py:87
  74.9 34.7 %collective-permute-done = bf16[1024,2048]{1,0:T(8,128)(2,1)} collective-permute-done((bf16[1024,2048]{1,0:T(8,128)(2,1)}, bf16[1024,2048]{1,0:T(8,128)(2,1)}, u32[]{:S(2)}, u32[]{:S(2)}) %collective-permute-start) | collective-permute-done | bytes 4194336 | tf_op jit(solution)/shard_map/ppermute | solution.py:21
  109.6 6.9 %fusion.11 = f32[1024,2048]{1,0:T(8,128)S(1)} fusion(bf16[1024,2048]{1,0:T(8,128)(2,1)} %collective-permute-done, bf16[1024,2048]{1,0:T(8,128)(2,1)} %multiply_convert_fusion.4, s32[]{:T(128)S(6)} %select_n.8), kind=kOutput, calls=%fused_computation.17 | convolution fusion | flops 4294967296 | bytes 14680068 | tf_op jit(solution)/shard_map/dot_general | solution.py:86
  116.6 0.0 collective-permute-done.2
  116.6 0.0 collective-permute-done.4
  116.6 6.3 %multiply_convert_fusion.3 = bf16[1024,2048]{1,0:T(8,128)(2,1)} fusion(f32[1024,2048]{1,0:T(8,128)S(1)} %fusion.11, f32[1024,2048]{1,0:T(8,128)S(1)} %fusion.16, bf16[512,2048]{1,0:T(8,128)(2,1)S(1)} %collective-permute-done.2, bf16[512,2048]{1,0:T(8,128)(2,1)} %collective-permute-done.4, bf16[1024,2048]{1,0:T(8,128)(2,1)} %multiply_convert_fusion.4, ...), kind=kOutput, calls=%fused_computation.5 | convolution fusion | flops 2156920832 | bytes 26214404 | tf_op jit(solution)/shard_map/dot_general | solution.py:88
  122.9 12.7 %collective-permute-start.7 = (bf16[1024,2048]{1,0:T(8,128)(2,1)}, bf16[1024,2048]{1,0:T(8,128)(2,1)}, u32[]{:S(2)}, u32[]{:S(2)}) collective-permute-start(bf16[1024,2048]{1,0:T(8,128)(2,1)} %multiply_convert_fusion.3), channel_id=1, source_target_pairs={{0,5},{1,4},{2,7},{3,6},{8,13},{9,12},{10,15},{11,14},{16,21},{17,... | collective-permute-start | bytes 12582920 | tf_op jit(solution)/shard_map/ppermute | solution.py:21
  135.6 2.0 slice.55
  137.6 2.3 collective-permute-start.8
  139.8 4.5 %collective-permute-start.5 = (bf16[1024,2048]{1,0:T(8,128)(2,1)}, bf16[1024,2048]{1,0:T(8,128)(2,1)}, u32[]{:S(2)}, u32[]{:S(2)}) collective-permute-start(bf16[1024,2048]{1,0:T(8,128)(2,1)} %multiply_convert_fusion.3), channel_id=1, source_target_pairs={{0,4},{1,5},{2,6},{3,7},{4,8},{5,9},{6,10},{7,11},{8,12},{9,13},{1... | collective-permute-start | bytes 12582920 | tf_op jit(solution)/shard_map/ppermute | solution.py:21
  144.3 1.5 slice.53
  145.8 1.3 collective-permute-start.6
  147.1 0.0 collective-permute-done.8
  147.1 1.5 collective-permute-start.9
  148.6 62.4 %collective-permute-done.6 = bf16[352,2048]{1,0:T(8,128)(2,1)S(1)} collective-permute-done((bf16[352,2048]{1,0:T(8,128)(2,1)S(1)}, bf16[352,2048]{1,0:T(8,128)(2,1)S(1)}, u32[]{:S(2)}, u32[]{:S(2)}) %collective-permute-start.6) | collective-permute-done | bytes 1441824 | tf_op jit(solution)/shard_map/ppermute | solution.py:21
  211.0 11.6 %collective-permute-done.7 = bf16[1024,2048]{1,0:T(8,128)(2,1)} collective-permute-done((bf16[1024,2048]{1,0:T(8,128)(2,1)}, bf16[1024,2048]{1,0:T(8,128)(2,1)}, u32[]{:S(2)}, u32[]{:S(2)}) %collective-permute-start.7) | collective-permute-done | bytes 4194336 | tf_op jit(solution)/shard_map/ppermute | solution.py:21
  222.5 4.1 %fusion.14 = f32[1024,2048]{1,0:T(8,128)S(1)} fusion(bf16[352,2048]{1,0:T(8,128)(2,1)S(1)} %collective-permute-done.6, bf16[1024,2048]{1,0:T(8,128)(2,1)} %collective-permute-done.7, bf16[1024,2048]{1,0:T(8,128)(2,1)} %multiply_convert_fusion.3, s32[]{:T(128)S(6)} %select_n.8), kind=kOutput, calls=%fused_computation.21 | convolution fusion | flops 1477115904 | bytes 12058628 | tf_op jit(solution)/shard_map/dot_general | solution.py:102
  226.6 36.1 %collective-permute-done.5 = bf16[1024,2048]{1,0:T(8,128)(2,1)} collective-permute-done((bf16[1024,2048]{1,0:T(8,128)(2,1)}, bf16[1024,2048]{1,0:T(8,128)(2,1)}, u32[]{:S(2)}, u32[]{:S(2)}) %collective-permute-start.5) | collective-permute-done | bytes 4194336 | tf_op jit(solution)/shard_map/ppermute | solution.py:21
  262.7 10.5 %fusion.8 = f32[1024,2048]{1,0:T(8,128)} fusion(bf16[1024,2048]{1,0:T(8,128)(2,1)} %collective-permute-done.5, bf16[1024,2048]{1,0:T(8,128)(2,1)} %multiply_convert_fusion.3, s32[]{:T(128)S(6)} %select_n.9), kind=kOutput, calls=%fused_computation.14 | convolution fusion | flops 4294967296 | bytes 14680068 | tf_op jit(solution)/shard_map/dot_general | solution.py:101
  273.3 20.9 %collective-permute-done.9 = bf16[672,2048]{1,0:T(8,128)(2,1)} collective-permute-done((bf16[672,2048]{1,0:T(8,128)(2,1)}, bf16[672,2048]{1,0:T(8,128)(2,1)}, u32[]{:S(2)}, u32[]{:S(2)}) %collective-permute-start.9) | collective-permute-done | bytes 2752544 | tf_op jit(solution)/shard_map/ppermute | solution.py:21
  294.1 0.0 copy-start.1
  294.1 11.4 %fusion.3 = bf16[1,1024,2048]{2,1,0:T(8,128)(2,1)} fusion(f32[1024,2048]{1,0:T(8,128)} %fusion.8, f32[1024,2048]{1,0:T(8,128)S(1)} %fusion.14, bf16[672,2048]{1,0:T(8,128)(2,1)} %collective-permute-done.9, bf16[1024,2048]{1,0:T(8,128)(2,1)} %collective-permute-done.7, bf16[1024,2048]{1,0:T(8,128)(2,1)} %multiply_convert_fusion.3, s32[]{:T(128)S(6)} %add.39), kind=kOutput, calls=%fused_computation.8 | convolution fusion | flops 2828337152 | bytes 28049412 | tf_op jit(solution)/shard_map/dot_general | solution.py:103
  305.6 0.0 copy-done.1
  (1 shorter events, 0.0 us)
Async XLA Ops:
  0.0 0.9 copy-start
  15.7 94.0 %collective-permute-start = (bf16[1024,2048]{1,0:T(8,128)(2,1)}, bf16[1024,2048]{1,0:T(8,128)(2,1)}, u32[]{:S(2)}, u32[]{:S(2)}) collective-permute-start(bf16[1024,2048]{1,0:T(8,128)(2,1)} %multiply_convert_fusion.4), channel_id=1, source_target_pairs={{0,3},{1,2},{2,5},{3,4},{4,7},{5,6},{6,9},{7,8},{8,11},{9,10},{10,... | collective-permute-start | bytes 12582920 | tf_op jit(solution)/shard_map/ppermute | solution.py:21
  21.3 6.6 %collective-permute-start.3 = (bf16[512,2048]{1,0:T(8,128)(2,1)}, bf16[512,2048]{1,0:T(8,128)(2,1)}, u32[]{:S(2)}, u32[]{:S(2)}) collective-permute-start(bf16[512,2048]{1,0:T(8,128)(2,1)} %get-tuple-element.5), channel_id=1, source_target_pairs={{30,6},{31,7},{62,38},{63,39},{94,70},{95,71},{126,102},{127,103}} | collective-permute-start | bytes 6291464 | tf_op jit(solution)/shard_map/ppermute | solution.py:21
  23.3 47.4 %collective-permute-start.1 = (bf16[512,2048]{1,0:T(8,128)(2,1)}, bf16[512,2048]{1,0:T(8,128)(2,1)}, u32[]{:S(2)}, u32[]{:S(2)}) collective-permute-start(bf16[512,2048]{1,0:T(8,128)(2,1)} %get-tuple-element.6), channel_id=1, source_target_pairs={{0,2},{1,3},{2,4},{3,5},{4,6},{5,7},{6,8},{7,9},{8,10},{9,11},{10,... | collective-permute-start | bytes 6291464 | tf_op jit(solution)/shard_map/ppermute | solution.py:21
  24.8 91.8 %collective-permute-start.2 = (bf16[512,2048]{1,0:T(8,128)(2,1)}, bf16[512,2048]{1,0:T(8,128)(2,1)S(1)}, u32[]{:S(2)}, u32[]{:S(2)}) collective-permute-start(bf16[512,2048]{1,0:T(8,128)(2,1)} %get-tuple-element.5), channel_id=1, source_target_pairs={{0,2},{1,3},{2,4},{3,5},{4,6},{5,7},{6,8},{7,9},{8,10},{9,11},{10,... | collective-permute-start | bytes 6291464 | tf_op jit(solution)/shard_map/ppermute | solution.py:21
  27.9 88.7 %collective-permute-start.4 = (bf16[512,2048]{1,0:T(8,128)(2,1)}, bf16[512,2048]{1,0:T(8,128)(2,1)}, u32[]{:S(2)}, u32[]{:S(2)}) collective-permute-start(bf16[512,2048]{1,0:T(8,128)(2,1)} %collective-permute-done.3), channel_id=1, source_target_pairs={{6,32},{7,33},{38,64},{39,65},{70,96},{71,97},{102,0},{103,1}} | collective-permute-start | bytes 6291464 | tf_op jit(solution)/shard_map/ppermute | solution.py:21
  122.9 99.7 %collective-permute-start.7 = (bf16[1024,2048]{1,0:T(8,128)(2,1)}, bf16[1024,2048]{1,0:T(8,128)(2,1)}, u32[]{:S(2)}, u32[]{:S(2)}) collective-permute-start(bf16[1024,2048]{1,0:T(8,128)(2,1)} %multiply_convert_fusion.3), channel_id=1, source_target_pairs={{0,5},{1,4},{2,7},{3,6},{8,13},{9,12},{10,15},{11,14},{16,21},{17,... | collective-permute-start | bytes 12582920 | tf_op jit(solution)/shard_map/ppermute | solution.py:21
  137.6 9.6 %collective-permute-start.8 = (bf16[672,2048]{1,0:T(8,128)(2,1)S(1)}, bf16[672,2048]{1,0:T(8,128)(2,1)}, u32[]{:S(2)}, u32[]{:S(2)}) collective-permute-start(bf16[672,2048]{1,0:T(8,128)(2,1)S(1)} %slice.55), channel_id=1, source_target_pairs={{4,12},{5,13},{6,14},{7,15},{12,20},{13,21},{14,22},{15,23},{20,28... | collective-permute-start | bytes 8257544 | tf_op jit(solution)/shard_map/ppermute | solution.py:21
  139.8 122.9 %collective-permute-start.5 = (bf16[1024,2048]{1,0:T(8,128)(2,1)}, bf16[1024,2048]{1,0:T(8,128)(2,1)}, u32[]{:S(2)}, u32[]{:S(2)}) collective-permute-start(bf16[1024,2048]{1,0:T(8,128)(2,1)} %multiply_convert_fusion.3), channel_id=1, source_target_pairs={{0,4},{1,5},{2,6},{3,7},{4,8},{5,9},{6,10},{7,11},{8,12},{9,13},{1... | collective-permute-start | bytes 12582920 | tf_op jit(solution)/shard_map/ppermute | solution.py:21
  145.8 65.1 %collective-permute-start.6 = (bf16[352,2048]{1,0:T(8,128)(2,1)S(1)}, bf16[352,2048]{1,0:T(8,128)(2,1)S(1)}, u32[]{:S(2)}, u32[]{:S(2)}) collective-permute-start(bf16[352,2048]{1,0:T(8,128)(2,1)S(1)} %slice.53), channel_id=1, source_target_pairs={{4,9},{5,8},{6,11},{7,10},{12,17},{13,16},{14,19},{15,18},{20,25},... | collective-permute-start | bytes 4325384 | tf_op jit(solution)/shard_map/ppermute | solution.py:21
  147.1 147.0 %collective-permute-start.9 = (bf16[672,2048]{1,0:T(8,128)(2,1)}, bf16[672,2048]{1,0:T(8,128)(2,1)}, u32[]{:S(2)}, u32[]{:S(2)}) collective-permute-start(bf16[672,2048]{1,0:T(8,128)(2,1)} %collective-permute-done.8), channel_id=1, source_target_pairs={{4,33},{5,32},{6,35},{7,34},{12,9},{13,8},{14,11},{15,10},{20,17},... | collective-permute-start | bytes 8257544 | tf_op jit(solution)/shard_map/ppermute | solution.py:21
  294.1 11.4 %copy-start.1 = (f32[16,2048]{1,0:T(8,128)S(1)}, f32[16,2048]{1,0:T(8,128)}, u32[]{:S(2)}) copy-start(f32[16,2048]{1,0:T(8,128)} %param.7) | copy-start | bytes 393220

commit v6 on v5

--- a/solution.py
+++ b/solution.py
@@ -53,6 +53,14 @@
     return lambda t, r, n, m: route(t, r, n, m) if y_low(t) == low else None
 
 
+def combined(later, earlier, row, half, norm_scale):
+    own_columns = lax.dynamic_slice_in_dim(later, row * half, half, axis=1)
+    other_columns = lax.dynamic_slice_in_dim(later, (1 - row) * half, half, axis=1)
+    columns = jnp.concatenate([own_columns, other_columns], axis=1)
+    total = jnp.dot(columns, earlier, preferred_element_type=jnp.float32)
+    return (total * norm_scale).astype(jnp.bfloat16)
+
+
 def shards(slice_ops, base_op, load_table, phase_idx, step_counts):
     state_size = base_op.shape[0]
     norm_scale = 1.0 / math.sqrt(state_size)
@@ -81,12 +89,8 @@
     wrapped = sent(current[split_rows:], boundary)
     same_bottom = same_bottom + sent(wrapped, boundary_exit)
     other = sent(current, direct(1, 1))
-    own_columns = lax.dynamic_slice_in_dim(current, row * half, half, axis=1)
-    other_columns = lax.dynamic_slice_in_dim(current, (1 - row) * half, half, axis=1)
-    total = jnp.dot(other_columns, other, preferred_element_type=jnp.float32)
-    total = total + jnp.dot(own_columns[:, :split_rows], same_top, preferred_element_type=jnp.float32)
-    total = total + jnp.dot(own_columns[:, split_rows:], same_bottom, preferred_element_type=jnp.float32)
-    current = (total * norm_scale).astype(jnp.bfloat16)
+    earlier = jnp.concatenate([same_top, same_bottom, other], axis=0)
+    current = combined(current, earlier, row, half, norm_scale)
 
     direct_rows = DIRECT_ROWS
     same = sent(current, direct(2, 0))
@@ -96,12 +100,8 @@
     other_bottom = sent(ring_first, ring_first_exit)
     other_top = other_top + other_near[:direct_rows]
     other_bottom = other_bottom + other_near[direct_rows:]
-    own_columns = lax.dynamic_slice_in_dim(current, row * half, half, axis=1)
-    other_columns = lax.dynamic_slice_in_dim(current, (1 - row) * half, half, axis=1)
-    total = jnp.dot(own_columns, same, preferred_element_type=jnp.float32)
-    total = total + jnp.dot(other_columns[:, :direct_rows], other_top, preferred_element_type=jnp.float32)
-    total = total + jnp.dot(other_columns[:, direct_rows:], other_bottom, preferred_element_type=jnp.float32)
-    current = (total * norm_scale).astype(jnp.bfloat16)
+    earlier = jnp.concatenate([same, other_top, other_bottom], axis=0)
+    current = combined(current, earlier, row, half, norm_scale)
     return current[None]
 
 

time: 306 us -> 315 us (1.029)
  the two profiles are of different devices: /device:TPU:119 before, /device:TPU:33 now
where the time goes in v6:
time: 315 us
  waiting for transfers between devices  244 us (77%)
  matrix products  36 us (11%)
  starting transfers between devices  22.2 us (7%)
  local copies, waits for them, and re-layouts  8.42 us (3%)
  other arithmetic  3.47 us (1%)
    ppermute x10, waiting for transfers between devices, sent(): return lax.ppermute(value, ('tm', 'row'), pairs)  244 us
    ppermute x10, starting transfers between devices, sent(): return lax.ppermute(value, ('tm', 'row'), pairs)  22.2 us
    dot_general x2, matrix products, combined(): total = jnp.dot(columns, earlier, preferred_element_type=jnp.float32)  21.3 us
    dot_general x1, matrix products, shards(): jnp.dot(left_factor, right_factor, preferred_element_type=jnp.float32)  13.8 us
  transfers between devices with their start and end apart: 10, of which 3 were waited for; matrix products, arithmetic and copies ran while one was open for 2% of the time, Pallas kernels for 0%

profile of v6, /device:TPU:33, one launch (start us, length us, event | category | flops | bytes accessed | tf_op | source)
XLA Modules:
  0.0 314.7 jit_solution(4495401943996615703)
XLA Ops:
  0.0 0.0 copy-start
  0.0 0.7 multiply_bitcast_fusion
  0.7 0.2 copy-done
  0.9 0.9 fusion.33
  1.8 13.8 %multiply_convert_fusion.4 = bf16[1024,2048]{1,0:T(8,128)(2,1)} fusion(bf16[2048,2048]{1,0:T(8,128)(2,1)} %param.6, f32[2048]{0:T(1024)S(1)} %bitcast.15, bf16[1,1024,2048]{2,1,0:T(8,128)(2,1)} %param.5, f32[2048]{0:T(1024)S(1)} %bitcast.14), kind=kOutput, calls=%fused_computation.18 | convolution fusion | flops 8613003264 | bytes 16793600 | tf_op jit(solution)/shard_map/dot_general | solution.py:80
  15.7 4.8 %fusion.39 = (bf16[512,2048]{1,0:T(8,128)(2,1)}, bf16[512,2048]{1,0:T(8,128)(2,1)}) fusion(bf16[1024,2048]{1,0:T(8,128)(2,1)} %multiply_convert_fusion.4), kind=kLoop, calls=%fused_computation.43 | loop fusion | bytes 8388608 | tf_op jit(solution)/shard_map/slice | solution.py:87
  20.4 2.0 collective-permute-start.2
  22.4 3.3 %collective-permute-start.4 = (bf16[1024,2048]{1,0:T(8,128)(2,1)}, bf16[1024,2048]{1,0:T(8,128)(2,1)}, u32[]{:S(2)}, u32[]{:S(2)}) collective-permute-start(bf16[1024,2048]{1,0:T(8,128)(2,1)} %multiply_convert_fusion.4), channel_id=1, source_target_pairs={{0,3},{1,2},{2,5},{3,4},{4,7},{5,6},{6,9},{7,8},{8,11},{9,10},{10,... | collective-permute-start | bytes 12582920 | tf_op jit(solution)/shard_map/ppermute | solution.py:21
  25.7 2.2 collective-permute-start.1
  27.9 0.0 collective-permute-done.2
  27.9 2.0 collective-permute-start.3
  29.9 1.3 collective-permute-start
  31.3 2.7 constant_dynamic-slice_fusion.3
  33.9 39.8 %collective-permute-done.1 = bf16[512,2048]{1,0:T(8,128)(2,1)S(1)} collective-permute-done((bf16[512,2048]{1,0:T(8,128)(2,1)}, bf16[512,2048]{1,0:T(8,128)(2,1)S(1)}, u32[]{:S(2)}, u32[]{:S(2)}) %collective-permute-start.1) | collective-permute-done | bytes 2097184 | tf_op jit(solution)/shard_map/ppermute | solution.py:21
  73.7 0.0 collective-permute-done.3
  73.7 2.4 add.19
  76.1 40.6 %collective-permute-done = bf16[512,2048]{1,0:T(8,128)(2,1)} collective-permute-done((bf16[512,2048]{1,0:T(8,128)(2,1)}, bf16[512,2048]{1,0:T(8,128)(2,1)}, u32[]{:S(2)}, u32[]{:S(2)}) %collective-permute-start) | collective-permute-done | bytes 2097184 | tf_op jit(solution)/shard_map/ppermute | solution.py:21
  116.7 0.0 collective-permute-done.4
  116.7 10.9 %multiply_convert_fusion.3 = bf16[1024,2048]{1,0:T(8,128)(2,1)S(1)} fusion(bf16[1024,2048]{1,0:T(8,128)(2,1)} %collective-permute-done.4, bf16[512,2048]{1,0:T(8,128)(2,1)S(1)} %add.19, bf16[512,2048]{1,0:T(8,128)(2,1)} %collective-permute-done, bf16[1024,1024]{1,0:T(8,128)(2,1)S(1)} %get-tuple-element.8, bf16[1024,1024]{1,0:T(8,128)(2,1)S(1)} %get-tuple-element.7), kind=kOutput, calls=%fused_computation.17 | convolution fusion | flops 8627683328 | bytes 16777216 | tf_op jit(solution)/shard_map/dot_general | solution.py:60
  127.6 0.2 slice.39
  127.8 0.8 collective-permute-start.8
  128.6 6.6 %collective-permute-start.7 = (bf16[1024,2048]{1,0:T(8,128)(2,1)S(1)}, bf16[1024,2048]{1,0:T(8,128)(2,1)S(1)}, u32[]{:S(2)}, u32[]{:S(2)}) collective-permute-start(bf16[1024,2048]{1,0:T(8,128)(2,1)S(1)} %multiply_convert_fusion.3), channel_id=1, source_target_pairs={{0,5},{1,4},{2,7},{3,6},{8,13},{9,12},{10,15},{11,14},{16,21},{17,... | collective-permute-start | bytes 12582920 | tf_op jit(solution)/shard_map/ppermute | solution.py:21
  135.2 1.2 collective-permute-start.5
  136.5 0.0 collective-permute-done.8
  136.5 1.3 collective-permute-start.9
  137.8 0.1 slice.37
  137.9 1.5 collective-permute-start.6
  139.3 0.5 constant_dynamic-slice_fusion.1
  139.8 164.1 %collective-permute-done.6 = bf16[352,2048]{1,0:T(8,128)(2,1)S(1)} collective-permute-done((bf16[352,2048]{1,0:T(8,128)(2,1)S(1)}, bf16[352,2048]{1,0:T(8,128)(2,1)S(1)}, u32[]{:S(2)}, u32[]{:S(2)}) %collective-permute-start.6) | collective-permute-done | bytes 1441824 | tf_op jit(solution)/shard_map/ppermute | solution.py:21
  303.9 0.0 collective-permute-done.7
  303.9 0.1 slice_add_fusion.1
  304.0 0.0 collective-permute-done.9
  304.0 0.3 slice_add_fusion
  304.3 0.0 collective-permute-done.5
  304.3 0.0 copy-start.1
  304.4 10.3 %fusion.28 = bf16[1,1024,2048]{2,1,0:T(8,128)(2,1)} fusion(bf16[672,2048]{1,0:T(8,128)(2,1)S(1)} %slice_add_fusion, bf16[352,2048]{1,0:T(8,128)(2,1)S(1)} %slice_add_fusion.1, bf16[1024,2048]{1,0:T(8,128)(2,1)S(1)} %collective-permute-done.5, bf16[1024,1024]{1,0:T(8,128)(2,1)S(1)} %get-tuple-element.6, bf16[1024,1024]{1,0:T(8,128)(2,1)S(1)} %get-tuple-element.5), kind=kOutput, calls=%fused_computation.28 | convolution fusion | flops 8627683328 | bytes 16777216 | tf_op jit(solution)/shard_map/dot_general | solution.py:60
  314.7 0.0 copy-done.1
  (1 shorter events, 0.0 us)
Async XLA Ops:
  0.0 0.9 copy-start
  20.4 7.5 %collective-permute-start.2 = (bf16[512,2048]{1,0:T(8,128)(2,1)}, bf16[512,2048]{1,0:T(8,128)(2,1)}, u32[]{:S(2)}, u32[]{:S(2)}) collective-permute-start(bf16[512,2048]{1,0:T(8,128)(2,1)} %get-tuple-element.10), channel_id=1, source_target_pairs={{30,6},{31,7},{62,38},{63,39},{94,70},{95,71},{126,102},{127,103}} | collective-permute-start | bytes 6291464 | tf_op jit(solution)/shard_map/ppermute | solution.py:21
  22.4 94.2 %collective-permute-start.4 = (bf16[1024,2048]{1,0:T(8,128)(2,1)}, bf16[1024,2048]{1,0:T(8,128)(2,1)}, u32[]{:S(2)}, u32[]{:S(2)}) collective-permute-start(bf16[1024,2048]{1,0:T(8,128)(2,1)} %multiply_convert_fusion.4), channel_id=1, source_target_pairs={{0,3},{1,2},{2,5},{3,4},{4,7},{5,6},{6,9},{7,8},{8,11},{9,10},{10,... | collective-permute-start | bytes 12582920 | tf_op jit(solution)/shard_map/ppermute | solution.py:21
  25.7 48.0 %collective-permute-start.1 = (bf16[512,2048]{1,0:T(8,128)(2,1)}, bf16[512,2048]{1,0:T(8,128)(2,1)S(1)}, u32[]{:S(2)}, u32[]{:S(2)}) collective-permute-start(bf16[512,2048]{1,0:T(8,128)(2,1)} %get-tuple-element.10), channel_id=1, source_target_pairs={{0,2},{1,3},{2,4},{3,5},{4,6},{5,7},{6,8},{7,9},{8,10},{9,11},{10,... | collective-permute-start | bytes 6291464 | tf_op jit(solution)/shard_map/ppermute | solution.py:21
  27.9 45.8 %collective-permute-start.3 = (bf16[512,2048]{1,0:T(8,128)(2,1)}, bf16[512,2048]{1,0:T(8,128)(2,1)}, u32[]{:S(2)}, u32[]{:S(2)}) collective-permute-start(bf16[512,2048]{1,0:T(8,128)(2,1)} %collective-permute-done.2), channel_id=1, source_target_pairs={{6,32},{7,33},{38,64},{39,65},{70,96},{71,97},{102,0},{103,1}} | collective-permute-start | bytes 6291464 | tf_op jit(solution)/shard_map/ppermute | solution.py:21
  29.9 86.7 %collective-permute-start = (bf16[512,2048]{1,0:T(8,128)(2,1)}, bf16[512,2048]{1,0:T(8,128)(2,1)}, u32[]{:S(2)}, u32[]{:S(2)}) collective-permute-start(bf16[512,2048]{1,0:T(8,128)(2,1)} %get-tuple-element.9), channel_id=1, source_target_pairs={{0,2},{1,3},{2,4},{3,5},{4,6},{5,7},{6,8},{7,9},{8,10},{9,11},{10,... | collective-permute-start | bytes 6291464 | tf_op jit(solution)/shard_map/ppermute | solution.py:21
  127.8 8.7 %collective-permute-start.8 = (bf16[672,2048]{1,0:T(8,128)(2,1)S(1)}, bf16[672,2048]{1,0:T(8,128)(2,1)S(1)}, u32[]{:S(2)}, u32[]{:S(2)}) collective-permute-start(bf16[672,2048]{1,0:T(8,128)(2,1)S(1)} %slice.39), channel_id=1, source_target_pairs={{4,12},{5,13},{6,14},{7,15},{12,20},{13,21},{14,22},{15,23},{20,28... | collective-permute-start | bytes 8257544 | tf_op jit(solution)/shard_map/ppermute | solution.py:21
  128.6 175.2 %collective-permute-start.7 = (bf16[1024,2048]{1,0:T(8,128)(2,1)S(1)}, bf16[1024,2048]{1,0:T(8,128)(2,1)S(1)}, u32[]{:S(2)}, u32[]{:S(2)}) collective-permute-start(bf16[1024,2048]{1,0:T(8,128)(2,1)S(1)} %multiply_convert_fusion.3), channel_id=1, source_target_pairs={{0,5},{1,4},{2,7},{3,6},{8,13},{9,12},{10,15},{11,14},{16,21},{17,... | collective-permute-start | bytes 12582920 | tf_op jit(solution)/shard_map/ppermute | solution.py:21
  135.2 169.1 %collective-permute-start.5 = (bf16[1024,2048]{1,0:T(8,128)(2,1)S(1)}, bf16[1024,2048]{1,0:T(8,128)(2,1)S(1)}, u32[]{:S(2)}, u32[]{:S(2)}) collective-permute-start(bf16[1024,2048]{1,0:T(8,128)(2,1)S(1)} %multiply_convert_fusion.3), channel_id=1, source_target_pairs={{0,4},{1,5},{2,6},{3,7},{4,8},{5,9},{6,10},{7,11},{8,12},{9,13},{1... | collective-permute-start | bytes 12582920 | tf_op jit(solution)/shard_map/ppermute | solution.py:21
  136.5 167.6 %collective-permute-start.9 = (bf16[672,2048]{1,0:T(8,128)(2,1)S(1)}, bf16[672,2048]{1,0:T(8,128)(2,1)S(1)}, u32[]{:S(2)}, u32[]{:S(2)}) collective-permute-start(bf16[672,2048]{1,0:T(8,128)(2,1)S(1)} %collective-permute-done.8), channel_id=1, source_target_pairs={{4,33},{5,32},{6,35},{7,34},{12,9},{13,8},{14,11},{15,10},{20,17},... | collective-permute-start | bytes 8257544 | tf_op jit(solution)/shard_map/ppermute | solution.py:21
  137.9 166.0 %collective-permute-start.6 = (bf16[352,2048]{1,0:T(8,128)(2,1)S(1)}, bf16[352,2048]{1,0:T(8,128)(2,1)S(1)}, u32[]{:S(2)}, u32[]{:S(2)}) collective-permute-start(bf16[352,2048]{1,0:T(8,128)(2,1)S(1)} %slice.37), channel_id=1, source_target_pairs={{4,9},{5,8},{6,11},{7,10},{12,17},{13,16},{14,19},{15,18},{20,25},... | collective-permute-start | bytes 4325384 | tf_op jit(solution)/shard_map/ppermute | solution.py:21
  304.3 10.3 %copy-start.1 = (f32[16,2048]{1,0:T(8,128)S(1)}, f32[16,2048]{1,0:T(8,128)}, u32[]{:S(2)}) copy-start(f32[16,2048]{1,0:T(8,128)} %param.7) | copy-start | bytes 393220

commit v7 on v6

--- a/solution.py
+++ b/solution.py
@@ -6,7 +6,8 @@
 from jax.sharding import PartitionSpec as P
 
 LEVELS = 2
-DIRECT_ROWS = 352
+DIRECT_ROWS = 208
+RELAY_ROWS = (416, 400)
 
 
 def sent(value, route):
@@ -53,11 +54,13 @@
     return lambda t, r, n, m: route(t, r, n, m) if y_low(t) == low else None
 
 
-def combined(later, earlier, row, half, norm_scale):
-    own_columns = lax.dynamic_slice_in_dim(later, row * half, half, axis=1)
-    other_columns = lax.dynamic_slice_in_dim(later, (1 - row) * half, half, axis=1)
-    columns = jnp.concatenate([own_columns, other_columns], axis=1)
-    total = jnp.dot(columns, earlier, preferred_element_type=jnp.float32)
+def combined(later, own_rows, other_rows, row, norm_scale):
+    earlier = jnp.where(
+        row == 0,
+        jnp.concatenate(own_rows + other_rows, axis=0),
+        jnp.concatenate(other_rows + own_rows, axis=0),
+    )
+    total = jnp.dot(later, earlier, preferred_element_type=jnp.float32)
     return (total * norm_scale).astype(jnp.bfloat16)
 
 
@@ -89,19 +92,17 @@
     wrapped = sent(current[split_rows:], boundary)
     same_bottom = same_bottom + sent(wrapped, boundary_exit)
     other = sent(current, direct(1, 1))
-    earlier = jnp.concatenate([same_top, same_bottom, other], axis=0)
-    current = combined(current, earlier, row, half, norm_scale)
+    current = combined(current, [same_top, same_bottom], [other], row, norm_scale)
 
-    direct_rows = DIRECT_ROWS
     same = sent(current, direct(2, 0))
     other_near = sent(current, when_low(0, direct(2, 1)))
-    other_top = sent(current[:direct_rows], when_low(1, direct(2, 1)))
-    ring_first = sent(current[direct_rows:], ring_first_hop)
-    other_bottom = sent(ring_first, ring_first_exit)
-    other_top = other_top + other_near[:direct_rows]
-    other_bottom = other_bottom + other_near[direct_rows:]
-    earlier = jnp.concatenate([same, other_top, other_bottom], axis=0)
-    current = combined(current, earlier, row, half, norm_scale)
+    other_rows = [sent(current[:DIRECT_ROWS], when_low(1, direct(2, 1))) + other_near[:DIRECT_ROWS]]
+    begin = DIRECT_ROWS
+    for size in RELAY_ROWS:
+        ring_first = sent(current[begin:begin + size], ring_first_hop)
+        other_rows.append(sent(ring_first, ring_first_exit) + other_near[begin:begin + size])
+        begin += size
+    current = combined(current, [same], other_rows, row, norm_scale)
     return current[None]
 
 

time: 315 us -> 309 us (0.981)
  the two profiles are of different devices: /device:TPU:33 before, /device:TPU:81 now
where the time goes in v7:
time: 309 us
  waiting for transfers between devices  212 us (69%)
  matrix products  43.8 us (14%)
  starting transfers between devices  38.7 us (13%)
  other arithmetic  8.23 us (3%)
  local copies, waits for them, and re-layouts  5.43 us (2%)
    ppermute x12, waiting for transfers between devices, sent(): return lax.ppermute(value, ('tm', 'row'), pairs)  212 us
    ppermute x12, starting transfers between devices, sent(): return lax.ppermute(value, ('tm', 'row'), pairs)  38.7 us
    dot_general x2, matrix products, combined(): total = jnp.dot(later, earlier, preferred_element_type=jnp.float32)  29.1 us
    dot_general x1, matrix products, shards(): jnp.dot(left_factor, right_factor, preferred_element_type=jnp.float32)  13.8 us
  transfers between devices with their start and end apart: 12, of which 5 were waited for; matrix products, arithmetic and copies ran while one was open for 3% of the time, Pallas kernels for 0%

profile of v7, /device:TPU:81, one launch (start us, length us, event | category | flops | bytes accessed | tf_op | source)
XLA Modules:
  0.0 308.9 jit_solution(7933767290819542776)
XLA Ops:
  0.0 0.0 copy-start
  0.0 0.7 multiply_bitcast_fusion
  0.7 0.2 copy-done
  0.9 0.9 fusion.33
  1.8 13.8 %multiply_convert_fusion.4 = bf16[1024,2048]{1,0:T(8,128)(2,1)} fusion(bf16[2048,2048]{1,0:T(8,128)(2,1)} %param.6, f32[2048]{0:T(1024)S(1)} %bitcast.17, bf16[1,1024,2048]{2,1,0:T(8,128)(2,1)} %param.5, f32[2048]{0:T(1024)S(1)} %bitcast.16), kind=kOutput, calls=%fused_computation.32 | convolution fusion | flops 8613003264 | bytes 16793600 | tf_op jit(solution)/shard_map/dot_general | solution.py:83
  15.7 4.9 %fusion.39 = (bf16[512,2048]{1,0:T(8,128)(2,1)}, bf16[512,2048]{1,0:T(8,128)(2,1)}) fusion(bf16[1024,2048]{1,0:T(8,128)(2,1)} %multiply_convert_fusion.4), kind=kLoop, calls=%fused_computation.50 | loop fusion | bytes 8388608 | tf_op jit(solution)/shard_map/slice | solution.py:90
  20.6 2.0 collective-permute-start.2
  22.6 0.7 collective-permute-start.4
  23.3 3.4 %collective-permute-start.1 = (bf16[512,2048]{1,0:T(8,128)(2,1)}, bf16[512,2048]{1,0:T(8,128)(2,1)S(1)}, u32[]{:S(2)}, u32[]{:S(2)}) collective-permute-start(bf16[512,2048]{1,0:T(8,128)(2,1)} %get-tuple-element.6), channel_id=1, source_target_pairs={{0,2},{1,3},{2,4},{3,5},{4,6},{5,7},{6,8},{7,9},{8,10},{9,11},{10,... | collective-permute-start | bytes 6291464 | tf_op jit(solution)/shard_map/ppermute | solution.py:22
  26.7 0.0 collective-permute-done.2
  26.7 2.0 collective-permute-start.3
  28.7 0.7 collective-permute-start
  29.5 43.1 %collective-permute-done.1 = bf16[512,2048]{1,0:T(8,128)(2,1)S(1)} collective-permute-done((bf16[512,2048]{1,0:T(8,128)(2,1)}, bf16[512,2048]{1,0:T(8,128)(2,1)S(1)}, u32[]{:S(2)}, u32[]{:S(2)}) %collective-permute-start.1) | collective-permute-done | bytes 2097184 | tf_op jit(solution)/shard_map/ppermute | solution.py:22
  72.5 0.0 collective-permute-done.3
  72.5 3.7 %add.12 = bf16[512,2048]{1,0:T(8,128)(2,1)} add(bf16[512,2048]{1,0:T(8,128)(2,1)S(1)} %collective-permute-done.1, bf16[512,2048]{1,0:T(8,128)(2,1)} %collective-permute-done.3) | non-fusion elementwise | flops 1048576 | bytes 6291456 | tf_op jit(solution)/shard_map/add | solution.py:93
  76.3 37.9 %collective-permute-done = bf16[512,2048]{1,0:T(8,128)(2,1)} collective-permute-done((bf16[512,2048]{1,0:T(8,128)(2,1)}, bf16[512,2048]{1,0:T(8,128)(2,1)}, u32[]{:S(2)}, u32[]{:S(2)}) %collective-permute-start) | collective-permute-done | bytes 2097184 | tf_op jit(solution)/shard_map/ppermute | solution.py:22
  114.2 1.4 collective-permute-done.4
  115.6 13.9 %multiply_convert_fusion.3 = bf16[1024,2048]{1,0:T(8,128)(2,1)S(1)} fusion(bf16[1024,2048]{1,0:T(8,128)(2,1)} %multiply_convert_fusion.4, bf16[1024,2048]{1,0:T(8,128)(2,1)} %collective-permute-done.4, bf16[512,2048]{1,0:T(8,128)(2,1)} %add.12, bf16[512,2048]{1,0:T(8,128)(2,1)} %collective-permute-done, pred[]{:T(512)S(6)} %eq.17), kind=kOutput, calls=%fused_computation.31 | convolution fusion | flops 8648654848 | bytes 16777216 | tf_op jit(solution)/shard_map/dot_general | solution.py:63
  129.5 0.0 copy-start.2
  129.5 6.0 %collective-permute-start.7 = (bf16[1024,2048]{1,0:T(8,128)(2,1)S(1)}, bf16[1024,2048]{1,0:T(8,128)(2,1)S(1)}, u32[]{:S(2)}, u32[]{:S(2)}) collective-permute-start(bf16[1024,2048]{1,0:T(8,128)(2,1)S(1)} %multiply_convert_fusion.3), channel_id=1, source_target_pairs={{0,5},{1,4},{2,7},{3,6},{8,13},{9,12},{10,15},{11,14},{16,21},{17,... | collective-permute-start | bytes 12582920 | tf_op jit(solution)/shard_map/ppermute | solution.py:22
  135.6 0.1 slice.49
  135.7 0.8 collective-permute-start.10
  136.5 18.2 %collective-permute-start.5 = (bf16[1024,2048]{1,0:T(8,128)(2,1)S(1)}, bf16[1024,2048]{1,0:T(8,128)(2,1)}, u32[]{:S(2)}, u32[]{:S(2)}) collective-permute-start(bf16[1024,2048]{1,0:T(8,128)(2,1)S(1)} %multiply_convert_fusion.3), channel_id=1, source_target_pairs={{0,4},{1,5},{2,6},{3,7},{4,8},{5,9},{6,10},{7,11},{8,12},{9,13},{1... | collective-permute-start | bytes 12582920 | tf_op jit(solution)/shard_map/ppermute | solution.py:22
  154.6 0.1 slice.47
  154.8 0.8 collective-permute-start.8
  155.5 0.0 collective-permute-done.10
  155.6 1.3 collective-permute-start.11
  156.9 0.1 slice.45
  156.9 1.3 collective-permute-start.6
  158.2 0.0 collective-permute-done.8
  158.2 1.5 collective-permute-start.9
  159.7 89.6 %collective-permute-done.6 = bf16[208,2048]{1,0:T(8,128)(2,1)S(1)} collective-permute-done((bf16[208,2048]{1,0:T(8,128)(2,1)S(1)}, bf16[208,2048]{1,0:T(8,128)(2,1)S(1)}, u32[]{:S(2)}, u32[]{:S(2)}) %collective-permute-start.6) | collective-permute-done | bytes 852000 | tf_op jit(solution)/shard_map/ppermute | solution.py:22
  249.3 0.0 collective-permute-done.7
  249.3 1.1 slice_add_fusion.2
  250.3 0.0 collective-permute-done.11
  250.3 1.3 slice_add_fusion.1
  251.7 40.5 %collective-permute-done.9 = bf16[416,2048]{1,0:T(8,128)(2,1)S(1)} collective-permute-done((bf16[416,2048]{1,0:T(8,128)(2,1)S(1)}, bf16[416,2048]{1,0:T(8,128)(2,1)S(1)}, u32[]{:S(2)}, u32[]{:S(2)}) %collective-permute-start.9) | collective-permute-done | bytes 1703968 | tf_op jit(solution)/shard_map/ppermute | solution.py:22
  292.2 1.4 slice_add_fusion
  293.6 0.0 copy-done.2
  293.6 0.0 collective-permute-done.5
  293.6 0.0 copy-start.1
  293.6 15.1 %fusion.29 = bf16[1,1024,2048]{2,1,0:T(8,128)(2,1)} fusion(bf16[1024,2048]{1,0:T(8,128)(2,1)} %copy-done.2, bf16[400,2048]{1,0:T(8,128)(2,1)} %slice_add_fusion.1, bf16[416,2048]{1,0:T(8,128)(2,1)} %slice_add_fusion, bf16[208,2048]{1,0:T(8,128)(2,1)} %slice_add_fusion.2, bf16[1024,2048]{1,0:T(8,128)(2,1)} %collective-permute-done.5, pred[]{:T(512)S(6)} %eq.17), kind=kOutput, calls=%fused_computation.36 | convolution fusion | flops 8665432064 | bytes 16777216 | tf_op jit(solution)/shard_map/dot_general | solution.py:63
  308.7 0.0 copy-done.1
  (1 shorter events, 0.0 us)
Async XLA Ops:
  0.0 0.9 copy-start
  20.6 6.1 %collective-permute-start.2 = (bf16[512,2048]{1,0:T(8,128)(2,1)}, bf16[512,2048]{1,0:T(8,128)(2,1)}, u32[]{:S(2)}, u32[]{:S(2)}) collective-permute-start(bf16[512,2048]{1,0:T(8,128)(2,1)} %get-tuple-element.6), channel_id=1, source_target_pairs={{30,6},{31,7},{62,38},{63,39},{94,70},{95,71},{126,102},{127,103}} | collective-permute-start | bytes 6291464 | tf_op jit(solution)/shard_map/ppermute | solution.py:22
  22.6 93.0 %collective-permute-start.4 = (bf16[1024,2048]{1,0:T(8,128)(2,1)}, bf16[1024,2048]{1,0:T(8,128)(2,1)}, u32[]{:S(2)}, u32[]{:S(2)}) collective-permute-start(bf16[1024,2048]{1,0:T(8,128)(2,1)} %multiply_convert_fusion.4), channel_id=1, source_target_pairs={{0,3},{1,2},{2,5},{3,4},{4,7},{5,6},{6,9},{7,8},{8,11},{9,10},{10,... | collective-permute-start | bytes 12582920 | tf_op jit(solution)/shard_map/ppermute | solution.py:22
  23.3 49.2 %collective-permute-start.1 = (bf16[512,2048]{1,0:T(8,128)(2,1)}, bf16[512,2048]{1,0:T(8,128)(2,1)S(1)}, u32[]{:S(2)}, u32[]{:S(2)}) collective-permute-start(bf16[512,2048]{1,0:T(8,128)(2,1)} %get-tuple-element.6), channel_id=1, source_target_pairs={{0,2},{1,3},{2,4},{3,5},{4,6},{5,7},{6,8},{7,9},{8,10},{9,11},{10,... | collective-permute-start | bytes 6291464 | tf_op jit(solution)/shard_map/ppermute | solution.py:22
  26.7 45.8 %collective-permute-start.3 = (bf16[512,2048]{1,0:T(8,128)(2,1)}, bf16[512,2048]{1,0:T(8,128)(2,1)}, u32[]{:S(2)}, u32[]{:S(2)}) collective-permute-start(bf16[512,2048]{1,0:T(8,128)(2,1)} %collective-permute-done.2), channel_id=1, source_target_pairs={{6,32},{7,33},{38,64},{39,65},{70,96},{71,97},{102,0},{103,1}} | collective-permute-start | bytes 6291464 | tf_op jit(solution)/shard_map/ppermute | solution.py:22
  28.7 85.4 %collective-permute-start = (bf16[512,2048]{1,0:T(8,128)(2,1)}, bf16[512,2048]{1,0:T(8,128)(2,1)}, u32[]{:S(2)}, u32[]{:S(2)}) collective-permute-start(bf16[512,2048]{1,0:T(8,128)(2,1)} %get-tuple-element.5), channel_id=1, source_target_pairs={{0,2},{1,3},{2,4},{3,5},{4,6},{5,7},{6,8},{7,9},{8,10},{9,11},{10,... | collective-permute-start | bytes 6291464 | tf_op jit(solution)/shard_map/ppermute | solution.py:22
  129.5 164.0 %copy-start.2 = (bf16[1024,2048]{1,0:T(8,128)(2,1)}, bf16[1024,2048]{1,0:T(8,128)(2,1)S(1)}, u32[]{:S(2)}) copy-start(bf16[1024,2048]{1,0:T(8,128)(2,1)S(1)} %multiply_convert_fusion.3) | copy-start | bytes 12582916
  129.5 119.7 %collective-permute-start.7 = (bf16[1024,2048]{1,0:T(8,128)(2,1)S(1)}, bf16[1024,2048]{1,0:T(8,128)(2,1)S(1)}, u32[]{:S(2)}, u32[]{:S(2)}) collective-permute-start(bf16[1024,2048]{1,0:T(8,128)(2,1)S(1)} %multiply_convert_fusion.3), channel_id=1, source_target_pairs={{0,5},{1,4},{2,7},{3,6},{8,13},{9,12},{10,15},{11,14},{16,21},{17,... | collective-permute-start | bytes 12582920 | tf_op jit(solution)/shard_map/ppermute | solution.py:22
  135.7 19.8 %collective-permute-start.10 = (bf16[400,2048]{1,0:T(8,128)(2,1)S(1)}, bf16[400,2048]{1,0:T(8,128)(2,1)S(1)}, u32[]{:S(2)}, u32[]{:S(2)}) collective-permute-start(bf16[400,2048]{1,0:T(8,128)(2,1)S(1)} %slice.49), channel_id=1, source_target_pairs={{4,12},{5,13},{6,14},{7,15},{12,20},{13,21},{14,22},{15,23},{20,28... | collective-permute-start | bytes 4915208 | tf_op jit(solution)/shard_map/ppermute | solution.py:22
  136.5 157.1 %collective-permute-start.5 = (bf16[1024,2048]{1,0:T(8,128)(2,1)S(1)}, bf16[1024,2048]{1,0:T(8,128)(2,1)}, u32[]{:S(2)}, u32[]{:S(2)}) collective-permute-start(bf16[1024,2048]{1,0:T(8,128)(2,1)S(1)} %multiply_convert_fusion.3), channel_id=1, source_target_pairs={{0,4},{1,5},{2,6},{3,7},{4,8},{5,9},{6,10},{7,11},{8,12},{9,13},{1... | collective-permute-start | bytes 12582920 | tf_op jit(solution)/shard_map/ppermute | solution.py:22
  154.8 3.5 %collective-permute-start.8 = (bf16[416,2048]{1,0:T(8,128)(2,1)S(1)}, bf16[416,2048]{1,0:T(8,128)(2,1)S(1)}, u32[]{:S(2)}, u32[]{:S(2)}) collective-permute-start(bf16[416,2048]{1,0:T(8,128)(2,1)S(1)} %slice.47), channel_id=1, source_target_pairs={{4,12},{5,13},{6,14},{7,15},{12,20},{13,21},{14,22},{15,23},{20,28... | collective-permute-start | bytes 5111816 | tf_op jit(solution)/shard_map/ppermute | solution.py:22
  155.6 94.8 %collective-permute-start.11 = (bf16[400,2048]{1,0:T(8,128)(2,1)S(1)}, bf16[400,2048]{1,0:T(8,128)(2,1)S(1)}, u32[]{:S(2)}, u32[]{:S(2)}) collective-permute-start(bf16[400,2048]{1,0:T(8,128)(2,1)S(1)} %collective-permute-done.10), channel_id=1, source_target_pairs={{4,33},{5,32},{6,35},{7,34},{12,9},{13,8},{14,11},{15,10},{20,17},... | collective-permute-start | bytes 4915208 | tf_op jit(solution)/shard_map/ppermute | solution.py:22
  156.9 92.4 %collective-permute-start.6 = (bf16[208,2048]{1,0:T(8,128)(2,1)S(1)}, bf16[208,2048]{1,0:T(8,128)(2,1)S(1)}, u32[]{:S(2)}, u32[]{:S(2)}) collective-permute-start(bf16[208,2048]{1,0:T(8,128)(2,1)S(1)} %slice.45), channel_id=1, source_target_pairs={{4,9},{5,8},{6,11},{7,10},{12,17},{13,16},{14,19},{15,18},{20,25},... | collective-permute-start | bytes 2555912 | tf_op jit(solution)/shard_map/ppermute | solution.py:22
  158.2 133.9 %collective-permute-start.9 = (bf16[416,2048]{1,0:T(8,128)(2,1)S(1)}, bf16[416,2048]{1,0:T(8,128)(2,1)S(1)}, u32[]{:S(2)}, u32[]{:S(2)}) collective-permute-start(bf16[416,2048]{1,0:T(8,128)(2,1)S(1)} %collective-permute-done.8), channel_id=1, source_target_pairs={{4,33},{5,32},{6,35},{7,34},{12,9},{13,8},{14,11},{15,10},{20,17},... | collective-permute-start | bytes 5111816 | tf_op jit(solution)/shard_map/ppermute | solution.py:22
  293.6 15.2 %copy-start.1 = (f32[16,2048]{1,0:T(8,128)S(1)}, f32[16,2048]{1,0:T(8,128)}, u32[]{:S(2)}) copy-start(f32[16,2048]{1,0:T(8,128)} %param.7) | copy-start | bytes 393220

commit v8 on v7

--- a/solution.py
+++ b/solution.py
@@ -6,8 +6,7 @@
 from jax.sharding import PartitionSpec as P
 
 LEVELS = 2
-DIRECT_ROWS = 208
-RELAY_ROWS = (416, 400)
+DIRECT_ROWS = 96
 
 
 def sent(value, route):
@@ -54,12 +53,15 @@
     return lambda t, r, n, m: route(t, r, n, m) if y_low(t) == low else None
 
 
-def combined(later, own_rows, other_rows, row, norm_scale):
-    earlier = jnp.where(
+def natural(own_rows, other_rows, row):
+    return jnp.where(
         row == 0,
         jnp.concatenate(own_rows + other_rows, axis=0),
         jnp.concatenate(other_rows + own_rows, axis=0),
     )
+
+
+def level_product(later, earlier, norm_scale):
     total = jnp.dot(later, earlier, preferred_element_type=jnp.float32)
     return (total * norm_scale).astype(jnp.bfloat16)
 
@@ -80,29 +82,33 @@
     gain_rows = jnp.exp(0.1 * count_row[:, None] * table_rows)
     right_factor = (base_op * gain_rows[0]).astype(jnp.bfloat16)
     left_factor = (slice_ops[0] * gain_rows[1]).astype(jnp.bfloat16)
-    product = jnp.dot(left_factor, right_factor, preferred_element_type=jnp.float32)
-    current = (product * norm_scale).astype(jnp.bfloat16)
+    chunk_rows = half // 2
+    chunks = []
+    for c in range(2):
+        product = jnp.dot(left_factor[c * chunk_rows:(c + 1) * chunk_rows], right_factor,
+                          preferred_element_type=jnp.float32)
+        chunks.append((product * norm_scale).astype(jnp.bfloat16))
 
-    split_rows = half // 2
     boundary = lambda t, r, n, m: ((t - 12) % n, r) if ring_of(t) == 3 and t % 4 == 3 else None
     boundary_exit = lambda t, r, n, m: ((t + 13) % n, r) if ring_of(t) == 0 and t % 4 == 3 else None
     not_boundary = lambda t, r, n, m: None if ring_of(t) == 3 and t % 4 == 3 else ((t + 1) % n, r)
-    same_top = sent(current[:split_rows], direct(1, 0))
-    same_bottom = sent(current[split_rows:], not_boundary)
-    wrapped = sent(current[split_rows:], boundary)
-    same_bottom = same_bottom + sent(wrapped, boundary_exit)
-    other = sent(current, direct(1, 1))
-    current = combined(current, [same_top, same_bottom], [other], row, norm_scale)
+    own_rows = [sent(chunks[0], direct(1, 0))]
+    other_rows = [sent(chunks[0], direct(1, 1))]
+    own_rows.append(sent(chunks[1], not_boundary) + sent(sent(chunks[1], boundary), boundary_exit))
+    other_rows.append(sent(chunks[1], direct(1, 1)))
+    earlier = natural(own_rows, other_rows, row)
+    chunks = [level_product(chunk, earlier, norm_scale) for chunk in chunks]
 
-    same = sent(current, direct(2, 0))
-    other_near = sent(current, when_low(0, direct(2, 1)))
-    other_rows = [sent(current[:DIRECT_ROWS], when_low(1, direct(2, 1))) + other_near[:DIRECT_ROWS]]
-    begin = DIRECT_ROWS
-    for size in RELAY_ROWS:
-        ring_first = sent(current[begin:begin + size], ring_first_hop)
-        other_rows.append(sent(ring_first, ring_first_exit) + other_near[begin:begin + size])
-        begin += size
-    current = combined(current, [same], other_rows, row, norm_scale)
+    own_rows = []
+    other_rows = []
+    for chunk in chunks:
+        own_rows.append(sent(chunk, direct(2, 0)))
+        other_near = sent(chunk, when_low(0, direct(2, 1)))
+        other_rows.append(sent(chunk[:DIRECT_ROWS], when_low(1, direct(2, 1))) + other_near[:DIRECT_ROWS])
+        ring_first = sent(chunk[DIRECT_ROWS:], ring_first_hop)
+        other_rows.append(sent(ring_first, ring_first_exit) + other_near[DIRECT_ROWS:])
+    earlier = natural(own_rows, other_rows, row)
+    current = level_product(jnp.concatenate(chunks, axis=0), earlier, norm_scale)
     return current[None]
 
 

time: 309 us -> 323 us (1.045)
  the two profiles are of different devices: /device:TPU:81 before, /device:TPU:96 now
where the time goes in v8:
time: 323 us; the launch traced here: 320 us
  waiting for transfers between devices  166 us (51%)
  starting transfers between devices  98.2 us (30%)
  matrix products  35.8 us (11%)
  other arithmetic  15.4 us (5%)
  local copies, waits for them, and re-layouts  4.4 us (1%)
    ppermute x16, waiting for transfers between devices, sent(): return lax.ppermute(value, ('tm', 'row'), pairs)  166 us
    ppermute x16, starting transfers between devices, sent(): return lax.ppermute(value, ('tm', 'row'), pairs)  98.2 us
    dot_general x3, matrix products, level_product(): total = jnp.dot(later, earlier, preferred_element_type=jnp.float32)  23.1 us
    dot_general x2, matrix products, shards(): jnp.dot(left_factor[c * chunk_rows:(c + 1) * chunk_rows], right_factor, p...  11.4 us
  transfers between devices with their start and end apart: 16, of which 7 were waited for; matrix products, arithmetic and copies ran while one was open for 5% of the time, Pallas kernels for 0%

profile of v8, /device:TPU:96, one launch (start us, length us, event | category | flops | bytes accessed | tf_op | source)
XLA Modules:
  0.0 320.3 jit_solution(6696708912810610959)
XLA Ops:
  0.0 0.0 copy-start
  0.0 0.0 copy-start.3
  0.0 0.8 multiply_bitcast_fusion
  0.8 0.1 copy-done
  0.9 1.3 fusion.14
  2.2 3.5 %fusion = bf16[1024,2048]{1,0:T(8,128)(2,1)S(1)} fusion(bf16[1,1024,2048]{2,1,0:T(8,128)(2,1)} %param.5, f32[2048]{0:T(1024)S(1)} %bitcast.15), kind=kLoop, calls=%fused_computation.3 | loop fusion | flops 6291456 | bytes 8396800 | tf_op jit(solution)/shard_map/convert_element_type | solution.py:84
  5.8 0.0 copy-done.3
  5.8 5.7 %multiply_convert_fusion.6 = bf16[512,2048]{1,0:T(8,128)(2,1)} fusion(bf16[2048,2048]{1,0:T(8,128)(2,1)S(1)} %copy-done.3, f32[2048]{0:T(1024)S(1)} %bitcast.16, bf16[1024,2048]{1,0:T(8,128)(2,1)S(1)} %fusion), kind=kOutput, calls=%fused_computation.16 | convolution fusion | flops 4309647360 | bytes 12591104 | tf_op jit(solution)/shard_map/dot_general | solution.py:88
  11.5 2.0 collective-permute-start.2
  13.5 1.9 collective-permute-start.1
  15.5 4.3 %collective-permute-start.5 = (bf16[512,2048]{1,0:T(8,128)(2,1)}, bf16[512,2048]{1,0:T(8,128)(2,1)S(1)}, u32[]{:S(2)}, u32[]{:S(2)}) collective-permute-start(bf16[512,2048]{1,0:T(8,128)(2,1)} %multiply_convert_fusion.6), channel_id=1, source_target_pairs={{0,3},{1,2},{2,5},{3,4},{4,7},{5,6},{6,9},{7,8},{8,11},{9,10},{10,... | collective-permute-start | bytes 6291464 | tf_op jit(solution)/shard_map/ppermute | solution.py:21
  19.7 0.0 collective-permute-done.2
  19.7 2.1 collective-permute-start.3
  21.8 5.7 %multiply_convert_fusion.7 = bf16[512,2048]{1,0:T(8,128)(2,1)} fusion(bf16[2048,2048]{1,0:T(8,128)(2,1)S(1)} %copy-done.3, f32[2048]{0:T(1024)S(1)} %bitcast.17, bf16[1024,2048]{1,0:T(8,128)(2,1)S(1)} %fusion), kind=kOutput, calls=%fused_computation.17 | convolution fusion | flops 4309647360 | bytes 12591104 | tf_op jit(solution)/shard_map/dot_general | solution.py:88
  27.5 0.0 collective-permute-start
  27.5 0.7 collective-permute-start.4
  28.1 34.4 %collective-permute-done.1 = bf16[512,2048]{1,0:T(8,128)(2,1)} collective-permute-done((bf16[512,2048]{1,0:T(8,128)(2,1)}, bf16[512,2048]{1,0:T(8,128)(2,1)}, u32[]{:S(2)}, u32[]{:S(2)}) %collective-permute-start.1) | collective-permute-done | bytes 2097184 | tf_op jit(solution)/shard_map/ppermute | solution.py:21
  62.5 0.0 collective-permute-done.3
  62.5 3.1 add.15
  65.6 6.9 %collective-permute-done.5 = bf16[512,2048]{1,0:T(8,128)(2,1)S(1)} collective-permute-done((bf16[512,2048]{1,0:T(8,128)(2,1)}, bf16[512,2048]{1,0:T(8,128)(2,1)S(1)}, u32[]{:S(2)}, u32[]{:S(2)}) %collective-permute-start.5) | collective-permute-done | bytes 2097184 | tf_op jit(solution)/shard_map/ppermute | solution.py:21
  72.5 34.9 %collective-permute-done = bf16[512,2048]{1,0:T(8,128)(2,1)} collective-permute-done((bf16[512,2048]{1,0:T(8,128)(2,1)}, bf16[512,2048]{1,0:T(8,128)(2,1)}, u32[]{:S(2)}, u32[]{:S(2)}) %collective-permute-start) | collective-permute-done | bytes 2097184 | tf_op jit(solution)/shard_map/ppermute | solution.py:21
  107.5 13.6 %collective-permute-done.4 = bf16[512,2048]{1,0:T(8,128)(2,1)} collective-permute-done((bf16[512,2048]{1,0:T(8,128)(2,1)}, bf16[512,2048]{1,0:T(8,128)(2,1)}, u32[]{:S(2)}, u32[]{:S(2)}) %collective-permute-start.4) | collective-permute-done | bytes 2097184 | tf_op jit(solution)/shard_map/ppermute | solution.py:21
  121.0 6.4 %maximum_select_fusion = bf16[2048,2048]{1,0:T(8,128)(2,1)S(1)} fusion(bf16[512,2048]{1,0:T(8,128)(2,1)S(1)} %collective-permute-done.5, bf16[512,2048]{1,0:T(8,128)(2,1)} %collective-permute-done.4, bf16[512,2048]{1,0:T(8,128)(2,1)S(1)} %add.15, bf16[512,2048]{1,0:T(8,128)(2,1)} %collective-permute-done, pred[]{:T(512)S(6)} %eq.17), kind=kLoop, calls=%fused_computation.1 | loop fusion | flops 71303168 | bytes 16777216 | tf_op jit(solution)/shard_map/jit(_where)/select_n | solution.py:57
  127.4 6.3 %multiply_convert_fusion.5 = bf16[512,2048]{1,0:T(8,128)(2,1)S(1)} fusion(bf16[512,2048]{1,0:T(8,128)(2,1)} %multiply_convert_fusion.7, bf16[2048,2048]{1,0:T(8,128)(2,1)S(1)} %maximum_select_fusion), kind=kOutput, calls=%fused_computation.15 | convolution fusion | flops 4297064448 | bytes 12582912 | tf_op jit(solution)/shard_map/dot_general | solution.py:65
  133.7 0.1 slice.54
  133.8 0.8 collective-permute-start.10
  134.6 6.3 %multiply_convert_fusion.4 = bf16[512,2048]{1,0:T(8,128)(2,1)S(1)} fusion(bf16[512,2048]{1,0:T(8,128)(2,1)} %multiply_convert_fusion.6, bf16[2048,2048]{1,0:T(8,128)(2,1)S(1)} %maximum_select_fusion), kind=kOutput, calls=%fused_computation.14 | convolution fusion | flops 4297064448 | bytes 12582912 | tf_op jit(solution)/shard_map/dot_general | solution.py:65
  140.9 0.1 slice.58
  141.0 1.0 collective-permute-start.14
  142.0 12.6 %collective-permute-start.6 = (bf16[512,2048]{1,0:T(8,128)(2,1)S(1)}, bf16[512,2048]{1,0:T(8,128)(2,1)S(1)}, u32[]{:S(2)}, u32[]{:S(2)}) collective-permute-start(bf16[512,2048]{1,0:T(8,128)(2,1)S(1)} %multiply_convert_fusion.5), channel_id=1, source_target_pairs={{0,4},{1,5},{2,6},{3,7},{4,8},{5,9},{6,10},{7,11},{8,12},{9,13},{1... | collective-permute-start | bytes 6291464 | tf_op jit(solution)/shard_map/ppermute | solution.py:21
  154.6 0.1 collective-permute-start.7
  154.7 6.1 %collective-permute-start.9 = (bf16[512,2048]{1,0:T(8,128)(2,1)S(1)}, bf16[512,2048]{1,0:T(8,128)(2,1)S(1)}, u32[]{:S(2)}, u32[]{:S(2)}) collective-permute-start(bf16[512,2048]{1,0:T(8,128)(2,1)S(1)} %multiply_convert_fusion.5), channel_id=1, source_target_pairs={{0,5},{1,4},{2,7},{3,6},{8,13},{9,12},{10,15},{11,14},{16,21},{17,... | collective-permute-start | bytes 6291464 | tf_op jit(solution)/shard_map/ppermute | solution.py:21
  160.8 0.0 collective-permute-done.10
  160.8 1.3 collective-permute-start.11
  162.1 0.0 collective-permute-done.14
  162.1 61.5 %collective-permute-start.13 = (bf16[512,2048]{1,0:T(8,128)(2,1)S(1)}, bf16[512,2048]{1,0:T(8,128)(2,1)S(1)}, u32[]{:S(2)}, u32[]{:S(2)}) collective-permute-start(bf16[512,2048]{1,0:T(8,128)(2,1)S(1)} %multiply_convert_fusion.4), channel_id=1, source_target_pairs={{0,5},{1,4},{2,7},{3,6},{8,13},{9,12},{10,15},{11,14},{16,21},{17,... | collective-permute-start | bytes 6291464 | tf_op jit(solution)/shard_map/ppermute | solution.py:21
  223.7 0.0 collective-permute-done.6
  223.7 1.3 collective-permute-start.8
  225.0 0.1 constant_dynamic-update-slice_fusion.1
  225.2 29.0 %collective-permute-done.7 = bf16[512,2048]{1,0:T(8,128)(2,1)S(1)} collective-permute-done((bf16[512,2048]{1,0:T(8,128)(2,1)S(1)}, bf16[512,2048]{1,0:T(8,128)(2,1)S(1)}, u32[]{:S(2)}, u32[]{:S(2)}) %collective-permute-start.7) | collective-permute-done | bytes 2097184 | tf_op jit(solution)/shard_map/ppermute | solution.py:21
  254.2 1.3 collective-permute-start.15
  255.5 0.1 constant_dynamic-update-slice_fusion
  255.7 0.0 collective-permute-done.8
  255.7 1.3 collective-permute-start.12
  257.0 0.0 collective-permute-done.9
  257.0 0.1 fusion.21
  257.1 0.0 collective-permute-done.11
  257.1 0.7 fusion.17
  257.8 46.4 %collective-permute-done.12 = bf16[96,2048]{1,0:T(8,128)(2,1)S(1)} collective-permute-done((bf16[96,2048]{1,0:T(8,128)(2,1)S(1)}, bf16[96,2048]{1,0:T(8,128)(2,1)S(1)}, u32[]{:S(2)}, u32[]{:S(2)}) %collective-permute-start.12) | collective-permute-done | bytes 393248 | tf_op jit(solution)/shard_map/ppermute | solution.py:21
  304.2 0.0 collective-permute-done.13
  304.2 0.1 fusion.23
  304.3 1.0 collective-permute-done.15
  305.3 0.7 fusion.19
  306.0 0.2 constant_dynamic-update-slice_fusion.3
  306.3 0.2 constant_dynamic-update-slice_fusion.2
  306.5 0.0 copy-start.2
  306.5 3.2 %copy-done.2 = bf16[2048,2048]{1,0:T(8,128)(2,1)} copy-done((bf16[2048,2048]{1,0:T(8,128)(2,1)}, bf16[2048,2048]{1,0:T(8,128)(2,1)S(1)}, u32[]{:S(2)}) %copy-start.2) | copy-done | bytes 8388632
  309.8 0.0 copy-start.1
  309.8 10.5 %fusion.6 = bf16[1,1024,2048]{2,1,0:T(8,128)(2,1)} fusion(bf16[2048,2048]{1,0:T(8,128)(2,1)S(1)} %get-tuple-element.6, bf16[2048,2048]{1,0:T(8,128)(2,1)} %copy-done.2, pred[]{:T(512)S(6)} %eq.17, bf16[512,2048]{1,0:T(8,128)(2,1)S(1)} %multiply_convert_fusion.4, bf16[512,2048]{1,0:T(8,128)(2,1)S(1)} %multiply_convert_fusion.5), kind=kOutput, calls=%fused_computation.10 | convolution fusion | flops 8606711808 | bytes 25165824 | tf_op jit(solution)/shard_map/dot_general | solution.py:65
  320.3 0.0 copy-done.1
  (3 shorter events, 0.1 us)
Async XLA Ops:
  0.0 0.9 copy-start
  0.0 5.8 %copy-start.3 = (bf16[2048,2048]{1,0:T(8,128)(2,1)S(1)}, bf16[2048,2048]{1,0:T(8,128)(2,1)}, u32[]{:S(2)}) copy-start(bf16[2048,2048]{1,0:T(8,128)(2,1)} %param.6) | copy-start | bytes 25165828
  11.5 8.2 %collective-permute-start.2 = (bf16[512,2048]{1,0:T(8,128)(2,1)}, bf16[512,2048]{1,0:T(8,128)(2,1)}, u32[]{:S(2)}, u32[]{:S(2)}) collective-permute-start(bf16[512,2048]{1,0:T(8,128)(2,1)} %multiply_convert_fusion.6), channel_id=1, source_target_pairs={{30,6},{31,7},{62,38},{63,39},{94,70},{95,71},{126,102},{127,103}} | collective-permute-start | bytes 6291464 | tf_op jit(solution)/shard_map/ppermute | solution.py:21
  13.5 49.0 %collective-permute-start.1 = (bf16[512,2048]{1,0:T(8,128)(2,1)}, bf16[512,2048]{1,0:T(8,128)(2,1)}, u32[]{:S(2)}, u32[]{:S(2)}) collective-permute-start(bf16[512,2048]{1,0:T(8,128)(2,1)} %multiply_convert_fusion.6), channel_id=1, source_target_pairs={{0,2},{1,3},{2,4},{3,5},{4,6},{5,7},{6,8},{7,9},{8,10},{9,11},{10,... | collective-permute-start | bytes 6291464 | tf_op jit(solution)/shard_map/ppermute | solution.py:21
  15.5 57.1 %collective-permute-start.5 = (bf16[512,2048]{1,0:T(8,128)(2,1)}, bf16[512,2048]{1,0:T(8,128)(2,1)S(1)}, u32[]{:S(2)}, u32[]{:S(2)}) collective-permute-start(bf16[512,2048]{1,0:T(8,128)(2,1)} %multiply_convert_fusion.6), channel_id=1, source_target_pairs={{0,3},{1,2},{2,5},{3,4},{4,7},{5,6},{6,9},{7,8},{8,11},{9,10},{10,... | collective-permute-start | bytes 6291464 | tf_op jit(solution)/shard_map/ppermute | solution.py:21
  19.7 42.8 %collective-permute-start.3 = (bf16[512,2048]{1,0:T(8,128)(2,1)}, bf16[512,2048]{1,0:T(8,128)(2,1)}, u32[]{:S(2)}, u32[]{:S(2)}) collective-permute-start(bf16[512,2048]{1,0:T(8,128)(2,1)} %collective-permute-done.2), channel_id=1, source_target_pairs={{6,32},{7,33},{38,64},{39,65},{70,96},{71,97},{102,0},{103,1}} | collective-permute-start | bytes 6291464 | tf_op jit(solution)/shard_map/ppermute | solution.py:21
  27.5 80.0 %collective-permute-start = (bf16[512,2048]{1,0:T(8,128)(2,1)}, bf16[512,2048]{1,0:T(8,128)(2,1)}, u32[]{:S(2)}, u32[]{:S(2)}) collective-permute-start(bf16[512,2048]{1,0:T(8,128)(2,1)} %multiply_convert_fusion.7), channel_id=1, source_target_pairs={{0,2},{1,3},{2,4},{3,5},{4,6},{5,7},{6,8},{7,9},{8,10},{9,11},{10,... | collective-permute-start | bytes 6291464 | tf_op jit(solution)/shard_map/ppermute | solution.py:21
  27.5 93.6 %collective-permute-start.4 = (bf16[512,2048]{1,0:T(8,128)(2,1)}, bf16[512,2048]{1,0:T(8,128)(2,1)}, u32[]{:S(2)}, u32[]{:S(2)}) collective-permute-start(bf16[512,2048]{1,0:T(8,128)(2,1)} %multiply_convert_fusion.7), channel_id=1, source_target_pairs={{0,3},{1,2},{2,5},{3,4},{4,7},{5,6},{6,9},{7,8},{8,11},{9,10},{10,... | collective-permute-start | bytes 6291464 | tf_op jit(solution)/shard_map/ppermute | solution.py:21
  133.8 27.0 %collective-permute-start.10 = (bf16[416,2048]{1,0:T(8,128)(2,1)S(1)}, bf16[416,2048]{1,0:T(8,128)(2,1)S(1)}, u32[]{:S(2)}, u32[]{:S(2)}) collective-permute-start(bf16[416,2048]{1,0:T(8,128)(2,1)S(1)} %slice.54), channel_id=1, source_target_pairs={{4,12},{5,13},{6,14},{7,15},{12,20},{13,21},{14,22},{15,23},{20,28... | collective-permute-start | bytes 5111816 | tf_op jit(solution)/shard_map/ppermute | solution.py:21
  141.0 21.1 %collective-permute-start.14 = (bf16[416,2048]{1,0:T(8,128)(2,1)S(1)}, bf16[416,2048]{1,0:T(8,128)(2,1)S(1)}, u32[]{:S(2)}, u32[]{:S(2)}) collective-permute-start(bf16[416,2048]{1,0:T(8,128)(2,1)S(1)} %slice.58), channel_id=1, source_target_pairs={{4,12},{5,13},{6,14},{7,15},{12,20},{13,21},{14,22},{15,23},{20,28... | collective-permute-start | bytes 5111816 | tf_op jit(solution)/shard_map/ppermute | solution.py:21
  142.0 81.8 %collective-permute-start.6 = (bf16[512,2048]{1,0:T(8,128)(2,1)S(1)}, bf16[512,2048]{1,0:T(8,128)(2,1)S(1)}, u32[]{:S(2)}, u32[]{:S(2)}) collective-permute-start(bf16[512,2048]{1,0:T(8,128)(2,1)S(1)} %multiply_convert_fusion.5), channel_id=1, source_target_pairs={{0,4},{1,5},{2,6},{3,7},{4,8},{5,9},{6,10},{7,11},{8,12},{9,13},{1... | collective-permute-start | bytes 6291464 | tf_op jit(solution)/shard_map/ppermute | solution.py:21
  154.6 99.6 %collective-permute-start.7 = (bf16[512,2048]{1,0:T(8,128)(2,1)S(1)}, bf16[512,2048]{1,0:T(8,128)(2,1)S(1)}, u32[]{:S(2)}, u32[]{:S(2)}) collective-permute-start(bf16[512,2048]{1,0:T(8,128)(2,1)S(1)} %multiply_convert_fusion.4), channel_id=1, source_target_pairs={{0,4},{1,5},{2,6},{3,7},{4,8},{5,9},{6,10},{7,11},{8,12},{9,13},{1... | collective-permute-start | bytes 6291464 | tf_op jit(solution)/shard_map/ppermute | solution.py:21
  154.7 102.3 %collective-permute-start.9 = (bf16[512,2048]{1,0:T(8,128)(2,1)S(1)}, bf16[512,2048]{1,0:T(8,128)(2,1)S(1)}, u32[]{:S(2)}, u32[]{:S(2)}) collective-permute-start(bf16[512,2048]{1,0:T(8,128)(2,1)S(1)} %multiply_convert_fusion.5), channel_id=1, source_target_pairs={{0,5},{1,4},{2,7},{3,6},{8,13},{9,12},{10,15},{11,14},{16,21},{17,... | collective-permute-start | bytes 6291464 | tf_op jit(solution)/shard_map/ppermute | solution.py:21
  160.8 96.3 %collective-permute-start.11 = (bf16[416,2048]{1,0:T(8,128)(2,1)S(1)}, bf16[416,2048]{1,0:T(8,128)(2,1)S(1)}, u32[]{:S(2)}, u32[]{:S(2)}) collective-permute-start(bf16[416,2048]{1,0:T(8,128)(2,1)S(1)} %collective-permute-done.10), channel_id=1, source_target_pairs={{4,33},{5,32},{6,35},{7,34},{12,9},{13,8},{14,11},{15,10},{20,17},... | collective-permute-start | bytes 5111816 | tf_op jit(solution)/shard_map/ppermute | solution.py:21
  162.1 142.1 %collective-permute-start.13 = (bf16[512,2048]{1,0:T(8,128)(2,1)S(1)}, bf16[512,2048]{1,0:T(8,128)(2,1)S(1)}, u32[]{:S(2)}, u32[]{:S(2)}) collective-permute-start(bf16[512,2048]{1,0:T(8,128)(2,1)S(1)} %multiply_convert_fusion.4), channel_id=1, source_target_pairs={{0,5},{1,4},{2,7},{3,6},{8,13},{9,12},{10,15},{11,14},{16,21},{17,... | collective-permute-start | bytes 6291464 | tf_op jit(solution)/shard_map/ppermute | solution.py:21
  223.7 31.9 %collective-permute-start.8 = (bf16[96,2048]{1,0:T(8,128)(2,1)S(1)}, bf16[96,2048]{1,0:T(8,128)(2,1)S(1)}, u32[]{:S(2)}, u32[]{:S(2)}) collective-permute-start(bf16[96,2048]{1,0:T(8,128)(2,1)S(1)} %slice.52), channel_id=1, source_target_pairs={{4,9},{5,8},{6,11},{7,10},{12,17},{13,16},{14,19},{15,18},{20,25},... | collective-permute-start | bytes 1179656 | tf_op jit(solution)/shard_map/ppermute | solution.py:21
  254.2 51.1 %collective-permute-start.15 = (bf16[416,2048]{1,0:T(8,128)(2,1)S(1)}, bf16[416,2048]{1,0:T(8,128)(2,1)S(1)}, u32[]{:S(2)}, u32[]{:S(2)}) collective-permute-start(bf16[416,2048]{1,0:T(8,128)(2,1)S(1)} %collective-permute-done.14), channel_id=1, source_target_pairs={{4,33},{5,32},{6,35},{7,34},{12,9},{13,8},{14,11},{15,10},{20,17},... | collective-permute-start | bytes 5111816 | tf_op jit(solution)/shard_map/ppermute | solution.py:21
  255.7 48.6 %collective-permute-start.12 = (bf16[96,2048]{1,0:T(8,128)(2,1)S(1)}, bf16[96,2048]{1,0:T(8,128)(2,1)S(1)}, u32[]{:S(2)}, u32[]{:S(2)}) collective-permute-start(bf16[96,2048]{1,0:T(8,128)(2,1)S(1)} %slice.56), channel_id=1, source_target_pairs={{4,9},{5,8},{6,11},{7,10},{12,17},{13,16},{14,19},{15,18},{20,25},... | collective-permute-start | bytes 1179656 | tf_op jit(solution)/shard_map/ppermute | solution.py:21
  306.5 3.3 %copy-start.2 = (bf16[2048,2048]{1,0:T(8,128)(2,1)}, bf16[2048,2048]{1,0:T(8,128)(2,1)S(1)}, u32[]{:S(2)}) copy-start(bf16[2048,2048]{1,0:T(8,128)(2,1)S(1)} %constant_dynamic-update-slice_fusion.2) | copy-start | bytes 25165828
  309.8 10.5 %copy-start.1 = (f32[16,2048]{1,0:T(8,128)S(1)}, f32[16,2048]{1,0:T(8,128)}, u32[]{:S(2)}) copy-start(f32[16,2048]{1,0:T(8,128)} %param.7) | copy-start | bytes 393220

commit v9 on v8

--- a/solution.py
+++ b/solution.py
@@ -6,7 +6,8 @@
 from jax.sharding import PartitionSpec as P
 
 LEVELS = 2
-DIRECT_ROWS = 96
+DIRECT_ROWS = 208
+RELAY_ROWS = (416, 400)
 
 
 def sent(value, route):
@@ -97,18 +98,17 @@
     own_rows.append(sent(chunks[1], not_boundary) + sent(sent(chunks[1], boundary), boundary_exit))
     other_rows.append(sent(chunks[1], direct(1, 1)))
     earlier = natural(own_rows, other_rows, row)
-    chunks = [level_product(chunk, earlier, norm_scale) for chunk in chunks]
+    current = level_product(jnp.concatenate(chunks, axis=0), earlier, norm_scale)
 
-    own_rows = []
-    other_rows = []
-    for chunk in chunks:
-        own_rows.append(sent(chunk, direct(2, 0)))
-        other_near = sent(chunk, when_low(0, direct(2, 1)))
-        other_rows.append(sent(chunk[:DIRECT_ROWS], when_low(1, direct(2, 1))) + other_near[:DIRECT_ROWS])
-        ring_first = sent(chunk[DIRECT_ROWS:], ring_first_hop)
-        other_rows.append(sent(ring_first, ring_first_exit) + other_near[DIRECT_ROWS:])
-    earlier = natural(own_rows, other_rows, row)
-    current = level_product(jnp.concatenate(chunks, axis=0), earlier, norm_scale)
+    same = sent(current, direct(2, 0))
+    other_near = sent(current, when_low(0, direct(2, 1)))
+    other_rows = [sent(current[:DIRECT_ROWS], when_low(1, direct(2, 1))) + other_near[:DIRECT_ROWS]]
+    begin = DIRECT_ROWS
+    for size in RELAY_ROWS:
+        ring_first = sent(current[begin:begin + size], ring_first_hop)
+        other_rows.append(sent(ring_first, ring_first_exit) + other_near[begin:begin + size])
+        begin += size
+    current = level_product(current, natural([same], other_rows, row), norm_scale)
     return current[None]
 
 

time: 323 us -> 300 us (0.929)
  starting transfers between devices: 98.2 us -> 49.5 us
  waiting for transfers between devices: 166 us -> 199 us
  other arithmetic: 15.4 us -> 8.14 us
  local copies, waits for them, and re-layouts: 4.4 us -> 0.4 us
  matrix products: 35.8 us -> 39.3 us
    ppermute x16 -> x13, starting transfers between devices: 98.2 us -> 49.5 us  [sent(): return lax.ppermute(value, ('tm', 'row'), pairs)]
    ppermute x16 -> x13, waiting for transfers between devices: 166 us -> 199 us  [sent(): return lax.ppermute(value, ('tm', 'row'), pairs)]
    select_n x1 -> x0, other arithmetic: 6.37 us -> none  [natural(): jnp.where(row == 0, jnp.concatenate(own_rows + other_rows, axis=0), jnp.c...]
    unnamed x11 -> x8, local copies, waits for them, and re-layouts: 3.86 us -> 0.11 us
    dot_general x3 -> x2, matrix products: 23.1 us -> 26.5 us  [level_product(): total = jnp.dot(later, earlier, preferred_element_type=jnp.float32)]
  transfers between devices with their start and end apart: 16 -> 13, of which waited for: 7 -> 7; matrix products, arithmetic and copies ran while one was open for 5% -> 3% of each run, Pallas kernels for 0% -> 0%
where the time goes in v9:
time: 300 us; the launch traced here: 296 us
  waiting for transfers between devices  199 us (66%)
  starting transfers between devices  49.5 us (16%)
  matrix products  39.3 us (13%)
  other arithmetic  8.14 us (3%)
    ppermute x13, waiting for transfers between devices, sent(): return lax.ppermute(value, ('tm', 'row'), pairs)  199 us
    ppermute x13, starting transfers between devices, sent(): return lax.ppermute(value, ('tm', 'row'), pairs)  49.5 us
    dot_general x2, matrix products, level_product(): total = jnp.dot(later, earlier, preferred_element_type=jnp.float32)  26.5 us
    dot_general x2, matrix products, shards(): jnp.dot(left_factor[c * chunk_rows:(c + 1) * chunk_rows], right_factor, p...  11.5 us
  transfers between devices with their start and end apart: 13, of which 7 were waited for; matrix products, arithmetic and copies ran while one was open for 3% of the time, Pallas kernels for 0%

profile of v9, /device:TPU:96, one launch (start us, length us, event | category | flops | bytes accessed | tf_op | source)
XLA Modules:
  0.0 296.5 jit_solution(14764521786261126961)
XLA Ops:
  0.0 0.0 copy-start
  0.0 0.0 copy-start.3
  0.0 0.8 multiply_bitcast_fusion
  0.8 0.1 copy-done
  0.9 1.3 fusion.39
  2.2 3.5 %fusion.28 = bf16[1024,2048]{1,0:T(8,128)(2,1)S(1)} fusion(bf16[1,1024,2048]{2,1,0:T(8,128)(2,1)} %param.5, f32[2048]{0:T(1024)S(1)} %bitcast.12), kind=kLoop, calls=%fused_computation.32 | loop fusion | flops 6291456 | bytes 8396800 | tf_op jit(solution)/shard_map/convert_element_type | solution.py:85
  5.8 0.0 copy-done.3
  5.8 5.7 %multiply_convert_fusion.5 = bf16[512,2048]{1,0:T(8,128)(2,1)} fusion(bf16[2048,2048]{1,0:T(8,128)(2,1)S(1)} %copy-done.3, f32[2048]{0:T(1024)S(1)} %bitcast.13, bf16[1024,2048]{1,0:T(8,128)(2,1)S(1)} %fusion.28), kind=kOutput, calls=%fused_computation.43 | convolution fusion | flops 4309647360 | bytes 12591104 | tf_op jit(solution)/shard_map/dot_general | solution.py:89
  11.5 2.0 collective-permute-start.2
  13.5 1.9 collective-permute-start.1
  15.4 0.0 collective-permute-done.2
  15.4 2.0 collective-permute-start.3
  17.5 5.8 %multiply_convert_fusion.6 = bf16[512,2048]{1,0:T(8,128)(2,1)} fusion(bf16[2048,2048]{1,0:T(8,128)(2,1)S(1)} %copy-done.3, f32[2048]{0:T(1024)S(1)} %bitcast.14, bf16[1024,2048]{1,0:T(8,128)(2,1)S(1)} %fusion.28), kind=kOutput, calls=%fused_computation.44 | convolution fusion | flops 4309647360 | bytes 12591104 | tf_op jit(solution)/shard_map/dot_general | solution.py:89
  23.3 4.2 %collective-permute-start.4 = (bf16[512,2048]{1,0:T(8,128)(2,1)}, bf16[512,2048]{1,0:T(8,128)(2,1)}, u32[]{:S(2)}, u32[]{:S(2)}) collective-permute-start(bf16[512,2048]{1,0:T(8,128)(2,1)} %multiply_convert_fusion.6), channel_id=1, source_target_pairs={{0,3},{1,2},{2,5},{3,4},{4,7},{5,6},{6,9},{7,8},{8,11},{9,10},{10,... | collective-permute-start | bytes 6291464 | tf_op jit(solution)/shard_map/ppermute | solution.py:22
  27.4 0.0 collective-permute-start
  27.4 21.3 %collective-permute-start.5 = (bf16[512,2048]{1,0:T(8,128)(2,1)}, bf16[512,2048]{1,0:T(8,128)(2,1)}, u32[]{:S(2)}, u32[]{:S(2)}) collective-permute-start(bf16[512,2048]{1,0:T(8,128)(2,1)} %multiply_convert_fusion.5), channel_id=1, source_target_pairs={{0,3},{1,2},{2,5},{3,4},{4,7},{5,6},{6,9},{7,8},{8,11},{9,10},{10,... | collective-permute-start | bytes 6291464 | tf_op jit(solution)/shard_map/ppermute | solution.py:22
  48.7 5.9 %collective-permute-done.1 = bf16[512,2048]{1,0:T(8,128)(2,1)S(1)} collective-permute-done((bf16[512,2048]{1,0:T(8,128)(2,1)}, bf16[512,2048]{1,0:T(8,128)(2,1)S(1)}, u32[]{:S(2)}, u32[]{:S(2)}) %collective-permute-start.1) | collective-permute-done | bytes 2097184 | tf_op jit(solution)/shard_map/ppermute | solution.py:22
  54.7 0.0 collective-permute-done.3
  54.7 2.4 add.12
  57.0 22.7 %collective-permute-done.4 = bf16[512,2048]{1,0:T(8,128)(2,1)} collective-permute-done((bf16[512,2048]{1,0:T(8,128)(2,1)}, bf16[512,2048]{1,0:T(8,128)(2,1)}, u32[]{:S(2)}, u32[]{:S(2)}) %collective-permute-start.4) | collective-permute-done | bytes 2097184 | tf_op jit(solution)/shard_map/ppermute | solution.py:22
  79.7 20.0 %collective-permute-done = bf16[512,2048]{1,0:T(8,128)(2,1)} collective-permute-done((bf16[512,2048]{1,0:T(8,128)(2,1)}, bf16[512,2048]{1,0:T(8,128)(2,1)}, u32[]{:S(2)}, u32[]{:S(2)}) %collective-permute-start) | collective-permute-done | bytes 2097184 | tf_op jit(solution)/shard_map/ppermute | solution.py:22
  99.7 25.2 %collective-permute-done.5 = bf16[512,2048]{1,0:T(8,128)(2,1)} collective-permute-done((bf16[512,2048]{1,0:T(8,128)(2,1)}, bf16[512,2048]{1,0:T(8,128)(2,1)}, u32[]{:S(2)}, u32[]{:S(2)}) %collective-permute-start.5) | collective-permute-done | bytes 2097184 | tf_op jit(solution)/shard_map/ppermute | solution.py:22
  125.0 12.8 %multiply_convert_fusion.2 = bf16[1024,2048]{1,0:T(8,128)(2,1)S(1)} fusion(bf16[512,2048]{1,0:T(8,128)(2,1)} %collective-permute-done.5, bf16[512,2048]{1,0:T(8,128)(2,1)} %collective-permute-done.4, bf16[512,2048]{1,0:T(8,128)(2,1)S(1)} %add.12, bf16[512,2048]{1,0:T(8,128)(2,1)} %collective-permute-done, pred[]{:T(512)S(6)} %eq.17, ...), kind=kOutput, calls=%fused_computation.34 | convolution fusion | flops 8673820672 | bytes 16777216 | tf_op jit(solution)/shard_map/dot_general | solution.py:66
  137.8 0.0 copy-start.2
  137.8 1.6 collective-permute-start.8
  139.4 0.1 slice.48
  139.5 0.8 collective-permute-start.11
  140.3 10.9 %collective-permute-start.6 = (bf16[1024,2048]{1,0:T(8,128)(2,1)S(1)}, bf16[1024,2048]{1,0:T(8,128)(2,1)}, u32[]{:S(2)}, u32[]{:S(2)}) collective-permute-start(bf16[1024,2048]{1,0:T(8,128)(2,1)S(1)} %multiply_convert_fusion.2), channel_id=1, source_target_pairs={{0,4},{1,5},{2,6},{3,7},{4,8},{5,9},{6,10},{7,11},{8,12},{9,13},{1... | collective-permute-start | bytes 12582920 | tf_op jit(solution)/shard_map/ppermute | solution.py:22
  151.2 0.1 slice.46
  151.3 0.8 collective-permute-start.9
  152.1 0.0 collective-permute-done.11
  152.1 1.3 collective-permute-start.12
  153.4 0.1 slice.44
  153.5 1.3 collective-permute-start.7
  154.8 0.0 collective-permute-done.9
  154.8 1.5 collective-permute-start.10
  156.3 63.9 %collective-permute-done.7 = bf16[208,2048]{1,0:T(8,128)(2,1)S(1)} collective-permute-done((bf16[208,2048]{1,0:T(8,128)(2,1)S(1)}, bf16[208,2048]{1,0:T(8,128)(2,1)S(1)}, u32[]{:S(2)}, u32[]{:S(2)}) %collective-permute-start.7) | collective-permute-done | bytes 852000 | tf_op jit(solution)/shard_map/ppermute | solution.py:22
  220.1 0.0 collective-permute-done.8
  220.1 1.1 slice_add_fusion.2
  221.2 5.3 %collective-permute-done.12 = bf16[400,2048]{1,0:T(8,128)(2,1)S(1)} collective-permute-done((bf16[400,2048]{1,0:T(8,128)(2,1)S(1)}, bf16[400,2048]{1,0:T(8,128)(2,1)S(1)}, u32[]{:S(2)}, u32[]{:S(2)}) %collective-permute-start.12) | collective-permute-done | bytes 1638432 | tf_op jit(solution)/shard_map/ppermute | solution.py:22
  226.5 0.2 slice_add_fusion.1
  226.7 55.8 %collective-permute-done.10 = bf16[416,2048]{1,0:T(8,128)(2,1)S(1)} collective-permute-done((bf16[416,2048]{1,0:T(8,128)(2,1)S(1)}, bf16[416,2048]{1,0:T(8,128)(2,1)S(1)}, u32[]{:S(2)}, u32[]{:S(2)}) %collective-permute-start.10) | collective-permute-done | bytes 1703968 | tf_op jit(solution)/shard_map/ppermute | solution.py:22
  282.6 0.2 slice_add_fusion
  282.7 0.0 copy-done.2
  282.7 0.0 collective-permute-done.6
  282.7 0.0 copy-start.1
  282.8 13.7 %fusion.33 = bf16[1,1024,2048]{2,1,0:T(8,128)(2,1)} fusion(bf16[1024,2048]{1,0:T(8,128)(2,1)} %copy-done.2, bf16[400,2048]{1,0:T(8,128)(2,1)S(1)} %slice_add_fusion.1, bf16[416,2048]{1,0:T(8,128)(2,1)S(1)} %slice_add_fusion, bf16[208,2048]{1,0:T(8,128)(2,1)} %slice_add_fusion.2, bf16[1024,2048]{1,0:T(8,128)(2,1)} %collective-permute-done.6, pred[]{:T(512)S(6)} %eq.17), kind=kOutput, calls=%fused_computation.39 | convolution fusion | flops 8665432064 | bytes 16777216 | tf_op jit(solution)/shard_map/dot_general | solution.py:66
  296.5 0.0 copy-done.1
  (1 shorter events, 0.0 us)
Async XLA Ops:
  0.0 0.9 copy-start
  0.0 5.8 %copy-start.3 = (bf16[2048,2048]{1,0:T(8,128)(2,1)S(1)}, bf16[2048,2048]{1,0:T(8,128)(2,1)}, u32[]{:S(2)}) copy-start(bf16[2048,2048]{1,0:T(8,128)(2,1)} %param.6) | copy-start | bytes 25165828
  11.5 3.9 %collective-permute-start.2 = (bf16[512,2048]{1,0:T(8,128)(2,1)}, bf16[512,2048]{1,0:T(8,128)(2,1)}, u32[]{:S(2)}, u32[]{:S(2)}) collective-permute-start(bf16[512,2048]{1,0:T(8,128)(2,1)} %multiply_convert_fusion.5), channel_id=1, source_target_pairs={{30,6},{31,7},{62,38},{63,39},{94,70},{95,71},{126,102},{127,103}} | collective-permute-start | bytes 6291464 | tf_op jit(solution)/shard_map/ppermute | solution.py:22
  13.5 41.2 %collective-permute-start.1 = (bf16[512,2048]{1,0:T(8,128)(2,1)}, bf16[512,2048]{1,0:T(8,128)(2,1)S(1)}, u32[]{:S(2)}, u32[]{:S(2)}) collective-permute-start(bf16[512,2048]{1,0:T(8,128)(2,1)} %multiply_convert_fusion.5), channel_id=1, source_target_pairs={{0,2},{1,3},{2,4},{3,5},{4,6},{5,7},{6,8},{7,9},{8,10},{9,11},{10,... | collective-permute-start | bytes 6291464 | tf_op jit(solution)/shard_map/ppermute | solution.py:22
  15.4 39.2 %collective-permute-start.3 = (bf16[512,2048]{1,0:T(8,128)(2,1)}, bf16[512,2048]{1,0:T(8,128)(2,1)}, u32[]{:S(2)}, u32[]{:S(2)}) collective-permute-start(bf16[512,2048]{1,0:T(8,128)(2,1)} %collective-permute-done.2), channel_id=1, source_target_pairs={{6,32},{7,33},{38,64},{39,65},{70,96},{71,97},{102,0},{103,1}} | collective-permute-start | bytes 6291464 | tf_op jit(solution)/shard_map/ppermute | solution.py:22
  23.3 56.5 %collective-permute-start.4 = (bf16[512,2048]{1,0:T(8,128)(2,1)}, bf16[512,2048]{1,0:T(8,128)(2,1)}, u32[]{:S(2)}, u32[]{:S(2)}) collective-permute-start(bf16[512,2048]{1,0:T(8,128)(2,1)} %multiply_convert_fusion.6), channel_id=1, source_target_pairs={{0,3},{1,2},{2,5},{3,4},{4,7},{5,6},{6,9},{7,8},{8,11},{9,10},{10,... | collective-permute-start | bytes 6291464 | tf_op jit(solution)/shard_map/ppermute | solution.py:22
  27.4 72.3 %collective-permute-start = (bf16[512,2048]{1,0:T(8,128)(2,1)}, bf16[512,2048]{1,0:T(8,128)(2,1)}, u32[]{:S(2)}, u32[]{:S(2)}) collective-permute-start(bf16[512,2048]{1,0:T(8,128)(2,1)} %multiply_convert_fusion.6), channel_id=1, source_target_pairs={{0,2},{1,3},{2,4},{3,5},{4,6},{5,7},{6,8},{7,9},{8,10},{9,11},{10,... | collective-permute-start | bytes 6291464 | tf_op jit(solution)/shard_map/ppermute | solution.py:22
  27.4 97.5 %collective-permute-start.5 = (bf16[512,2048]{1,0:T(8,128)(2,1)}, bf16[512,2048]{1,0:T(8,128)(2,1)}, u32[]{:S(2)}, u32[]{:S(2)}) collective-permute-start(bf16[512,2048]{1,0:T(8,128)(2,1)} %multiply_convert_fusion.5), channel_id=1, source_target_pairs={{0,3},{1,2},{2,5},{3,4},{4,7},{5,6},{6,9},{7,8},{8,11},{9,10},{10,... | collective-permute-start | bytes 6291464 | tf_op jit(solution)/shard_map/ppermute | solution.py:22
  137.8 144.9 %copy-start.2 = (bf16[1024,2048]{1,0:T(8,128)(2,1)}, bf16[1024,2048]{1,0:T(8,128)(2,1)S(1)}, u32[]{:S(2)}) copy-start(bf16[1024,2048]{1,0:T(8,128)(2,1)S(1)} %multiply_convert_fusion.2) | copy-start | bytes 12582916
  137.8 82.3 %collective-permute-start.8 = (bf16[1024,2048]{1,0:T(8,128)(2,1)S(1)}, bf16[1024,2048]{1,0:T(8,128)(2,1)S(1)}, u32[]{:S(2)}, u32[]{:S(2)}) collective-permute-start(bf16[1024,2048]{1,0:T(8,128)(2,1)S(1)} %multiply_convert_fusion.2), channel_id=1, source_target_pairs={{0,5},{1,4},{2,7},{3,6},{8,13},{9,12},{10,15},{11,14},{16,21},{17,... | collective-permute-start | bytes 12582920 | tf_op jit(solution)/shard_map/ppermute | solution.py:22
  139.5 12.6 %collective-permute-start.11 = (bf16[400,2048]{1,0:T(8,128)(2,1)S(1)}, bf16[400,2048]{1,0:T(8,128)(2,1)S(1)}, u32[]{:S(2)}, u32[]{:S(2)}) collective-permute-start(bf16[400,2048]{1,0:T(8,128)(2,1)S(1)} %slice.48), channel_id=1, source_target_pairs={{4,12},{5,13},{6,14},{7,15},{12,20},{13,21},{14,22},{15,23},{20,28... | collective-permute-start | bytes 4915208 | tf_op jit(solution)/shard_map/ppermute | solution.py:22
  140.3 142.5 %collective-permute-start.6 = (bf16[1024,2048]{1,0:T(8,128)(2,1)S(1)}, bf16[1024,2048]{1,0:T(8,128)(2,1)}, u32[]{:S(2)}, u32[]{:S(2)}) collective-permute-start(bf16[1024,2048]{1,0:T(8,128)(2,1)S(1)} %multiply_convert_fusion.2), channel_id=1, source_target_pairs={{0,4},{1,5},{2,6},{3,7},{4,8},{5,9},{6,10},{7,11},{8,12},{9,13},{1... | collective-permute-start | bytes 12582920 | tf_op jit(solution)/shard_map/ppermute | solution.py:22
  151.3 3.5 %collective-permute-start.9 = (bf16[416,2048]{1,0:T(8,128)(2,1)S(1)}, bf16[416,2048]{1,0:T(8,128)(2,1)S(1)}, u32[]{:S(2)}, u32[]{:S(2)}) collective-permute-start(bf16[416,2048]{1,0:T(8,128)(2,1)S(1)} %slice.46), channel_id=1, source_target_pairs={{4,12},{5,13},{6,14},{7,15},{12,20},{13,21},{14,22},{15,23},{20,28... | collective-permute-start | bytes 5111816 | tf_op jit(solution)/shard_map/ppermute | solution.py:22
  152.1 74.4 %collective-permute-start.12 = (bf16[400,2048]{1,0:T(8,128)(2,1)S(1)}, bf16[400,2048]{1,0:T(8,128)(2,1)S(1)}, u32[]{:S(2)}, u32[]{:S(2)}) collective-permute-start(bf16[400,2048]{1,0:T(8,128)(2,1)S(1)} %collective-permute-done.11), channel_id=1, source_target_pairs={{4,33},{5,32},{6,35},{7,34},{12,9},{13,8},{14,11},{15,10},{20,17},... | collective-permute-start | bytes 4915208 | tf_op jit(solution)/shard_map/ppermute | solution.py:22
  153.5 66.7 %collective-permute-start.7 = (bf16[208,2048]{1,0:T(8,128)(2,1)S(1)}, bf16[208,2048]{1,0:T(8,128)(2,1)S(1)}, u32[]{:S(2)}, u32[]{:S(2)}) collective-permute-start(bf16[208,2048]{1,0:T(8,128)(2,1)S(1)} %slice.44), channel_id=1, source_target_pairs={{4,9},{5,8},{6,11},{7,10},{12,17},{13,16},{14,19},{15,18},{20,25},... | collective-permute-start | bytes 2555912 | tf_op jit(solution)/shard_map/ppermute | solution.py:22
  154.8 127.8 %collective-permute-start.10 = (bf16[416,2048]{1,0:T(8,128)(2,1)S(1)}, bf16[416,2048]{1,0:T(8,128)(2,1)S(1)}, u32[]{:S(2)}, u32[]{:S(2)}) collective-permute-start(bf16[416,2048]{1,0:T(8,128)(2,1)S(1)} %collective-permute-done.9), channel_id=1, source_target_pairs={{4,33},{5,32},{6,35},{7,34},{12,9},{13,8},{14,11},{15,10},{20,17},... | collective-permute-start | bytes 5111816 | tf_op jit(solution)/shard_map/ppermute | solution.py:22
  282.7 13.7 %copy-start.1 = (f32[16,2048]{1,0:T(8,128)S(1)}, f32[16,2048]{1,0:T(8,128)}, u32[]{:S(2)}) copy-start(f32[16,2048]{1,0:T(8,128)} %param.7) | copy-start | bytes 393220

commit v10 on v8

--- a/solution.py
+++ b/solution.py
@@ -6,7 +6,6 @@
 from jax.sharding import PartitionSpec as P
 
 LEVELS = 2
-DIRECT_ROWS = 96
 
 
 def sent(value, route):
@@ -41,12 +40,14 @@
     return ((t + 4) % n, r)
 
 
-def ring_first_exit(t, r, n, m):
-    if y_low(t) != 1:
-        return None
-    if ring_of(t) == 0:
-        return ((t + 14) % n, 1 - r)
-    return ((t - 2) % n, 1 - r)
+def handed_on(row_offset):
+    def route(t, r, n, m):
+        if y_low(t) != 1:
+            return None
+        if ring_of(t) == 0:
+            return ((t + 14) % n, (r + row_offset) % m)
+        return ((t - 2) % n, (r + row_offset) % m)
+    return route
 
 
 def when_low(low, route):
@@ -99,15 +100,14 @@
     earlier = natural(own_rows, other_rows, row)
     chunks = [level_product(chunk, earlier, norm_scale) for chunk in chunks]
 
-    own_rows = []
-    other_rows = []
-    for chunk in chunks:
-        own_rows.append(sent(chunk, direct(2, 0)))
-        other_near = sent(chunk, when_low(0, direct(2, 1)))
-        other_rows.append(sent(chunk[:DIRECT_ROWS], when_low(1, direct(2, 1))) + other_near[:DIRECT_ROWS])
-        ring_first = sent(chunk[DIRECT_ROWS:], ring_first_hop)
-        other_rows.append(sent(ring_first, ring_first_exit) + other_near[DIRECT_ROWS:])
-    earlier = natural(own_rows, other_rows, row)
+    straight, handed = chunks
+    crossed = sent(handed, ring_first_hop)
+    same_straight = sent(straight, direct(2, 0))
+    other_straight = sent(straight, direct(2, 1))
+    onward = jnp.where(lax.axis_index("tm") // 2 % 2 == 0, handed, crossed)
+    same_handed = sent(onward, lambda t, r, n, m: direct(2, 0)(t, r, n, m) if y_low(t) == 0 else handed_on(0)(t, r, n, m))
+    other_handed = sent(onward, lambda t, r, n, m: direct(2, 1)(t, r, n, m) if y_low(t) == 0 else handed_on(1)(t, r, n, m))
+    earlier = natural([same_straight, same_handed], [other_straight, other_handed], row)
     current = level_product(jnp.concatenate(chunks, axis=0), earlier, norm_scale)
     return current[None]
 

time: 323 us -> 306 us (0.947)
  starting transfers between devices: 98.2 us -> 83.9 us
  matrix products: 35.8 us -> 40.2 us
  local copies, waits for them, and re-layouts: 4.4 us -> 0.12 us
    ppermute x16 -> x11, starting transfers between devices: 98.2 us -> 83.9 us  [sent(): return lax.ppermute(value, ('tm', 'row'), pairs)]
    dot_general x3, matrix products: 23.1 us -> 27.4 us  [level_product(): total = jnp.dot(later, earlier, preferred_element_type=jnp.float32)]
    unnamed x11 -> x6, local copies, waits for them, and re-layouts: 3.86 us -> 0.1 us
    ppermute x16 -> x11, waiting for transfers between devices: 166 us -> 166 us  [sent(): return lax.ppermute(value, ('tm', 'row'), pairs)]
  transfers between devices with their start and end apart: 16 -> 11, of which waited for: 7 -> 8; matrix products, arithmetic and copies ran while one was open for 5% -> 6% of each run, Pallas kernels for 0% -> 0%
where the time goes in v10:
time: 306 us; the launch traced here: 304 us
  waiting for transfers between devices  166 us (54%)
  starting transfers between devices  83.9 us (27%)
  matrix products  40.2 us (13%)
  other arithmetic  13.7 us (4%)
    ppermute x11, waiting for transfers between devices, sent(): return lax.ppermute(value, ('tm', 'row'), pairs)  166 us
    ppermute x11, starting transfers between devices, sent(): return lax.ppermute(value, ('tm', 'row'), pairs)  83.9 us
    dot_general x3, matrix products, level_product(): total = jnp.dot(later, earlier, preferred_element_type=jnp.float32)  27.4 us
    dot_general x2, matrix products, shards(): jnp.dot(left_factor[c * chunk_rows:(c + 1) * chunk_rows], right_factor, p...  11.6 us
    select_n x1, other arithmetic, natural(): jnp.where(row == 0, jnp.concatenate(own_rows + other_rows, axis=0), jnp.c...  6.75 us
  transfers between devices with their start and end apart: 11, of which 8 were waited for; matrix products, arithmetic and copies ran while one was open for 6% of the time, Pallas kernels for 0%

profile of v10, /device:TPU:96, one launch (start us, length us, event | category | flops | bytes accessed | tf_op | source)
XLA Modules:
  0.0 304.0 jit_solution(11683847311047528109)
XLA Ops:
  0.0 0.0 copy-start
  0.0 0.0 copy-start.2
  0.0 0.8 multiply_bitcast_fusion
  0.8 0.1 copy-done
  0.9 1.3 fusion.24
  2.2 3.5 %fusion.14 = bf16[1024,2048]{1,0:T(8,128)(2,1)S(1)} fusion(bf16[1,1024,2048]{2,1,0:T(8,128)(2,1)} %param.5, f32[2048]{0:T(1024)S(1)} %bitcast.15), kind=kLoop, calls=%fused_computation.18 | loop fusion | flops 6291456 | bytes 8396800 | tf_op jit(solution)/shard_map/convert_element_type | solution.py:85
  5.8 0.0 copy-done.2
  5.8 5.8 %multiply_convert_fusion.6 = bf16[512,2048]{1,0:T(8,128)(2,1)} fusion(bf16[2048,2048]{1,0:T(8,128)(2,1)S(1)} %copy-done.2, f32[2048]{0:T(1024)S(1)} %bitcast.16, bf16[1024,2048]{1,0:T(8,128)(2,1)S(1)} %fusion.14), kind=kOutput, calls=%fused_computation.29 | convolution fusion | flops 4309647360 | bytes 12591104 | tf_op jit(solution)/shard_map/dot_general | solution.py:89
  11.6 2.0 collective-permute-start.2
  13.6 1.9 collective-permute-start.1
  15.5 0.0 collective-permute-done.2
  15.5 2.0 collective-permute-start.3
  17.5 5.8 %multiply_convert_fusion.7 = bf16[512,2048]{1,0:T(8,128)(2,1)} fusion(bf16[2048,2048]{1,0:T(8,128)(2,1)S(1)} %copy-done.2, f32[2048]{0:T(1024)S(1)} %bitcast.17, bf16[1024,2048]{1,0:T(8,128)(2,1)S(1)} %fusion.14), kind=kOutput, calls=%fused_computation.30 | convolution fusion | flops 4309647360 | bytes 12591104 | tf_op jit(solution)/shard_map/dot_general | solution.py:89
  23.3 4.2 %collective-permute-start.4 = (bf16[512,2048]{1,0:T(8,128)(2,1)}, bf16[512,2048]{1,0:T(8,128)(2,1)}, u32[]{:S(2)}, u32[]{:S(2)}) collective-permute-start(bf16[512,2048]{1,0:T(8,128)(2,1)} %multiply_convert_fusion.7), channel_id=1, source_target_pairs={{0,3},{1,2},{2,5},{3,4},{4,7},{5,6},{6,9},{7,8},{8,11},{9,10},{10,... | collective-permute-start | bytes 6291464 | tf_op jit(solution)/shard_map/ppermute | solution.py:20
  27.5 0.0 collective-permute-start
  27.5 21.3 %collective-permute-start.5 = (bf16[512,2048]{1,0:T(8,128)(2,1)}, bf16[512,2048]{1,0:T(8,128)(2,1)}, u32[]{:S(2)}, u32[]{:S(2)}) collective-permute-start(bf16[512,2048]{1,0:T(8,128)(2,1)} %multiply_convert_fusion.6), channel_id=1, source_target_pairs={{0,3},{1,2},{2,5},{3,4},{4,7},{5,6},{6,9},{7,8},{8,11},{9,10},{10,... | collective-permute-start | bytes 6291464 | tf_op jit(solution)/shard_map/ppermute | solution.py:20
  48.8 6.0 %collective-permute-done.1 = bf16[512,2048]{1,0:T(8,128)(2,1)S(1)} collective-permute-done((bf16[512,2048]{1,0:T(8,128)(2,1)}, bf16[512,2048]{1,0:T(8,128)(2,1)S(1)}, u32[]{:S(2)}, u32[]{:S(2)}) %collective-permute-start.1) | collective-permute-done | bytes 2097184 | tf_op jit(solution)/shard_map/ppermute | solution.py:20
  54.8 0.0 collective-permute-done.3
  54.8 2.4 add.8
  57.1 22.6 %collective-permute-done.4 = bf16[512,2048]{1,0:T(8,128)(2,1)} collective-permute-done((bf16[512,2048]{1,0:T(8,128)(2,1)}, bf16[512,2048]{1,0:T(8,128)(2,1)}, u32[]{:S(2)}, u32[]{:S(2)}) %collective-permute-start.4) | collective-permute-done | bytes 2097184 | tf_op jit(solution)/shard_map/ppermute | solution.py:20
  79.7 20.1 %collective-permute-done = bf16[512,2048]{1,0:T(8,128)(2,1)} collective-permute-done((bf16[512,2048]{1,0:T(8,128)(2,1)}, bf16[512,2048]{1,0:T(8,128)(2,1)}, u32[]{:S(2)}, u32[]{:S(2)}) %collective-permute-start) | collective-permute-done | bytes 2097184 | tf_op jit(solution)/shard_map/ppermute | solution.py:20
  99.8 25.2 %collective-permute-done.5 = bf16[512,2048]{1,0:T(8,128)(2,1)} collective-permute-done((bf16[512,2048]{1,0:T(8,128)(2,1)}, bf16[512,2048]{1,0:T(8,128)(2,1)}, u32[]{:S(2)}, u32[]{:S(2)}) %collective-permute-start.5) | collective-permute-done | bytes 2097184 | tf_op jit(solution)/shard_map/ppermute | solution.py:20
  125.0 6.7 %maximum_select_fusion = bf16[2048,2048]{1,0:T(8,128)(2,1)S(1)} fusion(bf16[512,2048]{1,0:T(8,128)(2,1)} %collective-permute-done.5, bf16[512,2048]{1,0:T(8,128)(2,1)} %collective-permute-done.4, bf16[512,2048]{1,0:T(8,128)(2,1)S(1)} %add.8, bf16[512,2048]{1,0:T(8,128)(2,1)} %collective-permute-done, pred[]{:T(512)S(6)} %eq.22), kind=kLoop, calls=%fused_computation.1 | loop fusion | flops 71303168 | bytes 16777216 | tf_op jit(solution)/shard_map/jit(_where)/select_n | solution.py:58
  131.8 0.0 copy-start.1
  131.8 7.9 %multiply_convert_fusion.4 = bf16[512,2048]{1,0:T(8,128)(2,1)S(1)} fusion(bf16[512,2048]{1,0:T(8,128)(2,1)} %multiply_convert_fusion.6, bf16[2048,2048]{1,0:T(8,128)(2,1)S(1)} %maximum_select_fusion), kind=kOutput, calls=%fused_computation.27 | convolution fusion | flops 4297064448 | bytes 12582912 | tf_op jit(solution)/shard_map/dot_general | solution.py:66
  139.7 0.0 copy-done.1
  139.7 2.0 collective-permute-start.7
  141.7 8.5 %multiply_convert_fusion.5 = bf16[512,2048]{1,0:T(8,128)(2,1)S(1)} fusion(bf16[512,2048]{1,0:T(8,128)(2,1)} %multiply_convert_fusion.7, bf16[2048,2048]{1,0:T(8,128)(2,1)} %copy-done.1), kind=kOutput, calls=%fused_computation.28 | convolution fusion | flops 4297064448 | bytes 12582912 | tf_op jit(solution)/shard_map/dot_general | solution.py:66
  150.2 11.9 %collective-permute-start.9 = (bf16[512,2048]{1,0:T(8,128)(2,1)S(1)}, bf16[512,2048]{1,0:T(8,128)(2,1)S(1)}, u32[]{:S(2)}, u32[]{:S(2)}) collective-permute-start(bf16[512,2048]{1,0:T(8,128)(2,1)S(1)} %multiply_convert_fusion.5), channel_id=1, source_target_pairs={{0,5},{1,4},{2,7},{3,6},{4,9},{5,8},{6,11},{7,10},{8,13},{9,12},{1... | collective-permute-start | bytes 6291464 | tf_op jit(solution)/shard_map/ppermute | solution.py:20
  162.1 3.7 %collective-permute-start.6 = (bf16[512,2048]{1,0:T(8,128)(2,1)S(1)}, bf16[512,2048]{1,0:T(8,128)(2,1)S(1)}, u32[]{:S(2)}, u32[]{:S(2)}) collective-permute-start(bf16[512,2048]{1,0:T(8,128)(2,1)S(1)} %multiply_convert_fusion.5), channel_id=1, source_target_pairs={{0,4},{1,5},{2,6},{3,7},{4,8},{5,9},{6,10},{7,11},{8,12},{9,13},{1... | collective-permute-start | bytes 6291464 | tf_op jit(solution)/shard_map/ppermute | solution.py:20
  165.8 0.0 collective-permute-done.7
  165.8 0.2 broadcast_select_fusion
  166.0 34.9 %collective-permute-start.10 = (bf16[512,2048]{1,0:T(8,128)(2,1)S(1)}, bf16[512,2048]{1,0:T(8,128)(2,1)S(1)}, u32[]{:S(2)}, u32[]{:S(2)}) collective-permute-start(bf16[512,2048]{1,0:T(8,128)(2,1)S(1)} %broadcast_select_fusion), channel_id=1, source_target_pairs={{0,5},{1,4},{2,7},{3,6},{4,33},{5,32},{6,35},{7,34},{8,13},{9,12},... | collective-permute-start | bytes 6291464 | tf_op jit(solution)/shard_map/ppermute | solution.py:20
  201.0 0.0 collective-permute-start.8
  201.0 11.4 %collective-permute-done.9 = bf16[512,2048]{1,0:T(8,128)(2,1)S(1)} collective-permute-done((bf16[512,2048]{1,0:T(8,128)(2,1)S(1)}, bf16[512,2048]{1,0:T(8,128)(2,1)S(1)}, u32[]{:S(2)}, u32[]{:S(2)}) %collective-permute-start.9) | collective-permute-done | bytes 2097184 | tf_op jit(solution)/shard_map/ppermute | solution.py:20
  212.4 33.7 %collective-permute-done.6 = bf16[512,2048]{1,0:T(8,128)(2,1)S(1)} collective-permute-done((bf16[512,2048]{1,0:T(8,128)(2,1)S(1)}, bf16[512,2048]{1,0:T(8,128)(2,1)S(1)}, u32[]{:S(2)}, u32[]{:S(2)}) %collective-permute-start.6) | collective-permute-done | bytes 2097184 | tf_op jit(solution)/shard_map/ppermute | solution.py:20
  246.1 9.7 %collective-permute-done.10 = bf16[512,2048]{1,0:T(8,128)(2,1)S(1)} collective-permute-done((bf16[512,2048]{1,0:T(8,128)(2,1)S(1)}, bf16[512,2048]{1,0:T(8,128)(2,1)S(1)}, u32[]{:S(2)}, u32[]{:S(2)}) %collective-permute-start.10) | collective-permute-done | bytes 2097184 | tf_op jit(solution)/shard_map/ppermute | solution.py:20
  255.8 37.2 %collective-permute-done.8 = bf16[512,2048]{1,0:T(8,128)(2,1)S(1)} collective-permute-done((bf16[512,2048]{1,0:T(8,128)(2,1)S(1)}, bf16[512,2048]{1,0:T(8,128)(2,1)S(1)}, u32[]{:S(2)}, u32[]{:S(2)}) %collective-permute-start.8) | collective-permute-done | bytes 2097184 | tf_op jit(solution)/shard_map/ppermute | solution.py:20
  293.0 11.0 %fusion.18 = bf16[1,1024,2048]{2,1,0:T(8,128)(2,1)} fusion(bf16[512,2048]{1,0:T(8,128)(2,1)S(1)} %collective-permute-done.10, bf16[512,2048]{1,0:T(8,128)(2,1)S(1)} %collective-permute-done.9, bf16[512,2048]{1,0:T(8,128)(2,1)S(1)} %collective-permute-done.8, bf16[512,2048]{1,0:T(8,128)(2,1)S(1)} %collective-permute-done.6, pred[]{:T(512)S(6)} %eq.22, ...), kind=kOutput, calls=%fused_computation.23 | convolution fusion | flops 8673820672 | bytes 16777216 | tf_op jit(solution)/shard_map/dot_general | solution.py:66
  (1 shorter events, 0.0 us)
Async XLA Ops:
  0.0 0.9 copy-start
  0.0 5.8 %copy-start.2 = (bf16[2048,2048]{1,0:T(8,128)(2,1)S(1)}, bf16[2048,2048]{1,0:T(8,128)(2,1)}, u32[]{:S(2)}) copy-start(bf16[2048,2048]{1,0:T(8,128)(2,1)} %param.6) | copy-start | bytes 25165828
  11.6 3.9 %collective-permute-start.2 = (bf16[512,2048]{1,0:T(8,128)(2,1)}, bf16[512,2048]{1,0:T(8,128)(2,1)}, u32[]{:S(2)}, u32[]{:S(2)}) collective-permute-start(bf16[512,2048]{1,0:T(8,128)(2,1)} %multiply_convert_fusion.6), channel_id=1, source_target_pairs={{30,6},{31,7},{62,38},{63,39},{94,70},{95,71},{126,102},{127,103}} | collective-permute-start | bytes 6291464 | tf_op jit(solution)/shard_map/ppermute | solution.py:20
  13.6 41.2 %collective-permute-start.1 = (bf16[512,2048]{1,0:T(8,128)(2,1)}, bf16[512,2048]{1,0:T(8,128)(2,1)S(1)}, u32[]{:S(2)}, u32[]{:S(2)}) collective-permute-start(bf16[512,2048]{1,0:T(8,128)(2,1)} %multiply_convert_fusion.6), channel_id=1, source_target_pairs={{0,2},{1,3},{2,4},{3,5},{4,6},{5,7},{6,8},{7,9},{8,10},{9,11},{10,... | collective-permute-start | bytes 6291464 | tf_op jit(solution)/shard_map/ppermute | solution.py:20
  15.5 39.3 %collective-permute-start.3 = (bf16[512,2048]{1,0:T(8,128)(2,1)}, bf16[512,2048]{1,0:T(8,128)(2,1)}, u32[]{:S(2)}, u32[]{:S(2)}) collective-permute-start(bf16[512,2048]{1,0:T(8,128)(2,1)} %collective-permute-done.2), channel_id=1, source_target_pairs={{6,32},{7,33},{38,64},{39,65},{70,96},{71,97},{102,0},{103,1}} | collective-permute-start | bytes 6291464 | tf_op jit(solution)/shard_map/ppermute | solution.py:20
  23.3 56.5 %collective-permute-start.4 = (bf16[512,2048]{1,0:T(8,128)(2,1)}, bf16[512,2048]{1,0:T(8,128)(2,1)}, u32[]{:S(2)}, u32[]{:S(2)}) collective-permute-start(bf16[512,2048]{1,0:T(8,128)(2,1)} %multiply_convert_fusion.7), channel_id=1, source_target_pairs={{0,3},{1,2},{2,5},{3,4},{4,7},{5,6},{6,9},{7,8},{8,11},{9,10},{10,... | collective-permute-start | bytes 6291464 | tf_op jit(solution)/shard_map/ppermute | solution.py:20
  27.5 72.3 %collective-permute-start = (bf16[512,2048]{1,0:T(8,128)(2,1)}, bf16[512,2048]{1,0:T(8,128)(2,1)}, u32[]{:S(2)}, u32[]{:S(2)}) collective-permute-start(bf16[512,2048]{1,0:T(8,128)(2,1)} %multiply_convert_fusion.7), channel_id=1, source_target_pairs={{0,2},{1,3},{2,4},{3,5},{4,6},{5,7},{6,8},{7,9},{8,10},{9,11},{10,... | collective-permute-start | bytes 6291464 | tf_op jit(solution)/shard_map/ppermute | solution.py:20
  27.5 97.6 %collective-permute-start.5 = (bf16[512,2048]{1,0:T(8,128)(2,1)}, bf16[512,2048]{1,0:T(8,128)(2,1)}, u32[]{:S(2)}, u32[]{:S(2)}) collective-permute-start(bf16[512,2048]{1,0:T(8,128)(2,1)} %multiply_convert_fusion.6), channel_id=1, source_target_pairs={{0,3},{1,2},{2,5},{3,4},{4,7},{5,6},{6,9},{7,8},{8,11},{9,10},{10,... | collective-permute-start | bytes 6291464 | tf_op jit(solution)/shard_map/ppermute | solution.py:20
  131.8 7.9 %copy-start.1 = (bf16[2048,2048]{1,0:T(8,128)(2,1)}, bf16[2048,2048]{1,0:T(8,128)(2,1)S(1)}, u32[]{:S(2)}) copy-start(bf16[2048,2048]{1,0:T(8,128)(2,1)S(1)} %maximum_select_fusion) | copy-start | bytes 25165828
  139.7 26.1 %collective-permute-start.7 = (bf16[512,2048]{1,0:T(8,128)(2,1)S(1)}, bf16[512,2048]{1,0:T(8,128)(2,1)}, u32[]{:S(2)}, u32[]{:S(2)}) collective-permute-start(bf16[512,2048]{1,0:T(8,128)(2,1)S(1)} %multiply_convert_fusion.4), channel_id=1, source_target_pairs={{4,12},{5,13},{6,14},{7,15},{12,20},{13,21},{14,22},{15,23},{20,28... | collective-permute-start | bytes 6291464 | tf_op jit(solution)/shard_map/ppermute | solution.py:20
  150.2 62.2 %collective-permute-start.9 = (bf16[512,2048]{1,0:T(8,128)(2,1)S(1)}, bf16[512,2048]{1,0:T(8,128)(2,1)S(1)}, u32[]{:S(2)}, u32[]{:S(2)}) collective-permute-start(bf16[512,2048]{1,0:T(8,128)(2,1)S(1)} %multiply_convert_fusion.5), channel_id=1, source_target_pairs={{0,5},{1,4},{2,7},{3,6},{4,9},{5,8},{6,11},{7,10},{8,13},{9,12},{1... | collective-permute-start | bytes 6291464 | tf_op jit(solution)/shard_map/ppermute | solution.py:20
  162.1 84.0 %collective-permute-start.6 = (bf16[512,2048]{1,0:T(8,128)(2,1)S(1)}, bf16[512,2048]{1,0:T(8,128)(2,1)S(1)}, u32[]{:S(2)}, u32[]{:S(2)}) collective-permute-start(bf16[512,2048]{1,0:T(8,128)(2,1)S(1)} %multiply_convert_fusion.5), channel_id=1, source_target_pairs={{0,4},{1,5},{2,6},{3,7},{4,8},{5,9},{6,10},{7,11},{8,12},{9,13},{1... | collective-permute-start | bytes 6291464 | tf_op jit(solution)/shard_map/ppermute | solution.py:20
  166.0 89.8 %collective-permute-start.10 = (bf16[512,2048]{1,0:T(8,128)(2,1)S(1)}, bf16[512,2048]{1,0:T(8,128)(2,1)S(1)}, u32[]{:S(2)}, u32[]{:S(2)}) collective-permute-start(bf16[512,2048]{1,0:T(8,128)(2,1)S(1)} %broadcast_select_fusion), channel_id=1, source_target_pairs={{0,5},{1,4},{2,7},{3,6},{4,33},{5,32},{6,35},{7,34},{8,13},{9,12},... | collective-permute-start | bytes 6291464 | tf_op jit(solution)/shard_map/ppermute | solution.py:20
  201.0 92.0 %collective-permute-start.8 = (bf16[512,2048]{1,0:T(8,128)(2,1)S(1)}, bf16[512,2048]{1,0:T(8,128)(2,1)S(1)}, u32[]{:S(2)}, u32[]{:S(2)}) collective-permute-start(bf16[512,2048]{1,0:T(8,128)(2,1)S(1)} %broadcast_select_fusion), channel_id=1, source_target_pairs={{0,4},{1,5},{2,6},{3,7},{4,32},{5,33},{6,34},{7,35},{8,12},{9,13},... | collective-permute-start | bytes 6291464 | tf_op jit(solution)/shard_map/ppermute | solution.py:20

commit v11 on v9

--- a/solution.py
+++ b/solution.py
@@ -6,8 +6,7 @@
 from jax.sharding import PartitionSpec as P
 
 LEVELS = 2
-DIRECT_ROWS = 208
-RELAY_ROWS = (416, 400)
+RELAY_ROWS = (512, 512)
 
 
 def sent(value, route):
@@ -102,8 +101,8 @@
 
     same = sent(current, direct(2, 0))
     other_near = sent(current, when_low(0, direct(2, 1)))
-    other_rows = [sent(current[:DIRECT_ROWS], when_low(1, direct(2, 1))) + other_near[:DIRECT_ROWS]]
-    begin = DIRECT_ROWS
+    other_rows = []
+    begin = 0
     for size in RELAY_ROWS:
         ring_first = sent(current[begin:begin + size], ring_first_hop)
         other_rows.append(sent(ring_first, ring_first_exit) + other_near[begin:begin + size])

time: 300 us -> 314 us (1.047)
  waiting for transfers between devices: 199 us -> 205 us
  local copies, waits for them, and re-layouts: 0.4 us -> 3.7 us
    ppermute x13 -> x12, waiting for transfers between devices: 199 us -> 205 us  [sent(): return lax.ppermute(value, ('tm', 'row'), pairs)]
    unnamed x8, local copies, waits for them, and re-layouts: 0.11 us -> 3.37 us
    ppermute x13 -> x12, starting transfers between devices: 49.5 us -> 52 us  [sent(): return lax.ppermute(value, ('tm', 'row'), pairs)]
  transfers between devices with their start and end apart: 13 -> 12, of which waited for: 7 -> 6; matrix products, arithmetic and copies ran while one was open for 3% -> 3% of each run, Pallas kernels for 0% -> 0%
where the time goes in v11:
time: 314 us; the launch traced here: 309 us
  waiting for transfers between devices  205 us (65%)
  starting transfers between devices  52 us (17%)
  matrix products  39.3 us (13%)
  other arithmetic  8.89 us (3%)
  local copies, waits for them, and re-layouts  3.7 us (1%)
    ppermute x12, waiting for transfers between devices, sent(): return lax.ppermute(value, ('tm', 'row'), pairs)  205 us
    ppermute x12, starting transfers between devices, sent(): return lax.ppermute(value, ('tm', 'row'), pairs)  52 us
    dot_general x2, matrix products, level_product(): total = jnp.dot(later, earlier, preferred_element_type=jnp.float32)  27 us
    dot_general x2, matrix products, shards(): jnp.dot(left_factor[c * chunk_rows:(c + 1) * chunk_rows], right_factor, p...  11.4 us
  transfers between devices with their start and end apart: 12, of which 6 were waited for; matrix products, arithmetic and copies ran while one was open for 3% of the time, Pallas kernels for 0%

profile of v11, /device:TPU:96, one launch (start us, length us, event | category | flops | bytes accessed | tf_op | source)
XLA Modules:
  0.0 309.4 jit_solution(12084720368244852943)
XLA Ops:
  0.0 0.0 copy-start
  0.0 0.7 multiply_bitcast_fusion
  0.7 0.2 copy-done
  0.9 0.9 fusion.35
  1.8 0.0 copy-start.2
  1.8 3.4 %fusion.24 = bf16[1024,2048]{1,0:T(8,128)(2,1)S(1)} fusion(bf16[1,1024,2048]{2,1,0:T(8,128)(2,1)} %param.5, f32[2048]{0:T(1024)S(1)} %bitcast.12), kind=kLoop, calls=%fused_computation.28 | loop fusion | flops 6291456 | bytes 8396800 | tf_op jit(solution)/shard_map/convert_element_type | solution.py:84
  5.3 1.2 copy-done.2
  6.5 5.7 %multiply_convert_fusion.5 = bf16[512,2048]{1,0:T(8,128)(2,1)} fusion(bf16[2048,2048]{1,0:T(8,128)(2,1)S(1)} %copy-done.2, f32[2048]{0:T(1024)S(1)} %bitcast.13, bf16[1024,2048]{1,0:T(8,128)(2,1)S(1)} %fusion.24), kind=kOutput, calls=%fused_computation.39 | convolution fusion | flops 4309647360 | bytes 12591104 | tf_op jit(solution)/shard_map/dot_general | solution.py:88
  12.2 2.0 collective-permute-start.2
  14.2 1.9 collective-permute-start.1
  16.1 0.0 collective-permute-done.2
  16.1 2.1 collective-permute-start.3
  18.2 5.7 %multiply_convert_fusion.6 = bf16[512,2048]{1,0:T(8,128)(2,1)} fusion(bf16[2048,2048]{1,0:T(8,128)(2,1)S(1)} %copy-done.2, f32[2048]{0:T(1024)S(1)} %bitcast.14, bf16[1024,2048]{1,0:T(8,128)(2,1)S(1)} %fusion.24), kind=kOutput, calls=%fused_computation.40 | convolution fusion | flops 4309647360 | bytes 12591104 | tf_op jit(solution)/shard_map/dot_general | solution.py:88
  23.9 4.2 %collective-permute-start.4 = (bf16[512,2048]{1,0:T(8,128)(2,1)}, bf16[512,2048]{1,0:T(8,128)(2,1)}, u32[]{:S(2)}, u32[]{:S(2)}) collective-permute-start(bf16[512,2048]{1,0:T(8,128)(2,1)} %multiply_convert_fusion.6), channel_id=1, source_target_pairs={{0,3},{1,2},{2,5},{3,4},{4,7},{5,6},{6,9},{7,8},{8,11},{9,10},{10,... | collective-permute-start | bytes 6291464 | tf_op jit(solution)/shard_map/ppermute | solution.py:21
  28.1 0.0 collective-permute-start
  28.1 21.3 %collective-permute-start.5 = (bf16[512,2048]{1,0:T(8,128)(2,1)}, bf16[512,2048]{1,0:T(8,128)(2,1)}, u32[]{:S(2)}, u32[]{:S(2)}) collective-permute-start(bf16[512,2048]{1,0:T(8,128)(2,1)} %multiply_convert_fusion.5), channel_id=1, source_target_pairs={{0,3},{1,2},{2,5},{3,4},{4,7},{5,6},{6,9},{7,8},{8,11},{9,10},{10,... | collective-permute-start | bytes 6291464 | tf_op jit(solution)/shard_map/ppermute | solution.py:21
  49.4 6.0 %collective-permute-done.1 = bf16[512,2048]{1,0:T(8,128)(2,1)S(1)} collective-permute-done((bf16[512,2048]{1,0:T(8,128)(2,1)}, bf16[512,2048]{1,0:T(8,128)(2,1)S(1)}, u32[]{:S(2)}, u32[]{:S(2)}) %collective-permute-start.1) | collective-permute-done | bytes 2097184 | tf_op jit(solution)/shard_map/ppermute | solution.py:21
  55.4 0.0 collective-permute-done.3
  55.4 2.4 add.9
  57.8 22.6 %collective-permute-done.4 = bf16[512,2048]{1,0:T(8,128)(2,1)} collective-permute-done((bf16[512,2048]{1,0:T(8,128)(2,1)}, bf16[512,2048]{1,0:T(8,128)(2,1)}, u32[]{:S(2)}, u32[]{:S(2)}) %collective-permute-start.4) | collective-permute-done | bytes 2097184 | tf_op jit(solution)/shard_map/ppermute | solution.py:21
  80.4 20.1 %collective-permute-done = bf16[512,2048]{1,0:T(8,128)(2,1)} collective-permute-done((bf16[512,2048]{1,0:T(8,128)(2,1)}, bf16[512,2048]{1,0:T(8,128)(2,1)}, u32[]{:S(2)}, u32[]{:S(2)}) %collective-permute-start) | collective-permute-done | bytes 2097184 | tf_op jit(solution)/shard_map/ppermute | solution.py:21
  100.4 25.2 %collective-permute-done.5 = bf16[512,2048]{1,0:T(8,128)(2,1)} collective-permute-done((bf16[512,2048]{1,0:T(8,128)(2,1)}, bf16[512,2048]{1,0:T(8,128)(2,1)}, u32[]{:S(2)}, u32[]{:S(2)}) %collective-permute-start.5) | collective-permute-done | bytes 2097184 | tf_op jit(solution)/shard_map/ppermute | solution.py:21
  125.7 12.9 %multiply_convert_fusion.2 = bf16[1024,2048]{1,0:T(8,128)(2,1)S(1)} fusion(bf16[512,2048]{1,0:T(8,128)(2,1)} %collective-permute-done.5, bf16[512,2048]{1,0:T(8,128)(2,1)} %collective-permute-done.4, bf16[512,2048]{1,0:T(8,128)(2,1)S(1)} %add.9, bf16[512,2048]{1,0:T(8,128)(2,1)} %collective-permute-done, pred[]{:T(512)S(6)} %eq.17, ...), kind=kOutput, calls=%fused_computation.30 | convolution fusion | flops 8673820672 | bytes 16777216 | tf_op jit(solution)/shard_map/dot_general | solution.py:65
  138.6 0.3 fusion.43
  138.9 0.8 collective-permute-start.7
  139.7 0.8 collective-permute-start.10
  140.5 16.1 %collective-permute-start.9 = (bf16[1024,2048]{1,0:T(8,128)(2,1)S(1)}, bf16[1024,2048]{1,0:T(8,128)(2,1)S(1)}, u32[]{:S(2)}, u32[]{:S(2)}) collective-permute-start(bf16[1024,2048]{1,0:T(8,128)(2,1)S(1)} %multiply_convert_fusion.2), channel_id=1, source_target_pairs={{0,5},{1,4},{2,7},{3,6},{8,13},{9,12},{10,15},{11,14},{16,21},{17,... | collective-permute-start | bytes 12582920 | tf_op jit(solution)/shard_map/ppermute | solution.py:21
  156.6 0.1 collective-permute-start.6
  156.7 0.0 collective-permute-done.7
  156.7 1.3 collective-permute-start.8
  158.0 0.0 collective-permute-done.10
  158.0 1.5 collective-permute-start.11
  159.5 86.5 %collective-permute-done.8 = bf16[512,2048]{1,0:T(8,128)(2,1)S(1)} collective-permute-done((bf16[512,2048]{1,0:T(8,128)(2,1)S(1)}, bf16[512,2048]{1,0:T(8,128)(2,1)S(1)}, u32[]{:S(2)}, u32[]{:S(2)}) %collective-permute-start.8) | collective-permute-done | bytes 2097184 | tf_op jit(solution)/shard_map/ppermute | solution.py:21
  246.0 44.9 %collective-permute-done.11 = bf16[512,2048]{1,0:T(8,128)(2,1)S(1)} collective-permute-done((bf16[512,2048]{1,0:T(8,128)(2,1)S(1)}, bf16[512,2048]{1,0:T(8,128)(2,1)S(1)}, u32[]{:S(2)}, u32[]{:S(2)}) %collective-permute-start.11) | collective-permute-done | bytes 2097184 | tf_op jit(solution)/shard_map/ppermute | solution.py:21
  290.9 0.0 collective-permute-done.9
  290.9 2.4 slice_add_fusion.1
  293.3 0.0 collective-permute-done.6
  293.3 0.0 copy-start.3
  293.3 2.0 copy-done.3
  295.3 0.0 copy-start.1
  295.3 14.1 %fusion.29 = bf16[1,1024,2048]{2,1,0:T(8,128)(2,1)} fusion(bf16[1024,2048]{1,0:T(8,128)(2,1)S(1)} %multiply_convert_fusion.2, bf16[512,2048]{1,0:T(8,128)(2,1)} %get-tuple-element.6, bf16[512,2048]{1,0:T(8,128)(2,1)} %get-tuple-element.5, bf16[1024,2048]{1,0:T(8,128)(2,1)} %copy-done.3, pred[]{:T(512)S(6)} %eq.17), kind=kOutput, calls=%fused_computation.35 | convolution fusion | flops 8648654848 | bytes 16777216 | tf_op jit(solution)/shard_map/dot_general | solution.py:65
  309.4 0.0 copy-done.1
  (1 shorter events, 0.0 us)
Async XLA Ops:
  0.0 0.9 copy-start
  1.8 4.6 %copy-start.2 = (bf16[2048,2048]{1,0:T(8,128)(2,1)S(1)}, bf16[2048,2048]{1,0:T(8,128)(2,1)}, u32[]{:S(2)}) copy-start(bf16[2048,2048]{1,0:T(8,128)(2,1)} %param.6) | copy-start | bytes 25165828
  12.2 3.9 %collective-permute-start.2 = (bf16[512,2048]{1,0:T(8,128)(2,1)}, bf16[512,2048]{1,0:T(8,128)(2,1)}, u32[]{:S(2)}, u32[]{:S(2)}) collective-permute-start(bf16[512,2048]{1,0:T(8,128)(2,1)} %multiply_convert_fusion.5), channel_id=1, source_target_pairs={{30,6},{31,7},{62,38},{63,39},{94,70},{95,71},{126,102},{127,103}} | collective-permute-start | bytes 6291464 | tf_op jit(solution)/shard_map/ppermute | solution.py:21
  14.2 41.2 %collective-permute-start.1 = (bf16[512,2048]{1,0:T(8,128)(2,1)}, bf16[512,2048]{1,0:T(8,128)(2,1)S(1)}, u32[]{:S(2)}, u32[]{:S(2)}) collective-permute-start(bf16[512,2048]{1,0:T(8,128)(2,1)} %multiply_convert_fusion.5), channel_id=1, source_target_pairs={{0,2},{1,3},{2,4},{3,5},{4,6},{5,7},{6,8},{7,9},{8,10},{9,11},{10,... | collective-permute-start | bytes 6291464 | tf_op jit(solution)/shard_map/ppermute | solution.py:21
  16.1 39.3 %collective-permute-start.3 = (bf16[512,2048]{1,0:T(8,128)(2,1)}, bf16[512,2048]{1,0:T(8,128)(2,1)}, u32[]{:S(2)}, u32[]{:S(2)}) collective-permute-start(bf16[512,2048]{1,0:T(8,128)(2,1)} %collective-permute-done.2), channel_id=1, source_target_pairs={{6,32},{7,33},{38,64},{39,65},{70,96},{71,97},{102,0},{103,1}} | collective-permute-start | bytes 6291464 | tf_op jit(solution)/shard_map/ppermute | solution.py:21
  23.9 56.5 %collective-permute-start.4 = (bf16[512,2048]{1,0:T(8,128)(2,1)}, bf16[512,2048]{1,0:T(8,128)(2,1)}, u32[]{:S(2)}, u32[]{:S(2)}) collective-permute-start(bf16[512,2048]{1,0:T(8,128)(2,1)} %multiply_convert_fusion.6), channel_id=1, source_target_pairs={{0,3},{1,2},{2,5},{3,4},{4,7},{5,6},{6,9},{7,8},{8,11},{9,10},{10,... | collective-permute-start | bytes 6291464 | tf_op jit(solution)/shard_map/ppermute | solution.py:21
  28.1 72.4 %collective-permute-start = (bf16[512,2048]{1,0:T(8,128)(2,1)}, bf16[512,2048]{1,0:T(8,128)(2,1)}, u32[]{:S(2)}, u32[]{:S(2)}) collective-permute-start(bf16[512,2048]{1,0:T(8,128)(2,1)} %multiply_convert_fusion.6), channel_id=1, source_target_pairs={{0,2},{1,3},{2,4},{3,5},{4,6},{5,7},{6,8},{7,9},{8,10},{9,11},{10,... | collective-permute-start | bytes 6291464 | tf_op jit(solution)/shard_map/ppermute | solution.py:21
  28.1 97.6 %collective-permute-start.5 = (bf16[512,2048]{1,0:T(8,128)(2,1)}, bf16[512,2048]{1,0:T(8,128)(2,1)}, u32[]{:S(2)}, u32[]{:S(2)}) collective-permute-start(bf16[512,2048]{1,0:T(8,128)(2,1)} %multiply_convert_fusion.5), channel_id=1, source_target_pairs={{0,3},{1,2},{2,5},{3,4},{4,7},{5,6},{6,9},{7,8},{8,11},{9,10},{10,... | collective-permute-start | bytes 6291464 | tf_op jit(solution)/shard_map/ppermute | solution.py:21
  138.9 17.8 %collective-permute-start.7 = (bf16[512,2048]{1,0:T(8,128)(2,1)S(1)}, bf16[512,2048]{1,0:T(8,128)(2,1)S(1)}, u32[]{:S(2)}, u32[]{:S(2)}) collective-permute-start(bf16[512,2048]{1,0:T(8,128)(2,1)S(1)} %get-tuple-element.7), channel_id=1, source_target_pairs={{4,12},{5,13},{6,14},{7,15},{12,20},{13,21},{14,22},{15,23},{20,28... | collective-permute-start | bytes 6291464 | tf_op jit(solution)/shard_map/ppermute | solution.py:21
  139.7 18.3 %collective-permute-start.10 = (bf16[512,2048]{1,0:T(8,128)(2,1)S(1)}, bf16[512,2048]{1,0:T(8,128)(2,1)S(1)}, u32[]{:S(2)}, u32[]{:S(2)}) collective-permute-start(bf16[512,2048]{1,0:T(8,128)(2,1)S(1)} %get-tuple-element.8), channel_id=1, source_target_pairs={{4,12},{5,13},{6,14},{7,15},{12,20},{13,21},{14,22},{15,23},{20,28... | collective-permute-start | bytes 6291464 | tf_op jit(solution)/shard_map/ppermute | solution.py:21
  140.5 150.4 %collective-permute-start.9 = (bf16[1024,2048]{1,0:T(8,128)(2,1)S(1)}, bf16[1024,2048]{1,0:T(8,128)(2,1)S(1)}, u32[]{:S(2)}, u32[]{:S(2)}) collective-permute-start(bf16[1024,2048]{1,0:T(8,128)(2,1)S(1)} %multiply_convert_fusion.2), channel_id=1, source_target_pairs={{0,5},{1,4},{2,7},{3,6},{8,13},{9,12},{10,15},{11,14},{16,21},{17,... | collective-permute-start | bytes 12582920 | tf_op jit(solution)/shard_map/ppermute | solution.py:21
  156.6 136.7 %collective-permute-start.6 = (bf16[1024,2048]{1,0:T(8,128)(2,1)S(1)}, bf16[1024,2048]{1,0:T(8,128)(2,1)S(1)}, u32[]{:S(2)}, u32[]{:S(2)}) collective-permute-start(bf16[1024,2048]{1,0:T(8,128)(2,1)S(1)} %multiply_convert_fusion.2), channel_id=1, source_target_pairs={{0,4},{1,5},{2,6},{3,7},{4,8},{5,9},{6,10},{7,11},{8,12},{9,13},{1... | collective-permute-start | bytes 12582920 | tf_op jit(solution)/shard_map/ppermute | solution.py:21
  156.7 89.3 %collective-permute-start.8 = (bf16[512,2048]{1,0:T(8,128)(2,1)S(1)}, bf16[512,2048]{1,0:T(8,128)(2,1)S(1)}, u32[]{:S(2)}, u32[]{:S(2)}) collective-permute-start(bf16[512,2048]{1,0:T(8,128)(2,1)S(1)} %collective-permute-done.7), channel_id=1, source_target_pairs={{4,33},{5,32},{6,35},{7,34},{12,9},{13,8},{14,11},{15,10},{20,17},... | collective-permute-start | bytes 6291464 | tf_op jit(solution)/shard_map/ppermute | solution.py:21
  158.0 132.9 %collective-permute-start.11 = (bf16[512,2048]{1,0:T(8,128)(2,1)S(1)}, bf16[512,2048]{1,0:T(8,128)(2,1)S(1)}, u32[]{:S(2)}, u32[]{:S(2)}) collective-permute-start(bf16[512,2048]{1,0:T(8,128)(2,1)S(1)} %collective-permute-done.10), channel_id=1, source_target_pairs={{4,33},{5,32},{6,35},{7,34},{12,9},{13,8},{14,11},{15,10},{20,17},... | collective-permute-start | bytes 6291464 | tf_op jit(solution)/shard_map/ppermute | solution.py:21
  293.3 2.0 copy-start.3
  295.3 14.1 %copy-start.1 = (f32[16,2048]{1,0:T(8,128)S(1)}, f32[16,2048]{1,0:T(8,128)}, u32[]{:S(2)}) copy-start(f32[16,2048]{1,0:T(8,128)} %param.7) | copy-start | bytes 393220

commit v12 on v9

--- a/solution.py
+++ b/solution.py
@@ -6,8 +6,8 @@
 from jax.sharding import PartitionSpec as P
 
 LEVELS = 2
-DIRECT_ROWS = 208
-RELAY_ROWS = (416, 400)
+DIRECT_ROWS = 304
+RELAY_ROWS = (368, 352)
 
 
 def sent(value, route):

time: 300 us -> 294 us (0.980)
  starting transfers between devices: 49.5 us -> 38.7 us
  waiting for transfers between devices: 199 us -> 206 us
    ppermute x13, starting transfers between devices: 49.5 us -> 38.7 us  [sent(): return lax.ppermute(value, ('tm', 'row'), pairs)]
    ppermute x13, waiting for transfers between devices: 199 us -> 206 us  [sent(): return lax.ppermute(value, ('tm', 'row'), pairs)]
where the time goes in v12:
time: 294 us; the launch traced here: 293 us
  waiting for transfers between devices  206 us (70%)
  matrix products  38.9 us (13%)
  starting transfers between devices  38.7 us (13%)
  other arithmetic  8.04 us (3%)
    ppermute x13, waiting for transfers between devices, sent(): return lax.ppermute(value, ('tm', 'row'), pairs)  206 us
    ppermute x13, starting transfers between devices, sent(): return lax.ppermute(value, ('tm', 'row'), pairs)  38.7 us
    dot_general x2, matrix products, level_product(): total = jnp.dot(later, earlier, preferred_element_type=jnp.float32)  26.5 us
    dot_general x2, matrix products, shards(): jnp.dot(left_factor[c * chunk_rows:(c + 1) * chunk_rows], right_factor, p...  11.5 us
  transfers between devices with their start and end apart: 13, of which 7 were waited for; matrix products, arithmetic and copies ran while one was open for 3% of the time, Pallas kernels for 0%

profile of v12, /device:TPU:96, one launch (start us, length us, event | category | flops | bytes accessed | tf_op | source)
XLA Modules:
  0.0 293.3 jit_solution(12895108660293553159)
XLA Ops:
  0.0 0.0 copy-start
  0.0 0.7 multiply_bitcast_fusion
  0.7 0.2 copy-done
  0.9 0.9 fusion.39
  1.8 0.0 copy-start.3
  1.8 3.4 %fusion.28 = bf16[1024,2048]{1,0:T(8,128)(2,1)S(1)} fusion(bf16[1,1024,2048]{2,1,0:T(8,128)(2,1)} %param.5, f32[2048]{0:T(1024)S(1)} %bitcast.12), kind=kLoop, calls=%fused_computation.32 | loop fusion | flops 6291456 | bytes 8396800 | tf_op jit(solution)/shard_map/convert_element_type | solution.py:85
  5.3 1.2 copy-done.3
  6.5 5.7 %multiply_convert_fusion.5 = bf16[512,2048]{1,0:T(8,128)(2,1)} fusion(bf16[2048,2048]{1,0:T(8,128)(2,1)S(1)} %copy-done.3, f32[2048]{0:T(1024)S(1)} %bitcast.13, bf16[1024,2048]{1,0:T(8,128)(2,1)S(1)} %fusion.28), kind=kOutput, calls=%fused_computation.43 | convolution fusion | flops 4309647360 | bytes 12591104 | tf_op jit(solution)/shard_map/dot_general | solution.py:89
  12.2 2.0 collective-permute-start.2
  14.2 1.9 collective-permute-start.1
  16.1 0.0 collective-permute-done.2
  16.1 2.0 collective-permute-start.3
  18.2 5.8 %multiply_convert_fusion.6 = bf16[512,2048]{1,0:T(8,128)(2,1)} fusion(bf16[2048,2048]{1,0:T(8,128)(2,1)S(1)} %copy-done.3, f32[2048]{0:T(1024)S(1)} %bitcast.14, bf16[1024,2048]{1,0:T(8,128)(2,1)S(1)} %fusion.28), kind=kOutput, calls=%fused_computation.44 | convolution fusion | flops 4309647360 | bytes 12591104 | tf_op jit(solution)/shard_map/dot_general | solution.py:89
  23.9 4.2 %collective-permute-start.4 = (bf16[512,2048]{1,0:T(8,128)(2,1)}, bf16[512,2048]{1,0:T(8,128)(2,1)}, u32[]{:S(2)}, u32[]{:S(2)}) collective-permute-start(bf16[512,2048]{1,0:T(8,128)(2,1)} %multiply_convert_fusion.6), channel_id=1, source_target_pairs={{0,3},{1,2},{2,5},{3,4},{4,7},{5,6},{6,9},{7,8},{8,11},{9,10},{10,... | collective-permute-start | bytes 6291464 | tf_op jit(solution)/shard_map/ppermute | solution.py:22
  28.1 0.0 collective-permute-start
  28.1 21.3 %collective-permute-start.5 = (bf16[512,2048]{1,0:T(8,128)(2,1)}, bf16[512,2048]{1,0:T(8,128)(2,1)}, u32[]{:S(2)}, u32[]{:S(2)}) collective-permute-start(bf16[512,2048]{1,0:T(8,128)(2,1)} %multiply_convert_fusion.5), channel_id=1, source_target_pairs={{0,3},{1,2},{2,5},{3,4},{4,7},{5,6},{6,9},{7,8},{8,11},{9,10},{10,... | collective-permute-start | bytes 6291464 | tf_op jit(solution)/shard_map/ppermute | solution.py:22
  49.4 5.9 %collective-permute-done.1 = bf16[512,2048]{1,0:T(8,128)(2,1)S(1)} collective-permute-done((bf16[512,2048]{1,0:T(8,128)(2,1)}, bf16[512,2048]{1,0:T(8,128)(2,1)S(1)}, u32[]{:S(2)}, u32[]{:S(2)}) %collective-permute-start.1) | collective-permute-done | bytes 2097184 | tf_op jit(solution)/shard_map/ppermute | solution.py:22
  55.3 0.0 collective-permute-done.3
  55.4 2.4 add.12
  57.7 22.7 %collective-permute-done.4 = bf16[512,2048]{1,0:T(8,128)(2,1)} collective-permute-done((bf16[512,2048]{1,0:T(8,128)(2,1)}, bf16[512,2048]{1,0:T(8,128)(2,1)}, u32[]{:S(2)}, u32[]{:S(2)}) %collective-permute-start.4) | collective-permute-done | bytes 2097184 | tf_op jit(solution)/shard_map/ppermute | solution.py:22
  80.4 20.0 %collective-permute-done = bf16[512,2048]{1,0:T(8,128)(2,1)} collective-permute-done((bf16[512,2048]{1,0:T(8,128)(2,1)}, bf16[512,2048]{1,0:T(8,128)(2,1)}, u32[]{:S(2)}, u32[]{:S(2)}) %collective-permute-start) | collective-permute-done | bytes 2097184 | tf_op jit(solution)/shard_map/ppermute | solution.py:22
  100.4 25.2 %collective-permute-done.5 = bf16[512,2048]{1,0:T(8,128)(2,1)} collective-permute-done((bf16[512,2048]{1,0:T(8,128)(2,1)}, bf16[512,2048]{1,0:T(8,128)(2,1)}, u32[]{:S(2)}, u32[]{:S(2)}) %collective-permute-start.5) | collective-permute-done | bytes 2097184 | tf_op jit(solution)/shard_map/ppermute | solution.py:22
  125.6 12.8 %multiply_convert_fusion.2 = bf16[1024,2048]{1,0:T(8,128)(2,1)S(1)} fusion(bf16[512,2048]{1,0:T(8,128)(2,1)} %collective-permute-done.5, bf16[512,2048]{1,0:T(8,128)(2,1)} %collective-permute-done.4, bf16[512,2048]{1,0:T(8,128)(2,1)S(1)} %add.12, bf16[512,2048]{1,0:T(8,128)(2,1)} %collective-permute-done, pred[]{:T(512)S(6)} %eq.17, ...), kind=kOutput, calls=%fused_computation.34 | convolution fusion | flops 8673820672 | bytes 16777216 | tf_op jit(solution)/shard_map/dot_general | solution.py:66
  138.5 0.0 copy-start.2
  138.5 1.6 collective-permute-start.8
  140.0 0.1 collective-permute-start.6
  140.1 0.2 slice.48
  140.3 0.8 collective-permute-start.11
  141.0 0.2 slice.46
  141.2 0.8 collective-permute-start.9
  142.0 0.1 slice.44
  142.1 1.3 collective-permute-start.7
  143.4 0.0 collective-permute-done.11
  143.4 1.3 collective-permute-start.12
  144.7 0.0 collective-permute-done.9
  144.7 1.5 collective-permute-start.10
  146.2 60.4 %collective-permute-done.7 = bf16[304,2048]{1,0:T(8,128)(2,1)S(1)} collective-permute-done((bf16[304,2048]{1,0:T(8,128)(2,1)S(1)}, bf16[304,2048]{1,0:T(8,128)(2,1)S(1)}, u32[]{:S(2)}, u32[]{:S(2)}) %collective-permute-start.7) | collective-permute-done | bytes 1245216 | tf_op jit(solution)/shard_map/ppermute | solution.py:22
  206.5 13.9 %collective-permute-done.8 = bf16[1024,2048]{1,0:T(8,128)(2,1)S(1)} collective-permute-done((bf16[1024,2048]{1,0:T(8,128)(2,1)S(1)}, bf16[1024,2048]{1,0:T(8,128)(2,1)S(1)}, u32[]{:S(2)}, u32[]{:S(2)}) %collective-permute-start.8) | collective-permute-done | bytes 4194336 | tf_op jit(solution)/shard_map/ppermute | solution.py:22
  220.5 1.3 slice_add_fusion.2
  221.7 0.0 copy-done.2
  221.7 0.0 collective-permute-done.12
  221.7 0.1 slice_add_fusion.1
  221.9 57.6 %collective-permute-done.10 = bf16[368,2048]{1,0:T(8,128)(2,1)S(1)} collective-permute-done((bf16[368,2048]{1,0:T(8,128)(2,1)S(1)}, bf16[368,2048]{1,0:T(8,128)(2,1)S(1)}, u32[]{:S(2)}, u32[]{:S(2)}) %collective-permute-start.10) | collective-permute-done | bytes 1507360 | tf_op jit(solution)/shard_map/ppermute | solution.py:22
  279.4 0.2 slice_add_fusion
  279.6 0.0 collective-permute-done.6
  279.6 0.0 copy-start.1
  279.6 13.7 %fusion.33 = bf16[1,1024,2048]{2,1,0:T(8,128)(2,1)} fusion(bf16[1024,2048]{1,0:T(8,128)(2,1)} %copy-done.2, bf16[352,2048]{1,0:T(8,128)(2,1)S(1)} %slice_add_fusion.1, bf16[368,2048]{1,0:T(8,128)(2,1)S(1)} %slice_add_fusion, bf16[304,2048]{1,0:T(8,128)(2,1)} %slice_add_fusion.2, bf16[1024,2048]{1,0:T(8,128)(2,1)} %collective-permute-done.6, pred[]{:T(512)S(6)} %eq.17), kind=kOutput, calls=%fused_computation.39 | convolution fusion | flops 8665432064 | bytes 16777216 | tf_op jit(solution)/shard_map/dot_general | solution.py:66
  293.3 0.0 copy-done.1
  (1 shorter events, 0.0 us)
Async XLA Ops:
  0.0 0.9 copy-start
  1.8 4.6 %copy-start.3 = (bf16[2048,2048]{1,0:T(8,128)(2,1)S(1)}, bf16[2048,2048]{1,0:T(8,128)(2,1)}, u32[]{:S(2)}) copy-start(bf16[2048,2048]{1,0:T(8,128)(2,1)} %param.6) | copy-start | bytes 25165828
  12.2 3.9 %collective-permute-start.2 = (bf16[512,2048]{1,0:T(8,128)(2,1)}, bf16[512,2048]{1,0:T(8,128)(2,1)}, u32[]{:S(2)}, u32[]{:S(2)}) collective-permute-start(bf16[512,2048]{1,0:T(8,128)(2,1)} %multiply_convert_fusion.5), channel_id=1, source_target_pairs={{30,6},{31,7},{62,38},{63,39},{94,70},{95,71},{126,102},{127,103}} | collective-permute-start | bytes 6291464 | tf_op jit(solution)/shard_map/ppermute | solution.py:22
  14.2 41.2 %collective-permute-start.1 = (bf16[512,2048]{1,0:T(8,128)(2,1)}, bf16[512,2048]{1,0:T(8,128)(2,1)S(1)}, u32[]{:S(2)}, u32[]{:S(2)}) collective-permute-start(bf16[512,2048]{1,0:T(8,128)(2,1)} %multiply_convert_fusion.5), channel_id=1, source_target_pairs={{0,2},{1,3},{2,4},{3,5},{4,6},{5,7},{6,8},{7,9},{8,10},{9,11},{10,... | collective-permute-start | bytes 6291464 | tf_op jit(solution)/shard_map/ppermute | solution.py:22
  16.1 39.2 %collective-permute-start.3 = (bf16[512,2048]{1,0:T(8,128)(2,1)}, bf16[512,2048]{1,0:T(8,128)(2,1)}, u32[]{:S(2)}, u32[]{:S(2)}) collective-permute-start(bf16[512,2048]{1,0:T(8,128)(2,1)} %collective-permute-done.2), channel_id=1, source_target_pairs={{6,32},{7,33},{38,64},{39,65},{70,96},{71,97},{102,0},{103,1}} | collective-permute-start | bytes 6291464 | tf_op jit(solution)/shard_map/ppermute | solution.py:22
  23.9 56.5 %collective-permute-start.4 = (bf16[512,2048]{1,0:T(8,128)(2,1)}, bf16[512,2048]{1,0:T(8,128)(2,1)}, u32[]{:S(2)}, u32[]{:S(2)}) collective-permute-start(bf16[512,2048]{1,0:T(8,128)(2,1)} %multiply_convert_fusion.6), channel_id=1, source_target_pairs={{0,3},{1,2},{2,5},{3,4},{4,7},{5,6},{6,9},{7,8},{8,11},{9,10},{10,... | collective-permute-start | bytes 6291464 | tf_op jit(solution)/shard_map/ppermute | solution.py:22
  28.1 72.3 %collective-permute-start = (bf16[512,2048]{1,0:T(8,128)(2,1)}, bf16[512,2048]{1,0:T(8,128)(2,1)}, u32[]{:S(2)}, u32[]{:S(2)}) collective-permute-start(bf16[512,2048]{1,0:T(8,128)(2,1)} %multiply_convert_fusion.6), channel_id=1, source_target_pairs={{0,2},{1,3},{2,4},{3,5},{4,6},{5,7},{6,8},{7,9},{8,10},{9,11},{10,... | collective-permute-start | bytes 6291464 | tf_op jit(solution)/shard_map/ppermute | solution.py:22
  28.1 97.5 %collective-permute-start.5 = (bf16[512,2048]{1,0:T(8,128)(2,1)}, bf16[512,2048]{1,0:T(8,128)(2,1)}, u32[]{:S(2)}, u32[]{:S(2)}) collective-permute-start(bf16[512,2048]{1,0:T(8,128)(2,1)} %multiply_convert_fusion.5), channel_id=1, source_target_pairs={{0,3},{1,2},{2,5},{3,4},{4,7},{5,6},{6,9},{7,8},{8,11},{9,10},{10,... | collective-permute-start | bytes 6291464 | tf_op jit(solution)/shard_map/ppermute | solution.py:22
  138.5 83.3 %copy-start.2 = (bf16[1024,2048]{1,0:T(8,128)(2,1)}, bf16[1024,2048]{1,0:T(8,128)(2,1)S(1)}, u32[]{:S(2)}) copy-start(bf16[1024,2048]{1,0:T(8,128)(2,1)S(1)} %multiply_convert_fusion.2) | copy-start | bytes 12582916
  138.5 82.0 %collective-permute-start.8 = (bf16[1024,2048]{1,0:T(8,128)(2,1)S(1)}, bf16[1024,2048]{1,0:T(8,128)(2,1)S(1)}, u32[]{:S(2)}, u32[]{:S(2)}) collective-permute-start(bf16[1024,2048]{1,0:T(8,128)(2,1)S(1)} %multiply_convert_fusion.2), channel_id=1, source_target_pairs={{0,5},{1,4},{2,7},{3,6},{8,13},{9,12},{10,15},{11,14},{16,21},{17,... | collective-permute-start | bytes 12582920 | tf_op jit(solution)/shard_map/ppermute | solution.py:22
  140.0 139.6 %collective-permute-start.6 = (bf16[1024,2048]{1,0:T(8,128)(2,1)S(1)}, bf16[1024,2048]{1,0:T(8,128)(2,1)}, u32[]{:S(2)}, u32[]{:S(2)}) collective-permute-start(bf16[1024,2048]{1,0:T(8,128)(2,1)S(1)} %multiply_convert_fusion.2), channel_id=1, source_target_pairs={{0,4},{1,5},{2,6},{3,7},{4,8},{5,9},{6,10},{7,11},{8,12},{9,13},{1... | collective-permute-start | bytes 12582920 | tf_op jit(solution)/shard_map/ppermute | solution.py:22
  140.3 3.1 %collective-permute-start.11 = (bf16[352,2048]{1,0:T(8,128)(2,1)S(1)}, bf16[352,2048]{1,0:T(8,128)(2,1)S(1)}, u32[]{:S(2)}, u32[]{:S(2)}) collective-permute-start(bf16[352,2048]{1,0:T(8,128)(2,1)S(1)} %slice.48), channel_id=1, source_target_pairs={{4,12},{5,13},{6,14},{7,15},{12,20},{13,21},{14,22},{15,23},{20,28... | collective-permute-start | bytes 4325384 | tf_op jit(solution)/shard_map/ppermute | solution.py:22
  141.2 3.5 %collective-permute-start.9 = (bf16[368,2048]{1,0:T(8,128)(2,1)S(1)}, bf16[368,2048]{1,0:T(8,128)(2,1)S(1)}, u32[]{:S(2)}, u32[]{:S(2)}) collective-permute-start(bf16[368,2048]{1,0:T(8,128)(2,1)S(1)} %slice.46), channel_id=1, source_target_pairs={{4,12},{5,13},{6,14},{7,15},{12,20},{13,21},{14,22},{15,23},{20,28... | collective-permute-start | bytes 4521992 | tf_op jit(solution)/shard_map/ppermute | solution.py:22
  142.1 64.5 %collective-permute-start.7 = (bf16[304,2048]{1,0:T(8,128)(2,1)S(1)}, bf16[304,2048]{1,0:T(8,128)(2,1)S(1)}, u32[]{:S(2)}, u32[]{:S(2)}) collective-permute-start(bf16[304,2048]{1,0:T(8,128)(2,1)S(1)} %slice.44), channel_id=1, source_target_pairs={{4,9},{5,8},{6,11},{7,10},{12,17},{13,16},{14,19},{15,18},{20,25},... | collective-permute-start | bytes 3735560 | tf_op jit(solution)/shard_map/ppermute | solution.py:22
  143.4 78.4 %collective-permute-start.12 = (bf16[352,2048]{1,0:T(8,128)(2,1)S(1)}, bf16[352,2048]{1,0:T(8,128)(2,1)S(1)}, u32[]{:S(2)}, u32[]{:S(2)}) collective-permute-start(bf16[352,2048]{1,0:T(8,128)(2,1)S(1)} %collective-permute-done.11), channel_id=1, source_target_pairs={{4,33},{5,32},{6,35},{7,34},{12,9},{13,8},{14,11},{15,10},{20,17},... | collective-permute-start | bytes 4325384 | tf_op jit(solution)/shard_map/ppermute | solution.py:22
  144.7 134.8 %collective-permute-start.10 = (bf16[368,2048]{1,0:T(8,128)(2,1)S(1)}, bf16[368,2048]{1,0:T(8,128)(2,1)S(1)}, u32[]{:S(2)}, u32[]{:S(2)}) collective-permute-start(bf16[368,2048]{1,0:T(8,128)(2,1)S(1)} %collective-permute-done.9), channel_id=1, source_target_pairs={{4,33},{5,32},{6,35},{7,34},{12,9},{13,8},{14,11},{15,10},{20,17},... | collective-permute-start | bytes 4521992 | tf_op jit(solution)/shard_map/ppermute | solution.py:22
  279.6 13.7 %copy-start.1 = (f32[16,2048]{1,0:T(8,128)S(1)}, f32[16,2048]{1,0:T(8,128)}, u32[]{:S(2)}) copy-start(f32[16,2048]{1,0:T(8,128)} %param.7) | copy-start | bytes 393220

commit v13 on v12

--- a/solution.py
+++ b/solution.py
@@ -6,8 +6,8 @@
 from jax.sharding import PartitionSpec as P
 
 LEVELS = 2
-DIRECT_ROWS = 304
-RELAY_ROWS = (368, 352)
+DIRECT_ROWS = 400
+RELAY_ROWS = (320, 304)
 
 
 def sent(value, route):

time: 294 us -> 301 us (1.024)
  the two profiles are of different devices: /device:TPU:96 before, /device:TPU:0 now
where the time goes in v13:
time: 301 us
  waiting for transfers between devices  208 us (69%)
  starting transfers between devices  43.5 us (14%)
  matrix products  38.9 us (13%)
  other arithmetic  8.09 us (3%)
    ppermute x13, waiting for transfers between devices, sent(): return lax.ppermute(value, ('tm', 'row'), pairs)  208 us
    ppermute x13, starting transfers between devices, sent(): return lax.ppermute(value, ('tm', 'row'), pairs)  43.5 us
    dot_general x2, matrix products, level_product(): total = jnp.dot(later, earlier, preferred_element_type=jnp.float32)  26.5 us
    dot_general x2, matrix products, shards(): jnp.dot(left_factor[c * chunk_rows:(c + 1) * chunk_rows], right_factor, p...  11.5 us
  transfers between devices with their start and end apart: 13, of which 7 were waited for; matrix products, arithmetic and copies ran while one was open for 3% of the time, Pallas kernels for 0%

profile of v13, /device:TPU:0, one launch (start us, length us, event | category | flops | bytes accessed | tf_op | source)
XLA Modules:
  0.0 300.7 jit_solution(8588195324462461547)
XLA Ops:
  0.0 0.0 copy-start
  0.0 0.7 multiply_bitcast_fusion
  0.7 0.2 copy-done
  0.9 0.9 fusion.39
  1.8 0.0 copy-start.3
  1.8 3.4 %fusion.28 = bf16[1024,2048]{1,0:T(8,128)(2,1)S(1)} fusion(bf16[1,1024,2048]{2,1,0:T(8,128)(2,1)} %param.5, f32[2048]{0:T(1024)S(1)} %bitcast.12), kind=kLoop, calls=%fused_computation.32 | loop fusion | flops 6291456 | bytes 8396800 | tf_op jit(solution)/shard_map/convert_element_type | solution.py:85
  5.3 1.2 copy-done.3
  6.5 5.7 %multiply_convert_fusion.5 = bf16[512,2048]{1,0:T(8,128)(2,1)} fusion(bf16[2048,2048]{1,0:T(8,128)(2,1)S(1)} %copy-done.3, f32[2048]{0:T(1024)S(1)} %bitcast.13, bf16[1024,2048]{1,0:T(8,128)(2,1)S(1)} %fusion.28), kind=kOutput, calls=%fused_computation.43 | convolution fusion | flops 4309647360 | bytes 12591104 | tf_op jit(solution)/shard_map/dot_general | solution.py:89
  12.2 2.0 collective-permute-start.2
  14.2 1.4 collective-permute-start.1
  15.6 0.0 collective-permute-done.2
  15.6 1.3 collective-permute-start.3
  16.9 5.8 %multiply_convert_fusion.6 = bf16[512,2048]{1,0:T(8,128)(2,1)} fusion(bf16[2048,2048]{1,0:T(8,128)(2,1)S(1)} %copy-done.3, f32[2048]{0:T(1024)S(1)} %bitcast.14, bf16[1024,2048]{1,0:T(8,128)(2,1)S(1)} %fusion.28), kind=kOutput, calls=%fused_computation.44 | convolution fusion | flops 4309647360 | bytes 12591104 | tf_op jit(solution)/shard_map/dot_general | solution.py:89
  22.7 5.5 %collective-permute-start.4 = (bf16[512,2048]{1,0:T(8,128)(2,1)}, bf16[512,2048]{1,0:T(8,128)(2,1)}, u32[]{:S(2)}, u32[]{:S(2)}) collective-permute-start(bf16[512,2048]{1,0:T(8,128)(2,1)} %multiply_convert_fusion.6), channel_id=1, source_target_pairs={{0,3},{1,2},{2,5},{3,4},{4,7},{5,6},{6,9},{7,8},{8,11},{9,10},{10,... | collective-permute-start | bytes 6291464 | tf_op jit(solution)/shard_map/ppermute | solution.py:22
  28.2 0.0 collective-permute-start
  28.2 26.1 %collective-permute-start.5 = (bf16[512,2048]{1,0:T(8,128)(2,1)}, bf16[512,2048]{1,0:T(8,128)(2,1)}, u32[]{:S(2)}, u32[]{:S(2)}) collective-permute-start(bf16[512,2048]{1,0:T(8,128)(2,1)} %multiply_convert_fusion.5), channel_id=1, source_target_pairs={{0,3},{1,2},{2,5},{3,4},{4,7},{5,6},{6,9},{7,8},{8,11},{9,10},{10,... | collective-permute-start | bytes 6291464 | tf_op jit(solution)/shard_map/ppermute | solution.py:22
  54.3 0.0 collective-permute-done.1
  54.3 15.3 %collective-permute-done.3 = bf16[512,2048]{1,0:T(8,128)(2,1)} collective-permute-done((bf16[512,2048]{1,0:T(8,128)(2,1)}, bf16[512,2048]{1,0:T(8,128)(2,1)}, u32[]{:S(2)}, u32[]{:S(2)}) %collective-permute-start.3) | collective-permute-done | bytes 2097184 | tf_op jit(solution)/shard_map/ppermute | solution.py:22
  69.6 2.3 add.12
  72.0 20.0 %collective-permute-done.4 = bf16[512,2048]{1,0:T(8,128)(2,1)} collective-permute-done((bf16[512,2048]{1,0:T(8,128)(2,1)}, bf16[512,2048]{1,0:T(8,128)(2,1)}, u32[]{:S(2)}, u32[]{:S(2)}) %collective-permute-start.4) | collective-permute-done | bytes 2097184 | tf_op jit(solution)/shard_map/ppermute | solution.py:22
  92.0 20.8 %collective-permute-done = bf16[512,2048]{1,0:T(8,128)(2,1)} collective-permute-done((bf16[512,2048]{1,0:T(8,128)(2,1)}, bf16[512,2048]{1,0:T(8,128)(2,1)}, u32[]{:S(2)}, u32[]{:S(2)}) %collective-permute-start) | collective-permute-done | bytes 2097184 | tf_op jit(solution)/shard_map/ppermute | solution.py:22
  112.7 31.6 %collective-permute-done.5 = bf16[512,2048]{1,0:T(8,128)(2,1)} collective-permute-done((bf16[512,2048]{1,0:T(8,128)(2,1)}, bf16[512,2048]{1,0:T(8,128)(2,1)}, u32[]{:S(2)}, u32[]{:S(2)}) %collective-permute-start.5) | collective-permute-done | bytes 2097184 | tf_op jit(solution)/shard_map/ppermute | solution.py:22
  144.3 12.8 %multiply_convert_fusion.2 = bf16[1024,2048]{1,0:T(8,128)(2,1)S(1)} fusion(bf16[512,2048]{1,0:T(8,128)(2,1)} %collective-permute-done.5, bf16[512,2048]{1,0:T(8,128)(2,1)} %collective-permute-done.4, bf16[512,2048]{1,0:T(8,128)(2,1)S(1)} %add.12, bf16[512,2048]{1,0:T(8,128)(2,1)} %collective-permute-done, pred[]{:T(512)S(6)} %eq.17, ...), kind=kOutput, calls=%fused_computation.34 | convolution fusion | flops 8673820672 | bytes 16777216 | tf_op jit(solution)/shard_map/dot_general | solution.py:66
  157.2 0.0 copy-start.2
  157.2 1.6 collective-permute-start.8
  158.7 0.1 collective-permute-start.6
  158.8 0.1 slice.48
  158.9 0.7 collective-permute-start.11
  159.7 0.1 slice.46
  159.7 0.7 collective-permute-start.9
  160.5 0.0 collective-permute-done.11
  160.5 1.3 collective-permute-start.12
  161.8 0.0 collective-permute-done.9
  161.8 1.3 collective-permute-start.10
  163.1 0.1 slice.44
  163.2 1.5 collective-permute-start.7
  164.7 50.5 %collective-permute-done.12 = bf16[304,2048]{1,0:T(8,128)(2,1)S(1)} collective-permute-done((bf16[304,2048]{1,0:T(8,128)(2,1)S(1)}, bf16[304,2048]{1,0:T(8,128)(2,1)S(1)}, u32[]{:S(2)}, u32[]{:S(2)}) %collective-permute-start.12) | collective-permute-done | bytes 1245216 | tf_op jit(solution)/shard_map/ppermute | solution.py:22
  215.2 29.0 %collective-permute-done.8 = bf16[1024,2048]{1,0:T(8,128)(2,1)S(1)} collective-permute-done((bf16[1024,2048]{1,0:T(8,128)(2,1)S(1)}, bf16[1024,2048]{1,0:T(8,128)(2,1)S(1)}, u32[]{:S(2)}, u32[]{:S(2)}) %collective-permute-start.8) | collective-permute-done | bytes 4194336 | tf_op jit(solution)/shard_map/ppermute | solution.py:22
  244.2 1.3 slice_add_fusion.2
  245.4 0.0 copy-done.2
  245.4 0.0 collective-permute-done.10
  245.5 0.2 slice_add_fusion.1
  245.6 41.2 %collective-permute-done.7 = bf16[400,2048]{1,0:T(8,128)(2,1)S(1)} collective-permute-done((bf16[400,2048]{1,0:T(8,128)(2,1)S(1)}, bf16[400,2048]{1,0:T(8,128)(2,1)S(1)}, u32[]{:S(2)}, u32[]{:S(2)}) %collective-permute-start.7) | collective-permute-done | bytes 1638432 | tf_op jit(solution)/shard_map/ppermute | solution.py:22
  286.9 0.2 slice_add_fusion
  287.0 0.0 collective-permute-done.6
  287.0 0.0 copy-start.1
  287.1 13.7 %fusion.33 = bf16[1,1024,2048]{2,1,0:T(8,128)(2,1)} fusion(bf16[1024,2048]{1,0:T(8,128)(2,1)} %copy-done.2, bf16[304,2048]{1,0:T(8,128)(2,1)} %slice_add_fusion.2, bf16[320,2048]{1,0:T(8,128)(2,1)S(1)} %slice_add_fusion.1, bf16[400,2048]{1,0:T(8,128)(2,1)S(1)} %slice_add_fusion, bf16[1024,2048]{1,0:T(8,128)(2,1)} %collective-permute-done.6, pred[]{:T(512)S(6)} %eq.17), kind=kOutput, calls=%fused_computation.39 | convolution fusion | flops 8665432064 | bytes 16777216 | tf_op jit(solution)/shard_map/dot_general | solution.py:66
  300.7 0.0 copy-done.1
  (1 shorter events, 0.0 us)
Async XLA Ops:
  0.0 0.9 copy-start
  1.8 4.6 %copy-start.3 = (bf16[2048,2048]{1,0:T(8,128)(2,1)S(1)}, bf16[2048,2048]{1,0:T(8,128)(2,1)}, u32[]{:S(2)}) copy-start(bf16[2048,2048]{1,0:T(8,128)(2,1)} %param.6) | copy-start | bytes 25165828
  12.2 3.4 %collective-permute-start.2 = (bf16[512,2048]{1,0:T(8,128)(2,1)}, bf16[512,2048]{1,0:T(8,128)(2,1)}, u32[]{:S(2)}, u32[]{:S(2)}) collective-permute-start(bf16[512,2048]{1,0:T(8,128)(2,1)} %multiply_convert_fusion.5), channel_id=1, source_target_pairs={{30,6},{31,7},{62,38},{63,39},{94,70},{95,71},{126,102},{127,103}} | collective-permute-start | bytes 6291464 | tf_op jit(solution)/shard_map/ppermute | solution.py:22
  14.2 40.2 %collective-permute-start.1 = (bf16[512,2048]{1,0:T(8,128)(2,1)}, bf16[512,2048]{1,0:T(8,128)(2,1)S(1)}, u32[]{:S(2)}, u32[]{:S(2)}) collective-permute-start(bf16[512,2048]{1,0:T(8,128)(2,1)} %multiply_convert_fusion.5), channel_id=1, source_target_pairs={{0,2},{1,3},{2,4},{3,5},{4,6},{5,7},{6,8},{7,9},{8,10},{9,11},{10,... | collective-permute-start | bytes 6291464 | tf_op jit(solution)/shard_map/ppermute | solution.py:22
  15.6 54.0 %collective-permute-start.3 = (bf16[512,2048]{1,0:T(8,128)(2,1)}, bf16[512,2048]{1,0:T(8,128)(2,1)}, u32[]{:S(2)}, u32[]{:S(2)}) collective-permute-start(bf16[512,2048]{1,0:T(8,128)(2,1)} %collective-permute-done.2), channel_id=1, source_target_pairs={{6,32},{7,33},{38,64},{39,65},{70,96},{71,97},{102,0},{103,1}} | collective-permute-start | bytes 6291464 | tf_op jit(solution)/shard_map/ppermute | solution.py:22
  22.7 69.3 %collective-permute-start.4 = (bf16[512,2048]{1,0:T(8,128)(2,1)}, bf16[512,2048]{1,0:T(8,128)(2,1)}, u32[]{:S(2)}, u32[]{:S(2)}) collective-permute-start(bf16[512,2048]{1,0:T(8,128)(2,1)} %multiply_convert_fusion.6), channel_id=1, source_target_pairs={{0,3},{1,2},{2,5},{3,4},{4,7},{5,6},{6,9},{7,8},{8,11},{9,10},{10,... | collective-permute-start | bytes 6291464 | tf_op jit(solution)/shard_map/ppermute | solution.py:22
  28.2 84.5 %collective-permute-start = (bf16[512,2048]{1,0:T(8,128)(2,1)}, bf16[512,2048]{1,0:T(8,128)(2,1)}, u32[]{:S(2)}, u32[]{:S(2)}) collective-permute-start(bf16[512,2048]{1,0:T(8,128)(2,1)} %multiply_convert_fusion.6), channel_id=1, source_target_pairs={{0,2},{1,3},{2,4},{3,5},{4,6},{5,7},{6,8},{7,9},{8,10},{9,11},{10,... | collective-permute-start | bytes 6291464 | tf_op jit(solution)/shard_map/ppermute | solution.py:22
  28.2 116.1 %collective-permute-start.5 = (bf16[512,2048]{1,0:T(8,128)(2,1)}, bf16[512,2048]{1,0:T(8,128)(2,1)}, u32[]{:S(2)}, u32[]{:S(2)}) collective-permute-start(bf16[512,2048]{1,0:T(8,128)(2,1)} %multiply_convert_fusion.5), channel_id=1, source_target_pairs={{0,3},{1,2},{2,5},{3,4},{4,7},{5,6},{6,9},{7,8},{8,11},{9,10},{10,... | collective-permute-start | bytes 6291464 | tf_op jit(solution)/shard_map/ppermute | solution.py:22
  157.2 88.3 %copy-start.2 = (bf16[1024,2048]{1,0:T(8,128)(2,1)}, bf16[1024,2048]{1,0:T(8,128)(2,1)S(1)}, u32[]{:S(2)}) copy-start(bf16[1024,2048]{1,0:T(8,128)(2,1)S(1)} %multiply_convert_fusion.2) | copy-start | bytes 12582916
  157.2 87.0 %collective-permute-start.8 = (bf16[1024,2048]{1,0:T(8,128)(2,1)S(1)}, bf16[1024,2048]{1,0:T(8,128)(2,1)S(1)}, u32[]{:S(2)}, u32[]{:S(2)}) collective-permute-start(bf16[1024,2048]{1,0:T(8,128)(2,1)S(1)} %multiply_convert_fusion.2), channel_id=1, source_target_pairs={{0,5},{1,4},{2,7},{3,6},{8,13},{9,12},{10,15},{11,14},{16,21},{17,... | collective-permute-start | bytes 12582920 | tf_op jit(solution)/shard_map/ppermute | solution.py:22
  158.7 128.3 %collective-permute-start.6 = (bf16[1024,2048]{1,0:T(8,128)(2,1)S(1)}, bf16[1024,2048]{1,0:T(8,128)(2,1)}, u32[]{:S(2)}, u32[]{:S(2)}) collective-permute-start(bf16[1024,2048]{1,0:T(8,128)(2,1)S(1)} %multiply_convert_fusion.2), channel_id=1, source_target_pairs={{0,4},{1,5},{2,6},{3,7},{4,8},{5,9},{6,10},{7,11},{8,12},{9,13},{1... | collective-permute-start | bytes 12582920 | tf_op jit(solution)/shard_map/ppermute | solution.py:22
  158.9 1.6 collective-permute-start.11
  159.7 2.1 collective-permute-start.9
  160.5 54.7 %collective-permute-start.12 = (bf16[304,2048]{1,0:T(8,128)(2,1)S(1)}, bf16[304,2048]{1,0:T(8,128)(2,1)S(1)}, u32[]{:S(2)}, u32[]{:S(2)}) collective-permute-start(bf16[304,2048]{1,0:T(8,128)(2,1)S(1)} %collective-permute-done.11), channel_id=1, source_target_pairs={{4,33},{5,32},{6,35},{7,34},{12,9},{13,8},{14,11},{15,10},{20,17},... | collective-permute-start | bytes 3735560 | tf_op jit(solution)/shard_map/ppermute | solution.py:22
  161.8 83.6 %collective-permute-start.10 = (bf16[320,2048]{1,0:T(8,128)(2,1)S(1)}, bf16[320,2048]{1,0:T(8,128)(2,1)S(1)}, u32[]{:S(2)}, u32[]{:S(2)}) collective-permute-start(bf16[320,2048]{1,0:T(8,128)(2,1)S(1)} %collective-permute-done.9), channel_id=1, source_target_pairs={{4,33},{5,32},{6,35},{7,34},{12,9},{13,8},{14,11},{15,10},{20,17},... | collective-permute-start | bytes 3932168 | tf_op jit(solution)/shard_map/ppermute | solution.py:22
  163.2 123.6 %collective-permute-start.7 = (bf16[400,2048]{1,0:T(8,128)(2,1)S(1)}, bf16[400,2048]{1,0:T(8,128)(2,1)S(1)}, u32[]{:S(2)}, u32[]{:S(2)}) collective-permute-start(bf16[400,2048]{1,0:T(8,128)(2,1)S(1)} %slice.44), channel_id=1, source_target_pairs={{4,9},{5,8},{6,11},{7,10},{12,17},{13,16},{14,19},{15,18},{20,25},... | collective-permute-start | bytes 4915208 | tf_op jit(solution)/shard_map/ppermute | solution.py:22
  287.0 13.7 %copy-start.1 = (f32[16,2048]{1,0:T(8,128)S(1)}, f32[16,2048]{1,0:T(8,128)}, u32[]{:S(2)}) copy-start(f32[16,2048]{1,0:T(8,128)} %param.7) | copy-start | bytes 393220

commit v14 on v13

--- a/solution.py
+++ b/solution.py
@@ -6,8 +6,8 @@
 from jax.sharding import PartitionSpec as P
 
 LEVELS = 2
-DIRECT_ROWS = 400
-RELAY_ROWS = (320, 304)
+DIRECT_ROWS = 256
+RELAY_ROWS = (384, 384)
 
 
 def sent(value, route):

time: 301 us -> 297 us (0.987)
  the two profiles are of different devices: /device:TPU:0 before, /device:TPU:96 now
where the time goes in v14:
time: 297 us
  waiting for transfers between devices  207 us (70%)
  matrix products  38.8 us (13%)
  starting transfers between devices  38.7 us (13%)
  other arithmetic  8.02 us (3%)
  local copies, waits for them, and re-layouts  3.87 us (1%)
    ppermute x13, waiting for transfers between devices, sent(): return lax.ppermute(value, ('tm', 'row'), pairs)  207 us
    ppermute x13, starting transfers between devices, sent(): return lax.ppermute(value, ('tm', 'row'), pairs)  38.7 us
    dot_general x2, matrix products, level_product(): total = jnp.dot(later, earlier, preferred_element_type=jnp.float32)  26.5 us
    dot_general x2, matrix products, shards(): jnp.dot(left_factor[c * chunk_rows:(c + 1) * chunk_rows], right_factor, p...  11.4 us
  transfers between devices with their start and end apart: 13, of which 8 were waited for; matrix products, arithmetic and copies ran while one was open for 3% of the time, Pallas kernels for 0%

profile of v14, /device:TPU:96, one launch (start us, length us, event | category | flops | bytes accessed | tf_op | source)
XLA Modules:
  0.0 297.0 jit_solution(7014160781358438034)
XLA Ops:
  0.0 0.0 copy-start
  0.0 0.7 multiply_bitcast_fusion
  0.7 0.2 copy-done
  0.9 0.9 fusion.39
  1.8 0.0 copy-start.3
  1.8 3.4 %fusion.28 = bf16[1024,2048]{1,0:T(8,128)(2,1)S(1)} fusion(bf16[1,1024,2048]{2,1,0:T(8,128)(2,1)} %param.5, f32[2048]{0:T(1024)S(1)} %bitcast.12), kind=kLoop, calls=%fused_computation.32 | loop fusion | flops 6291456 | bytes 8396800 | tf_op jit(solution)/shard_map/convert_element_type | solution.py:85
  5.3 1.2 copy-done.3
  6.5 5.7 %multiply_convert_fusion.5 = bf16[512,2048]{1,0:T(8,128)(2,1)} fusion(bf16[2048,2048]{1,0:T(8,128)(2,1)S(1)} %copy-done.3, f32[2048]{0:T(1024)S(1)} %bitcast.13, bf16[1024,2048]{1,0:T(8,128)(2,1)S(1)} %fusion.28), kind=kOutput, calls=%fused_computation.43 | convolution fusion | flops 4309647360 | bytes 12591104 | tf_op jit(solution)/shard_map/dot_general | solution.py:89
  12.2 2.0 collective-permute-start.2
  14.2 1.9 collective-permute-start.1
  16.1 0.0 collective-permute-done.2
  16.1 2.1 collective-permute-start.3
  18.2 5.7 %multiply_convert_fusion.6 = bf16[512,2048]{1,0:T(8,128)(2,1)} fusion(bf16[2048,2048]{1,0:T(8,128)(2,1)S(1)} %copy-done.3, f32[2048]{0:T(1024)S(1)} %bitcast.14, bf16[1024,2048]{1,0:T(8,128)(2,1)S(1)} %fusion.28), kind=kOutput, calls=%fused_computation.44 | convolution fusion | flops 4309647360 | bytes 12591104 | tf_op jit(solution)/shard_map/dot_general | solution.py:89
  23.9 4.2 %collective-permute-start.4 = (bf16[512,2048]{1,0:T(8,128)(2,1)}, bf16[512,2048]{1,0:T(8,128)(2,1)}, u32[]{:S(2)}, u32[]{:S(2)}) collective-permute-start(bf16[512,2048]{1,0:T(8,128)(2,1)} %multiply_convert_fusion.6), channel_id=1, source_target_pairs={{0,3},{1,2},{2,5},{3,4},{4,7},{5,6},{6,9},{7,8},{8,11},{9,10},{10,... | collective-permute-start | bytes 6291464 | tf_op jit(solution)/shard_map/ppermute | solution.py:22
  28.1 0.0 collective-permute-start
  28.1 21.3 %collective-permute-start.5 = (bf16[512,2048]{1,0:T(8,128)(2,1)}, bf16[512,2048]{1,0:T(8,128)(2,1)}, u32[]{:S(2)}, u32[]{:S(2)}) collective-permute-start(bf16[512,2048]{1,0:T(8,128)(2,1)} %multiply_convert_fusion.5), channel_id=1, source_target_pairs={{0,3},{1,2},{2,5},{3,4},{4,7},{5,6},{6,9},{7,8},{8,11},{9,10},{10,... | collective-permute-start | bytes 6291464 | tf_op jit(solution)/shard_map/ppermute | solution.py:22
  49.4 6.0 %collective-permute-done.1 = bf16[512,2048]{1,0:T(8,128)(2,1)S(1)} collective-permute-done((bf16[512,2048]{1,0:T(8,128)(2,1)}, bf16[512,2048]{1,0:T(8,128)(2,1)S(1)}, u32[]{:S(2)}, u32[]{:S(2)}) %collective-permute-start.1) | collective-permute-done | bytes 2097184 | tf_op jit(solution)/shard_map/ppermute | solution.py:22
  55.4 0.0 collective-permute-done.3
  55.4 2.4 add.12
  57.8 22.6 %collective-permute-done.4 = bf16[512,2048]{1,0:T(8,128)(2,1)} collective-permute-done((bf16[512,2048]{1,0:T(8,128)(2,1)}, bf16[512,2048]{1,0:T(8,128)(2,1)}, u32[]{:S(2)}, u32[]{:S(2)}) %collective-permute-start.4) | collective-permute-done | bytes 2097184 | tf_op jit(solution)/shard_map/ppermute | solution.py:22
  80.3 20.1 %collective-permute-done = bf16[512,2048]{1,0:T(8,128)(2,1)} collective-permute-done((bf16[512,2048]{1,0:T(8,128)(2,1)}, bf16[512,2048]{1,0:T(8,128)(2,1)}, u32[]{:S(2)}, u32[]{:S(2)}) %collective-permute-start) | collective-permute-done | bytes 2097184 | tf_op jit(solution)/shard_map/ppermute | solution.py:22
  100.4 25.2 %collective-permute-done.5 = bf16[512,2048]{1,0:T(8,128)(2,1)} collective-permute-done((bf16[512,2048]{1,0:T(8,128)(2,1)}, bf16[512,2048]{1,0:T(8,128)(2,1)}, u32[]{:S(2)}, u32[]{:S(2)}) %collective-permute-start.5) | collective-permute-done | bytes 2097184 | tf_op jit(solution)/shard_map/ppermute | solution.py:22
  125.7 12.9 %multiply_convert_fusion.2 = bf16[1024,2048]{1,0:T(8,128)(2,1)S(1)} fusion(bf16[512,2048]{1,0:T(8,128)(2,1)} %collective-permute-done.5, bf16[512,2048]{1,0:T(8,128)(2,1)} %collective-permute-done.4, bf16[512,2048]{1,0:T(8,128)(2,1)S(1)} %add.12, bf16[512,2048]{1,0:T(8,128)(2,1)} %collective-permute-done, pred[]{:T(512)S(6)} %eq.17, ...), kind=kOutput, calls=%fused_computation.34 | convolution fusion | flops 8673820672 | bytes 16777216 | tf_op jit(solution)/shard_map/dot_general | solution.py:66
  138.6 0.0 copy-start.2
  138.6 1.6 collective-permute-start.8
  140.1 0.1 collective-permute-start.6
  140.2 0.4 fusion.47
  140.6 0.8 collective-permute-start.9
  141.4 0.8 collective-permute-start.11
  142.1 0.1 slice.44
  142.2 0.0 copy-done.2
  142.3 1.3 collective-permute-start.7
  143.6 0.0 collective-permute-done.9
  143.6 1.3 collective-permute-start.10
  144.9 0.0 collective-permute-done.11
  144.9 1.5 collective-permute-start.12
  146.4 53.0 %collective-permute-done.7 = bf16[256,2048]{1,0:T(8,128)(2,1)S(1)} collective-permute-done((bf16[256,2048]{1,0:T(8,128)(2,1)S(1)}, bf16[256,2048]{1,0:T(8,128)(2,1)S(1)}, u32[]{:S(2)}, u32[]{:S(2)}) %collective-permute-start.7) | collective-permute-done | bytes 1048608 | tf_op jit(solution)/shard_map/ppermute | solution.py:22
  199.3 21.4 %collective-permute-done.8 = bf16[1024,2048]{1,0:T(8,128)(2,1)S(1)} collective-permute-done((bf16[1024,2048]{1,0:T(8,128)(2,1)S(1)}, bf16[1024,2048]{1,0:T(8,128)(2,1)S(1)}, u32[]{:S(2)}, u32[]{:S(2)}) %collective-permute-start.8) | collective-permute-done | bytes 4194336 | tf_op jit(solution)/shard_map/ppermute | solution.py:22
  220.7 1.2 slice_add_fusion.2
  221.9 2.9 collective-permute-done.10
  224.8 56.2 %collective-permute-done.12 = bf16[384,2048]{1,0:T(8,128)(2,1)S(1)} collective-permute-done((bf16[384,2048]{1,0:T(8,128)(2,1)S(1)}, bf16[384,2048]{1,0:T(8,128)(2,1)S(1)}, u32[]{:S(2)}, u32[]{:S(2)}) %collective-permute-start.12) | collective-permute-done | bytes 1572896 | tf_op jit(solution)/shard_map/ppermute | solution.py:22
  281.0 0.3 slice_add_fusion.1
  281.3 0.0 collective-permute-done.6
  281.4 0.0 copy-start.4
  281.4 2.0 copy-done.4
  283.3 0.0 copy-start.1
  283.3 13.6 %fusion.33 = bf16[1,1024,2048]{2,1,0:T(8,128)(2,1)} fusion(bf16[1024,2048]{1,0:T(8,128)(2,1)} %copy-done.2, bf16[384,2048]{1,0:T(8,128)(2,1)S(1)} %get-tuple-element.6, bf16[384,2048]{1,0:T(8,128)(2,1)S(1)} %get-tuple-element.5, bf16[256,2048]{1,0:T(8,128)(2,1)} %slice_add_fusion.2, bf16[1024,2048]{1,0:T(8,128)(2,1)} %copy-done.4, pred[]{:T(512)S(6)} %eq.17), kind=kOutput, calls=%fused_computation.39 | convolution fusion | flops 8665432064 | bytes 16777216 | tf_op jit(solution)/shard_map/dot_general | solution.py:66
  297.0 0.0 copy-done.1
  (1 shorter events, 0.0 us)
Async XLA Ops:
  0.0 0.9 copy-start
  1.8 4.6 %copy-start.3 = (bf16[2048,2048]{1,0:T(8,128)(2,1)S(1)}, bf16[2048,2048]{1,0:T(8,128)(2,1)}, u32[]{:S(2)}) copy-start(bf16[2048,2048]{1,0:T(8,128)(2,1)} %param.6) | copy-start | bytes 25165828
  12.2 3.9 %collective-permute-start.2 = (bf16[512,2048]{1,0:T(8,128)(2,1)}, bf16[512,2048]{1,0:T(8,128)(2,1)}, u32[]{:S(2)}, u32[]{:S(2)}) collective-permute-start(bf16[512,2048]{1,0:T(8,128)(2,1)} %multiply_convert_fusion.5), channel_id=1, source_target_pairs={{30,6},{31,7},{62,38},{63,39},{94,70},{95,71},{126,102},{127,103}} | collective-permute-start | bytes 6291464 | tf_op jit(solution)/shard_map/ppermute | solution.py:22
  14.2 41.2 %collective-permute-start.1 = (bf16[512,2048]{1,0:T(8,128)(2,1)}, bf16[512,2048]{1,0:T(8,128)(2,1)S(1)}, u32[]{:S(2)}, u32[]{:S(2)}) collective-permute-start(bf16[512,2048]{1,0:T(8,128)(2,1)} %multiply_convert_fusion.5), channel_id=1, source_target_pairs={{0,2},{1,3},{2,4},{3,5},{4,6},{5,7},{6,8},{7,9},{8,10},{9,11},{10,... | collective-permute-start | bytes 6291464 | tf_op jit(solution)/shard_map/ppermute | solution.py:22
  16.1 39.3 %collective-permute-start.3 = (bf16[512,2048]{1,0:T(8,128)(2,1)}, bf16[512,2048]{1,0:T(8,128)(2,1)}, u32[]{:S(2)}, u32[]{:S(2)}) collective-permute-start(bf16[512,2048]{1,0:T(8,128)(2,1)} %collective-permute-done.2), channel_id=1, source_target_pairs={{6,32},{7,33},{38,64},{39,65},{70,96},{71,97},{102,0},{103,1}} | collective-permute-start | bytes 6291464 | tf_op jit(solution)/shard_map/ppermute | solution.py:22
  23.9 56.5 %collective-permute-start.4 = (bf16[512,2048]{1,0:T(8,128)(2,1)}, bf16[512,2048]{1,0:T(8,128)(2,1)}, u32[]{:S(2)}, u32[]{:S(2)}) collective-permute-start(bf16[512,2048]{1,0:T(8,128)(2,1)} %multiply_convert_fusion.6), channel_id=1, source_target_pairs={{0,3},{1,2},{2,5},{3,4},{4,7},{5,6},{6,9},{7,8},{8,11},{9,10},{10,... | collective-permute-start | bytes 6291464 | tf_op jit(solution)/shard_map/ppermute | solution.py:22
  28.1 72.4 %collective-permute-start = (bf16[512,2048]{1,0:T(8,128)(2,1)}, bf16[512,2048]{1,0:T(8,128)(2,1)}, u32[]{:S(2)}, u32[]{:S(2)}) collective-permute-start(bf16[512,2048]{1,0:T(8,128)(2,1)} %multiply_convert_fusion.6), channel_id=1, source_target_pairs={{0,2},{1,3},{2,4},{3,5},{4,6},{5,7},{6,8},{7,9},{8,10},{9,11},{10,... | collective-permute-start | bytes 6291464 | tf_op jit(solution)/shard_map/ppermute | solution.py:22
  28.1 97.6 %collective-permute-start.5 = (bf16[512,2048]{1,0:T(8,128)(2,1)}, bf16[512,2048]{1,0:T(8,128)(2,1)}, u32[]{:S(2)}, u32[]{:S(2)}) collective-permute-start(bf16[512,2048]{1,0:T(8,128)(2,1)} %multiply_convert_fusion.5), channel_id=1, source_target_pairs={{0,3},{1,2},{2,5},{3,4},{4,7},{5,6},{6,9},{7,8},{8,11},{9,10},{10,... | collective-permute-start | bytes 6291464 | tf_op jit(solution)/shard_map/ppermute | solution.py:22
  138.6 3.7 %copy-start.2 = (bf16[1024,2048]{1,0:T(8,128)(2,1)}, bf16[1024,2048]{1,0:T(8,128)(2,1)S(1)}, u32[]{:S(2)}) copy-start(bf16[1024,2048]{1,0:T(8,128)(2,1)S(1)} %multiply_convert_fusion.2) | copy-start | bytes 12582916
  138.6 82.1 %collective-permute-start.8 = (bf16[1024,2048]{1,0:T(8,128)(2,1)S(1)}, bf16[1024,2048]{1,0:T(8,128)(2,1)S(1)}, u32[]{:S(2)}, u32[]{:S(2)}) collective-permute-start(bf16[1024,2048]{1,0:T(8,128)(2,1)S(1)} %multiply_convert_fusion.2), channel_id=1, source_target_pairs={{0,5},{1,4},{2,7},{3,6},{8,13},{9,12},{10,15},{11,14},{16,21},{17,... | collective-permute-start | bytes 12582920 | tf_op jit(solution)/shard_map/ppermute | solution.py:22
  140.1 141.2 %collective-permute-start.6 = (bf16[1024,2048]{1,0:T(8,128)(2,1)S(1)}, bf16[1024,2048]{1,0:T(8,128)(2,1)S(1)}, u32[]{:S(2)}, u32[]{:S(2)}) collective-permute-start(bf16[1024,2048]{1,0:T(8,128)(2,1)S(1)} %multiply_convert_fusion.2), channel_id=1, source_target_pairs={{0,4},{1,5},{2,6},{3,7},{4,8},{5,9},{6,10},{7,11},{8,12},{9,13},{1... | collective-permute-start | bytes 12582920 | tf_op jit(solution)/shard_map/ppermute | solution.py:22
  140.6 3.0 collective-permute-start.9
  141.4 3.5 %collective-permute-start.11 = (bf16[384,2048]{1,0:T(8,128)(2,1)S(1)}, bf16[384,2048]{1,0:T(8,128)(2,1)S(1)}, u32[]{:S(2)}, u32[]{:S(2)}) collective-permute-start(bf16[384,2048]{1,0:T(8,128)(2,1)S(1)} %get-tuple-element.8), channel_id=1, source_target_pairs={{4,12},{5,13},{6,14},{7,15},{12,20},{13,21},{14,22},{15,23},{20,28... | collective-permute-start | bytes 4718600 | tf_op jit(solution)/shard_map/ppermute | solution.py:22
  142.3 57.1 %collective-permute-start.7 = (bf16[256,2048]{1,0:T(8,128)(2,1)S(1)}, bf16[256,2048]{1,0:T(8,128)(2,1)S(1)}, u32[]{:S(2)}, u32[]{:S(2)}) collective-permute-start(bf16[256,2048]{1,0:T(8,128)(2,1)S(1)} %slice.44), channel_id=1, source_target_pairs={{4,9},{5,8},{6,11},{7,10},{12,17},{13,16},{14,19},{15,18},{20,25},... | collective-permute-start | bytes 3145736 | tf_op jit(solution)/shard_map/ppermute | solution.py:22
  143.6 81.3 %collective-permute-start.10 = (bf16[384,2048]{1,0:T(8,128)(2,1)S(1)}, bf16[384,2048]{1,0:T(8,128)(2,1)S(1)}, u32[]{:S(2)}, u32[]{:S(2)}) collective-permute-start(bf16[384,2048]{1,0:T(8,128)(2,1)S(1)} %collective-permute-done.9), channel_id=1, source_target_pairs={{4,33},{5,32},{6,35},{7,34},{12,9},{13,8},{14,11},{15,10},{20,17},... | collective-permute-start | bytes 4718600 | tf_op jit(solution)/shard_map/ppermute | solution.py:22
  144.9 136.2 %collective-permute-start.12 = (bf16[384,2048]{1,0:T(8,128)(2,1)S(1)}, bf16[384,2048]{1,0:T(8,128)(2,1)S(1)}, u32[]{:S(2)}, u32[]{:S(2)}) collective-permute-start(bf16[384,2048]{1,0:T(8,128)(2,1)S(1)} %collective-permute-done.11), channel_id=1, source_target_pairs={{4,33},{5,32},{6,35},{7,34},{12,9},{13,8},{14,11},{15,10},{20,17},... | collective-permute-start | bytes 4718600 | tf_op jit(solution)/shard_map/ppermute | solution.py:22
  281.4 2.0 copy-start.4
  283.3 13.6 %copy-start.1 = (f32[16,2048]{1,0:T(8,128)S(1)}, f32[16,2048]{1,0:T(8,128)}, u32[]{:S(2)}) copy-start(f32[16,2048]{1,0:T(8,128)} %param.7) | copy-start | bytes 393220

commit v15 on v12

--- a/solution.py
+++ b/solution.py
@@ -90,13 +90,16 @@
                           preferred_element_type=jnp.float32)
         chunks.append((product * norm_scale).astype(jnp.bfloat16))
 
-    boundary = lambda t, r, n, m: ((t - 12) % n, r) if ring_of(t) == 3 and t % 4 == 3 else None
     boundary_exit = lambda t, r, n, m: ((t + 13) % n, r) if ring_of(t) == 0 and t % 4 == 3 else None
     not_boundary = lambda t, r, n, m: None if ring_of(t) == 3 and t % 4 == 3 else ((t + 1) % n, r)
     own_rows = [sent(chunks[0], direct(1, 0))]
     other_rows = [sent(chunks[0], direct(1, 1))]
-    own_rows.append(sent(chunks[1], not_boundary) + sent(sent(chunks[1], boundary), boundary_exit))
-    other_rows.append(sent(chunks[1], direct(1, 1)))
+    crossing = lambda t, r, n, m: (((t - 12) if ring_of(t) == 3 else (t + 4)) % n, r) if t % 4 == 3 else None
+    handed = lambda t, r, n, m: ((((t + 13) if ring_of(t) == 0 else (t - 3)) % n), 1 - r) if t % 4 == 3 else None
+    not_cross = lambda t, r, n, m: None if t % 4 == 3 else ((t + 1) % n, 1 - r)
+    crossed = sent(chunks[1], crossing)
+    own_rows.append(sent(chunks[1], not_boundary) + sent(crossed, boundary_exit))
+    other_rows.append(sent(chunks[1], not_cross) + sent(crossed, handed))
     earlier = natural(own_rows, other_rows, row)
     current = level_product(jnp.concatenate(chunks, axis=0), earlier, norm_scale)
 

time: 294 us -> 294 us (level)
  waiting for transfers between devices: 206 us -> 194 us
  starting transfers between devices: 38.7 us -> 45.5 us
  other arithmetic: 8.04 us -> 11 us
    ppermute x13 -> x14, waiting for transfers between devices: 206 us -> 194 us  [sent(): return lax.ppermute(value, ('tm', 'row'), pairs)]
    ppermute x13 -> x14, starting transfers between devices: 38.7 us -> 45.5 us  [sent(): return lax.ppermute(value, ('tm', 'row'), pairs)]
    add x1 -> x2, other arithmetic: 2.35 us -> 5.35 us  [the longest x1 3 us: shards(): other_rows.append(sent(chunks[1], not_cross) + sent(crossed, handed))]
  transfers between devices with their start and end apart: 13 -> 14, of which waited for: 7 -> 6; matrix products, arithmetic and copies ran while one was open for 3% -> 4% of each run, Pallas kernels for 0% -> 0%
where the time goes in v15:
time: 294 us; the launch traced here: 291 us
  waiting for transfers between devices  194 us (66%)
  starting transfers between devices  45.5 us (15%)
  matrix products  38.7 us (13%)
  other arithmetic  11 us (4%)
    ppermute x14, waiting for transfers between devices, sent(): return lax.ppermute(value, ('tm', 'row'), pairs)  194 us
    ppermute x14, starting transfers between devices, sent(): return lax.ppermute(value, ('tm', 'row'), pairs)  45.5 us
    dot_general x2, matrix products, level_product(): total = jnp.dot(later, earlier, preferred_element_type=jnp.float32)  26.4 us
    dot_general x2, matrix products, shards(): jnp.dot(left_factor[c * chunk_rows:(c + 1) * chunk_rows], right_factor, p...  11.4 us
  transfers between devices with their start and end apart: 14, of which 6 were waited for; matrix products, arithmetic and copies ran while one was open for 4% of the time, Pallas kernels for 0%

profile of v15, /device:TPU:96, one launch (start us, length us, event | category | flops | bytes accessed | tf_op | source)
XLA Modules:
  0.0 290.8 jit_solution(8446784050481063513)
XLA Ops:
  0.0 0.0 copy-start
  0.0 0.7 multiply_bitcast_fusion
  0.7 0.2 copy-done
  0.9 0.9 fusion.39
  1.8 0.0 copy-start.3
  1.8 3.4 %fusion.28 = bf16[1024,2048]{1,0:T(8,128)(2,1)S(1)} fusion(bf16[1,1024,2048]{2,1,0:T(8,128)(2,1)} %param.5, f32[2048]{0:T(1024)S(1)} %bitcast.12), kind=kLoop, calls=%fused_computation.32 | loop fusion | flops 6291456 | bytes 8396800 | tf_op jit(solution)/shard_map/convert_element_type | solution.py:85
  5.3 1.2 copy-done.3
  6.5 5.7 %multiply_convert_fusion.5 = bf16[512,2048]{1,0:T(8,128)(2,1)} fusion(bf16[2048,2048]{1,0:T(8,128)(2,1)S(1)} %copy-done.3, f32[2048]{0:T(1024)S(1)} %bitcast.13, bf16[1024,2048]{1,0:T(8,128)(2,1)S(1)} %fusion.28), kind=kOutput, calls=%fused_computation.43 | convolution fusion | flops 4309647360 | bytes 12591104 | tf_op jit(solution)/shard_map/dot_general | solution.py:89
  12.2 2.0 collective-permute-start.2
  14.2 5.9 %collective-permute-start.5 = (bf16[512,2048]{1,0:T(8,128)(2,1)}, bf16[512,2048]{1,0:T(8,128)(2,1)}, u32[]{:S(2)}, u32[]{:S(2)}) collective-permute-start(bf16[512,2048]{1,0:T(8,128)(2,1)} %multiply_convert_fusion.5), channel_id=1, source_target_pairs={{0,3},{1,2},{2,5},{3,4},{4,7},{5,6},{8,11},{9,10},{10,13},{11,12},... | collective-permute-start | bytes 6291464 | tf_op jit(solution)/shard_map/ppermute | solution.py:22
  20.1 1.9 collective-permute-start.1
  22.0 0.0 collective-permute-done.2
  22.0 1.3 collective-permute-start.6
  23.3 5.7 %multiply_convert_fusion.6 = bf16[512,2048]{1,0:T(8,128)(2,1)} fusion(bf16[2048,2048]{1,0:T(8,128)(2,1)S(1)} %copy-done.3, f32[2048]{0:T(1024)S(1)} %bitcast.14, bf16[1024,2048]{1,0:T(8,128)(2,1)S(1)} %fusion.28), kind=kOutput, calls=%fused_computation.44 | convolution fusion | flops 4309647360 | bytes 12591104 | tf_op jit(solution)/shard_map/dot_general | solution.py:89
  29.1 2.0 collective-permute-start.3
  31.1 1.5 collective-permute-start.4
  32.5 32.1 %collective-permute-done.5 = bf16[512,2048]{1,0:T(8,128)(2,1)} collective-permute-done((bf16[512,2048]{1,0:T(8,128)(2,1)}, bf16[512,2048]{1,0:T(8,128)(2,1)}, u32[]{:S(2)}, u32[]{:S(2)}) %collective-permute-start.5) | collective-permute-done | bytes 2097184 | tf_op jit(solution)/shard_map/ppermute | solution.py:22
  64.6 22.8 %collective-permute-start = (bf16[512,2048]{1,0:T(8,128)(2,1)}, bf16[512,2048]{1,0:T(8,128)(2,1)}, u32[]{:S(2)}, u32[]{:S(2)}) collective-permute-start(bf16[512,2048]{1,0:T(8,128)(2,1)} %multiply_convert_fusion.6), channel_id=1, source_target_pairs={{0,2},{1,3},{2,4},{3,5},{4,6},{5,7},{6,8},{7,9},{8,10},{9,11},{10,... | collective-permute-start | bytes 6291464 | tf_op jit(solution)/shard_map/ppermute | solution.py:22
  87.4 33.6 %collective-permute-done.6 = bf16[512,2048]{1,0:T(8,128)(2,1)} collective-permute-done((bf16[512,2048]{1,0:T(8,128)(2,1)}, bf16[512,2048]{1,0:T(8,128)(2,1)}, u32[]{:S(2)}, u32[]{:S(2)}) %collective-permute-start.6) | collective-permute-done | bytes 2097184 | tf_op jit(solution)/shard_map/ppermute | solution.py:22
  121.0 3.0 %add.16 = bf16[512,2048]{1,0:T(8,128)(2,1)S(1)} add(bf16[512,2048]{1,0:T(8,128)(2,1)} %collective-permute-done.5, bf16[512,2048]{1,0:T(8,128)(2,1)} %collective-permute-done.6) | non-fusion elementwise | flops 1048576 | bytes 6291456 | tf_op jit(solution)/shard_map/add | solution.py:102
  124.0 0.0 collective-permute-done.1
  124.0 0.0 collective-permute-done.3
  124.0 2.4 add.15
  126.4 0.4 collective-permute-done.4
  126.8 0.0 collective-permute-done
  126.8 12.7 %multiply_convert_fusion.2 = bf16[1024,2048]{1,0:T(8,128)(2,1)S(1)} fusion(bf16[512,2048]{1,0:T(8,128)(2,1)S(1)} %add.16, bf16[512,2048]{1,0:T(8,128)(2,1)} %collective-permute-done.4, bf16[512,2048]{1,0:T(8,128)(2,1)S(1)} %add.15, bf16[512,2048]{1,0:T(8,128)(2,1)} %collective-permute-done, pred[]{:T(512)S(6)} %eq.17, ...), kind=kOutput, calls=%fused_computation.34 | convolution fusion | flops 8673820672 | bytes 16777216 | tf_op jit(solution)/shard_map/dot_general | solution.py:66
  139.5 0.0 copy-start.2
  139.5 2.7 collective-permute-start.9
  142.2 0.1 collective-permute-start.7
  142.3 0.2 slice.48
  142.4 0.8 collective-permute-start.12
  143.2 0.2 slice.46
  143.4 0.8 collective-permute-start.10
  144.1 0.1 slice.44
  144.2 0.0 copy-done.2
  144.2 1.3 collective-permute-start.8
  145.5 0.0 collective-permute-done.12
  145.5 1.3 collective-permute-start.13
  146.8 0.0 collective-permute-done.10
  146.8 1.3 collective-permute-start.11
  148.1 55.1 %collective-permute-done.8 = bf16[304,2048]{1,0:T(8,128)(2,1)S(1)} collective-permute-done((bf16[304,2048]{1,0:T(8,128)(2,1)S(1)}, bf16[304,2048]{1,0:T(8,128)(2,1)S(1)}, u32[]{:S(2)}, u32[]{:S(2)}) %collective-permute-start.8) | collective-permute-done | bytes 1245216 | tf_op jit(solution)/shard_map/ppermute | solution.py:22
  203.2 27.4 %collective-permute-done.9 = bf16[1024,2048]{1,0:T(8,128)(2,1)S(1)} collective-permute-done((bf16[1024,2048]{1,0:T(8,128)(2,1)S(1)}, bf16[1024,2048]{1,0:T(8,128)(2,1)S(1)}, u32[]{:S(2)}, u32[]{:S(2)}) %collective-permute-start.9) | collective-permute-done | bytes 4194336 | tf_op jit(solution)/shard_map/ppermute | solution.py:22
  230.7 1.2 slice_add_fusion.2
  231.9 0.0 collective-permute-done.13
  231.9 0.1 slice_add_fusion.1
  232.1 44.9 %collective-permute-done.11 = bf16[368,2048]{1,0:T(8,128)(2,1)S(1)} collective-permute-done((bf16[368,2048]{1,0:T(8,128)(2,1)S(1)}, bf16[368,2048]{1,0:T(8,128)(2,1)S(1)}, u32[]{:S(2)}, u32[]{:S(2)}) %collective-permute-start.11) | collective-permute-done | bytes 1507360 | tf_op jit(solution)/shard_map/ppermute | solution.py:22
  277.0 0.2 slice_add_fusion
  277.1 0.0 collective-permute-done.7
  277.1 0.0 copy-start.1
  277.2 13.7 %fusion.33 = bf16[1,1024,2048]{2,1,0:T(8,128)(2,1)} fusion(bf16[1024,2048]{1,0:T(8,128)(2,1)} %copy-done.2, bf16[352,2048]{1,0:T(8,128)(2,1)S(1)} %slice_add_fusion.1, bf16[368,2048]{1,0:T(8,128)(2,1)S(1)} %slice_add_fusion, bf16[304,2048]{1,0:T(8,128)(2,1)} %slice_add_fusion.2, bf16[1024,2048]{1,0:T(8,128)(2,1)} %collective-permute-done.7, pred[]{:T(512)S(6)} %eq.17), kind=kOutput, calls=%fused_computation.39 | convolution fusion | flops 8665432064 | bytes 16777216 | tf_op jit(solution)/shard_map/dot_general | solution.py:66
  290.8 0.0 copy-done.1
  (1 shorter events, 0.0 us)
Async XLA Ops:
  0.0 0.9 copy-start
  1.8 4.6 %copy-start.3 = (bf16[2048,2048]{1,0:T(8,128)(2,1)S(1)}, bf16[2048,2048]{1,0:T(8,128)(2,1)}, u32[]{:S(2)}) copy-start(bf16[2048,2048]{1,0:T(8,128)(2,1)} %param.6) | copy-start | bytes 25165828
  12.2 9.8 %collective-permute-start.2 = (bf16[512,2048]{1,0:T(8,128)(2,1)}, bf16[512,2048]{1,0:T(8,128)(2,1)}, u32[]{:S(2)}, u32[]{:S(2)}) collective-permute-start(bf16[512,2048]{1,0:T(8,128)(2,1)} %multiply_convert_fusion.5), channel_id=1, source_target_pairs={{6,14},{7,15},{14,22},{15,23},{22,30},{23,31},{30,6},{31,7},{38,46... | collective-permute-start | bytes 6291464 | tf_op jit(solution)/shard_map/ppermute | solution.py:22
  14.2 50.5 %collective-permute-start.5 = (bf16[512,2048]{1,0:T(8,128)(2,1)}, bf16[512,2048]{1,0:T(8,128)(2,1)}, u32[]{:S(2)}, u32[]{:S(2)}) collective-permute-start(bf16[512,2048]{1,0:T(8,128)(2,1)} %multiply_convert_fusion.5), channel_id=1, source_target_pairs={{0,3},{1,2},{2,5},{3,4},{4,7},{5,6},{8,11},{9,10},{10,13},{11,12},... | collective-permute-start | bytes 6291464 | tf_op jit(solution)/shard_map/ppermute | solution.py:22
  20.1 103.9 %collective-permute-start.1 = (bf16[512,2048]{1,0:T(8,128)(2,1)}, bf16[512,2048]{1,0:T(8,128)(2,1)S(1)}, u32[]{:S(2)}, u32[]{:S(2)}) collective-permute-start(bf16[512,2048]{1,0:T(8,128)(2,1)} %multiply_convert_fusion.5), channel_id=1, source_target_pairs={{0,2},{1,3},{2,4},{3,5},{4,6},{5,7},{6,8},{7,9},{8,10},{9,11},{10,... | collective-permute-start | bytes 6291464 | tf_op jit(solution)/shard_map/ppermute | solution.py:22
  22.0 98.9 %collective-permute-start.6 = (bf16[512,2048]{1,0:T(8,128)(2,1)}, bf16[512,2048]{1,0:T(8,128)(2,1)}, u32[]{:S(2)}, u32[]{:S(2)}) collective-permute-start(bf16[512,2048]{1,0:T(8,128)(2,1)} %collective-permute-done.2), channel_id=1, source_target_pairs={{6,33},{7,32},{14,9},{15,8},{22,17},{23,16},{30,25},{31,24},{38,65... | collective-permute-start | bytes 6291464 | tf_op jit(solution)/shard_map/ppermute | solution.py:22
  29.1 94.9 %collective-permute-start.3 = (bf16[512,2048]{1,0:T(8,128)(2,1)}, bf16[512,2048]{1,0:T(8,128)(2,1)}, u32[]{:S(2)}, u32[]{:S(2)}) collective-permute-start(bf16[512,2048]{1,0:T(8,128)(2,1)} %collective-permute-done.2), channel_id=1, source_target_pairs={{6,32},{7,33},{38,64},{39,65},{70,96},{71,97},{102,0},{103,1}} | collective-permute-start | bytes 6291464 | tf_op jit(solution)/shard_map/ppermute | solution.py:22
  31.1 95.7 %collective-permute-start.4 = (bf16[512,2048]{1,0:T(8,128)(2,1)}, bf16[512,2048]{1,0:T(8,128)(2,1)}, u32[]{:S(2)}, u32[]{:S(2)}) collective-permute-start(bf16[512,2048]{1,0:T(8,128)(2,1)} %multiply_convert_fusion.6), channel_id=1, source_target_pairs={{0,3},{1,2},{2,5},{3,4},{4,7},{5,6},{6,9},{7,8},{8,11},{9,10},{10,... | collective-permute-start | bytes 6291464 | tf_op jit(solution)/shard_map/ppermute | solution.py:22
  64.6 62.1 %collective-permute-start = (bf16[512,2048]{1,0:T(8,128)(2,1)}, bf16[512,2048]{1,0:T(8,128)(2,1)}, u32[]{:S(2)}, u32[]{:S(2)}) collective-permute-start(bf16[512,2048]{1,0:T(8,128)(2,1)} %multiply_convert_fusion.6), channel_id=1, source_target_pairs={{0,2},{1,3},{2,4},{3,5},{4,6},{5,7},{6,8},{7,9},{8,10},{9,11},{10,... | collective-permute-start | bytes 6291464 | tf_op jit(solution)/shard_map/ppermute | solution.py:22
  139.5 4.7 %copy-start.2 = (bf16[1024,2048]{1,0:T(8,128)(2,1)}, bf16[1024,2048]{1,0:T(8,128)(2,1)S(1)}, u32[]{:S(2)}) copy-start(bf16[1024,2048]{1,0:T(8,128)(2,1)S(1)} %multiply_convert_fusion.2) | copy-start | bytes 12582916
  139.5 91.2 %collective-permute-start.9 = (bf16[1024,2048]{1,0:T(8,128)(2,1)S(1)}, bf16[1024,2048]{1,0:T(8,128)(2,1)S(1)}, u32[]{:S(2)}, u32[]{:S(2)}) collective-permute-start(bf16[1024,2048]{1,0:T(8,128)(2,1)S(1)} %multiply_convert_fusion.2), channel_id=1, source_target_pairs={{0,5},{1,4},{2,7},{3,6},{8,13},{9,12},{10,15},{11,14},{16,21},{17,... | collective-permute-start | bytes 12582920 | tf_op jit(solution)/shard_map/ppermute | solution.py:22
  142.2 134.9 %collective-permute-start.7 = (bf16[1024,2048]{1,0:T(8,128)(2,1)S(1)}, bf16[1024,2048]{1,0:T(8,128)(2,1)}, u32[]{:S(2)}, u32[]{:S(2)}) collective-permute-start(bf16[1024,2048]{1,0:T(8,128)(2,1)S(1)} %multiply_convert_fusion.2), channel_id=1, source_target_pairs={{0,4},{1,5},{2,6},{3,7},{4,8},{5,9},{6,10},{7,11},{8,12},{9,13},{1... | collective-permute-start | bytes 12582920 | tf_op jit(solution)/shard_map/ppermute | solution.py:22
  142.4 3.1 %collective-permute-start.12 = (bf16[352,2048]{1,0:T(8,128)(2,1)S(1)}, bf16[352,2048]{1,0:T(8,128)(2,1)S(1)}, u32[]{:S(2)}, u32[]{:S(2)}) collective-permute-start(bf16[352,2048]{1,0:T(8,128)(2,1)S(1)} %slice.48), channel_id=1, source_target_pairs={{4,12},{5,13},{6,14},{7,15},{12,20},{13,21},{14,22},{15,23},{20,28... | collective-permute-start | bytes 4325384 | tf_op jit(solution)/shard_map/ppermute | solution.py:22
  143.4 3.5 %collective-permute-start.10 = (bf16[368,2048]{1,0:T(8,128)(2,1)S(1)}, bf16[368,2048]{1,0:T(8,128)(2,1)S(1)}, u32[]{:S(2)}, u32[]{:S(2)}) collective-permute-start(bf16[368,2048]{1,0:T(8,128)(2,1)S(1)} %slice.46), channel_id=1, source_target_pairs={{4,12},{5,13},{6,14},{7,15},{12,20},{13,21},{14,22},{15,23},{20,28... | collective-permute-start | bytes 4521992 | tf_op jit(solution)/shard_map/ppermute | solution.py:22
  144.2 59.0 %collective-permute-start.8 = (bf16[304,2048]{1,0:T(8,128)(2,1)S(1)}, bf16[304,2048]{1,0:T(8,128)(2,1)S(1)}, u32[]{:S(2)}, u32[]{:S(2)}) collective-permute-start(bf16[304,2048]{1,0:T(8,128)(2,1)S(1)} %slice.44), channel_id=1, source_target_pairs={{4,9},{5,8},{6,11},{7,10},{12,17},{13,16},{14,19},{15,18},{20,25},... | collective-permute-start | bytes 3735560 | tf_op jit(solution)/shard_map/ppermute | solution.py:22
  145.5 86.4 %collective-permute-start.13 = (bf16[352,2048]{1,0:T(8,128)(2,1)S(1)}, bf16[352,2048]{1,0:T(8,128)(2,1)S(1)}, u32[]{:S(2)}, u32[]{:S(2)}) collective-permute-start(bf16[352,2048]{1,0:T(8,128)(2,1)S(1)} %collective-permute-done.12), channel_id=1, source_target_pairs={{4,33},{5,32},{6,35},{7,34},{12,9},{13,8},{14,11},{15,10},{20,17},... | collective-permute-start | bytes 4325384 | tf_op jit(solution)/shard_map/ppermute | solution.py:22
  146.8 130.1 %collective-permute-start.11 = (bf16[368,2048]{1,0:T(8,128)(2,1)S(1)}, bf16[368,2048]{1,0:T(8,128)(2,1)S(1)}, u32[]{:S(2)}, u32[]{:S(2)}) collective-permute-start(bf16[368,2048]{1,0:T(8,128)(2,1)S(1)} %collective-permute-done.10), channel_id=1, source_target_pairs={{4,33},{5,32},{6,35},{7,34},{12,9},{13,8},{14,11},{15,10},{20,17},... | collective-permute-start | bytes 4521992 | tf_op jit(solution)/shard_map/ppermute | solution.py:22
  277.1 13.7 %copy-start.1 = (f32[16,2048]{1,0:T(8,128)S(1)}, f32[16,2048]{1,0:T(8,128)}, u32[]{:S(2)}) copy-start(f32[16,2048]{1,0:T(8,128)} %param.7) | copy-start | bytes 393220

commit v16 on v15

--- a/solution.py
+++ b/solution.py
@@ -90,15 +90,15 @@
                           preferred_element_type=jnp.float32)
         chunks.append((product * norm_scale).astype(jnp.bfloat16))
 
-    boundary_exit = lambda t, r, n, m: ((t + 13) % n, r) if ring_of(t) == 0 and t % 4 == 3 else None
-    not_boundary = lambda t, r, n, m: None if ring_of(t) == 3 and t % 4 == 3 else ((t + 1) % n, r)
     own_rows = [sent(chunks[0], direct(1, 0))]
     other_rows = [sent(chunks[0], direct(1, 1))]
     crossing = lambda t, r, n, m: (((t - 12) if ring_of(t) == 3 else (t + 4)) % n, r) if t % 4 == 3 else None
     handed = lambda t, r, n, m: ((((t + 13) if ring_of(t) == 0 else (t - 3)) % n), 1 - r) if t % 4 == 3 else None
     not_cross = lambda t, r, n, m: None if t % 4 == 3 else ((t + 1) % n, 1 - r)
     crossed = sent(chunks[1], crossing)
-    own_rows.append(sent(chunks[1], not_boundary) + sent(crossed, boundary_exit))
+    handed_same = lambda t, r, n, m: ((((t + 13) if ring_of(t) == 0 else (t - 3)) % n), r) if t % 4 == 3 else None
+    same_not_cross = lambda t, r, n, m: None if t % 4 == 3 else ((t + 1) % n, r)
+    own_rows.append(sent(chunks[1], same_not_cross) + sent(crossed, handed_same))
     other_rows.append(sent(chunks[1], not_cross) + sent(crossed, handed))
     earlier = natural(own_rows, other_rows, row)
     current = level_product(jnp.concatenate(chunks, axis=0), earlier, norm_scale)

time: 294 us -> 297 us (1.010)
  waiting for transfers between devices: 194 us -> 213 us
  starting transfers between devices: 45.5 us -> 32.2 us
    ppermute x14, waiting for transfers between devices: 194 us -> 213 us  [sent(): return lax.ppermute(value, ('tm', 'row'), pairs)]
    ppermute x14, starting transfers between devices: 45.5 us -> 32.2 us  [sent(): return lax.ppermute(value, ('tm', 'row'), pairs)]
  transfers between devices with their start and end apart: 14 -> 14, of which waited for: 6 -> 7; matrix products, arithmetic and copies ran while one was open for 4% -> 4% of each run, Pallas kernels for 0% -> 0%
where the time goes in v16:
time: 297 us
  waiting for transfers between devices  213 us (72%)
  matrix products  38.7 us (13%)
  starting transfers between devices  32.2 us (11%)
  other arithmetic  11 us (4%)
    ppermute x14, waiting for transfers between devices, sent(): return lax.ppermute(value, ('tm', 'row'), pairs)  213 us
    ppermute x14, starting transfers between devices, sent(): return lax.ppermute(value, ('tm', 'row'), pairs)  32.2 us
    dot_general x2, matrix products, level_product(): total = jnp.dot(later, earlier, preferred_element_type=jnp.float32)  26.4 us
    dot_general x2, matrix products, shards(): jnp.dot(left_factor[c * chunk_rows:(c + 1) * chunk_rows], right_factor, p...  11.4 us
  transfers between devices with their start and end apart: 14, of which 7 were waited for; matrix products, arithmetic and copies ran while one was open for 4% of the time, Pallas kernels for 0%

profile of v16, /device:TPU:96, one launch (start us, length us, event | category | flops | bytes accessed | tf_op | source)
XLA Modules:
  0.0 296.6 jit_solution(159468726971455795)
XLA Ops:
  0.0 0.0 copy-start
  0.0 0.7 multiply_bitcast_fusion
  0.7 0.2 copy-done
  0.9 0.9 fusion.39
  1.8 0.0 copy-start.3
  1.8 3.4 %fusion.28 = bf16[1024,2048]{1,0:T(8,128)(2,1)S(1)} fusion(bf16[1,1024,2048]{2,1,0:T(8,128)(2,1)} %param.5, f32[2048]{0:T(1024)S(1)} %bitcast.12), kind=kLoop, calls=%fused_computation.32 | loop fusion | flops 6291456 | bytes 8396800 | tf_op jit(solution)/shard_map/convert_element_type | solution.py:85
  5.3 1.2 copy-done.3
  6.5 5.7 %multiply_convert_fusion.5 = bf16[512,2048]{1,0:T(8,128)(2,1)} fusion(bf16[2048,2048]{1,0:T(8,128)(2,1)S(1)} %copy-done.3, f32[2048]{0:T(1024)S(1)} %bitcast.13, bf16[1024,2048]{1,0:T(8,128)(2,1)S(1)} %fusion.28), kind=kOutput, calls=%fused_computation.43 | convolution fusion | flops 4309647360 | bytes 12591104 | tf_op jit(solution)/shard_map/dot_general | solution.py:89
  12.2 2.0 collective-permute-start.2
  14.2 5.9 %collective-permute-start.5 = (bf16[512,2048]{1,0:T(8,128)(2,1)}, bf16[512,2048]{1,0:T(8,128)(2,1)}, u32[]{:S(2)}, u32[]{:S(2)}) collective-permute-start(bf16[512,2048]{1,0:T(8,128)(2,1)} %multiply_convert_fusion.5), channel_id=1, source_target_pairs={{0,3},{1,2},{2,5},{3,4},{4,7},{5,6},{8,11},{9,10},{10,13},{11,12},... | collective-permute-start | bytes 6291464 | tf_op jit(solution)/shard_map/ppermute | solution.py:22
  20.1 1.4 collective-permute-start.1
  21.5 0.0 collective-permute-done.2
  21.5 1.3 collective-permute-start.6
  22.8 5.7 %multiply_convert_fusion.6 = bf16[512,2048]{1,0:T(8,128)(2,1)} fusion(bf16[2048,2048]{1,0:T(8,128)(2,1)S(1)} %copy-done.3, f32[2048]{0:T(1024)S(1)} %bitcast.14, bf16[1024,2048]{1,0:T(8,128)(2,1)S(1)} %fusion.28), kind=kOutput, calls=%fused_computation.44 | convolution fusion | flops 4309647360 | bytes 12591104 | tf_op jit(solution)/shard_map/dot_general | solution.py:89
  28.6 1.3 collective-permute-start.3
  29.9 2.7 collective-permute-start.4
  32.5 32.0 %collective-permute-done.5 = bf16[512,2048]{1,0:T(8,128)(2,1)} collective-permute-done((bf16[512,2048]{1,0:T(8,128)(2,1)}, bf16[512,2048]{1,0:T(8,128)(2,1)}, u32[]{:S(2)}, u32[]{:S(2)}) %collective-permute-start.5) | collective-permute-done | bytes 2097184 | tf_op jit(solution)/shard_map/ppermute | solution.py:22
  64.5 10.4 %collective-permute-start = (bf16[512,2048]{1,0:T(8,128)(2,1)}, bf16[512,2048]{1,0:T(8,128)(2,1)}, u32[]{:S(2)}, u32[]{:S(2)}) collective-permute-start(bf16[512,2048]{1,0:T(8,128)(2,1)} %multiply_convert_fusion.6), channel_id=1, source_target_pairs={{0,2},{1,3},{2,4},{3,5},{4,6},{5,7},{6,8},{7,9},{8,10},{9,11},{10,... | collective-permute-start | bytes 6291464 | tf_op jit(solution)/shard_map/ppermute | solution.py:22
  74.9 46.1 %collective-permute-done.6 = bf16[512,2048]{1,0:T(8,128)(2,1)} collective-permute-done((bf16[512,2048]{1,0:T(8,128)(2,1)}, bf16[512,2048]{1,0:T(8,128)(2,1)}, u32[]{:S(2)}, u32[]{:S(2)}) %collective-permute-start.6) | collective-permute-done | bytes 2097184 | tf_op jit(solution)/shard_map/ppermute | solution.py:22
  121.0 3.0 %add.16 = bf16[512,2048]{1,0:T(8,128)(2,1)S(1)} add(bf16[512,2048]{1,0:T(8,128)(2,1)} %collective-permute-done.5, bf16[512,2048]{1,0:T(8,128)(2,1)} %collective-permute-done.6) | non-fusion elementwise | flops 1048576 | bytes 6291456 | tf_op jit(solution)/shard_map/add | solution.py:102
  124.0 0.0 collective-permute-done.1
  124.0 0.0 collective-permute-done.3
  124.0 2.4 add.15
  126.4 8.4 %collective-permute-done.4 = bf16[512,2048]{1,0:T(8,128)(2,1)} collective-permute-done((bf16[512,2048]{1,0:T(8,128)(2,1)}, bf16[512,2048]{1,0:T(8,128)(2,1)}, u32[]{:S(2)}, u32[]{:S(2)}) %collective-permute-start.4) | collective-permute-done | bytes 2097184 | tf_op jit(solution)/shard_map/ppermute | solution.py:22
  134.8 5.3 %collective-permute-done = bf16[512,2048]{1,0:T(8,128)(2,1)} collective-permute-done((bf16[512,2048]{1,0:T(8,128)(2,1)}, bf16[512,2048]{1,0:T(8,128)(2,1)}, u32[]{:S(2)}, u32[]{:S(2)}) %collective-permute-start) | collective-permute-done | bytes 2097184 | tf_op jit(solution)/shard_map/ppermute | solution.py:22
  140.0 12.7 %multiply_convert_fusion.2 = bf16[1024,2048]{1,0:T(8,128)(2,1)S(1)} fusion(bf16[512,2048]{1,0:T(8,128)(2,1)S(1)} %add.16, bf16[512,2048]{1,0:T(8,128)(2,1)} %collective-permute-done.4, bf16[512,2048]{1,0:T(8,128)(2,1)S(1)} %add.15, bf16[512,2048]{1,0:T(8,128)(2,1)} %collective-permute-done, pred[]{:T(512)S(6)} %eq.17, ...), kind=kOutput, calls=%fused_computation.34 | convolution fusion | flops 8673820672 | bytes 16777216 | tf_op jit(solution)/shard_map/dot_general | solution.py:66
  152.8 0.0 copy-start.2
  152.8 1.7 collective-permute-start.9
  154.5 0.1 collective-permute-start.7
  154.6 0.2 slice.48
  154.8 0.8 collective-permute-start.12
  155.5 0.2 slice.46
  155.7 0.8 collective-permute-start.10
  156.5 0.1 slice.44
  156.5 0.0 copy-done.2
  156.6 1.3 collective-permute-start.8
  157.9 0.0 collective-permute-done.12
  157.9 1.3 collective-permute-start.13
  159.2 0.0 collective-permute-done.10
  159.2 1.3 collective-permute-start.11
  160.5 49.0 %collective-permute-done.8 = bf16[304,2048]{1,0:T(8,128)(2,1)S(1)} collective-permute-done((bf16[304,2048]{1,0:T(8,128)(2,1)S(1)}, bf16[304,2048]{1,0:T(8,128)(2,1)S(1)}, u32[]{:S(2)}, u32[]{:S(2)}) %collective-permute-start.8) | collective-permute-done | bytes 1245216 | tf_op jit(solution)/shard_map/ppermute | solution.py:22
  209.4 21.3 %collective-permute-done.9 = bf16[1024,2048]{1,0:T(8,128)(2,1)S(1)} collective-permute-done((bf16[1024,2048]{1,0:T(8,128)(2,1)S(1)}, bf16[1024,2048]{1,0:T(8,128)(2,1)S(1)}, u32[]{:S(2)}, u32[]{:S(2)}) %collective-permute-start.9) | collective-permute-done | bytes 4194336 | tf_op jit(solution)/shard_map/ppermute | solution.py:22
  230.7 1.2 slice_add_fusion.2
  231.9 0.0 collective-permute-done.13
  231.9 0.1 slice_add_fusion.1
  232.1 50.7 %collective-permute-done.11 = bf16[368,2048]{1,0:T(8,128)(2,1)S(1)} collective-permute-done((bf16[368,2048]{1,0:T(8,128)(2,1)S(1)}, bf16[368,2048]{1,0:T(8,128)(2,1)S(1)}, u32[]{:S(2)}, u32[]{:S(2)}) %collective-permute-start.11) | collective-permute-done | bytes 1507360 | tf_op jit(solution)/shard_map/ppermute | solution.py:22
  282.8 0.2 slice_add_fusion
  282.9 0.0 collective-permute-done.7
  282.9 0.0 copy-start.1
  282.9 13.7 %fusion.33 = bf16[1,1024,2048]{2,1,0:T(8,128)(2,1)} fusion(bf16[1024,2048]{1,0:T(8,128)(2,1)} %copy-done.2, bf16[352,2048]{1,0:T(8,128)(2,1)S(1)} %slice_add_fusion.1, bf16[368,2048]{1,0:T(8,128)(2,1)S(1)} %slice_add_fusion, bf16[304,2048]{1,0:T(8,128)(2,1)} %slice_add_fusion.2, bf16[1024,2048]{1,0:T(8,128)(2,1)} %collective-permute-done.7, pred[]{:T(512)S(6)} %eq.17), kind=kOutput, calls=%fused_computation.39 | convolution fusion | flops 8665432064 | bytes 16777216 | tf_op jit(solution)/shard_map/dot_general | solution.py:66
  296.6 0.0 copy-done.1
  (1 shorter events, 0.0 us)
Async XLA Ops:
  0.0 0.9 copy-start
  1.8 4.6 %copy-start.3 = (bf16[2048,2048]{1,0:T(8,128)(2,1)S(1)}, bf16[2048,2048]{1,0:T(8,128)(2,1)}, u32[]{:S(2)}) copy-start(bf16[2048,2048]{1,0:T(8,128)(2,1)} %param.6) | copy-start | bytes 25165828
  12.2 9.3 %collective-permute-start.2 = (bf16[512,2048]{1,0:T(8,128)(2,1)}, bf16[512,2048]{1,0:T(8,128)(2,1)}, u32[]{:S(2)}, u32[]{:S(2)}) collective-permute-start(bf16[512,2048]{1,0:T(8,128)(2,1)} %multiply_convert_fusion.5), channel_id=1, source_target_pairs={{6,14},{7,15},{14,22},{15,23},{22,30},{23,31},{30,6},{31,7},{38,46... | collective-permute-start | bytes 6291464 | tf_op jit(solution)/shard_map/ppermute | solution.py:22
  14.2 50.3 %collective-permute-start.5 = (bf16[512,2048]{1,0:T(8,128)(2,1)}, bf16[512,2048]{1,0:T(8,128)(2,1)}, u32[]{:S(2)}, u32[]{:S(2)}) collective-permute-start(bf16[512,2048]{1,0:T(8,128)(2,1)} %multiply_convert_fusion.5), channel_id=1, source_target_pairs={{0,3},{1,2},{2,5},{3,4},{4,7},{5,6},{8,11},{9,10},{10,13},{11,12},... | collective-permute-start | bytes 6291464 | tf_op jit(solution)/shard_map/ppermute | solution.py:22
  20.1 103.9 %collective-permute-start.1 = (bf16[512,2048]{1,0:T(8,128)(2,1)}, bf16[512,2048]{1,0:T(8,128)(2,1)S(1)}, u32[]{:S(2)}, u32[]{:S(2)}) collective-permute-start(bf16[512,2048]{1,0:T(8,128)(2,1)} %multiply_convert_fusion.5), channel_id=1, source_target_pairs={{0,2},{1,3},{2,4},{3,5},{4,6},{5,7},{8,10},{9,11},{10,12},{11,13},... | collective-permute-start | bytes 6291464 | tf_op jit(solution)/shard_map/ppermute | solution.py:22
  21.5 99.4 %collective-permute-start.6 = (bf16[512,2048]{1,0:T(8,128)(2,1)}, bf16[512,2048]{1,0:T(8,128)(2,1)}, u32[]{:S(2)}, u32[]{:S(2)}) collective-permute-start(bf16[512,2048]{1,0:T(8,128)(2,1)} %collective-permute-done.2), channel_id=1, source_target_pairs={{6,33},{7,32},{14,9},{15,8},{22,17},{23,16},{30,25},{31,24},{38,65... | collective-permute-start | bytes 6291464 | tf_op jit(solution)/shard_map/ppermute | solution.py:22
  28.6 95.4 %collective-permute-start.3 = (bf16[512,2048]{1,0:T(8,128)(2,1)}, bf16[512,2048]{1,0:T(8,128)(2,1)}, u32[]{:S(2)}, u32[]{:S(2)}) collective-permute-start(bf16[512,2048]{1,0:T(8,128)(2,1)} %collective-permute-done.2), channel_id=1, source_target_pairs={{6,32},{7,33},{14,8},{15,9},{22,16},{23,17},{30,24},{31,25},{38,64... | collective-permute-start | bytes 6291464 | tf_op jit(solution)/shard_map/ppermute | solution.py:22
  29.9 104.9 %collective-permute-start.4 = (bf16[512,2048]{1,0:T(8,128)(2,1)}, bf16[512,2048]{1,0:T(8,128)(2,1)}, u32[]{:S(2)}, u32[]{:S(2)}) collective-permute-start(bf16[512,2048]{1,0:T(8,128)(2,1)} %multiply_convert_fusion.6), channel_id=1, source_target_pairs={{0,3},{1,2},{2,5},{3,4},{4,7},{5,6},{6,9},{7,8},{8,11},{9,10},{10,... | collective-permute-start | bytes 6291464 | tf_op jit(solution)/shard_map/ppermute | solution.py:22
  64.5 75.5 %collective-permute-start = (bf16[512,2048]{1,0:T(8,128)(2,1)}, bf16[512,2048]{1,0:T(8,128)(2,1)}, u32[]{:S(2)}, u32[]{:S(2)}) collective-permute-start(bf16[512,2048]{1,0:T(8,128)(2,1)} %multiply_convert_fusion.6), channel_id=1, source_target_pairs={{0,2},{1,3},{2,4},{3,5},{4,6},{5,7},{6,8},{7,9},{8,10},{9,11},{10,... | collective-permute-start | bytes 6291464 | tf_op jit(solution)/shard_map/ppermute | solution.py:22
  152.8 3.8 %copy-start.2 = (bf16[1024,2048]{1,0:T(8,128)(2,1)}, bf16[1024,2048]{1,0:T(8,128)(2,1)S(1)}, u32[]{:S(2)}) copy-start(bf16[1024,2048]{1,0:T(8,128)(2,1)S(1)} %multiply_convert_fusion.2) | copy-start | bytes 12582916
  152.8 77.9 %collective-permute-start.9 = (bf16[1024,2048]{1,0:T(8,128)(2,1)S(1)}, bf16[1024,2048]{1,0:T(8,128)(2,1)S(1)}, u32[]{:S(2)}, u32[]{:S(2)}) collective-permute-start(bf16[1024,2048]{1,0:T(8,128)(2,1)S(1)} %multiply_convert_fusion.2), channel_id=1, source_target_pairs={{0,5},{1,4},{2,7},{3,6},{8,13},{9,12},{10,15},{11,14},{16,21},{17,... | collective-permute-start | bytes 12582920 | tf_op jit(solution)/shard_map/ppermute | solution.py:22
  154.5 128.4 %collective-permute-start.7 = (bf16[1024,2048]{1,0:T(8,128)(2,1)S(1)}, bf16[1024,2048]{1,0:T(8,128)(2,1)}, u32[]{:S(2)}, u32[]{:S(2)}) collective-permute-start(bf16[1024,2048]{1,0:T(8,128)(2,1)S(1)} %multiply_convert_fusion.2), channel_id=1, source_target_pairs={{0,4},{1,5},{2,6},{3,7},{4,8},{5,9},{6,10},{7,11},{8,12},{9,13},{1... | collective-permute-start | bytes 12582920 | tf_op jit(solution)/shard_map/ppermute | solution.py:22
  154.8 3.1 %collective-permute-start.12 = (bf16[352,2048]{1,0:T(8,128)(2,1)S(1)}, bf16[352,2048]{1,0:T(8,128)(2,1)S(1)}, u32[]{:S(2)}, u32[]{:S(2)}) collective-permute-start(bf16[352,2048]{1,0:T(8,128)(2,1)S(1)} %slice.48), channel_id=1, source_target_pairs={{4,12},{5,13},{6,14},{7,15},{12,20},{13,21},{14,22},{15,23},{20,28... | collective-permute-start | bytes 4325384 | tf_op jit(solution)/shard_map/ppermute | solution.py:22
  155.7 3.5 %collective-permute-start.10 = (bf16[368,2048]{1,0:T(8,128)(2,1)S(1)}, bf16[368,2048]{1,0:T(8,128)(2,1)S(1)}, u32[]{:S(2)}, u32[]{:S(2)}) collective-permute-start(bf16[368,2048]{1,0:T(8,128)(2,1)S(1)} %slice.46), channel_id=1, source_target_pairs={{4,12},{5,13},{6,14},{7,15},{12,20},{13,21},{14,22},{15,23},{20,28... | collective-permute-start | bytes 4521992 | tf_op jit(solution)/shard_map/ppermute | solution.py:22
  156.6 52.9 %collective-permute-start.8 = (bf16[304,2048]{1,0:T(8,128)(2,1)S(1)}, bf16[304,2048]{1,0:T(8,128)(2,1)S(1)}, u32[]{:S(2)}, u32[]{:S(2)}) collective-permute-start(bf16[304,2048]{1,0:T(8,128)(2,1)S(1)} %slice.44), channel_id=1, source_target_pairs={{4,9},{5,8},{6,11},{7,10},{12,17},{13,16},{14,19},{15,18},{20,25},... | collective-permute-start | bytes 3735560 | tf_op jit(solution)/shard_map/ppermute | solution.py:22
  157.9 74.1 %collective-permute-start.13 = (bf16[352,2048]{1,0:T(8,128)(2,1)S(1)}, bf16[352,2048]{1,0:T(8,128)(2,1)S(1)}, u32[]{:S(2)}, u32[]{:S(2)}) collective-permute-start(bf16[352,2048]{1,0:T(8,128)(2,1)S(1)} %collective-permute-done.12), channel_id=1, source_target_pairs={{4,33},{5,32},{6,35},{7,34},{12,9},{13,8},{14,11},{15,10},{20,17},... | collective-permute-start | bytes 4325384 | tf_op jit(solution)/shard_map/ppermute | solution.py:22
  159.2 123.6 %collective-permute-start.11 = (bf16[368,2048]{1,0:T(8,128)(2,1)S(1)}, bf16[368,2048]{1,0:T(8,128)(2,1)S(1)}, u32[]{:S(2)}, u32[]{:S(2)}) collective-permute-start(bf16[368,2048]{1,0:T(8,128)(2,1)S(1)} %collective-permute-done.10), channel_id=1, source_target_pairs={{4,33},{5,32},{6,35},{7,34},{12,9},{13,8},{14,11},{15,10},{20,17},... | collective-permute-start | bytes 4521992 | tf_op jit(solution)/shard_map/ppermute | solution.py:22
  282.9 13.7 %copy-start.1 = (f32[16,2048]{1,0:T(8,128)S(1)}, f32[16,2048]{1,0:T(8,128)}, u32[]{:S(2)}) copy-start(f32[16,2048]{1,0:T(8,128)} %param.7) | copy-start | bytes 393220

commit v17 on v9

--- a/solution.py
+++ b/solution.py
@@ -104,8 +104,13 @@
     other_near = sent(current, when_low(0, direct(2, 1)))
     other_rows = [sent(current[:DIRECT_ROWS], when_low(1, direct(2, 1))) + other_near[:DIRECT_ROWS]]
     begin = DIRECT_ROWS
+    previous = None
     for size in RELAY_ROWS:
-        ring_first = sent(current[begin:begin + size], ring_first_hop)
+        piece = current[begin:begin + size]
+        if previous is not None:
+            piece, _ = lax.optimization_barrier((piece, previous))
+        ring_first = sent(piece, ring_first_hop)
+        previous = ring_first
         other_rows.append(sent(ring_first, ring_first_exit) + other_near[begin:begin + size])
         begin += size
     current = level_product(current, natural([same], other_rows, row), norm_scale)

time: 300 us -> 304 us (1.013)
  waiting for transfers between devices: 199 us -> 204 us
    ppermute x13, waiting for transfers between devices: 199 us -> 204 us  [sent(): return lax.ppermute(value, ('tm', 'row'), pairs)]
  transfers between devices with their start and end apart: 13 -> 13, of which waited for: 7 -> 6; matrix products, arithmetic and copies ran while one was open for 3% -> 3% of each run, Pallas kernels for 0% -> 0%
where the time goes in v17:
time: 304 us; the launch traced here: 302 us
  waiting for transfers between devices  204 us (67%)
  starting transfers between devices  49.5 us (16%)
  matrix products  39.3 us (13%)
  other arithmetic  8.14 us (3%)
    ppermute x13, waiting for transfers between devices, sent(): return lax.ppermute(value, ('tm', 'row'), pairs)  204 us
    ppermute x13, starting transfers between devices, sent(): return lax.ppermute(value, ('tm', 'row'), pairs)  49.5 us
    dot_general x2, matrix products, level_product(): total = jnp.dot(later, earlier, preferred_element_type=jnp.float32)  26.5 us
    dot_general x2, matrix products, shards(): jnp.dot(left_factor[c * chunk_rows:(c + 1) * chunk_rows], right_factor, p...  11.5 us
  transfers between devices with their start and end apart: 13, of which 6 were waited for; matrix products, arithmetic and copies ran while one was open for 3% of the time, Pallas kernels for 0%

profile of v17, /device:TPU:96, one launch (start us, length us, event | category | flops | bytes accessed | tf_op | source)
XLA Modules:
  0.0 301.8 jit_solution(17198059758599162273)
XLA Ops:
  0.0 0.0 copy-start
  0.0 0.0 copy-start.3
  0.0 0.8 multiply_bitcast_fusion
  0.8 0.1 copy-done
  0.9 1.3 fusion.39
  2.2 3.5 %fusion.28 = bf16[1024,2048]{1,0:T(8,128)(2,1)S(1)} fusion(bf16[1,1024,2048]{2,1,0:T(8,128)(2,1)} %param.5, f32[2048]{0:T(1024)S(1)} %bitcast.12), kind=kLoop, calls=%fused_computation.32 | loop fusion | flops 6291456 | bytes 8396800 | tf_op jit(solution)/shard_map/convert_element_type | solution.py:85
  5.8 0.0 copy-done.3
  5.8 5.7 %multiply_convert_fusion.5 = bf16[512,2048]{1,0:T(8,128)(2,1)} fusion(bf16[2048,2048]{1,0:T(8,128)(2,1)S(1)} %copy-done.3, f32[2048]{0:T(1024)S(1)} %bitcast.13, bf16[1024,2048]{1,0:T(8,128)(2,1)S(1)} %fusion.28), kind=kOutput, calls=%fused_computation.43 | convolution fusion | flops 4309647360 | bytes 12591104 | tf_op jit(solution)/shard_map/dot_general | solution.py:89
  11.5 2.0 collective-permute-start.2
  13.5 1.9 collective-permute-start.1
  15.4 0.0 collective-permute-done.2
  15.4 2.0 collective-permute-start.3
  17.5 5.8 %multiply_convert_fusion.6 = bf16[512,2048]{1,0:T(8,128)(2,1)} fusion(bf16[2048,2048]{1,0:T(8,128)(2,1)S(1)} %copy-done.3, f32[2048]{0:T(1024)S(1)} %bitcast.14, bf16[1024,2048]{1,0:T(8,128)(2,1)S(1)} %fusion.28), kind=kOutput, calls=%fused_computation.44 | convolution fusion | flops 4309647360 | bytes 12591104 | tf_op jit(solution)/shard_map/dot_general | solution.py:89
  23.3 4.2 %collective-permute-start.4 = (bf16[512,2048]{1,0:T(8,128)(2,1)}, bf16[512,2048]{1,0:T(8,128)(2,1)}, u32[]{:S(2)}, u32[]{:S(2)}) collective-permute-start(bf16[512,2048]{1,0:T(8,128)(2,1)} %multiply_convert_fusion.6), channel_id=1, source_target_pairs={{0,3},{1,2},{2,5},{3,4},{4,7},{5,6},{6,9},{7,8},{8,11},{9,10},{10,... | collective-permute-start | bytes 6291464 | tf_op jit(solution)/shard_map/ppermute | solution.py:22
  27.4 0.0 collective-permute-start
  27.4 21.3 %collective-permute-start.5 = (bf16[512,2048]{1,0:T(8,128)(2,1)}, bf16[512,2048]{1,0:T(8,128)(2,1)}, u32[]{:S(2)}, u32[]{:S(2)}) collective-permute-start(bf16[512,2048]{1,0:T(8,128)(2,1)} %multiply_convert_fusion.5), channel_id=1, source_target_pairs={{0,3},{1,2},{2,5},{3,4},{4,7},{5,6},{6,9},{7,8},{8,11},{9,10},{10,... | collective-permute-start | bytes 6291464 | tf_op jit(solution)/shard_map/ppermute | solution.py:22
  48.7 5.9 %collective-permute-done.1 = bf16[512,2048]{1,0:T(8,128)(2,1)S(1)} collective-permute-done((bf16[512,2048]{1,0:T(8,128)(2,1)}, bf16[512,2048]{1,0:T(8,128)(2,1)S(1)}, u32[]{:S(2)}, u32[]{:S(2)}) %collective-permute-start.1) | collective-permute-done | bytes 2097184 | tf_op jit(solution)/shard_map/ppermute | solution.py:22
  54.7 0.0 collective-permute-done.3
  54.7 2.4 add.12
  57.0 22.7 %collective-permute-done.4 = bf16[512,2048]{1,0:T(8,128)(2,1)} collective-permute-done((bf16[512,2048]{1,0:T(8,128)(2,1)}, bf16[512,2048]{1,0:T(8,128)(2,1)}, u32[]{:S(2)}, u32[]{:S(2)}) %collective-permute-start.4) | collective-permute-done | bytes 2097184 | tf_op jit(solution)/shard_map/ppermute | solution.py:22
  79.7 20.0 %collective-permute-done = bf16[512,2048]{1,0:T(8,128)(2,1)} collective-permute-done((bf16[512,2048]{1,0:T(8,128)(2,1)}, bf16[512,2048]{1,0:T(8,128)(2,1)}, u32[]{:S(2)}, u32[]{:S(2)}) %collective-permute-start) | collective-permute-done | bytes 2097184 | tf_op jit(solution)/shard_map/ppermute | solution.py:22
  99.7 25.2 %collective-permute-done.5 = bf16[512,2048]{1,0:T(8,128)(2,1)} collective-permute-done((bf16[512,2048]{1,0:T(8,128)(2,1)}, bf16[512,2048]{1,0:T(8,128)(2,1)}, u32[]{:S(2)}, u32[]{:S(2)}) %collective-permute-start.5) | collective-permute-done | bytes 2097184 | tf_op jit(solution)/shard_map/ppermute | solution.py:22
  125.0 12.8 %multiply_convert_fusion.2 = bf16[1024,2048]{1,0:T(8,128)(2,1)S(1)} fusion(bf16[512,2048]{1,0:T(8,128)(2,1)} %collective-permute-done.5, bf16[512,2048]{1,0:T(8,128)(2,1)} %collective-permute-done.4, bf16[512,2048]{1,0:T(8,128)(2,1)S(1)} %add.12, bf16[512,2048]{1,0:T(8,128)(2,1)} %collective-permute-done, pred[]{:T(512)S(6)} %eq.17, ...), kind=kOutput, calls=%fused_computation.34 | convolution fusion | flops 8673820672 | bytes 16777216 | tf_op jit(solution)/shard_map/dot_general | solution.py:66
  137.8 0.0 copy-start.2
  137.8 1.6 collective-permute-start.8
  139.4 0.1 slice.46
  139.5 0.8 collective-permute-start.9
  140.3 10.9 %collective-permute-start.6 = (bf16[1024,2048]{1,0:T(8,128)(2,1)S(1)}, bf16[1024,2048]{1,0:T(8,128)(2,1)}, u32[]{:S(2)}, u32[]{:S(2)}) collective-permute-start(bf16[1024,2048]{1,0:T(8,128)(2,1)S(1)} %multiply_convert_fusion.2), channel_id=1, source_target_pairs={{0,4},{1,5},{2,6},{3,7},{4,8},{5,9},{6,10},{7,11},{8,12},{9,13},{1... | collective-permute-start | bytes 12582920 | tf_op jit(solution)/shard_map/ppermute | solution.py:22
  151.2 0.1 slice.48
  151.3 0.0 collective-permute-done.9
  151.3 0.8 collective-permute-start.11
  152.1 1.3 collective-permute-start.10
  153.4 0.1 slice.44
  153.5 1.3 collective-permute-start.7
  154.8 0.0 collective-permute-done.11
  154.8 1.5 collective-permute-start.12
  156.2 97.2 %collective-permute-done.7 = bf16[208,2048]{1,0:T(8,128)(2,1)S(1)} collective-permute-done((bf16[208,2048]{1,0:T(8,128)(2,1)S(1)}, bf16[208,2048]{1,0:T(8,128)(2,1)S(1)}, u32[]{:S(2)}, u32[]{:S(2)}) %collective-permute-start.7) | collective-permute-done | bytes 852000 | tf_op jit(solution)/shard_map/ppermute | solution.py:22
  253.5 0.0 collective-permute-done.8
  253.5 1.1 slice_add_fusion.2
  254.6 0.0 collective-permute-done.10
  254.6 0.2 slice_add_fusion
  254.7 33.1 %collective-permute-done.12 = bf16[400,2048]{1,0:T(8,128)(2,1)S(1)} collective-permute-done((bf16[400,2048]{1,0:T(8,128)(2,1)S(1)}, bf16[400,2048]{1,0:T(8,128)(2,1)S(1)}, u32[]{:S(2)}, u32[]{:S(2)}) %collective-permute-start.12) | collective-permute-done | bytes 1638432 | tf_op jit(solution)/shard_map/ppermute | solution.py:22
  287.9 0.2 slice_add_fusion.1
  288.1 0.0 copy-done.2
  288.1 0.0 collective-permute-done.6
  288.1 0.0 copy-start.1
  288.1 13.7 %fusion.33 = bf16[1,1024,2048]{2,1,0:T(8,128)(2,1)} fusion(bf16[1024,2048]{1,0:T(8,128)(2,1)} %copy-done.2, bf16[400,2048]{1,0:T(8,128)(2,1)S(1)} %slice_add_fusion.1, bf16[416,2048]{1,0:T(8,128)(2,1)S(1)} %slice_add_fusion, bf16[208,2048]{1,0:T(8,128)(2,1)} %slice_add_fusion.2, bf16[1024,2048]{1,0:T(8,128)(2,1)} %collective-permute-done.6, pred[]{:T(512)S(6)} %eq.17), kind=kOutput, calls=%fused_computation.39 | convolution fusion | flops 8665432064 | bytes 16777216 | tf_op jit(solution)/shard_map/dot_general | solution.py:66
  301.8 0.0 copy-done.1
  (1 shorter events, 0.0 us)
Async XLA Ops:
  0.0 0.9 copy-start
  0.0 5.8 %copy-start.3 = (bf16[2048,2048]{1,0:T(8,128)(2,1)S(1)}, bf16[2048,2048]{1,0:T(8,128)(2,1)}, u32[]{:S(2)}) copy-start(bf16[2048,2048]{1,0:T(8,128)(2,1)} %param.6) | copy-start | bytes 25165828
  11.5 3.9 %collective-permute-start.2 = (bf16[512,2048]{1,0:T(8,128)(2,1)}, bf16[512,2048]{1,0:T(8,128)(2,1)}, u32[]{:S(2)}, u32[]{:S(2)}) collective-permute-start(bf16[512,2048]{1,0:T(8,128)(2,1)} %multiply_convert_fusion.5), channel_id=1, source_target_pairs={{30,6},{31,7},{62,38},{63,39},{94,70},{95,71},{126,102},{127,103}} | collective-permute-start | bytes 6291464 | tf_op jit(solution)/shard_map/ppermute | solution.py:22
  13.5 41.2 %collective-permute-start.1 = (bf16[512,2048]{1,0:T(8,128)(2,1)}, bf16[512,2048]{1,0:T(8,128)(2,1)S(1)}, u32[]{:S(2)}, u32[]{:S(2)}) collective-permute-start(bf16[512,2048]{1,0:T(8,128)(2,1)} %multiply_convert_fusion.5), channel_id=1, source_target_pairs={{0,2},{1,3},{2,4},{3,5},{4,6},{5,7},{6,8},{7,9},{8,10},{9,11},{10,... | collective-permute-start | bytes 6291464 | tf_op jit(solution)/shard_map/ppermute | solution.py:22
  15.4 39.2 %collective-permute-start.3 = (bf16[512,2048]{1,0:T(8,128)(2,1)}, bf16[512,2048]{1,0:T(8,128)(2,1)}, u32[]{:S(2)}, u32[]{:S(2)}) collective-permute-start(bf16[512,2048]{1,0:T(8,128)(2,1)} %collective-permute-done.2), channel_id=1, source_target_pairs={{6,32},{7,33},{38,64},{39,65},{70,96},{71,97},{102,0},{103,1}} | collective-permute-start | bytes 6291464 | tf_op jit(solution)/shard_map/ppermute | solution.py:22
  23.3 56.5 %collective-permute-start.4 = (bf16[512,2048]{1,0:T(8,128)(2,1)}, bf16[512,2048]{1,0:T(8,128)(2,1)}, u32[]{:S(2)}, u32[]{:S(2)}) collective-permute-start(bf16[512,2048]{1,0:T(8,128)(2,1)} %multiply_convert_fusion.6), channel_id=1, source_target_pairs={{0,3},{1,2},{2,5},{3,4},{4,7},{5,6},{6,9},{7,8},{8,11},{9,10},{10,... | collective-permute-start | bytes 6291464 | tf_op jit(solution)/shard_map/ppermute | solution.py:22
  27.4 72.3 %collective-permute-start = (bf16[512,2048]{1,0:T(8,128)(2,1)}, bf16[512,2048]{1,0:T(8,128)(2,1)}, u32[]{:S(2)}, u32[]{:S(2)}) collective-permute-start(bf16[512,2048]{1,0:T(8,128)(2,1)} %multiply_convert_fusion.6), channel_id=1, source_target_pairs={{0,2},{1,3},{2,4},{3,5},{4,6},{5,7},{6,8},{7,9},{8,10},{9,11},{10,... | collective-permute-start | bytes 6291464 | tf_op jit(solution)/shard_map/ppermute | solution.py:22
  27.4 97.5 %collective-permute-start.5 = (bf16[512,2048]{1,0:T(8,128)(2,1)}, bf16[512,2048]{1,0:T(8,128)(2,1)}, u32[]{:S(2)}, u32[]{:S(2)}) collective-permute-start(bf16[512,2048]{1,0:T(8,128)(2,1)} %multiply_convert_fusion.5), channel_id=1, source_target_pairs={{0,3},{1,2},{2,5},{3,4},{4,7},{5,6},{6,9},{7,8},{8,11},{9,10},{10,... | collective-permute-start | bytes 6291464 | tf_op jit(solution)/shard_map/ppermute | solution.py:22
  137.8 150.2 %copy-start.2 = (bf16[1024,2048]{1,0:T(8,128)(2,1)}, bf16[1024,2048]{1,0:T(8,128)(2,1)S(1)}, u32[]{:S(2)}) copy-start(bf16[1024,2048]{1,0:T(8,128)(2,1)S(1)} %multiply_convert_fusion.2) | copy-start | bytes 12582916
  137.8 115.6 %collective-permute-start.8 = (bf16[1024,2048]{1,0:T(8,128)(2,1)S(1)}, bf16[1024,2048]{1,0:T(8,128)(2,1)S(1)}, u32[]{:S(2)}, u32[]{:S(2)}) collective-permute-start(bf16[1024,2048]{1,0:T(8,128)(2,1)S(1)} %multiply_convert_fusion.2), channel_id=1, source_target_pairs={{0,5},{1,4},{2,7},{3,6},{8,13},{9,12},{10,15},{11,14},{16,21},{17,... | collective-permute-start | bytes 12582920 | tf_op jit(solution)/shard_map/ppermute | solution.py:22
  139.5 11.8 %collective-permute-start.9 = (bf16[416,2048]{1,0:T(8,128)(2,1)S(1)}, bf16[416,2048]{1,0:T(8,128)(2,1)S(1)}, u32[]{:S(2)}, u32[]{:S(2)}) collective-permute-start(bf16[416,2048]{1,0:T(8,128)(2,1)S(1)} %slice.46), channel_id=1, source_target_pairs={{4,12},{5,13},{6,14},{7,15},{12,20},{13,21},{14,22},{15,23},{20,28... | collective-permute-start | bytes 5111816 | tf_op jit(solution)/shard_map/ppermute | solution.py:22
  140.3 147.8 %collective-permute-start.6 = (bf16[1024,2048]{1,0:T(8,128)(2,1)S(1)}, bf16[1024,2048]{1,0:T(8,128)(2,1)}, u32[]{:S(2)}, u32[]{:S(2)}) collective-permute-start(bf16[1024,2048]{1,0:T(8,128)(2,1)S(1)} %multiply_convert_fusion.2), channel_id=1, source_target_pairs={{0,4},{1,5},{2,6},{3,7},{4,8},{5,9},{6,10},{7,11},{8,12},{9,13},{1... | collective-permute-start | bytes 12582920 | tf_op jit(solution)/shard_map/ppermute | solution.py:22
  151.3 3.4 %collective-permute-start.11 = (bf16[400,2048]{1,0:T(8,128)(2,1)S(1)}, bf16[400,2048]{1,0:T(8,128)(2,1)S(1)}, u32[]{:S(2)}, u32[]{:S(2)}) collective-permute-start(bf16[400,2048]{1,0:T(8,128)(2,1)S(1)} %slice.48), channel_id=1, source_target_pairs={{4,12},{5,13},{6,14},{7,15},{12,20},{13,21},{14,22},{15,23},{20,28... | collective-permute-start | bytes 4915208 | tf_op jit(solution)/shard_map/ppermute | solution.py:22
  152.1 102.5 %collective-permute-start.10 = (bf16[416,2048]{1,0:T(8,128)(2,1)S(1)}, bf16[416,2048]{1,0:T(8,128)(2,1)S(1)}, u32[]{:S(2)}, u32[]{:S(2)}) collective-permute-start(bf16[416,2048]{1,0:T(8,128)(2,1)S(1)} %collective-permute-done.9), channel_id=1, source_target_pairs={{4,33},{5,32},{6,35},{7,34},{12,9},{13,8},{14,11},{15,10},{20,17},... | collective-permute-start | bytes 5111816 | tf_op jit(solution)/shard_map/ppermute | solution.py:22
  153.5 100.0 %collective-permute-start.7 = (bf16[208,2048]{1,0:T(8,128)(2,1)S(1)}, bf16[208,2048]{1,0:T(8,128)(2,1)S(1)}, u32[]{:S(2)}, u32[]{:S(2)}) collective-permute-start(bf16[208,2048]{1,0:T(8,128)(2,1)S(1)} %slice.44), channel_id=1, source_target_pairs={{4,9},{5,8},{6,11},{7,10},{12,17},{13,16},{14,19},{15,18},{20,25},... | collective-permute-start | bytes 2555912 | tf_op jit(solution)/shard_map/ppermute | solution.py:22
  154.8 133.1 %collective-permute-start.12 = (bf16[400,2048]{1,0:T(8,128)(2,1)S(1)}, bf16[400,2048]{1,0:T(8,128)(2,1)S(1)}, u32[]{:S(2)}, u32[]{:S(2)}) collective-permute-start(bf16[400,2048]{1,0:T(8,128)(2,1)S(1)} %collective-permute-done.11), channel_id=1, source_target_pairs={{4,33},{5,32},{6,35},{7,34},{12,9},{13,8},{14,11},{15,10},{20,17},... | collective-permute-start | bytes 4915208 | tf_op jit(solution)/shard_map/ppermute | solution.py:22
  288.1 13.7 %copy-start.1 = (f32[16,2048]{1,0:T(8,128)S(1)}, f32[16,2048]{1,0:T(8,128)}, u32[]{:S(2)}) copy-start(f32[16,2048]{1,0:T(8,128)} %param.7) | copy-start | bytes 393220

commit v18 on v12

--- a/solution.py
+++ b/solution.py
@@ -83,10 +83,11 @@
     gain_rows = jnp.exp(0.1 * count_row[:, None] * table_rows)
     right_factor = (base_op * gain_rows[0]).astype(jnp.bfloat16)
     left_factor = (slice_ops[0] * gain_rows[1]).astype(jnp.bfloat16)
-    chunk_rows = half // 2
+    first_rows = half * 3 // 8
+    bounds = ((0, first_rows), (first_rows, half))
     chunks = []
-    for c in range(2):
-        product = jnp.dot(left_factor[c * chunk_rows:(c + 1) * chunk_rows], right_factor,
+    for begin, end in bounds:
+        product = jnp.dot(left_factor[begin:end], right_factor,
                           preferred_element_type=jnp.float32)
         chunks.append((product * norm_scale).astype(jnp.bfloat16))
 

time: 294 us -> 307 us (1.044)
  starting transfers between devices: 38.7 us -> 44.4 us
  local copies, waits for them, and re-layouts: 1.83 us -> 5.68 us
    ppermute x13, starting transfers between devices: 38.7 us -> 44.4 us  [sent(): return lax.ppermute(value, ('tm', 'row'), pairs)]
  transfers between devices with their start and end apart: 13 -> 13, of which waited for: 7 -> 7; matrix products, arithmetic and copies ran while one was open for 3% -> 5% of each run, Pallas kernels for 0% -> 0%
where the time goes in v18:
time: 307 us; the launch traced here: 305 us
  waiting for transfers between devices  203 us (66%)
  starting transfers between devices  44.4 us (14%)
  matrix products  41.2 us (13%)
  other arithmetic  10.2 us (3%)
  local copies, waits for them, and re-layouts  5.68 us (2%)
    ppermute x13, waiting for transfers between devices, sent(): return lax.ppermute(value, ('tm', 'row'), pairs)  203 us
    ppermute x13, starting transfers between devices, sent(): return lax.ppermute(value, ('tm', 'row'), pairs)  44.4 us
    dot_general x2, matrix products, level_product(): total = jnp.dot(later, earlier, preferred_element_type=jnp.float32)  28.9 us
    dot_general x2, matrix products, shards(): jnp.dot(left_factor[begin:end], right_factor, preferred_element_type=jnp....  11.4 us
  transfers between devices with their start and end apart: 13, of which 7 were waited for; matrix products, arithmetic and copies ran while one was open for 5% of the time, Pallas kernels for 0%

profile of v18, /device:TPU:96, one launch (start us, length us, event | category | flops | bytes accessed | tf_op | source)
XLA Modules:
  0.0 304.7 jit_solution(12027697031443603753)
XLA Ops:
  0.0 0.0 copy-start
  0.0 0.7 multiply_bitcast_fusion
  0.7 0.2 copy-done
  0.9 0.9 fusion.40
  1.8 0.0 copy-start.2
  1.8 3.6 %fusion.28 = bf16[1024,2048]{1,0:T(8,128)(2,1)S(1)} fusion(bf16[1,1024,2048]{2,1,0:T(8,128)(2,1)} %param.5, f32[2048]{0:T(1024)S(1)} %bitcast.12), kind=kLoop, calls=%fused_computation.32 | loop fusion | flops 6291456 | bytes 8396800 | tf_op jit(solution)/shard_map/convert_element_type | solution.py:85
  5.4 1.0 copy-done.2
  6.5 6.9 %multiply_convert_fusion.5 = bf16[640,2048]{1,0:T(8,128)(2,1)} fusion(bf16[2048,2048]{1,0:T(8,128)(2,1)S(1)} %copy-done.2, f32[2048]{0:T(1024)S(1)} %bitcast.13, bf16[1024,2048]{1,0:T(8,128)(2,1)S(1)} %fusion.28), kind=kOutput, calls=%fused_computation.39 | convolution fusion | flops 5383913472 | bytes 13639680 | tf_op jit(solution)/shard_map/dot_general | solution.py:90
  13.3 2.2 collective-permute-start.2
  15.5 1.9 collective-permute-start.1
  17.5 0.0 collective-permute-done.2
  17.5 2.2 collective-permute-start.3
  19.6 4.2 %collective-permute-start.5 = (bf16[640,2048]{1,0:T(8,128)(2,1)}, bf16[640,2048]{1,0:T(8,128)(2,1)}, u32[]{:S(2)}, u32[]{:S(2)}) collective-permute-start(bf16[640,2048]{1,0:T(8,128)(2,1)} %multiply_convert_fusion.5), channel_id=1, source_target_pairs={{0,3},{1,2},{2,5},{3,4},{4,7},{5,6},{6,9},{7,8},{8,11},{9,10},{10,... | collective-permute-start | bytes 7864328 | tf_op jit(solution)/shard_map/ppermute | solution.py:22
  23.8 4.6 %multiply_convert_fusion.8 = bf16[384,2048]{1,0:T(8,128)(2,1)} fusion(bf16[2048,2048]{1,0:T(8,128)(2,1)S(1)} %copy-done.2, f32[2048]{0:T(1024)S(1)} %bitcast.14, bf16[1024,2048]{1,0:T(8,128)(2,1)S(1)} %fusion.28), kind=kOutput, calls=%fused_computation.44 | convolution fusion | flops 3235381248 | bytes 11542528 | tf_op jit(solution)/shard_map/dot_general | solution.py:90
  28.4 0.0 collective-permute-start
  28.4 26.7 %collective-permute-start.4 = (bf16[384,2048]{1,0:T(8,128)(2,1)}, bf16[384,2048]{1,0:T(8,128)(2,1)}, u32[]{:S(2)}, u32[]{:S(2)}) collective-permute-start(bf16[384,2048]{1,0:T(8,128)(2,1)} %multiply_convert_fusion.8), channel_id=1, source_target_pairs={{0,3},{1,2},{2,5},{3,4},{4,7},{5,6},{6,9},{7,8},{8,11},{9,10},{10,... | collective-permute-start | bytes 4718600 | tf_op jit(solution)/shard_map/ppermute | solution.py:22
  55.1 18.5 %collective-permute-done.1 = bf16[640,2048]{1,0:T(8,128)(2,1)S(1)} collective-permute-done((bf16[640,2048]{1,0:T(8,128)(2,1)}, bf16[640,2048]{1,0:T(8,128)(2,1)S(1)}, u32[]{:S(2)}, u32[]{:S(2)}) %collective-permute-start.1) | collective-permute-done | bytes 2621472 | tf_op jit(solution)/shard_map/ppermute | solution.py:22
  73.6 0.0 collective-permute-done.3
  73.6 4.3 %add.12 = bf16[640,2048]{1,0:T(8,128)(2,1)} add(bf16[640,2048]{1,0:T(8,128)(2,1)S(1)} %collective-permute-done.1, bf16[640,2048]{1,0:T(8,128)(2,1)} %collective-permute-done.3) | non-fusion elementwise | flops 1310720 | bytes 7864320 | tf_op jit(solution)/shard_map/add | solution.py:99
  77.9 29.5 %collective-permute-done = bf16[384,2048]{1,0:T(8,128)(2,1)} collective-permute-done((bf16[384,2048]{1,0:T(8,128)(2,1)}, bf16[384,2048]{1,0:T(8,128)(2,1)}, u32[]{:S(2)}, u32[]{:S(2)}) %collective-permute-start) | collective-permute-done | bytes 1572896 | tf_op jit(solution)/shard_map/ppermute | solution.py:22
  107.4 18.1 %collective-permute-done.4 = bf16[384,2048]{1,0:T(8,128)(2,1)} collective-permute-done((bf16[384,2048]{1,0:T(8,128)(2,1)}, bf16[384,2048]{1,0:T(8,128)(2,1)}, u32[]{:S(2)}, u32[]{:S(2)}) %collective-permute-start.4) | collective-permute-done | bytes 1572896 | tf_op jit(solution)/shard_map/ppermute | solution.py:22
  125.5 0.0 collective-permute-done.5
  125.5 15.2 %multiply_convert_fusion.2 = bf16[1024,2048]{1,0:T(8,128)(2,1)} fusion(bf16[640,2048]{1,0:T(8,128)(2,1)} %collective-permute-done.5, bf16[384,2048]{1,0:T(8,128)(2,1)} %collective-permute-done.4, bf16[640,2048]{1,0:T(8,128)(2,1)} %add.12, bf16[384,2048]{1,0:T(8,128)(2,1)} %collective-permute-done, pred[]{:T(512)S(6)} %eq.17, ...), kind=kOutput, calls=%fused_computation.34 | convolution fusion | flops 8673820672 | bytes 16777216 | tf_op jit(solution)/shard_map/dot_general | solution.py:66
  140.8 1.5 collective-permute-start.8
  142.3 0.3 collective-permute-start.6
  142.6 1.5 slice.48
  144.1 0.8 collective-permute-start.11
  144.8 1.5 slice.46
  146.3 0.8 collective-permute-start.9
  147.1 1.4 slice.44
  148.5 1.3 collective-permute-start.7
  149.8 0.0 collective-permute-done.11
  149.8 1.3 collective-permute-start.12
  151.1 0.0 collective-permute-done.9
  151.1 1.3 collective-permute-start.10
  152.4 63.4 %collective-permute-done.7 = bf16[304,2048]{1,0:T(8,128)(2,1)S(1)} collective-permute-done((bf16[304,2048]{1,0:T(8,128)(2,1)S(1)}, bf16[304,2048]{1,0:T(8,128)(2,1)S(1)}, u32[]{:S(2)}, u32[]{:S(2)}) %collective-permute-start.7) | collective-permute-done | bytes 1245216 | tf_op jit(solution)/shard_map/ppermute | solution.py:22
  215.9 6.1 %collective-permute-done.8 = bf16[1024,2048]{1,0:T(8,128)(2,1)S(1)} collective-permute-done((bf16[1024,2048]{1,0:T(8,128)(2,1)}, bf16[1024,2048]{1,0:T(8,128)(2,1)S(1)}, u32[]{:S(2)}, u32[]{:S(2)}) %collective-permute-start.8) | collective-permute-done | bytes 4194336 | tf_op jit(solution)/shard_map/ppermute | solution.py:22
  221.9 1.3 slice_add_fusion.2
  223.2 5.4 %collective-permute-done.12 = bf16[352,2048]{1,0:T(8,128)(2,1)S(1)} collective-permute-done((bf16[352,2048]{1,0:T(8,128)(2,1)S(1)}, bf16[352,2048]{1,0:T(8,128)(2,1)S(1)}, u32[]{:S(2)}, u32[]{:S(2)}) %collective-permute-start.12) | collective-permute-done | bytes 1441824 | tf_op jit(solution)/shard_map/ppermute | solution.py:22
  228.6 0.1 slice_add_fusion.1
  228.7 62.2 %collective-permute-done.10 = bf16[368,2048]{1,0:T(8,128)(2,1)S(1)} collective-permute-done((bf16[368,2048]{1,0:T(8,128)(2,1)S(1)}, bf16[368,2048]{1,0:T(8,128)(2,1)S(1)}, u32[]{:S(2)}, u32[]{:S(2)}) %collective-permute-start.10) | collective-permute-done | bytes 1507360 | tf_op jit(solution)/shard_map/ppermute | solution.py:22
  290.9 0.2 slice_add_fusion
  291.1 0.0 collective-permute-done.6
  291.1 0.0 copy-start.1
  291.1 13.7 %fusion.33 = bf16[1,1024,2048]{2,1,0:T(8,128)(2,1)} fusion(bf16[1024,2048]{1,0:T(8,128)(2,1)} %multiply_convert_fusion.2, bf16[352,2048]{1,0:T(8,128)(2,1)S(1)} %slice_add_fusion.1, bf16[368,2048]{1,0:T(8,128)(2,1)S(1)} %slice_add_fusion, bf16[304,2048]{1,0:T(8,128)(2,1)} %slice_add_fusion.2, bf16[1024,2048]{1,0:T(8,128)(2,1)} %collective-permute-done.6, ...), kind=kOutput, calls=%fused_computation.40 | convolution fusion | flops 8665432064 | bytes 16777216 | tf_op jit(solution)/shard_map/dot_general | solution.py:66
  304.7 0.0 copy-done.1
  (1 shorter events, 0.0 us)
Async XLA Ops:
  0.0 0.9 copy-start
  1.8 4.6 %copy-start.2 = (bf16[2048,2048]{1,0:T(8,128)(2,1)S(1)}, bf16[2048,2048]{1,0:T(8,128)(2,1)}, u32[]{:S(2)}) copy-start(bf16[2048,2048]{1,0:T(8,128)(2,1)} %param.6) | copy-start | bytes 25165828
  13.3 4.1 %collective-permute-start.2 = (bf16[640,2048]{1,0:T(8,128)(2,1)}, bf16[640,2048]{1,0:T(8,128)(2,1)}, u32[]{:S(2)}, u32[]{:S(2)}) collective-permute-start(bf16[640,2048]{1,0:T(8,128)(2,1)} %multiply_convert_fusion.5), channel_id=1, source_target_pairs={{30,6},{31,7},{62,38},{63,39},{94,70},{95,71},{126,102},{127,103}} | collective-permute-start | bytes 7864328 | tf_op jit(solution)/shard_map/ppermute | solution.py:22
  15.5 58.0 %collective-permute-start.1 = (bf16[640,2048]{1,0:T(8,128)(2,1)}, bf16[640,2048]{1,0:T(8,128)(2,1)S(1)}, u32[]{:S(2)}, u32[]{:S(2)}) collective-permute-start(bf16[640,2048]{1,0:T(8,128)(2,1)} %multiply_convert_fusion.5), channel_id=1, source_target_pairs={{0,2},{1,3},{2,4},{3,5},{4,6},{5,7},{6,8},{7,9},{8,10},{9,11},{10,... | collective-permute-start | bytes 7864328 | tf_op jit(solution)/shard_map/ppermute | solution.py:22
  17.5 56.1 %collective-permute-start.3 = (bf16[640,2048]{1,0:T(8,128)(2,1)}, bf16[640,2048]{1,0:T(8,128)(2,1)}, u32[]{:S(2)}, u32[]{:S(2)}) collective-permute-start(bf16[640,2048]{1,0:T(8,128)(2,1)} %collective-permute-done.2), channel_id=1, source_target_pairs={{6,32},{7,33},{38,64},{39,65},{70,96},{71,97},{102,0},{103,1}} | collective-permute-start | bytes 7864328 | tf_op jit(solution)/shard_map/ppermute | solution.py:22
  19.6 105.9 %collective-permute-start.5 = (bf16[640,2048]{1,0:T(8,128)(2,1)}, bf16[640,2048]{1,0:T(8,128)(2,1)}, u32[]{:S(2)}, u32[]{:S(2)}) collective-permute-start(bf16[640,2048]{1,0:T(8,128)(2,1)} %multiply_convert_fusion.5), channel_id=1, source_target_pairs={{0,3},{1,2},{2,5},{3,4},{4,7},{5,6},{6,9},{7,8},{8,11},{9,10},{10,... | collective-permute-start | bytes 7864328 | tf_op jit(solution)/shard_map/ppermute | solution.py:22
  28.4 79.0 %collective-permute-start = (bf16[384,2048]{1,0:T(8,128)(2,1)}, bf16[384,2048]{1,0:T(8,128)(2,1)}, u32[]{:S(2)}, u32[]{:S(2)}) collective-permute-start(bf16[384,2048]{1,0:T(8,128)(2,1)} %multiply_convert_fusion.8), channel_id=1, source_target_pairs={{0,2},{1,3},{2,4},{3,5},{4,6},{5,7},{6,8},{7,9},{8,10},{9,11},{10,... | collective-permute-start | bytes 4718600 | tf_op jit(solution)/shard_map/ppermute | solution.py:22
  28.4 97.1 %collective-permute-start.4 = (bf16[384,2048]{1,0:T(8,128)(2,1)}, bf16[384,2048]{1,0:T(8,128)(2,1)}, u32[]{:S(2)}, u32[]{:S(2)}) collective-permute-start(bf16[384,2048]{1,0:T(8,128)(2,1)} %multiply_convert_fusion.8), channel_id=1, source_target_pairs={{0,3},{1,2},{2,5},{3,4},{4,7},{5,6},{6,9},{7,8},{8,11},{9,10},{10,... | collective-permute-start | bytes 4718600 | tf_op jit(solution)/shard_map/ppermute | solution.py:22
  140.8 81.2 %collective-permute-start.8 = (bf16[1024,2048]{1,0:T(8,128)(2,1)}, bf16[1024,2048]{1,0:T(8,128)(2,1)S(1)}, u32[]{:S(2)}, u32[]{:S(2)}) collective-permute-start(bf16[1024,2048]{1,0:T(8,128)(2,1)} %multiply_convert_fusion.2), channel_id=1, source_target_pairs={{0,5},{1,4},{2,7},{3,6},{8,13},{9,12},{10,15},{11,14},{16,21},{17,... | collective-permute-start | bytes 12582920 | tf_op jit(solution)/shard_map/ppermute | solution.py:22
  142.3 148.7 %collective-permute-start.6 = (bf16[1024,2048]{1,0:T(8,128)(2,1)}, bf16[1024,2048]{1,0:T(8,128)(2,1)}, u32[]{:S(2)}, u32[]{:S(2)}) collective-permute-start(bf16[1024,2048]{1,0:T(8,128)(2,1)} %multiply_convert_fusion.2), channel_id=1, source_target_pairs={{0,4},{1,5},{2,6},{3,7},{4,8},{5,9},{6,10},{7,11},{8,12},{9,13},{1... | collective-permute-start | bytes 12582920 | tf_op jit(solution)/shard_map/ppermute | solution.py:22
  144.1 5.7 %collective-permute-start.11 = (bf16[352,2048]{1,0:T(8,128)(2,1)S(1)}, bf16[352,2048]{1,0:T(8,128)(2,1)S(1)}, u32[]{:S(2)}, u32[]{:S(2)}) collective-permute-start(bf16[352,2048]{1,0:T(8,128)(2,1)S(1)} %slice.48), channel_id=1, source_target_pairs={{4,12},{5,13},{6,14},{7,15},{12,20},{13,21},{14,22},{15,23},{20,28... | collective-permute-start | bytes 4325384 | tf_op jit(solution)/shard_map/ppermute | solution.py:22
  146.3 4.8 %collective-permute-start.9 = (bf16[368,2048]{1,0:T(8,128)(2,1)S(1)}, bf16[368,2048]{1,0:T(8,128)(2,1)S(1)}, u32[]{:S(2)}, u32[]{:S(2)}) collective-permute-start(bf16[368,2048]{1,0:T(8,128)(2,1)S(1)} %slice.46), channel_id=1, source_target_pairs={{4,12},{5,13},{6,14},{7,15},{12,20},{13,21},{14,22},{15,23},{20,28... | collective-permute-start | bytes 4521992 | tf_op jit(solution)/shard_map/ppermute | solution.py:22
  148.5 67.4 %collective-permute-start.7 = (bf16[304,2048]{1,0:T(8,128)(2,1)S(1)}, bf16[304,2048]{1,0:T(8,128)(2,1)S(1)}, u32[]{:S(2)}, u32[]{:S(2)}) collective-permute-start(bf16[304,2048]{1,0:T(8,128)(2,1)S(1)} %slice.44), channel_id=1, source_target_pairs={{4,9},{5,8},{6,11},{7,10},{12,17},{13,16},{14,19},{15,18},{20,25},... | collective-permute-start | bytes 3735560 | tf_op jit(solution)/shard_map/ppermute | solution.py:22
  149.8 78.8 %collective-permute-start.12 = (bf16[352,2048]{1,0:T(8,128)(2,1)S(1)}, bf16[352,2048]{1,0:T(8,128)(2,1)S(1)}, u32[]{:S(2)}, u32[]{:S(2)}) collective-permute-start(bf16[352,2048]{1,0:T(8,128)(2,1)S(1)} %collective-permute-done.11), channel_id=1, source_target_pairs={{4,33},{5,32},{6,35},{7,34},{12,9},{13,8},{14,11},{15,10},{20,17},... | collective-permute-start | bytes 4325384 | tf_op jit(solution)/shard_map/ppermute | solution.py:22
  151.1 139.8 %collective-permute-start.10 = (bf16[368,2048]{1,0:T(8,128)(2,1)S(1)}, bf16[368,2048]{1,0:T(8,128)(2,1)S(1)}, u32[]{:S(2)}, u32[]{:S(2)}) collective-permute-start(bf16[368,2048]{1,0:T(8,128)(2,1)S(1)} %collective-permute-done.9), channel_id=1, source_target_pairs={{4,33},{5,32},{6,35},{7,34},{12,9},{13,8},{14,11},{15,10},{20,17},... | collective-permute-start | bytes 4521992 | tf_op jit(solution)/shard_map/ppermute | solution.py:22
  291.1 13.7 %copy-start.1 = (f32[16,2048]{1,0:T(8,128)S(1)}, f32[16,2048]{1,0:T(8,128)}, u32[]{:S(2)}) copy-start(f32[16,2048]{1,0:T(8,128)} %param.7) | copy-start | bytes 393220

commit v19 on v12

--- a/solution.py
+++ b/solution.py
@@ -90,12 +90,9 @@
                           preferred_element_type=jnp.float32)
         chunks.append((product * norm_scale).astype(jnp.bfloat16))
 
-    boundary = lambda t, r, n, m: ((t - 12) % n, r) if ring_of(t) == 3 and t % 4 == 3 else None
-    boundary_exit = lambda t, r, n, m: ((t + 13) % n, r) if ring_of(t) == 0 and t % 4 == 3 else None
-    not_boundary = lambda t, r, n, m: None if ring_of(t) == 3 and t % 4 == 3 else ((t + 1) % n, r)
     own_rows = [sent(chunks[0], direct(1, 0))]
     other_rows = [sent(chunks[0], direct(1, 1))]
-    own_rows.append(sent(chunks[1], not_boundary) + sent(sent(chunks[1], boundary), boundary_exit))
+    own_rows.append(sent(chunks[1], direct(1, 0)))
     other_rows.append(sent(chunks[1], direct(1, 1)))
     earlier = natural(own_rows, other_rows, row)
     current = level_product(jnp.concatenate(chunks, axis=0), earlier, norm_scale)

time: 294 us -> 293 us (level)
  waiting for transfers between devices: 206 us -> 233 us
  starting transfers between devices: 38.7 us -> 14.8 us
    ppermute x13 -> x11, waiting for transfers between devices: 206 us -> 233 us  [sent(): return lax.ppermute(value, ('tm', 'row'), pairs)]
    ppermute x13 -> x11, starting transfers between devices: 38.7 us -> 14.8 us  [sent(): return lax.ppermute(value, ('tm', 'row'), pairs)]
  transfers between devices with their start and end apart: 13 -> 11, of which waited for: 7 -> 6; matrix products, arithmetic and copies ran while one was open for 3% -> 3% of each run, Pallas kernels for 0% -> 0%
where the time goes in v19:
time: 293 us
  waiting for transfers between devices  233 us (80%)
  matrix products  37.6 us (13%)
  starting transfers between devices  14.8 us (5%)
  other arithmetic  5.7 us (2%)
    ppermute x11, waiting for transfers between devices, sent(): return lax.ppermute(value, ('tm', 'row'), pairs)  233 us
    dot_general x2, matrix products, level_product(): total = jnp.dot(later, earlier, preferred_element_type=jnp.float32)  26.2 us
    ppermute x11, starting transfers between devices, sent(): return lax.ppermute(value, ('tm', 'row'), pairs)  14.8 us
    dot_general x2, matrix products, shards(): jnp.dot(left_factor[c * chunk_rows:(c + 1) * chunk_rows], right_factor, p...  10.6 us
  transfers between devices with their start and end apart: 11, of which 6 were waited for; matrix products, arithmetic and copies ran while one was open for 3% of the time, Pallas kernels for 0%

profile of v19, /device:TPU:96, one launch (start us, length us, event | category | flops | bytes accessed | tf_op | source)
XLA Modules:
  0.0 292.9 jit_solution(3255764803096496340)
XLA Ops:
  0.0 0.0 copy-start
  0.0 0.7 multiply_bitcast_fusion
  0.7 0.2 copy-done
  0.9 0.9 fusion.39
  1.8 0.0 copy-start.2
  1.8 3.4 %fusion.28 = bf16[1024,2048]{1,0:T(8,128)(2,1)S(1)} fusion(bf16[1,1024,2048]{2,1,0:T(8,128)(2,1)} %param.5, f32[2048]{0:T(1024)S(1)} %bitcast.12), kind=kLoop, calls=%fused_computation.32 | loop fusion | flops 6291456 | bytes 8396800 | tf_op jit(solution)/shard_map/convert_element_type | solution.py:85
  5.3 1.2 copy-done.2
  6.5 4.8 %multiply_convert_fusion.6 = bf16[512,2048]{1,0:T(8,128)(2,1)S(1)} fusion(bf16[2048,2048]{1,0:T(8,128)(2,1)S(1)} %copy-done.2, f32[2048]{0:T(1024)S(1)} %bitcast.13, bf16[1024,2048]{1,0:T(8,128)(2,1)S(1)} %fusion.28), kind=kOutput, calls=%fused_computation.44 | convolution fusion | flops 4309647360 | bytes 12591104 | tf_op jit(solution)/shard_map/dot_general | solution.py:89
  11.3 2.7 collective-permute-start.2
  14.0 0.5 collective-permute-start
  14.5 5.8 %multiply_convert_fusion.5 = bf16[512,2048]{1,0:T(8,128)(2,1)} fusion(bf16[2048,2048]{1,0:T(8,128)(2,1)S(1)} %copy-done.2, f32[2048]{0:T(1024)S(1)} %bitcast.14, bf16[1024,2048]{1,0:T(8,128)(2,1)S(1)} %fusion.28), kind=kOutput, calls=%fused_computation.43 | convolution fusion | flops 4309647360 | bytes 12591104 | tf_op jit(solution)/shard_map/dot_general | solution.py:89
  20.2 1.7 collective-permute-start.3
  22.0 0.0 collective-permute-start.1
  22.0 44.6 %collective-permute-done.2 = bf16[512,2048]{1,0:T(8,128)(2,1)} collective-permute-done((bf16[512,2048]{1,0:T(8,128)(2,1)S(1)}, bf16[512,2048]{1,0:T(8,128)(2,1)}, u32[]{:S(2)}, u32[]{:S(2)}) %collective-permute-start.2) | collective-permute-done | bytes 2097184 | tf_op jit(solution)/shard_map/ppermute | solution.py:22
  66.6 0.0 collective-permute-done
  66.6 51.9 %collective-permute-done.3 = bf16[512,2048]{1,0:T(8,128)(2,1)} collective-permute-done((bf16[512,2048]{1,0:T(8,128)(2,1)}, bf16[512,2048]{1,0:T(8,128)(2,1)}, u32[]{:S(2)}, u32[]{:S(2)}) %collective-permute-start.3) | collective-permute-done | bytes 2097184 | tf_op jit(solution)/shard_map/ppermute | solution.py:22
  118.5 0.0 collective-permute-done.1
  118.5 12.6 %multiply_convert_fusion.2 = bf16[1024,2048]{1,0:T(8,128)(2,1)S(1)} fusion(bf16[512,2048]{1,0:T(8,128)(2,1)} %collective-permute-done.3, bf16[512,2048]{1,0:T(8,128)(2,1)} %collective-permute-done.2, bf16[512,2048]{1,0:T(8,128)(2,1)} %collective-permute-done.1, bf16[512,2048]{1,0:T(8,128)(2,1)} %collective-permute-done, pred[]{:T(512)S(6)} %eq.17, ...), kind=kOutput, calls=%fused_computation.34 | convolution fusion | flops 8673820672 | bytes 16777216 | tf_op jit(solution)/shard_map/dot_general | solution.py:66
  131.1 0.0 copy-start.1
  131.1 4.2 %collective-permute-start.6 = (bf16[1024,2048]{1,0:T(8,128)(2,1)S(1)}, bf16[1024,2048]{1,0:T(8,128)(2,1)S(1)}, u32[]{:S(2)}, u32[]{:S(2)}) collective-permute-start(bf16[1024,2048]{1,0:T(8,128)(2,1)S(1)} %multiply_convert_fusion.2), channel_id=1, source_target_pairs={{0,5},{1,4},{2,7},{3,6},{8,13},{9,12},{10,15},{11,14},{16,21},{17,... | collective-permute-start | bytes 12582920 | tf_op jit(solution)/shard_map/ppermute | solution.py:22
  135.3 0.1 collective-permute-start.4
  135.4 0.2 slice.48
  135.5 0.8 collective-permute-start.9
  136.3 0.2 slice.46
  136.4 0.8 collective-permute-start.7
  137.2 0.1 slice.44
  137.3 1.3 collective-permute-start.5
  138.6 0.0 collective-permute-done.9
  138.6 1.3 collective-permute-start.10
  139.9 0.0 collective-permute-done.7
  139.9 1.5 collective-permute-start.8
  141.4 66.2 %collective-permute-done.5 = bf16[304,2048]{1,0:T(8,128)(2,1)S(1)} collective-permute-done((bf16[304,2048]{1,0:T(8,128)(2,1)S(1)}, bf16[304,2048]{1,0:T(8,128)(2,1)S(1)}, u32[]{:S(2)}, u32[]{:S(2)}) %collective-permute-start.5) | collective-permute-done | bytes 1245216 | tf_op jit(solution)/shard_map/ppermute | solution.py:22
  207.6 1.2 collective-permute-done.6
  208.8 1.3 slice_add_fusion.2
  210.0 0.0 copy-done.1
  210.0 8.7 %collective-permute-done.10 = bf16[352,2048]{1,0:T(8,128)(2,1)S(1)} collective-permute-done((bf16[352,2048]{1,0:T(8,128)(2,1)S(1)}, bf16[352,2048]{1,0:T(8,128)(2,1)S(1)}, u32[]{:S(2)}, u32[]{:S(2)}) %collective-permute-start.10) | collective-permute-done | bytes 1441824 | tf_op jit(solution)/shard_map/ppermute | solution.py:22
  218.8 0.1 slice_add_fusion.1
  218.9 60.1 %collective-permute-done.8 = bf16[368,2048]{1,0:T(8,128)(2,1)S(1)} collective-permute-done((bf16[368,2048]{1,0:T(8,128)(2,1)S(1)}, bf16[368,2048]{1,0:T(8,128)(2,1)S(1)}, u32[]{:S(2)}, u32[]{:S(2)}) %collective-permute-start.8) | collective-permute-done | bytes 1507360 | tf_op jit(solution)/shard_map/ppermute | solution.py:22
  279.1 0.2 slice_add_fusion
  279.2 0.0 collective-permute-done.4
  279.2 13.6 %fusion.33 = bf16[1,1024,2048]{2,1,0:T(8,128)(2,1)} fusion(bf16[1024,2048]{1,0:T(8,128)(2,1)} %copy-done.1, bf16[352,2048]{1,0:T(8,128)(2,1)S(1)} %slice_add_fusion.1, bf16[368,2048]{1,0:T(8,128)(2,1)S(1)} %slice_add_fusion, bf16[304,2048]{1,0:T(8,128)(2,1)} %slice_add_fusion.2, bf16[1024,2048]{1,0:T(8,128)(2,1)} %collective-permute-done.4, pred[]{:T(512)S(6)} %eq.17), kind=kOutput, calls=%fused_computation.39 | convolution fusion | flops 8665432064 | bytes 16777216 | tf_op jit(solution)/shard_map/dot_general | solution.py:66
  (1 shorter events, 0.0 us)
Async XLA Ops:
  0.0 0.9 copy-start
  1.8 4.6 %copy-start.2 = (bf16[2048,2048]{1,0:T(8,128)(2,1)S(1)}, bf16[2048,2048]{1,0:T(8,128)(2,1)}, u32[]{:S(2)}) copy-start(bf16[2048,2048]{1,0:T(8,128)(2,1)} %param.6) | copy-start | bytes 25165828
  11.3 55.3 %collective-permute-start.2 = (bf16[512,2048]{1,0:T(8,128)(2,1)S(1)}, bf16[512,2048]{1,0:T(8,128)(2,1)}, u32[]{:S(2)}, u32[]{:S(2)}) collective-permute-start(bf16[512,2048]{1,0:T(8,128)(2,1)S(1)} %multiply_convert_fusion.6), channel_id=1, source_target_pairs={{0,3},{1,2},{2,5},{3,4},{4,7},{5,6},{6,9},{7,8},{8,11},{9,10},{10,... | collective-permute-start | bytes 6291464 | tf_op jit(solution)/shard_map/ppermute | solution.py:22
  14.0 52.6 %collective-permute-start = (bf16[512,2048]{1,0:T(8,128)(2,1)S(1)}, bf16[512,2048]{1,0:T(8,128)(2,1)}, u32[]{:S(2)}, u32[]{:S(2)}) collective-permute-start(bf16[512,2048]{1,0:T(8,128)(2,1)S(1)} %multiply_convert_fusion.6), channel_id=1, source_target_pairs={{0,2},{1,3},{2,4},{3,5},{4,6},{5,7},{6,8},{7,9},{8,10},{9,11},{10,... | collective-permute-start | bytes 6291464 | tf_op jit(solution)/shard_map/ppermute | solution.py:22
  20.2 98.2 %collective-permute-start.3 = (bf16[512,2048]{1,0:T(8,128)(2,1)}, bf16[512,2048]{1,0:T(8,128)(2,1)}, u32[]{:S(2)}, u32[]{:S(2)}) collective-permute-start(bf16[512,2048]{1,0:T(8,128)(2,1)} %multiply_convert_fusion.5), channel_id=1, source_target_pairs={{0,3},{1,2},{2,5},{3,4},{4,7},{5,6},{6,9},{7,8},{8,11},{9,10},{10,... | collective-permute-start | bytes 6291464 | tf_op jit(solution)/shard_map/ppermute | solution.py:22
  22.0 96.5 %collective-permute-start.1 = (bf16[512,2048]{1,0:T(8,128)(2,1)}, bf16[512,2048]{1,0:T(8,128)(2,1)}, u32[]{:S(2)}, u32[]{:S(2)}) collective-permute-start(bf16[512,2048]{1,0:T(8,128)(2,1)} %multiply_convert_fusion.5), channel_id=1, source_target_pairs={{0,2},{1,3},{2,4},{3,5},{4,6},{5,7},{6,8},{7,9},{8,10},{9,11},{10,... | collective-permute-start | bytes 6291464 | tf_op jit(solution)/shard_map/ppermute | solution.py:22
  131.1 79.0 %copy-start.1 = (bf16[1024,2048]{1,0:T(8,128)(2,1)}, bf16[1024,2048]{1,0:T(8,128)(2,1)S(1)}, u32[]{:S(2)}) copy-start(bf16[1024,2048]{1,0:T(8,128)(2,1)S(1)} %multiply_convert_fusion.2) | copy-start | bytes 12582916
  131.1 77.7 %collective-permute-start.6 = (bf16[1024,2048]{1,0:T(8,128)(2,1)S(1)}, bf16[1024,2048]{1,0:T(8,128)(2,1)S(1)}, u32[]{:S(2)}, u32[]{:S(2)}) collective-permute-start(bf16[1024,2048]{1,0:T(8,128)(2,1)S(1)} %multiply_convert_fusion.2), channel_id=1, source_target_pairs={{0,5},{1,4},{2,7},{3,6},{8,13},{9,12},{10,15},{11,14},{16,21},{17,... | collective-permute-start | bytes 12582920 | tf_op jit(solution)/shard_map/ppermute | solution.py:22
  135.3 144.0 %collective-permute-start.4 = (bf16[1024,2048]{1,0:T(8,128)(2,1)S(1)}, bf16[1024,2048]{1,0:T(8,128)(2,1)}, u32[]{:S(2)}, u32[]{:S(2)}) collective-permute-start(bf16[1024,2048]{1,0:T(8,128)(2,1)S(1)} %multiply_convert_fusion.2), channel_id=1, source_target_pairs={{0,4},{1,5},{2,6},{3,7},{4,8},{5,9},{6,10},{7,11},{8,12},{9,13},{1... | collective-permute-start | bytes 12582920 | tf_op jit(solution)/shard_map/ppermute | solution.py:22
  135.5 3.1 %collective-permute-start.9 = (bf16[352,2048]{1,0:T(8,128)(2,1)S(1)}, bf16[352,2048]{1,0:T(8,128)(2,1)S(1)}, u32[]{:S(2)}, u32[]{:S(2)}) collective-permute-start(bf16[352,2048]{1,0:T(8,128)(2,1)S(1)} %slice.48), channel_id=1, source_target_pairs={{4,12},{5,13},{6,14},{7,15},{12,20},{13,21},{14,22},{15,23},{20,28... | collective-permute-start | bytes 4325384 | tf_op jit(solution)/shard_map/ppermute | solution.py:22
  136.4 3.5 %collective-permute-start.7 = (bf16[368,2048]{1,0:T(8,128)(2,1)S(1)}, bf16[368,2048]{1,0:T(8,128)(2,1)S(1)}, u32[]{:S(2)}, u32[]{:S(2)}) collective-permute-start(bf16[368,2048]{1,0:T(8,128)(2,1)S(1)} %slice.46), channel_id=1, source_target_pairs={{4,12},{5,13},{6,14},{7,15},{12,20},{13,21},{14,22},{15,23},{20,28... | collective-permute-start | bytes 4521992 | tf_op jit(solution)/shard_map/ppermute | solution.py:22
  137.3 70.3 %collective-permute-start.5 = (bf16[304,2048]{1,0:T(8,128)(2,1)S(1)}, bf16[304,2048]{1,0:T(8,128)(2,1)S(1)}, u32[]{:S(2)}, u32[]{:S(2)}) collective-permute-start(bf16[304,2048]{1,0:T(8,128)(2,1)S(1)} %slice.44), channel_id=1, source_target_pairs={{4,9},{5,8},{6,11},{7,10},{12,17},{13,16},{14,19},{15,18},{20,25},... | collective-permute-start | bytes 3735560 | tf_op jit(solution)/shard_map/ppermute | solution.py:22
  138.6 80.2 %collective-permute-start.10 = (bf16[352,2048]{1,0:T(8,128)(2,1)S(1)}, bf16[352,2048]{1,0:T(8,128)(2,1)S(1)}, u32[]{:S(2)}, u32[]{:S(2)}) collective-permute-start(bf16[352,2048]{1,0:T(8,128)(2,1)S(1)} %collective-permute-done.9), channel_id=1, source_target_pairs={{4,33},{5,32},{6,35},{7,34},{12,9},{13,8},{14,11},{15,10},{20,17},... | collective-permute-start | bytes 4325384 | tf_op jit(solution)/shard_map/ppermute | solution.py:22
  139.9 139.1 %collective-permute-start.8 = (bf16[368,2048]{1,0:T(8,128)(2,1)S(1)}, bf16[368,2048]{1,0:T(8,128)(2,1)S(1)}, u32[]{:S(2)}, u32[]{:S(2)}) collective-permute-start(bf16[368,2048]{1,0:T(8,128)(2,1)S(1)} %collective-permute-done.7), channel_id=1, source_target_pairs={{4,33},{5,32},{6,35},{7,34},{12,9},{13,8},{14,11},{15,10},{20,17},... | collective-permute-start | bytes 4521992 | tf_op jit(solution)/shard_map/ppermute | solution.py:22

commit v20 on v19

--- a/solution.py
+++ b/solution.py
@@ -6,8 +6,8 @@
 from jax.sharding import PartitionSpec as P
 
 LEVELS = 2
-DIRECT_ROWS = 304
-RELAY_ROWS = (368, 352)
+DIRECT_ROWS = 352
+RELAY_ROWS = (672,)
 
 
 def sent(value, route):

time: 293 us -> 296 us (1.010)
  the two profiles are of different devices: /device:TPU:96 before, /device:TPU:6 now
where the time goes in v20:
time: 296 us; the launch traced here: 295 us
  waiting for transfers between devices  240 us (81%)
  matrix products  37.6 us (13%)
  starting transfers between devices  10.2 us (3%)
  other arithmetic  6.12 us (2%)
    ppermute x9, waiting for transfers between devices, sent(): return lax.ppermute(value, ('tm', 'row'), pairs)  240 us
    dot_general x2, matrix products, level_product(): total = jnp.dot(later, earlier, preferred_element_type=jnp.float32)  26.2 us
    dot_general x2, matrix products, shards(): jnp.dot(left_factor[c * chunk_rows:(c + 1) * chunk_rows], right_factor, p...  10.5 us
    ppermute x9, starting transfers between devices, sent(): return lax.ppermute(value, ('tm', 'row'), pairs)  10.2 us
  transfers between devices with their start and end apart: 9, of which 5 were waited for; matrix products, arithmetic and copies ran while one was open for 3% of the time, Pallas kernels for 0%

profile of v20, /device:TPU:6, one launch (start us, length us, event | category | flops | bytes accessed | tf_op | source)
XLA Modules:
  0.0 295.5 jit_solution(11659738093973796973)
XLA Ops:
  0.0 0.0 copy-start
  0.0 0.7 multiply_bitcast_fusion
  0.7 0.2 copy-done
  0.9 0.9 fusion.35
  1.8 0.0 copy-start.1
  1.8 3.4 %fusion.24 = bf16[1024,2048]{1,0:T(8,128)(2,1)S(1)} fusion(bf16[1,1024,2048]{2,1,0:T(8,128)(2,1)} %param.5, f32[2048]{0:T(1024)S(1)} %bitcast.12), kind=kLoop, calls=%fused_computation.28 | loop fusion | flops 6291456 | bytes 8396800 | tf_op jit(solution)/shard_map/convert_element_type | solution.py:85
  5.3 1.2 copy-done.1
  6.5 4.8 %multiply_convert_fusion.6 = bf16[512,2048]{1,0:T(8,128)(2,1)S(1)} fusion(bf16[2048,2048]{1,0:T(8,128)(2,1)S(1)} %copy-done.1, f32[2048]{0:T(1024)S(1)} %bitcast.13, bf16[1024,2048]{1,0:T(8,128)(2,1)S(1)} %fusion.24), kind=kOutput, calls=%fused_computation.40 | convolution fusion | flops 4309647360 | bytes 12591104 | tf_op jit(solution)/shard_map/dot_general | solution.py:89
  11.3 2.7 collective-permute-start.2
  14.0 0.5 collective-permute-start
  14.5 5.8 %multiply_convert_fusion.5 = bf16[512,2048]{1,0:T(8,128)(2,1)} fusion(bf16[2048,2048]{1,0:T(8,128)(2,1)S(1)} %copy-done.1, f32[2048]{0:T(1024)S(1)} %bitcast.14, bf16[1024,2048]{1,0:T(8,128)(2,1)S(1)} %fusion.24), kind=kOutput, calls=%fused_computation.39 | convolution fusion | flops 4309647360 | bytes 12591104 | tf_op jit(solution)/shard_map/dot_general | solution.py:89
  20.2 1.7 collective-permute-start.3
  22.0 0.0 collective-permute-start.1
  22.0 41.7 %collective-permute-done.2 = bf16[512,2048]{1,0:T(8,128)(2,1)} collective-permute-done((bf16[512,2048]{1,0:T(8,128)(2,1)S(1)}, bf16[512,2048]{1,0:T(8,128)(2,1)}, u32[]{:S(2)}, u32[]{:S(2)}) %collective-permute-start.2) | collective-permute-done | bytes 2097184 | tf_op jit(solution)/shard_map/ppermute | solution.py:22
  63.7 20.2 %collective-permute-done = bf16[512,2048]{1,0:T(8,128)(2,1)} collective-permute-done((bf16[512,2048]{1,0:T(8,128)(2,1)S(1)}, bf16[512,2048]{1,0:T(8,128)(2,1)}, u32[]{:S(2)}, u32[]{:S(2)}) %collective-permute-start) | collective-permute-done | bytes 2097184 | tf_op jit(solution)/shard_map/ppermute | solution.py:22
  83.9 35.2 %collective-permute-done.3 = bf16[512,2048]{1,0:T(8,128)(2,1)} collective-permute-done((bf16[512,2048]{1,0:T(8,128)(2,1)}, bf16[512,2048]{1,0:T(8,128)(2,1)}, u32[]{:S(2)}, u32[]{:S(2)}) %collective-permute-start.3) | collective-permute-done | bytes 2097184 | tf_op jit(solution)/shard_map/ppermute | solution.py:22
  119.0 22.9 %collective-permute-done.1 = bf16[512,2048]{1,0:T(8,128)(2,1)} collective-permute-done((bf16[512,2048]{1,0:T(8,128)(2,1)}, bf16[512,2048]{1,0:T(8,128)(2,1)}, u32[]{:S(2)}, u32[]{:S(2)}) %collective-permute-start.1) | collective-permute-done | bytes 2097184 | tf_op jit(solution)/shard_map/ppermute | solution.py:22
  141.9 12.6 %multiply_convert_fusion.2 = bf16[1024,2048]{1,0:T(8,128)(2,1)S(1)} fusion(bf16[512,2048]{1,0:T(8,128)(2,1)} %collective-permute-done.3, bf16[512,2048]{1,0:T(8,128)(2,1)} %collective-permute-done.2, bf16[512,2048]{1,0:T(8,128)(2,1)} %collective-permute-done.1, bf16[512,2048]{1,0:T(8,128)(2,1)} %collective-permute-done, pred[]{:T(512)S(6)} %eq.17, ...), kind=kOutput, calls=%fused_computation.30 | convolution fusion | flops 8673820672 | bytes 16777216 | tf_op jit(solution)/shard_map/dot_general | solution.py:66
  154.6 0.2 slice.38
  154.8 0.8 collective-permute-start.7
  155.6 1.6 collective-permute-start.6
  157.2 0.1 collective-permute-start.4
  157.3 0.0 collective-permute-done.7
  157.3 1.3 collective-permute-start.8
  158.6 0.1 slice.36
  158.7 1.5 collective-permute-start.5
  160.2 119.8 %collective-permute-done.5 = bf16[352,2048]{1,0:T(8,128)(2,1)S(1)} collective-permute-done((bf16[352,2048]{1,0:T(8,128)(2,1)S(1)}, bf16[352,2048]{1,0:T(8,128)(2,1)S(1)}, u32[]{:S(2)}, u32[]{:S(2)}) %collective-permute-start.5) | collective-permute-done | bytes 1441824 | tf_op jit(solution)/shard_map/ppermute | solution.py:22
  279.9 0.0 collective-permute-done.6
  279.9 0.1 slice_add_fusion.1
  280.1 0.0 collective-permute-done.8
  280.1 1.8 slice_add_fusion
  281.9 0.0 collective-permute-done.4
  281.9 13.6 %fusion.29 = bf16[1,1024,2048]{2,1,0:T(8,128)(2,1)} fusion(bf16[1024,2048]{1,0:T(8,128)(2,1)S(1)} %multiply_convert_fusion.2, bf16[672,2048]{1,0:T(8,128)(2,1)} %slice_add_fusion, bf16[352,2048]{1,0:T(8,128)(2,1)S(1)} %slice_add_fusion.1, bf16[1024,2048]{1,0:T(8,128)(2,1)} %collective-permute-done.4, pred[]{:T(512)S(6)} %eq.17), kind=kOutput, calls=%fused_computation.35 | convolution fusion | flops 8648654848 | bytes 16777216 | tf_op jit(solution)/shard_map/dot_general | solution.py:66
  (1 shorter events, 0.0 us)
Async XLA Ops:
  0.0 0.9 copy-start
  1.8 4.6 %copy-start.1 = (bf16[2048,2048]{1,0:T(8,128)(2,1)S(1)}, bf16[2048,2048]{1,0:T(8,128)(2,1)}, u32[]{:S(2)}) copy-start(bf16[2048,2048]{1,0:T(8,128)(2,1)} %param.6) | copy-start | bytes 25165828
  11.3 52.4 %collective-permute-start.2 = (bf16[512,2048]{1,0:T(8,128)(2,1)S(1)}, bf16[512,2048]{1,0:T(8,128)(2,1)}, u32[]{:S(2)}, u32[]{:S(2)}) collective-permute-start(bf16[512,2048]{1,0:T(8,128)(2,1)S(1)} %multiply_convert_fusion.6), channel_id=1, source_target_pairs={{0,3},{1,2},{2,5},{3,4},{4,7},{5,6},{6,9},{7,8},{8,11},{9,10},{10,... | collective-permute-start | bytes 6291464 | tf_op jit(solution)/shard_map/ppermute | solution.py:22
  14.0 69.9 %collective-permute-start = (bf16[512,2048]{1,0:T(8,128)(2,1)S(1)}, bf16[512,2048]{1,0:T(8,128)(2,1)}, u32[]{:S(2)}, u32[]{:S(2)}) collective-permute-start(bf16[512,2048]{1,0:T(8,128)(2,1)S(1)} %multiply_convert_fusion.6), channel_id=1, source_target_pairs={{0,2},{1,3},{2,4},{3,5},{4,6},{5,7},{6,8},{7,9},{8,10},{9,11},{10,... | collective-permute-start | bytes 6291464 | tf_op jit(solution)/shard_map/ppermute | solution.py:22
  20.2 98.8 %collective-permute-start.3 = (bf16[512,2048]{1,0:T(8,128)(2,1)}, bf16[512,2048]{1,0:T(8,128)(2,1)}, u32[]{:S(2)}, u32[]{:S(2)}) collective-permute-start(bf16[512,2048]{1,0:T(8,128)(2,1)} %multiply_convert_fusion.5), channel_id=1, source_target_pairs={{0,3},{1,2},{2,5},{3,4},{4,7},{5,6},{6,9},{7,8},{8,11},{9,10},{10,... | collective-permute-start | bytes 6291464 | tf_op jit(solution)/shard_map/ppermute | solution.py:22
  22.0 120.0 %collective-permute-start.1 = (bf16[512,2048]{1,0:T(8,128)(2,1)}, bf16[512,2048]{1,0:T(8,128)(2,1)}, u32[]{:S(2)}, u32[]{:S(2)}) collective-permute-start(bf16[512,2048]{1,0:T(8,128)(2,1)} %multiply_convert_fusion.5), channel_id=1, source_target_pairs={{0,2},{1,3},{2,4},{3,5},{4,6},{5,7},{6,8},{7,9},{8,10},{9,11},{10,... | collective-permute-start | bytes 6291464 | tf_op jit(solution)/shard_map/ppermute | solution.py:22
  154.8 2.5 collective-permute-start.7
  155.6 124.3 %collective-permute-start.6 = (bf16[1024,2048]{1,0:T(8,128)(2,1)S(1)}, bf16[1024,2048]{1,0:T(8,128)(2,1)S(1)}, u32[]{:S(2)}, u32[]{:S(2)}) collective-permute-start(bf16[1024,2048]{1,0:T(8,128)(2,1)S(1)} %multiply_convert_fusion.2), channel_id=1, source_target_pairs={{0,5},{1,4},{2,7},{3,6},{8,13},{9,12},{10,15},{11,14},{16,21},{17,... | collective-permute-start | bytes 12582920 | tf_op jit(solution)/shard_map/ppermute | solution.py:22
  157.2 124.7 %collective-permute-start.4 = (bf16[1024,2048]{1,0:T(8,128)(2,1)S(1)}, bf16[1024,2048]{1,0:T(8,128)(2,1)}, u32[]{:S(2)}, u32[]{:S(2)}) collective-permute-start(bf16[1024,2048]{1,0:T(8,128)(2,1)S(1)} %multiply_convert_fusion.2), channel_id=1, source_target_pairs={{0,4},{1,5},{2,6},{3,7},{4,8},{5,9},{6,10},{7,11},{8,12},{9,13},{1... | collective-permute-start | bytes 12582920 | tf_op jit(solution)/shard_map/ppermute | solution.py:22
  157.3 122.8 %collective-permute-start.8 = (bf16[672,2048]{1,0:T(8,128)(2,1)S(1)}, bf16[672,2048]{1,0:T(8,128)(2,1)S(1)}, u32[]{:S(2)}, u32[]{:S(2)}) collective-permute-start(bf16[672,2048]{1,0:T(8,128)(2,1)S(1)} %collective-permute-done.7), channel_id=1, source_target_pairs={{4,33},{5,32},{6,35},{7,34},{12,9},{13,8},{14,11},{15,10},{20,17},... | collective-permute-start | bytes 8257544 | tf_op jit(solution)/shard_map/ppermute | solution.py:22
  158.7 121.2 %collective-permute-start.5 = (bf16[352,2048]{1,0:T(8,128)(2,1)S(1)}, bf16[352,2048]{1,0:T(8,128)(2,1)S(1)}, u32[]{:S(2)}, u32[]{:S(2)}) collective-permute-start(bf16[352,2048]{1,0:T(8,128)(2,1)S(1)} %slice.36), channel_id=1, source_target_pairs={{4,9},{5,8},{6,11},{7,10},{12,17},{13,16},{14,19},{15,18},{20,25},... | collective-permute-start | bytes 4325384 | tf_op jit(solution)/shard_map/ppermute | solution.py:22

commit v21 on v20

--- a/solution.py
+++ b/solution.py
@@ -6,8 +6,8 @@
 from jax.sharding import PartitionSpec as P
 
 LEVELS = 2
-DIRECT_ROWS = 352
-RELAY_ROWS = (672,)
+DIRECT_ROWS = 336
+RELAY_ROWS = (352, 336)
 
 
 def sent(value, route):

time: 296 us -> 305 us (1.030)
  the two profiles are of different devices: /device:TPU:6 before, /device:TPU:80 now
where the time goes in v21:
time: 305 us
  waiting for transfers between devices  246 us (81%)
  matrix products  37.6 us (12%)
  starting transfers between devices  12.4 us (4%)
  other arithmetic  5.72 us (2%)
  local copies, waits for them, and re-layouts  3.69 us (1%)
    ppermute x11, waiting for transfers between devices, sent(): return lax.ppermute(value, ('tm', 'row'), pairs)  246 us
    dot_general x2, matrix products, level_product(): total = jnp.dot(later, earlier, preferred_element_type=jnp.float32)  26.3 us
    ppermute x11, starting transfers between devices, sent(): return lax.ppermute(value, ('tm', 'row'), pairs)  12.4 us
    dot_general x2, matrix products, shards(): jnp.dot(left_factor[c * chunk_rows:(c + 1) * chunk_rows], right_factor, p...  10.5 us
  transfers between devices with their start and end apart: 11, of which 5 were waited for; matrix products, arithmetic and copies ran while one was open for 2% of the time, Pallas kernels for 0%

profile of v21, /device:TPU:80, one launch (start us, length us, event | category | flops | bytes accessed | tf_op | source)
XLA Modules:
  0.0 305.2 jit_solution(5444989020589908811)
XLA Ops:
  0.0 0.0 copy-start
  0.0 0.7 multiply_bitcast_fusion
  0.7 0.2 copy-done
  0.9 0.9 fusion.39
  1.8 0.0 copy-start.2
  1.8 3.4 %fusion.28 = bf16[1024,2048]{1,0:T(8,128)(2,1)S(1)} fusion(bf16[1,1024,2048]{2,1,0:T(8,128)(2,1)} %param.5, f32[2048]{0:T(1024)S(1)} %bitcast.12), kind=kLoop, calls=%fused_computation.32 | loop fusion | flops 6291456 | bytes 8396800 | tf_op jit(solution)/shard_map/convert_element_type | solution.py:85
  5.3 1.2 copy-done.2
  6.5 4.8 %multiply_convert_fusion.6 = bf16[512,2048]{1,0:T(8,128)(2,1)S(1)} fusion(bf16[2048,2048]{1,0:T(8,128)(2,1)S(1)} %copy-done.2, f32[2048]{0:T(1024)S(1)} %bitcast.13, bf16[1024,2048]{1,0:T(8,128)(2,1)S(1)} %fusion.28), kind=kOutput, calls=%fused_computation.44 | convolution fusion | flops 4309647360 | bytes 12591104 | tf_op jit(solution)/shard_map/dot_general | solution.py:89
  11.2 0.1 collective-permute-start.2
  11.3 0.6 collective-permute-start
  11.9 5.7 %multiply_convert_fusion.5 = bf16[512,2048]{1,0:T(8,128)(2,1)} fusion(bf16[2048,2048]{1,0:T(8,128)(2,1)S(1)} %copy-done.2, f32[2048]{0:T(1024)S(1)} %bitcast.14, bf16[1024,2048]{1,0:T(8,128)(2,1)S(1)} %fusion.28), kind=kOutput, calls=%fused_computation.43 | convolution fusion | flops 4309647360 | bytes 12591104 | tf_op jit(solution)/shard_map/dot_general | solution.py:89
  17.6 2.8 collective-permute-start.3
  20.4 0.0 collective-permute-start.1
  20.4 39.8 %collective-permute-done.2 = bf16[512,2048]{1,0:T(8,128)(2,1)} collective-permute-done((bf16[512,2048]{1,0:T(8,128)(2,1)S(1)}, bf16[512,2048]{1,0:T(8,128)(2,1)}, u32[]{:S(2)}, u32[]{:S(2)}) %collective-permute-start.2) | collective-permute-done | bytes 2097184 | tf_op jit(solution)/shard_map/ppermute | solution.py:22
  60.2 0.1 collective-permute-done
  60.3 44.9 %collective-permute-done.3 = bf16[512,2048]{1,0:T(8,128)(2,1)} collective-permute-done((bf16[512,2048]{1,0:T(8,128)(2,1)}, bf16[512,2048]{1,0:T(8,128)(2,1)}, u32[]{:S(2)}, u32[]{:S(2)}) %collective-permute-start.3) | collective-permute-done | bytes 2097184 | tf_op jit(solution)/shard_map/ppermute | solution.py:22
  105.2 0.0 collective-permute-done.1
  105.2 12.6 %multiply_convert_fusion.2 = bf16[1024,2048]{1,0:T(8,128)(2,1)S(1)} fusion(bf16[512,2048]{1,0:T(8,128)(2,1)} %collective-permute-done.3, bf16[512,2048]{1,0:T(8,128)(2,1)} %collective-permute-done.2, bf16[512,2048]{1,0:T(8,128)(2,1)} %collective-permute-done.1, bf16[512,2048]{1,0:T(8,128)(2,1)} %collective-permute-done, pred[]{:T(512)S(6)} %eq.17, ...), kind=kOutput, calls=%fused_computation.34 | convolution fusion | flops 8673820672 | bytes 16777216 | tf_op jit(solution)/shard_map/dot_general | solution.py:66
  117.8 0.0 copy-start.1
  117.8 3.3 %collective-permute-start.6 = (bf16[1024,2048]{1,0:T(8,128)(2,1)S(1)}, bf16[1024,2048]{1,0:T(8,128)(2,1)S(1)}, u32[]{:S(2)}, u32[]{:S(2)}) collective-permute-start(bf16[1024,2048]{1,0:T(8,128)(2,1)S(1)} %multiply_convert_fusion.2), channel_id=1, source_target_pairs={{0,5},{1,4},{2,7},{3,6},{8,13},{9,12},{10,15},{11,14},{16,21},{17,... | collective-permute-start | bytes 12582920 | tf_op jit(solution)/shard_map/ppermute | solution.py:22
  121.1 0.1 collective-permute-start.4
  121.2 0.1 slice.46
  121.3 0.8 collective-permute-start.7
  122.1 0.2 fusion.47
  122.3 0.0 copy-done.1
  122.3 0.7 collective-permute-start.9
  123.0 0.0 collective-permute-done.7
  123.0 1.3 collective-permute-start.8
  124.3 1.3 collective-permute-start.5
  125.6 0.0 collective-permute-done.9
  125.6 1.5 collective-permute-start.10
  127.1 98.7 %collective-permute-done.8 = bf16[352,2048]{1,0:T(8,128)(2,1)S(1)} collective-permute-done((bf16[352,2048]{1,0:T(8,128)(2,1)S(1)}, bf16[352,2048]{1,0:T(8,128)(2,1)S(1)}, u32[]{:S(2)}, u32[]{:S(2)}) %collective-permute-start.8) | collective-permute-done | bytes 1441824 | tf_op jit(solution)/shard_map/ppermute | solution.py:22
  225.9 0.0 collective-permute-done.6
  225.9 0.1 slice_add_fusion
  226.0 0.0 collective-permute-done.5
  226.0 62.1 %collective-permute-done.10 = bf16[336,2048]{1,0:T(8,128)(2,1)S(1)} collective-permute-done((bf16[336,2048]{1,0:T(8,128)(2,1)S(1)}, bf16[336,2048]{1,0:T(8,128)(2,1)S(1)}, u32[]{:S(2)}, u32[]{:S(2)}) %collective-permute-start.10) | collective-permute-done | bytes 1376288 | tf_op jit(solution)/shard_map/ppermute | solution.py:22
  288.1 1.4 slice_add_fusion.2
  289.5 0.0 collective-permute-done.4
  289.5 0.0 copy-start.3
  289.5 2.0 copy-done.3
  291.5 13.7 %fusion.33 = bf16[1,1024,2048]{2,1,0:T(8,128)(2,1)} fusion(bf16[1024,2048]{1,0:T(8,128)(2,1)} %copy-done.1, bf16[336,2048]{1,0:T(8,128)(2,1)} %get-tuple-element.6, bf16[352,2048]{1,0:T(8,128)(2,1)S(1)} %slice_add_fusion, bf16[336,2048]{1,0:T(8,128)(2,1)S(1)} %get-tuple-element.5, bf16[1024,2048]{1,0:T(8,128)(2,1)} %copy-done.3, pred[]{:T(512)S(6)} %eq.17), kind=kOutput, calls=%fused_computation.39 | convolution fusion | flops 8665432064 | bytes 16777216 | tf_op jit(solution)/shard_map/dot_general | solution.py:66
  (1 shorter events, 0.0 us)
Async XLA Ops:
  0.0 0.9 copy-start
  1.8 4.6 %copy-start.2 = (bf16[2048,2048]{1,0:T(8,128)(2,1)S(1)}, bf16[2048,2048]{1,0:T(8,128)(2,1)}, u32[]{:S(2)}) copy-start(bf16[2048,2048]{1,0:T(8,128)(2,1)} %param.6) | copy-start | bytes 25165828
  11.2 48.9 %collective-permute-start.2 = (bf16[512,2048]{1,0:T(8,128)(2,1)S(1)}, bf16[512,2048]{1,0:T(8,128)(2,1)}, u32[]{:S(2)}, u32[]{:S(2)}) collective-permute-start(bf16[512,2048]{1,0:T(8,128)(2,1)S(1)} %multiply_convert_fusion.6), channel_id=1, source_target_pairs={{0,3},{1,2},{2,5},{3,4},{4,7},{5,6},{6,9},{7,8},{8,11},{9,10},{10,... | collective-permute-start | bytes 6291464 | tf_op jit(solution)/shard_map/ppermute | solution.py:22
  11.3 49.0 %collective-permute-start = (bf16[512,2048]{1,0:T(8,128)(2,1)S(1)}, bf16[512,2048]{1,0:T(8,128)(2,1)}, u32[]{:S(2)}, u32[]{:S(2)}) collective-permute-start(bf16[512,2048]{1,0:T(8,128)(2,1)S(1)} %multiply_convert_fusion.6), channel_id=1, source_target_pairs={{0,2},{1,3},{2,4},{3,5},{4,6},{5,7},{6,8},{7,9},{8,10},{9,11},{10,... | collective-permute-start | bytes 6291464 | tf_op jit(solution)/shard_map/ppermute | solution.py:22
  17.6 87.6 %collective-permute-start.3 = (bf16[512,2048]{1,0:T(8,128)(2,1)}, bf16[512,2048]{1,0:T(8,128)(2,1)}, u32[]{:S(2)}, u32[]{:S(2)}) collective-permute-start(bf16[512,2048]{1,0:T(8,128)(2,1)} %multiply_convert_fusion.5), channel_id=1, source_target_pairs={{0,3},{1,2},{2,5},{3,4},{4,7},{5,6},{6,9},{7,8},{8,11},{9,10},{10,... | collective-permute-start | bytes 6291464 | tf_op jit(solution)/shard_map/ppermute | solution.py:22
  20.4 84.8 %collective-permute-start.1 = (bf16[512,2048]{1,0:T(8,128)(2,1)}, bf16[512,2048]{1,0:T(8,128)(2,1)}, u32[]{:S(2)}, u32[]{:S(2)}) collective-permute-start(bf16[512,2048]{1,0:T(8,128)(2,1)} %multiply_convert_fusion.5), channel_id=1, source_target_pairs={{0,2},{1,3},{2,4},{3,5},{4,6},{5,7},{6,8},{7,9},{8,10},{9,11},{10,... | collective-permute-start | bytes 6291464 | tf_op jit(solution)/shard_map/ppermute | solution.py:22
  117.8 4.5 %copy-start.1 = (bf16[1024,2048]{1,0:T(8,128)(2,1)}, bf16[1024,2048]{1,0:T(8,128)(2,1)S(1)}, u32[]{:S(2)}) copy-start(bf16[1024,2048]{1,0:T(8,128)(2,1)S(1)} %multiply_convert_fusion.2) | copy-start | bytes 12582916
  117.8 108.1 %collective-permute-start.6 = (bf16[1024,2048]{1,0:T(8,128)(2,1)S(1)}, bf16[1024,2048]{1,0:T(8,128)(2,1)S(1)}, u32[]{:S(2)}, u32[]{:S(2)}) collective-permute-start(bf16[1024,2048]{1,0:T(8,128)(2,1)S(1)} %multiply_convert_fusion.2), channel_id=1, source_target_pairs={{0,5},{1,4},{2,7},{3,6},{8,13},{9,12},{10,15},{11,14},{16,21},{17,... | collective-permute-start | bytes 12582920 | tf_op jit(solution)/shard_map/ppermute | solution.py:22
  121.1 168.4 %collective-permute-start.4 = (bf16[1024,2048]{1,0:T(8,128)(2,1)S(1)}, bf16[1024,2048]{1,0:T(8,128)(2,1)S(1)}, u32[]{:S(2)}, u32[]{:S(2)}) collective-permute-start(bf16[1024,2048]{1,0:T(8,128)(2,1)S(1)} %multiply_convert_fusion.2), channel_id=1, source_target_pairs={{0,4},{1,5},{2,6},{3,7},{4,8},{5,9},{6,10},{7,11},{8,12},{9,13},{1... | collective-permute-start | bytes 12582920 | tf_op jit(solution)/shard_map/ppermute | solution.py:22
  121.3 1.7 collective-permute-start.7
  122.3 3.4 %collective-permute-start.9 = (bf16[336,2048]{1,0:T(8,128)(2,1)S(1)}, bf16[336,2048]{1,0:T(8,128)(2,1)S(1)}, u32[]{:S(2)}, u32[]{:S(2)}) collective-permute-start(bf16[336,2048]{1,0:T(8,128)(2,1)S(1)} %get-tuple-element.8), channel_id=1, source_target_pairs={{4,12},{5,13},{6,14},{7,15},{12,20},{13,21},{14,22},{15,23},{20,28... | collective-permute-start | bytes 4128776 | tf_op jit(solution)/shard_map/ppermute | solution.py:22
  123.0 102.8 %collective-permute-start.8 = (bf16[352,2048]{1,0:T(8,128)(2,1)S(1)}, bf16[352,2048]{1,0:T(8,128)(2,1)S(1)}, u32[]{:S(2)}, u32[]{:S(2)}) collective-permute-start(bf16[352,2048]{1,0:T(8,128)(2,1)S(1)} %collective-permute-done.7), channel_id=1, source_target_pairs={{4,33},{5,32},{6,35},{7,34},{12,9},{13,8},{14,11},{15,10},{20,17},... | collective-permute-start | bytes 4325384 | tf_op jit(solution)/shard_map/ppermute | solution.py:22
  124.3 101.7 %collective-permute-start.5 = (bf16[336,2048]{1,0:T(8,128)(2,1)S(1)}, bf16[336,2048]{1,0:T(8,128)(2,1)S(1)}, u32[]{:S(2)}, u32[]{:S(2)}) collective-permute-start(bf16[336,2048]{1,0:T(8,128)(2,1)S(1)} %get-tuple-element.7), channel_id=1, source_target_pairs={{4,9},{5,8},{6,11},{7,10},{12,17},{13,16},{14,19},{15,18},{20,25},... | collective-permute-start | bytes 4128776 | tf_op jit(solution)/shard_map/ppermute | solution.py:22
  125.6 162.4 %collective-permute-start.10 = (bf16[336,2048]{1,0:T(8,128)(2,1)S(1)}, bf16[336,2048]{1,0:T(8,128)(2,1)S(1)}, u32[]{:S(2)}, u32[]{:S(2)}) collective-permute-start(bf16[336,2048]{1,0:T(8,128)(2,1)S(1)} %collective-permute-done.9), channel_id=1, source_target_pairs={{4,33},{5,32},{6,35},{7,34},{12,9},{13,8},{14,11},{15,10},{20,17},... | collective-permute-start | bytes 4128776 | tf_op jit(solution)/shard_map/ppermute | solution.py:22
  289.5 2.0 copy-start.3

commit v22 on v19

--- a/solution.py
+++ b/solution.py
@@ -7,7 +7,7 @@
 
 LEVELS = 2
 DIRECT_ROWS = 304
-RELAY_ROWS = (368, 352)
+RELAY_ROWS = (352, 368)
 
 
 def sent(value, route):

time: 293 us -> 293 us (level)
  no operation moved by 1% of the time
where the time goes in v22:
time: 293 us
  waiting for transfers between devices  233 us (80%)
  matrix products  37.6 us (13%)
  starting transfers between devices  14.8 us (5%)
  other arithmetic  5.7 us (2%)
    ppermute x11, waiting for transfers between devices, sent(): return lax.ppermute(value, ('tm', 'row'), pairs)  233 us
    dot_general x2, matrix products, level_product(): total = jnp.dot(later, earlier, preferred_element_type=jnp.float32)  26.2 us
    ppermute x11, starting transfers between devices, sent(): return lax.ppermute(value, ('tm', 'row'), pairs)  14.8 us
    dot_general x2, matrix products, shards(): jnp.dot(left_factor[c * chunk_rows:(c + 1) * chunk_rows], right_factor, p...  10.6 us
  transfers between devices with their start and end apart: 11, of which 6 were waited for; matrix products, arithmetic and copies ran while one was open for 3% of the time, Pallas kernels for 0%

profile of v22, /device:TPU:96, one launch (start us, length us, event | category | flops | bytes accessed | tf_op | source)
XLA Modules:
  0.0 292.9 jit_solution(9410423041761430886)
XLA Ops:
  0.0 0.0 copy-start
  0.0 0.7 multiply_bitcast_fusion
  0.7 0.2 copy-done
  0.9 0.9 fusion.39
  1.8 0.0 copy-start.2
  1.8 3.4 %fusion.28 = bf16[1024,2048]{1,0:T(8,128)(2,1)S(1)} fusion(bf16[1,1024,2048]{2,1,0:T(8,128)(2,1)} %param.5, f32[2048]{0:T(1024)S(1)} %bitcast.12), kind=kLoop, calls=%fused_computation.32 | loop fusion | flops 6291456 | bytes 8396800 | tf_op jit(solution)/shard_map/convert_element_type | solution.py:85
  5.3 1.2 copy-done.2
  6.5 4.8 %multiply_convert_fusion.6 = bf16[512,2048]{1,0:T(8,128)(2,1)S(1)} fusion(bf16[2048,2048]{1,0:T(8,128)(2,1)S(1)} %copy-done.2, f32[2048]{0:T(1024)S(1)} %bitcast.13, bf16[1024,2048]{1,0:T(8,128)(2,1)S(1)} %fusion.28), kind=kOutput, calls=%fused_computation.44 | convolution fusion | flops 4309647360 | bytes 12591104 | tf_op jit(solution)/shard_map/dot_general | solution.py:89
  11.3 2.7 collective-permute-start.2
  14.0 0.5 collective-permute-start
  14.5 5.8 %multiply_convert_fusion.5 = bf16[512,2048]{1,0:T(8,128)(2,1)} fusion(bf16[2048,2048]{1,0:T(8,128)(2,1)S(1)} %copy-done.2, f32[2048]{0:T(1024)S(1)} %bitcast.14, bf16[1024,2048]{1,0:T(8,128)(2,1)S(1)} %fusion.28), kind=kOutput, calls=%fused_computation.43 | convolution fusion | flops 4309647360 | bytes 12591104 | tf_op jit(solution)/shard_map/dot_general | solution.py:89
  20.2 1.7 collective-permute-start.3
  22.0 0.0 collective-permute-start.1
  22.0 44.6 %collective-permute-done.2 = bf16[512,2048]{1,0:T(8,128)(2,1)} collective-permute-done((bf16[512,2048]{1,0:T(8,128)(2,1)S(1)}, bf16[512,2048]{1,0:T(8,128)(2,1)}, u32[]{:S(2)}, u32[]{:S(2)}) %collective-permute-start.2) | collective-permute-done | bytes 2097184 | tf_op jit(solution)/shard_map/ppermute | solution.py:22
  66.6 0.0 collective-permute-done
  66.6 51.9 %collective-permute-done.3 = bf16[512,2048]{1,0:T(8,128)(2,1)} collective-permute-done((bf16[512,2048]{1,0:T(8,128)(2,1)}, bf16[512,2048]{1,0:T(8,128)(2,1)}, u32[]{:S(2)}, u32[]{:S(2)}) %collective-permute-start.3) | collective-permute-done | bytes 2097184 | tf_op jit(solution)/shard_map/ppermute | solution.py:22
  118.5 0.0 collective-permute-done.1
  118.5 12.6 %multiply_convert_fusion.2 = bf16[1024,2048]{1,0:T(8,128)(2,1)S(1)} fusion(bf16[512,2048]{1,0:T(8,128)(2,1)} %collective-permute-done.3, bf16[512,2048]{1,0:T(8,128)(2,1)} %collective-permute-done.2, bf16[512,2048]{1,0:T(8,128)(2,1)} %collective-permute-done.1, bf16[512,2048]{1,0:T(8,128)(2,1)} %collective-permute-done, pred[]{:T(512)S(6)} %eq.17, ...), kind=kOutput, calls=%fused_computation.34 | convolution fusion | flops 8673820672 | bytes 16777216 | tf_op jit(solution)/shard_map/dot_general | solution.py:66
  131.1 0.0 copy-start.1
  131.1 4.2 %collective-permute-start.6 = (bf16[1024,2048]{1,0:T(8,128)(2,1)S(1)}, bf16[1024,2048]{1,0:T(8,128)(2,1)S(1)}, u32[]{:S(2)}, u32[]{:S(2)}) collective-permute-start(bf16[1024,2048]{1,0:T(8,128)(2,1)S(1)} %multiply_convert_fusion.2), channel_id=1, source_target_pairs={{0,5},{1,4},{2,7},{3,6},{8,13},{9,12},{10,15},{11,14},{16,21},{17,... | collective-permute-start | bytes 12582920 | tf_op jit(solution)/shard_map/ppermute | solution.py:22
  135.3 0.1 collective-permute-start.4
  135.4 0.2 slice.46
  135.5 0.8 collective-permute-start.7
  136.3 0.2 slice.48
  136.4 0.8 collective-permute-start.9
  137.2 0.1 slice.44
  137.3 1.3 collective-permute-start.5
  138.6 0.0 collective-permute-done.7
  138.6 1.3 collective-permute-start.8
  139.9 0.0 collective-permute-done.9
  139.9 1.5 collective-permute-start.10
  141.4 66.2 %collective-permute-done.5 = bf16[304,2048]{1,0:T(8,128)(2,1)S(1)} collective-permute-done((bf16[304,2048]{1,0:T(8,128)(2,1)S(1)}, bf16[304,2048]{1,0:T(8,128)(2,1)S(1)}, u32[]{:S(2)}, u32[]{:S(2)}) %collective-permute-start.5) | collective-permute-done | bytes 1245216 | tf_op jit(solution)/shard_map/ppermute | solution.py:22
  207.6 1.2 collective-permute-done.6
  208.8 1.3 slice_add_fusion.2
  210.0 0.0 copy-done.1
  210.0 8.7 %collective-permute-done.8 = bf16[352,2048]{1,0:T(8,128)(2,1)S(1)} collective-permute-done((bf16[352,2048]{1,0:T(8,128)(2,1)S(1)}, bf16[352,2048]{1,0:T(8,128)(2,1)S(1)}, u32[]{:S(2)}, u32[]{:S(2)}) %collective-permute-start.8) | collective-permute-done | bytes 1441824 | tf_op jit(solution)/shard_map/ppermute | solution.py:22
  218.8 0.1 slice_add_fusion.1
  218.9 60.1 %collective-permute-done.10 = bf16[368,2048]{1,0:T(8,128)(2,1)S(1)} collective-permute-done((bf16[368,2048]{1,0:T(8,128)(2,1)S(1)}, bf16[368,2048]{1,0:T(8,128)(2,1)S(1)}, u32[]{:S(2)}, u32[]{:S(2)}) %collective-permute-start.10) | collective-permute-done | bytes 1507360 | tf_op jit(solution)/shard_map/ppermute | solution.py:22
  279.1 0.2 slice_add_fusion
  279.2 0.0 collective-permute-done.4
  279.2 13.6 %fusion.33 = bf16[1,1024,2048]{2,1,0:T(8,128)(2,1)} fusion(bf16[1024,2048]{1,0:T(8,128)(2,1)} %copy-done.1, bf16[368,2048]{1,0:T(8,128)(2,1)S(1)} %slice_add_fusion, bf16[352,2048]{1,0:T(8,128)(2,1)S(1)} %slice_add_fusion.1, bf16[304,2048]{1,0:T(8,128)(2,1)} %slice_add_fusion.2, bf16[1024,2048]{1,0:T(8,128)(2,1)} %collective-permute-done.4, pred[]{:T(512)S(6)} %eq.17), kind=kOutput, calls=%fused_computation.39 | convolution fusion | flops 8665432064 | bytes 16777216 | tf_op jit(solution)/shard_map/dot_general | solution.py:66
  (1 shorter events, 0.0 us)
Async XLA Ops:
  0.0 0.9 copy-start
  1.8 4.6 %copy-start.2 = (bf16[2048,2048]{1,0:T(8,128)(2,1)S(1)}, bf16[2048,2048]{1,0:T(8,128)(2,1)}, u32[]{:S(2)}) copy-start(bf16[2048,2048]{1,0:T(8,128)(2,1)} %param.6) | copy-start | bytes 25165828
  11.3 55.3 %collective-permute-start.2 = (bf16[512,2048]{1,0:T(8,128)(2,1)S(1)}, bf16[512,2048]{1,0:T(8,128)(2,1)}, u32[]{:S(2)}, u32[]{:S(2)}) collective-permute-start(bf16[512,2048]{1,0:T(8,128)(2,1)S(1)} %multiply_convert_fusion.6), channel_id=1, source_target_pairs={{0,3},{1,2},{2,5},{3,4},{4,7},{5,6},{6,9},{7,8},{8,11},{9,10},{10,... | collective-permute-start | bytes 6291464 | tf_op jit(solution)/shard_map/ppermute | solution.py:22
  14.0 52.6 %collective-permute-start = (bf16[512,2048]{1,0:T(8,128)(2,1)S(1)}, bf16[512,2048]{1,0:T(8,128)(2,1)}, u32[]{:S(2)}, u32[]{:S(2)}) collective-permute-start(bf16[512,2048]{1,0:T(8,128)(2,1)S(1)} %multiply_convert_fusion.6), channel_id=1, source_target_pairs={{0,2},{1,3},{2,4},{3,5},{4,6},{5,7},{6,8},{7,9},{8,10},{9,11},{10,... | collective-permute-start | bytes 6291464 | tf_op jit(solution)/shard_map/ppermute | solution.py:22
  20.2 98.2 %collective-permute-start.3 = (bf16[512,2048]{1,0:T(8,128)(2,1)}, bf16[512,2048]{1,0:T(8,128)(2,1)}, u32[]{:S(2)}, u32[]{:S(2)}) collective-permute-start(bf16[512,2048]{1,0:T(8,128)(2,1)} %multiply_convert_fusion.5), channel_id=1, source_target_pairs={{0,3},{1,2},{2,5},{3,4},{4,7},{5,6},{6,9},{7,8},{8,11},{9,10},{10,... | collective-permute-start | bytes 6291464 | tf_op jit(solution)/shard_map/ppermute | solution.py:22
  22.0 96.5 %collective-permute-start.1 = (bf16[512,2048]{1,0:T(8,128)(2,1)}, bf16[512,2048]{1,0:T(8,128)(2,1)}, u32[]{:S(2)}, u32[]{:S(2)}) collective-permute-start(bf16[512,2048]{1,0:T(8,128)(2,1)} %multiply_convert_fusion.5), channel_id=1, source_target_pairs={{0,2},{1,3},{2,4},{3,5},{4,6},{5,7},{6,8},{7,9},{8,10},{9,11},{10,... | collective-permute-start | bytes 6291464 | tf_op jit(solution)/shard_map/ppermute | solution.py:22
  131.1 79.0 %copy-start.1 = (bf16[1024,2048]{1,0:T(8,128)(2,1)}, bf16[1024,2048]{1,0:T(8,128)(2,1)S(1)}, u32[]{:S(2)}) copy-start(bf16[1024,2048]{1,0:T(8,128)(2,1)S(1)} %multiply_convert_fusion.2) | copy-start | bytes 12582916
  131.1 77.7 %collective-permute-start.6 = (bf16[1024,2048]{1,0:T(8,128)(2,1)S(1)}, bf16[1024,2048]{1,0:T(8,128)(2,1)S(1)}, u32[]{:S(2)}, u32[]{:S(2)}) collective-permute-start(bf16[1024,2048]{1,0:T(8,128)(2,1)S(1)} %multiply_convert_fusion.2), channel_id=1, source_target_pairs={{0,5},{1,4},{2,7},{3,6},{8,13},{9,12},{10,15},{11,14},{16,21},{17,... | collective-permute-start | bytes 12582920 | tf_op jit(solution)/shard_map/ppermute | solution.py:22
  135.3 144.0 %collective-permute-start.4 = (bf16[1024,2048]{1,0:T(8,128)(2,1)S(1)}, bf16[1024,2048]{1,0:T(8,128)(2,1)}, u32[]{:S(2)}, u32[]{:S(2)}) collective-permute-start(bf16[1024,2048]{1,0:T(8,128)(2,1)S(1)} %multiply_convert_fusion.2), channel_id=1, source_target_pairs={{0,4},{1,5},{2,6},{3,7},{4,8},{5,9},{6,10},{7,11},{8,12},{9,13},{1... | collective-permute-start | bytes 12582920 | tf_op jit(solution)/shard_map/ppermute | solution.py:22
  135.5 3.1 %collective-permute-start.7 = (bf16[352,2048]{1,0:T(8,128)(2,1)S(1)}, bf16[352,2048]{1,0:T(8,128)(2,1)S(1)}, u32[]{:S(2)}, u32[]{:S(2)}) collective-permute-start(bf16[352,2048]{1,0:T(8,128)(2,1)S(1)} %slice.46), channel_id=1, source_target_pairs={{4,12},{5,13},{6,14},{7,15},{12,20},{13,21},{14,22},{15,23},{20,28... | collective-permute-start | bytes 4325384 | tf_op jit(solution)/shard_map/ppermute | solution.py:22
  136.4 3.5 %collective-permute-start.9 = (bf16[368,2048]{1,0:T(8,128)(2,1)S(1)}, bf16[368,2048]{1,0:T(8,128)(2,1)S(1)}, u32[]{:S(2)}, u32[]{:S(2)}) collective-permute-start(bf16[368,2048]{1,0:T(8,128)(2,1)S(1)} %slice.48), channel_id=1, source_target_pairs={{4,12},{5,13},{6,14},{7,15},{12,20},{13,21},{14,22},{15,23},{20,28... | collective-permute-start | bytes 4521992 | tf_op jit(solution)/shard_map/ppermute | solution.py:22
  137.3 70.3 %collective-permute-start.5 = (bf16[304,2048]{1,0:T(8,128)(2,1)S(1)}, bf16[304,2048]{1,0:T(8,128)(2,1)S(1)}, u32[]{:S(2)}, u32[]{:S(2)}) collective-permute-start(bf16[304,2048]{1,0:T(8,128)(2,1)S(1)} %slice.44), channel_id=1, source_target_pairs={{4,9},{5,8},{6,11},{7,10},{12,17},{13,16},{14,19},{15,18},{20,25},... | collective-permute-start | bytes 3735560 | tf_op jit(solution)/shard_map/ppermute | solution.py:22
  138.6 80.2 %collective-permute-start.8 = (bf16[352,2048]{1,0:T(8,128)(2,1)S(1)}, bf16[352,2048]{1,0:T(8,128)(2,1)S(1)}, u32[]{:S(2)}, u32[]{:S(2)}) collective-permute-start(bf16[352,2048]{1,0:T(8,128)(2,1)S(1)} %collective-permute-done.7), channel_id=1, source_target_pairs={{4,33},{5,32},{6,35},{7,34},{12,9},{13,8},{14,11},{15,10},{20,17},... | collective-permute-start | bytes 4325384 | tf_op jit(solution)/shard_map/ppermute | solution.py:22
  139.9 139.1 %collective-permute-start.10 = (bf16[368,2048]{1,0:T(8,128)(2,1)S(1)}, bf16[368,2048]{1,0:T(8,128)(2,1)S(1)}, u32[]{:S(2)}, u32[]{:S(2)}) collective-permute-start(bf16[368,2048]{1,0:T(8,128)(2,1)S(1)} %collective-permute-done.9), channel_id=1, source_target_pairs={{4,33},{5,32},{6,35},{7,34},{12,9},{13,8},{14,11},{15,10},{20,17},... | collective-permute-start | bytes 4521992 | tf_op jit(solution)/shard_map/ppermute | solution.py:22

commit v23 on v22

--- a/solution.py
+++ b/solution.py
@@ -7,7 +7,7 @@
 
 LEVELS = 2
 DIRECT_ROWS = 304
-RELAY_ROWS = (352, 368)
+RELAY_ROWS = (320, 400)
 
 
 def sent(value, route):

time: 293 us -> 324 us (1.11)
  waiting for transfers between devices: 233 us -> 264 us
    ppermute x11, waiting for transfers between devices: 233 us -> 264 us  [sent(): return lax.ppermute(value, ('tm', 'row'), pairs)]
  transfers between devices with their start and end apart: 11 -> 11, of which waited for: 6 -> 6; matrix products, arithmetic and copies ran while one was open for 3% -> 2% of each run, Pallas kernels for 0% -> 0%
where the time goes in v23:
time: 324 us
  waiting for transfers between devices  264 us (81%)
  matrix products  37.6 us (12%)
  starting transfers between devices  14.8 us (5%)
  other arithmetic  5.76 us (2%)
    ppermute x11, waiting for transfers between devices, sent(): return lax.ppermute(value, ('tm', 'row'), pairs)  264 us
    dot_general x2, matrix products, level_product(): total = jnp.dot(later, earlier, preferred_element_type=jnp.float32)  26.2 us
    ppermute x11, starting transfers between devices, sent(): return lax.ppermute(value, ('tm', 'row'), pairs)  14.8 us
    dot_general x2, matrix products, shards(): jnp.dot(left_factor[c * chunk_rows:(c + 1) * chunk_rows], right_factor, p...  10.6 us
  transfers between devices with their start and end apart: 11, of which 6 were waited for; matrix products, arithmetic and copies ran while one was open for 2% of the time, Pallas kernels for 0%

profile of v23, /device:TPU:96, one launch (start us, length us, event | category | flops | bytes accessed | tf_op | source)
XLA Modules:
  0.0 323.7 jit_solution(2093435712302913597)
XLA Ops:
  0.0 0.0 copy-start
  0.0 0.7 multiply_bitcast_fusion
  0.7 0.2 copy-done
  0.9 0.9 fusion.39
  1.8 0.0 copy-start.2
  1.8 3.4 %fusion.28 = bf16[1024,2048]{1,0:T(8,128)(2,1)S(1)} fusion(bf16[1,1024,2048]{2,1,0:T(8,128)(2,1)} %param.5, f32[2048]{0:T(1024)S(1)} %bitcast.12), kind=kLoop, calls=%fused_computation.32 | loop fusion | flops 6291456 | bytes 8396800 | tf_op jit(solution)/shard_map/convert_element_type | solution.py:85
  5.3 1.2 copy-done.2
  6.5 4.8 %multiply_convert_fusion.6 = bf16[512,2048]{1,0:T(8,128)(2,1)S(1)} fusion(bf16[2048,2048]{1,0:T(8,128)(2,1)S(1)} %copy-done.2, f32[2048]{0:T(1024)S(1)} %bitcast.13, bf16[1024,2048]{1,0:T(8,128)(2,1)S(1)} %fusion.28), kind=kOutput, calls=%fused_computation.44 | convolution fusion | flops 4309647360 | bytes 12591104 | tf_op jit(solution)/shard_map/dot_general | solution.py:89
  11.3 2.7 collective-permute-start.2
  14.0 0.5 collective-permute-start
  14.5 5.8 %multiply_convert_fusion.5 = bf16[512,2048]{1,0:T(8,128)(2,1)} fusion(bf16[2048,2048]{1,0:T(8,128)(2,1)S(1)} %copy-done.2, f32[2048]{0:T(1024)S(1)} %bitcast.14, bf16[1024,2048]{1,0:T(8,128)(2,1)S(1)} %fusion.28), kind=kOutput, calls=%fused_computation.43 | convolution fusion | flops 4309647360 | bytes 12591104 | tf_op jit(solution)/shard_map/dot_general | solution.py:89
  20.2 1.7 collective-permute-start.3
  22.0 0.0 collective-permute-start.1
  22.0 44.6 %collective-permute-done.2 = bf16[512,2048]{1,0:T(8,128)(2,1)} collective-permute-done((bf16[512,2048]{1,0:T(8,128)(2,1)S(1)}, bf16[512,2048]{1,0:T(8,128)(2,1)}, u32[]{:S(2)}, u32[]{:S(2)}) %collective-permute-start.2) | collective-permute-done | bytes 2097184 | tf_op jit(solution)/shard_map/ppermute | solution.py:22
  66.6 0.0 collective-permute-done
  66.6 51.9 %collective-permute-done.3 = bf16[512,2048]{1,0:T(8,128)(2,1)} collective-permute-done((bf16[512,2048]{1,0:T(8,128)(2,1)}, bf16[512,2048]{1,0:T(8,128)(2,1)}, u32[]{:S(2)}, u32[]{:S(2)}) %collective-permute-start.3) | collective-permute-done | bytes 2097184 | tf_op jit(solution)/shard_map/ppermute | solution.py:22
  118.5 0.0 collective-permute-done.1
  118.5 12.6 %multiply_convert_fusion.2 = bf16[1024,2048]{1,0:T(8,128)(2,1)S(1)} fusion(bf16[512,2048]{1,0:T(8,128)(2,1)} %collective-permute-done.3, bf16[512,2048]{1,0:T(8,128)(2,1)} %collective-permute-done.2, bf16[512,2048]{1,0:T(8,128)(2,1)} %collective-permute-done.1, bf16[512,2048]{1,0:T(8,128)(2,1)} %collective-permute-done, pred[]{:T(512)S(6)} %eq.17, ...), kind=kOutput, calls=%fused_computation.34 | convolution fusion | flops 8673820672 | bytes 16777216 | tf_op jit(solution)/shard_map/dot_general | solution.py:66
  131.1 0.0 copy-start.1
  131.1 4.2 %collective-permute-start.6 = (bf16[1024,2048]{1,0:T(8,128)(2,1)S(1)}, bf16[1024,2048]{1,0:T(8,128)(2,1)S(1)}, u32[]{:S(2)}, u32[]{:S(2)}) collective-permute-start(bf16[1024,2048]{1,0:T(8,128)(2,1)S(1)} %multiply_convert_fusion.2), channel_id=1, source_target_pairs={{0,5},{1,4},{2,7},{3,6},{8,13},{9,12},{10,15},{11,14},{16,21},{17,... | collective-permute-start | bytes 12582920 | tf_op jit(solution)/shard_map/ppermute | solution.py:22
  135.3 0.1 collective-permute-start.4
  135.4 0.1 slice.48
  135.5 0.8 collective-permute-start.9
  136.2 0.1 slice.46
  136.3 0.7 collective-permute-start.7
  137.1 0.1 slice.44
  137.2 1.3 collective-permute-start.5
  138.5 0.0 collective-permute-done.7
  138.5 1.3 collective-permute-start.8
  139.8 0.0 collective-permute-done.9
  139.8 1.5 collective-permute-start.10
  141.3 65.4 %collective-permute-done.5 = bf16[304,2048]{1,0:T(8,128)(2,1)S(1)} collective-permute-done((bf16[304,2048]{1,0:T(8,128)(2,1)S(1)}, bf16[304,2048]{1,0:T(8,128)(2,1)S(1)}, u32[]{:S(2)}, u32[]{:S(2)}) %collective-permute-start.5) | collective-permute-done | bytes 1245216 | tf_op jit(solution)/shard_map/ppermute | solution.py:22
  206.7 2.1 collective-permute-done.6
  208.8 1.3 slice_add_fusion.2
  210.0 0.0 copy-done.1
  210.0 70.1 %collective-permute-done.8 = bf16[320,2048]{1,0:T(8,128)(2,1)S(1)} collective-permute-done((bf16[320,2048]{1,0:T(8,128)(2,1)S(1)}, bf16[320,2048]{1,0:T(8,128)(2,1)S(1)}, u32[]{:S(2)}, u32[]{:S(2)}) %collective-permute-start.8) | collective-permute-done | bytes 1310752 | tf_op jit(solution)/shard_map/ppermute | solution.py:22
  280.1 0.2 slice_add_fusion.1
  280.3 29.6 %collective-permute-done.10 = bf16[400,2048]{1,0:T(8,128)(2,1)S(1)} collective-permute-done((bf16[400,2048]{1,0:T(8,128)(2,1)S(1)}, bf16[400,2048]{1,0:T(8,128)(2,1)S(1)}, u32[]{:S(2)}, u32[]{:S(2)}) %collective-permute-start.10) | collective-permute-done | bytes 1638432 | tf_op jit(solution)/shard_map/ppermute | solution.py:22
  309.9 0.2 slice_add_fusion
  310.1 0.0 collective-permute-done.4
  310.1 13.6 %fusion.33 = bf16[1,1024,2048]{2,1,0:T(8,128)(2,1)} fusion(bf16[1024,2048]{1,0:T(8,128)(2,1)} %copy-done.1, bf16[400,2048]{1,0:T(8,128)(2,1)S(1)} %slice_add_fusion, bf16[320,2048]{1,0:T(8,128)(2,1)S(1)} %slice_add_fusion.1, bf16[304,2048]{1,0:T(8,128)(2,1)} %slice_add_fusion.2, bf16[1024,2048]{1,0:T(8,128)(2,1)} %collective-permute-done.4, pred[]{:T(512)S(6)} %eq.17), kind=kOutput, calls=%fused_computation.39 | convolution fusion | flops 8665432064 | bytes 16777216 | tf_op jit(solution)/shard_map/dot_general | solution.py:66
  (1 shorter events, 0.0 us)
Async XLA Ops:
  0.0 0.9 copy-start
  1.8 4.6 %copy-start.2 = (bf16[2048,2048]{1,0:T(8,128)(2,1)S(1)}, bf16[2048,2048]{1,0:T(8,128)(2,1)}, u32[]{:S(2)}) copy-start(bf16[2048,2048]{1,0:T(8,128)(2,1)} %param.6) | copy-start | bytes 25165828
  11.3 55.3 %collective-permute-start.2 = (bf16[512,2048]{1,0:T(8,128)(2,1)S(1)}, bf16[512,2048]{1,0:T(8,128)(2,1)}, u32[]{:S(2)}, u32[]{:S(2)}) collective-permute-start(bf16[512,2048]{1,0:T(8,128)(2,1)S(1)} %multiply_convert_fusion.6), channel_id=1, source_target_pairs={{0,3},{1,2},{2,5},{3,4},{4,7},{5,6},{6,9},{7,8},{8,11},{9,10},{10,... | collective-permute-start | bytes 6291464 | tf_op jit(solution)/shard_map/ppermute | solution.py:22
  14.0 52.6 %collective-permute-start = (bf16[512,2048]{1,0:T(8,128)(2,1)S(1)}, bf16[512,2048]{1,0:T(8,128)(2,1)}, u32[]{:S(2)}, u32[]{:S(2)}) collective-permute-start(bf16[512,2048]{1,0:T(8,128)(2,1)S(1)} %multiply_convert_fusion.6), channel_id=1, source_target_pairs={{0,2},{1,3},{2,4},{3,5},{4,6},{5,7},{6,8},{7,9},{8,10},{9,11},{10,... | collective-permute-start | bytes 6291464 | tf_op jit(solution)/shard_map/ppermute | solution.py:22
  20.2 98.2 %collective-permute-start.3 = (bf16[512,2048]{1,0:T(8,128)(2,1)}, bf16[512,2048]{1,0:T(8,128)(2,1)}, u32[]{:S(2)}, u32[]{:S(2)}) collective-permute-start(bf16[512,2048]{1,0:T(8,128)(2,1)} %multiply_convert_fusion.5), channel_id=1, source_target_pairs={{0,3},{1,2},{2,5},{3,4},{4,7},{5,6},{6,9},{7,8},{8,11},{9,10},{10,... | collective-permute-start | bytes 6291464 | tf_op jit(solution)/shard_map/ppermute | solution.py:22
  22.0 96.5 %collective-permute-start.1 = (bf16[512,2048]{1,0:T(8,128)(2,1)}, bf16[512,2048]{1,0:T(8,128)(2,1)}, u32[]{:S(2)}, u32[]{:S(2)}) collective-permute-start(bf16[512,2048]{1,0:T(8,128)(2,1)} %multiply_convert_fusion.5), channel_id=1, source_target_pairs={{0,2},{1,3},{2,4},{3,5},{4,6},{5,7},{6,8},{7,9},{8,10},{9,11},{10,... | collective-permute-start | bytes 6291464 | tf_op jit(solution)/shard_map/ppermute | solution.py:22
  131.1 79.0 %copy-start.1 = (bf16[1024,2048]{1,0:T(8,128)(2,1)}, bf16[1024,2048]{1,0:T(8,128)(2,1)S(1)}, u32[]{:S(2)}) copy-start(bf16[1024,2048]{1,0:T(8,128)(2,1)S(1)} %multiply_convert_fusion.2) | copy-start | bytes 12582916
  131.1 77.7 %collective-permute-start.6 = (bf16[1024,2048]{1,0:T(8,128)(2,1)S(1)}, bf16[1024,2048]{1,0:T(8,128)(2,1)S(1)}, u32[]{:S(2)}, u32[]{:S(2)}) collective-permute-start(bf16[1024,2048]{1,0:T(8,128)(2,1)S(1)} %multiply_convert_fusion.2), channel_id=1, source_target_pairs={{0,5},{1,4},{2,7},{3,6},{8,13},{9,12},{10,15},{11,14},{16,21},{17,... | collective-permute-start | bytes 12582920 | tf_op jit(solution)/shard_map/ppermute | solution.py:22
  135.3 174.8 %collective-permute-start.4 = (bf16[1024,2048]{1,0:T(8,128)(2,1)S(1)}, bf16[1024,2048]{1,0:T(8,128)(2,1)}, u32[]{:S(2)}, u32[]{:S(2)}) collective-permute-start(bf16[1024,2048]{1,0:T(8,128)(2,1)S(1)} %multiply_convert_fusion.2), channel_id=1, source_target_pairs={{0,4},{1,5},{2,6},{3,7},{4,8},{5,9},{6,10},{7,11},{8,12},{9,13},{1... | collective-permute-start | bytes 12582920 | tf_op jit(solution)/shard_map/ppermute | solution.py:22
  135.5 4.3 %collective-permute-start.9 = (bf16[400,2048]{1,0:T(8,128)(2,1)S(1)}, bf16[400,2048]{1,0:T(8,128)(2,1)S(1)}, u32[]{:S(2)}, u32[]{:S(2)}) collective-permute-start(bf16[400,2048]{1,0:T(8,128)(2,1)S(1)} %slice.48), channel_id=1, source_target_pairs={{4,12},{5,13},{6,14},{7,15},{12,20},{13,21},{14,22},{15,23},{20,28... | collective-permute-start | bytes 4915208 | tf_op jit(solution)/shard_map/ppermute | solution.py:22
  136.3 2.1 collective-permute-start.7
  137.2 69.5 %collective-permute-start.5 = (bf16[304,2048]{1,0:T(8,128)(2,1)S(1)}, bf16[304,2048]{1,0:T(8,128)(2,1)S(1)}, u32[]{:S(2)}, u32[]{:S(2)}) collective-permute-start(bf16[304,2048]{1,0:T(8,128)(2,1)S(1)} %slice.44), channel_id=1, source_target_pairs={{4,9},{5,8},{6,11},{7,10},{12,17},{13,16},{14,19},{15,18},{20,25},... | collective-permute-start | bytes 3735560 | tf_op jit(solution)/shard_map/ppermute | solution.py:22
  138.5 141.6 %collective-permute-start.8 = (bf16[320,2048]{1,0:T(8,128)(2,1)S(1)}, bf16[320,2048]{1,0:T(8,128)(2,1)S(1)}, u32[]{:S(2)}, u32[]{:S(2)}) collective-permute-start(bf16[320,2048]{1,0:T(8,128)(2,1)S(1)} %collective-permute-done.7), channel_id=1, source_target_pairs={{4,33},{5,32},{6,35},{7,34},{12,9},{13,8},{14,11},{15,10},{20,17},... | collective-permute-start | bytes 3932168 | tf_op jit(solution)/shard_map/ppermute | solution.py:22
  139.8 170.1 %collective-permute-start.10 = (bf16[400,2048]{1,0:T(8,128)(2,1)S(1)}, bf16[400,2048]{1,0:T(8,128)(2,1)S(1)}, u32[]{:S(2)}, u32[]{:S(2)}) collective-permute-start(bf16[400,2048]{1,0:T(8,128)(2,1)S(1)} %collective-permute-done.9), channel_id=1, source_target_pairs={{4,33},{5,32},{6,35},{7,34},{12,9},{13,8},{14,11},{15,10},{20,17},... | collective-permute-start | bytes 4915208 | tf_op jit(solution)/shard_map/ppermute | solution.py:22

commit v24 on v23

--- a/solution.py
+++ b/solution.py
@@ -6,8 +6,8 @@
 from jax.sharding import PartitionSpec as P
 
 LEVELS = 2
-DIRECT_ROWS = 304
-RELAY_ROWS = (320, 400)
+DIRECT_ROWS = 288
+RELAY_ROWS = (368, 368)
 
 
 def sent(value, route):

time: 324 us -> 295 us (0.910)
  waiting for transfers between devices: 264 us -> 233 us
    ppermute x11, waiting for transfers between devices: 264 us -> 233 us  [sent(): return lax.ppermute(value, ('tm', 'row'), pairs)]
  transfers between devices with their start and end apart: 11 -> 11, of which waited for: 6 -> 6; matrix products, arithmetic and copies ran while one was open for 2% -> 3% of each run, Pallas kernels for 0% -> 0%
where the time goes in v24:
time: 295 us
  waiting for transfers between devices  233 us (79%)
  matrix products  37.5 us (13%)
  starting transfers between devices  14.8 us (5%)
  other arithmetic  5.71 us (2%)
  local copies, waits for them, and re-layouts  3.87 us (1%)
    ppermute x11, waiting for transfers between devices, sent(): return lax.ppermute(value, ('tm', 'row'), pairs)  233 us
    dot_general x2, matrix products, level_product(): total = jnp.dot(later, earlier, preferred_element_type=jnp.float32)  26.2 us
    ppermute x11, starting transfers between devices, sent(): return lax.ppermute(value, ('tm', 'row'), pairs)  14.8 us
    dot_general x2, matrix products, shards(): jnp.dot(left_factor[c * chunk_rows:(c + 1) * chunk_rows], right_factor, p...  10.5 us
  transfers between devices with their start and end apart: 11, of which 6 were waited for; matrix products, arithmetic and copies ran while one was open for 3% of the time, Pallas kernels for 0%

profile of v24, /device:TPU:96, one launch (start us, length us, event | category | flops | bytes accessed | tf_op | source)
XLA Modules:
  0.0 295.1 jit_solution(10675254289851912785)
XLA Ops:
  0.0 0.0 copy-start
  0.0 0.7 multiply_bitcast_fusion
  0.7 0.2 copy-done
  0.9 0.9 fusion.39
  1.8 0.0 copy-start.2
  1.8 3.4 %fusion.28 = bf16[1024,2048]{1,0:T(8,128)(2,1)S(1)} fusion(bf16[1,1024,2048]{2,1,0:T(8,128)(2,1)} %param.5, f32[2048]{0:T(1024)S(1)} %bitcast.12), kind=kLoop, calls=%fused_computation.32 | loop fusion | flops 6291456 | bytes 8396800 | tf_op jit(solution)/shard_map/convert_element_type | solution.py:85
  5.3 1.2 copy-done.2
  6.5 4.8 %multiply_convert_fusion.6 = bf16[512,2048]{1,0:T(8,128)(2,1)S(1)} fusion(bf16[2048,2048]{1,0:T(8,128)(2,1)S(1)} %copy-done.2, f32[2048]{0:T(1024)S(1)} %bitcast.13, bf16[1024,2048]{1,0:T(8,128)(2,1)S(1)} %fusion.28), kind=kOutput, calls=%fused_computation.44 | convolution fusion | flops 4309647360 | bytes 12591104 | tf_op jit(solution)/shard_map/dot_general | solution.py:89
  11.2 2.7 collective-permute-start.2
  13.9 0.5 collective-permute-start
  14.4 5.7 %multiply_convert_fusion.5 = bf16[512,2048]{1,0:T(8,128)(2,1)} fusion(bf16[2048,2048]{1,0:T(8,128)(2,1)S(1)} %copy-done.2, f32[2048]{0:T(1024)S(1)} %bitcast.14, bf16[1024,2048]{1,0:T(8,128)(2,1)S(1)} %fusion.28), kind=kOutput, calls=%fused_computation.43 | convolution fusion | flops 4309647360 | bytes 12591104 | tf_op jit(solution)/shard_map/dot_general | solution.py:89
  20.2 1.7 collective-permute-start.3
  21.9 0.0 collective-permute-start.1
  21.9 44.6 %collective-permute-done.2 = bf16[512,2048]{1,0:T(8,128)(2,1)} collective-permute-done((bf16[512,2048]{1,0:T(8,128)(2,1)S(1)}, bf16[512,2048]{1,0:T(8,128)(2,1)}, u32[]{:S(2)}, u32[]{:S(2)}) %collective-permute-start.2) | collective-permute-done | bytes 2097184 | tf_op jit(solution)/shard_map/ppermute | solution.py:22
  66.5 0.0 collective-permute-done
  66.5 51.9 %collective-permute-done.3 = bf16[512,2048]{1,0:T(8,128)(2,1)} collective-permute-done((bf16[512,2048]{1,0:T(8,128)(2,1)}, bf16[512,2048]{1,0:T(8,128)(2,1)}, u32[]{:S(2)}, u32[]{:S(2)}) %collective-permute-start.3) | collective-permute-done | bytes 2097184 | tf_op jit(solution)/shard_map/ppermute | solution.py:22
  118.4 0.0 collective-permute-done.1
  118.4 12.6 %multiply_convert_fusion.2 = bf16[1024,2048]{1,0:T(8,128)(2,1)S(1)} fusion(bf16[512,2048]{1,0:T(8,128)(2,1)} %collective-permute-done.3, bf16[512,2048]{1,0:T(8,128)(2,1)} %collective-permute-done.2, bf16[512,2048]{1,0:T(8,128)(2,1)} %collective-permute-done.1, bf16[512,2048]{1,0:T(8,128)(2,1)} %collective-permute-done, pred[]{:T(512)S(6)} %eq.17, ...), kind=kOutput, calls=%fused_computation.34 | convolution fusion | flops 8673820672 | bytes 16777216 | tf_op jit(solution)/shard_map/dot_general | solution.py:66
  131.0 0.0 copy-start.1
  131.0 4.2 %collective-permute-start.6 = (bf16[1024,2048]{1,0:T(8,128)(2,1)S(1)}, bf16[1024,2048]{1,0:T(8,128)(2,1)S(1)}, u32[]{:S(2)}, u32[]{:S(2)}) collective-permute-start(bf16[1024,2048]{1,0:T(8,128)(2,1)S(1)} %multiply_convert_fusion.2), channel_id=1, source_target_pairs={{0,5},{1,4},{2,7},{3,6},{8,13},{9,12},{10,15},{11,14},{16,21},{17,... | collective-permute-start | bytes 12582920 | tf_op jit(solution)/shard_map/ppermute | solution.py:22
  135.2 0.1 collective-permute-start.4
  135.3 0.3 fusion.47
  135.6 0.8 collective-permute-start.7
  136.4 0.8 collective-permute-start.9
  137.2 0.1 slice.44
  137.3 0.0 copy-done.1
  137.3 1.3 collective-permute-start.5
  138.6 0.0 collective-permute-done.7
  138.6 1.3 collective-permute-start.8
  139.9 0.0 collective-permute-done.9
  139.9 1.5 collective-permute-start.10
  141.4 63.9 %collective-permute-done.5 = bf16[288,2048]{1,0:T(8,128)(2,1)S(1)} collective-permute-done((bf16[288,2048]{1,0:T(8,128)(2,1)S(1)}, bf16[288,2048]{1,0:T(8,128)(2,1)S(1)}, u32[]{:S(2)}, u32[]{:S(2)}) %collective-permute-start.5) | collective-permute-done | bytes 1179680 | tf_op jit(solution)/shard_map/ppermute | solution.py:22
  205.3 3.4 %collective-permute-done.6 = bf16[1024,2048]{1,0:T(8,128)(2,1)S(1)} collective-permute-done((bf16[1024,2048]{1,0:T(8,128)(2,1)S(1)}, bf16[1024,2048]{1,0:T(8,128)(2,1)S(1)}, u32[]{:S(2)}, u32[]{:S(2)}) %collective-permute-start.6) | collective-permute-done | bytes 4194336 | tf_op jit(solution)/shard_map/ppermute | solution.py:22
  208.7 1.3 slice_add_fusion.2
  210.0 11.6 %collective-permute-done.8 = bf16[368,2048]{1,0:T(8,128)(2,1)S(1)} collective-permute-done((bf16[368,2048]{1,0:T(8,128)(2,1)S(1)}, bf16[368,2048]{1,0:T(8,128)(2,1)S(1)}, u32[]{:S(2)}, u32[]{:S(2)}) %collective-permute-start.8) | collective-permute-done | bytes 1507360 | tf_op jit(solution)/shard_map/ppermute | solution.py:22
  221.6 57.6 %collective-permute-done.10 = bf16[368,2048]{1,0:T(8,128)(2,1)S(1)} collective-permute-done((bf16[368,2048]{1,0:T(8,128)(2,1)S(1)}, bf16[368,2048]{1,0:T(8,128)(2,1)S(1)}, u32[]{:S(2)}, u32[]{:S(2)}) %collective-permute-start.10) | collective-permute-done | bytes 1507360 | tf_op jit(solution)/shard_map/ppermute | solution.py:22
  279.2 0.3 slice_add_fusion.1
  279.5 0.0 collective-permute-done.4
  279.5 0.0 copy-start.3
  279.5 2.0 copy-done.3
  281.5 13.6 %fusion.33 = bf16[1,1024,2048]{2,1,0:T(8,128)(2,1)} fusion(bf16[1024,2048]{1,0:T(8,128)(2,1)} %copy-done.1, bf16[368,2048]{1,0:T(8,128)(2,1)S(1)} %get-tuple-element.6, bf16[368,2048]{1,0:T(8,128)(2,1)S(1)} %get-tuple-element.5, bf16[288,2048]{1,0:T(8,128)(2,1)} %slice_add_fusion.2, bf16[1024,2048]{1,0:T(8,128)(2,1)} %copy-done.3, pred[]{:T(512)S(6)} %eq.17), kind=kOutput, calls=%fused_computation.39 | convolution fusion | flops 8665432064 | bytes 16777216 | tf_op jit(solution)/shard_map/dot_general | solution.py:66
  (1 shorter events, 0.0 us)
Async XLA Ops:
  0.0 0.9 copy-start
  1.8 4.6 %copy-start.2 = (bf16[2048,2048]{1,0:T(8,128)(2,1)S(1)}, bf16[2048,2048]{1,0:T(8,128)(2,1)}, u32[]{:S(2)}) copy-start(bf16[2048,2048]{1,0:T(8,128)(2,1)} %param.6) | copy-start | bytes 25165828
  11.2 55.3 %collective-permute-start.2 = (bf16[512,2048]{1,0:T(8,128)(2,1)S(1)}, bf16[512,2048]{1,0:T(8,128)(2,1)}, u32[]{:S(2)}, u32[]{:S(2)}) collective-permute-start(bf16[512,2048]{1,0:T(8,128)(2,1)S(1)} %multiply_convert_fusion.6), channel_id=1, source_target_pairs={{0,3},{1,2},{2,5},{3,4},{4,7},{5,6},{6,9},{7,8},{8,11},{9,10},{10,... | collective-permute-start | bytes 6291464 | tf_op jit(solution)/shard_map/ppermute | solution.py:22
  13.9 52.6 %collective-permute-start = (bf16[512,2048]{1,0:T(8,128)(2,1)S(1)}, bf16[512,2048]{1,0:T(8,128)(2,1)}, u32[]{:S(2)}, u32[]{:S(2)}) collective-permute-start(bf16[512,2048]{1,0:T(8,128)(2,1)S(1)} %multiply_convert_fusion.6), channel_id=1, source_target_pairs={{0,2},{1,3},{2,4},{3,5},{4,6},{5,7},{6,8},{7,9},{8,10},{9,11},{10,... | collective-permute-start | bytes 6291464 | tf_op jit(solution)/shard_map/ppermute | solution.py:22
  20.2 98.3 %collective-permute-start.3 = (bf16[512,2048]{1,0:T(8,128)(2,1)}, bf16[512,2048]{1,0:T(8,128)(2,1)}, u32[]{:S(2)}, u32[]{:S(2)}) collective-permute-start(bf16[512,2048]{1,0:T(8,128)(2,1)} %multiply_convert_fusion.5), channel_id=1, source_target_pairs={{0,3},{1,2},{2,5},{3,4},{4,7},{5,6},{6,9},{7,8},{8,11},{9,10},{10,... | collective-permute-start | bytes 6291464 | tf_op jit(solution)/shard_map/ppermute | solution.py:22
  21.9 96.6 %collective-permute-start.1 = (bf16[512,2048]{1,0:T(8,128)(2,1)}, bf16[512,2048]{1,0:T(8,128)(2,1)}, u32[]{:S(2)}, u32[]{:S(2)}) collective-permute-start(bf16[512,2048]{1,0:T(8,128)(2,1)} %multiply_convert_fusion.5), channel_id=1, source_target_pairs={{0,2},{1,3},{2,4},{3,5},{4,6},{5,7},{6,8},{7,9},{8,10},{9,11},{10,... | collective-permute-start | bytes 6291464 | tf_op jit(solution)/shard_map/ppermute | solution.py:22
  131.0 6.3 %copy-start.1 = (bf16[1024,2048]{1,0:T(8,128)(2,1)}, bf16[1024,2048]{1,0:T(8,128)(2,1)S(1)}, u32[]{:S(2)}) copy-start(bf16[1024,2048]{1,0:T(8,128)(2,1)S(1)} %multiply_convert_fusion.2) | copy-start | bytes 12582916
  131.0 77.7 %collective-permute-start.6 = (bf16[1024,2048]{1,0:T(8,128)(2,1)S(1)}, bf16[1024,2048]{1,0:T(8,128)(2,1)S(1)}, u32[]{:S(2)}, u32[]{:S(2)}) collective-permute-start(bf16[1024,2048]{1,0:T(8,128)(2,1)S(1)} %multiply_convert_fusion.2), channel_id=1, source_target_pairs={{0,5},{1,4},{2,7},{3,6},{8,13},{9,12},{10,15},{11,14},{16,21},{17,... | collective-permute-start | bytes 12582920 | tf_op jit(solution)/shard_map/ppermute | solution.py:22
  135.2 144.3 %collective-permute-start.4 = (bf16[1024,2048]{1,0:T(8,128)(2,1)S(1)}, bf16[1024,2048]{1,0:T(8,128)(2,1)S(1)}, u32[]{:S(2)}, u32[]{:S(2)}) collective-permute-start(bf16[1024,2048]{1,0:T(8,128)(2,1)S(1)} %multiply_convert_fusion.2), channel_id=1, source_target_pairs={{0,4},{1,5},{2,6},{3,7},{4,8},{5,9},{6,10},{7,11},{8,12},{9,13},{1... | collective-permute-start | bytes 12582920 | tf_op jit(solution)/shard_map/ppermute | solution.py:22
  135.6 3.0 %collective-permute-start.7 = (bf16[368,2048]{1,0:T(8,128)(2,1)S(1)}, bf16[368,2048]{1,0:T(8,128)(2,1)S(1)}, u32[]{:S(2)}, u32[]{:S(2)}) collective-permute-start(bf16[368,2048]{1,0:T(8,128)(2,1)S(1)} %get-tuple-element.7), channel_id=1, source_target_pairs={{4,12},{5,13},{6,14},{7,15},{12,20},{13,21},{14,22},{15,23},{20,28... | collective-permute-start | bytes 4521992 | tf_op jit(solution)/shard_map/ppermute | solution.py:22
  136.4 3.5 %collective-permute-start.9 = (bf16[368,2048]{1,0:T(8,128)(2,1)S(1)}, bf16[368,2048]{1,0:T(8,128)(2,1)S(1)}, u32[]{:S(2)}, u32[]{:S(2)}) collective-permute-start(bf16[368,2048]{1,0:T(8,128)(2,1)S(1)} %get-tuple-element.8), channel_id=1, source_target_pairs={{4,12},{5,13},{6,14},{7,15},{12,20},{13,21},{14,22},{15,23},{20,28... | collective-permute-start | bytes 4521992 | tf_op jit(solution)/shard_map/ppermute | solution.py:22
  137.3 68.0 %collective-permute-start.5 = (bf16[288,2048]{1,0:T(8,128)(2,1)S(1)}, bf16[288,2048]{1,0:T(8,128)(2,1)S(1)}, u32[]{:S(2)}, u32[]{:S(2)}) collective-permute-start(bf16[288,2048]{1,0:T(8,128)(2,1)S(1)} %slice.44), channel_id=1, source_target_pairs={{4,9},{5,8},{6,11},{7,10},{12,17},{13,16},{14,19},{15,18},{20,25},... | collective-permute-start | bytes 3538952 | tf_op jit(solution)/shard_map/ppermute | solution.py:22
  138.6 83.0 %collective-permute-start.8 = (bf16[368,2048]{1,0:T(8,128)(2,1)S(1)}, bf16[368,2048]{1,0:T(8,128)(2,1)S(1)}, u32[]{:S(2)}, u32[]{:S(2)}) collective-permute-start(bf16[368,2048]{1,0:T(8,128)(2,1)S(1)} %collective-permute-done.7), channel_id=1, source_target_pairs={{4,33},{5,32},{6,35},{7,34},{12,9},{13,8},{14,11},{15,10},{20,17},... | collective-permute-start | bytes 4521992 | tf_op jit(solution)/shard_map/ppermute | solution.py:22
  139.9 139.3 %collective-permute-start.10 = (bf16[368,2048]{1,0:T(8,128)(2,1)S(1)}, bf16[368,2048]{1,0:T(8,128)(2,1)S(1)}, u32[]{:S(2)}, u32[]{:S(2)}) collective-permute-start(bf16[368,2048]{1,0:T(8,128)(2,1)S(1)} %collective-permute-done.9), channel_id=1, source_target_pairs={{4,33},{5,32},{6,35},{7,34},{12,9},{13,8},{14,11},{15,10},{20,17},... | collective-permute-start | bytes 4521992 | tf_op jit(solution)/shard_map/ppermute | solution.py:22
  279.5 2.0 copy-start.3
